TPU v7x, 256 devices: a whole 4x4x8 slice. The times are simulated.
256 devices in a mesh: gx: 32 (over z_lo, y, core), gy: 4 (over x), gz: 2 (over z_hi).
Axes of the slice: x: 4, y: 4, z: 8 (z_hi: 2, z_lo: 4; z = z_hi * 4 + z_lo), core: 2. Of those that a mesh axis runs over, the one named last changes fastest.
Arguments:
- f_pop: float32 [19, 128, 64, 256], P(None, 'gx', 'gy', 'gz'), may hold values from 0.02 to 0.1
- g_pop: float32 [19, 128, 64, 256], P(None, 'gx', 'gy', 'gz'), may hold values from -0.2 to 0.2
- displacement: int32 [1], replicated, may hold values from 33 to 47
Outputs:
- f_new: float32 [19, 128, 64, 256], P(None, 'gx', 'gy', 'gz')
- g_new: float32 [19, 128, 64, 256], P(None, 'gx', 'gy', 'gz')
All inputs are finite; a program needn't handle non-finite values.
Results may differ from a plain program's by a relative error of at most 0.0001.
Values sent between devices are 32-bit elements; how exact they have to be, the bound alone decides.
No kernel may reach another device: no remote copies, remote signals or barrier semaphores. Data moves between devices by JAX's collectives and lax.ppermute only.
A program may use at most 64 MiB of HBM per device.

v0:
```python
import jax
import jax.numpy as jnp
from jax import lax
from jax.sharding import PartitionSpec as P

VELOCITIES = [
    (0, 0, 0),
    (1, 0, 0),
    (1, 1, 0),
    (1, -1, 0),
    (1, 0, 1),
    (1, 0, -1),
    (-1, 0, 0),
    (-1, -1, 0),
    (-1, 1, 0),
    (-1, 0, -1),
    (-1, 0, 1),
    (0, 1, 0),
    (0, -1, 0),
    (0, 0, 1),
    (0, 0, -1),
    (0, 1, 1),
    (0, -1, -1),
    (0, 1, -1),
    (0, -1, 1),
]
BULK_COEF = 0.5
STIFFNESS = 0.5
TAU_FLUID = 0.8
TAU_ORDER = 0.9


def with_halo(cells, sides, width):
    for axis, dim in sides:
        count = lax.axis_size(axis)
        head = lax.slice_in_dim(cells, 0, width, axis=dim)
        tail = lax.slice_in_dim(cells, cells.shape[dim] - width, cells.shape[dim], axis=dim)
        cells = jnp.concatenate(
            [
                lax.ppermute(tail, axis, [(i, (i + 1) % count) for i in range(count)]),
                cells,
                lax.ppermute(head, axis, [((i + 1) % count, i) for i in range(count)]),
            ],
            axis=dim,
        )
    return cells


def lattice_weight(number):
    steps_sq = sum((abs(comp) for comp in VELOCITIES[number]))
    if steps_sq == 0:
        return 1.0 / 3.0
    if steps_sq == 1:
        return 1.0 / 18.0
    return 1.0 / 36.0


def along(number, values, base):
    result = jnp.zeros_like(base)
    for axis_id in range(3):
        comp = VELOCITIES[number][axis_id]
        if comp != 0:
            result = result + comp * values[axis_id]
    return result


def collide(f_pop, g_pop, order_field, laplace, slopes):
    density = jnp.sum(f_pop, axis=0)
    chemical = (
        BULK_COEF * (order_field * order_field * order_field - order_field) - STIFFNESS * laplace
    )
    forces = [chemical * slope for slope in slopes]
    moments = []
    for axis_id in range(3):
        moment = jnp.zeros_like(density)
        for number in range(19):
            comp = VELOCITIES[number][axis_id]
            if comp != 0:
                moment = moment + comp * f_pop[number]
        moments.append(moment)
    flows = [(moments[axis_id] + 0.5 * forces[axis_id]) / density for axis_id in range(3)]
    speed_sq = flows[0] * flows[0] + flows[1] * flows[1] + flows[2] * flows[2]
    flow_force = flows[0] * forces[0] + flows[1] * forces[1] + flows[2] * forces[2]
    f_posts = []
    g_eqs = []
    for number in range(19):
        weight = lattice_weight(number)
        proj_flow = along(number, flows, density)
        proj_force = along(number, forces, density)
        shape_term = 3.0 * proj_flow + 4.5 * proj_flow * proj_flow - 1.5 * speed_sq
        f_eq = weight * density * (1.0 + shape_term)
        source = (
            (1.0 - 0.5 / TAU_FLUID)
            * weight
            * (3.0 * (proj_force - flow_force) + 9.0 * proj_flow * proj_force)
        )
        f_posts.append(f_pop[number] - (f_pop[number] - f_eq) / TAU_FLUID + source)
        g_eqs.append(weight * (3.0 * chemical + order_field * shape_term))
    rest_eq = order_field
    for number in range(1, 19):
        rest_eq = rest_eq - g_eqs[number]
    g_eqs[0] = rest_eq
    g_posts = [g_pop[number] - (g_pop[number] - g_eqs[number]) / TAU_ORDER for number in range(19)]
    return (jnp.stack(f_posts), jnp.stack(g_posts))


def window(whole, begin, rows, whole_rows):
    begin = jnp.mod(begin, whole_rows)
    doubled = jnp.concatenate([whole, whole], axis=1)
    return lax.dynamic_slice_in_dim(doubled, begin, rows, 1)


def sliding(edges, shift):
    extended = with_halo(edges, (("gx", 1),), 1)
    below = extended[:, 0]
    above = extended[:, 3]
    whole_below, whole_above = (
        lax.all_gather(below, "gy", axis=1, tiled=True),
        lax.all_gather(above, "gy", axis=1, tiled=True),
    )
    rows = below.shape[1]
    whole_rows = whole_below.shape[1]
    start = lax.axis_index("gy") * rows
    return (
        window(whole_below, start - shift, rows, whole_rows),
        window(whole_above, start + shift, rows, whole_rows),
    )


def extend_x(posts, below, above):
    rows, layers = (posts.shape[2], posts.shape[3])
    lower = jnp.concatenate(
        [
            jnp.zeros((1, rows, layers), jnp.float32),
            below,
            jnp.zeros((13, rows, layers), jnp.float32),
        ],
        axis=0,
    )
    upper = jnp.concatenate(
        [
            jnp.zeros((6, rows, layers), jnp.float32),
            above,
            jnp.zeros((8, rows, layers), jnp.float32),
        ],
        axis=0,
    )
    return jnp.concatenate([lower[:, None], posts, upper[:, None]], axis=1)


def local(f_pop, g_pop, displacement):
    shift = displacement[0]
    width_x, width_y, width_z = (f_pop.shape[1], f_pop.shape[2], f_pop.shape[3])
    order_field = jnp.sum(g_pop, axis=0)
    phase_edges = jnp.stack([order_field[0], order_field[-1]])[None]
    phase_below, phase_above = sliding(phase_edges, shift)
    neigh_xm = jnp.concatenate([phase_below, order_field[:-1]], axis=0)
    neigh_xp = jnp.concatenate([order_field[1:], phase_above], axis=0)
    padded = with_halo(order_field, (("gy", 1), ("gz", 2)), 1)
    neigh_ym = padded[:, :-2, 1:-1]
    neigh_yp = padded[:, 2:, 1:-1]
    neigh_zm = padded[:, 1:-1, :-2]
    neigh_zp = padded[:, 1:-1, 2:]
    laplace = neigh_xm + neigh_xp + neigh_ym + neigh_yp + neigh_zm + neigh_zp - 6.0 * order_field
    slopes = [0.5 * (neigh_xp - neigh_xm), 0.5 * (neigh_yp - neigh_ym), 0.5 * (neigh_zp - neigh_zm)]
    f_post, g_post = collide(f_pop, g_pop, order_field, laplace, slopes)
    pop_edges = jnp.concatenate(
        [
            jnp.stack([f_post[6:11, 0], f_post[1:6, -1]], axis=1),
            jnp.stack([g_post[6:11, 0], g_post[1:6, -1]], axis=1),
        ],
        axis=0,
    )
    pop_below, pop_above = sliding(pop_edges, shift)
    layered = jnp.concatenate(
        [
            extend_x(f_post, pop_below[0:5], pop_above[0:5]),
            extend_x(g_post, pop_below[5:10], pop_above[5:10]),
        ],
        axis=0,
    )
    results = []
    padded_all = with_halo(layered, (("gy", 2), ("gz", 3)), 1)
    for number in range(38):
        vel_x, vel_y, vel_z = VELOCITIES[number % 19]
        results.append(
            padded_all[
                number,
                1 - vel_x : 1 - vel_x + width_x,
                1 - vel_y : 1 - vel_y + width_y,
                1 - vel_z : 1 - vel_z + width_z,
            ]
        )
    f_new = jnp.stack(results[:19])
    g_new = jnp.stack(results[19:])
    return (f_new, g_new)


def solution(mesh):
    return jax.shard_map(
        local,
        mesh=mesh,
        in_specs=(P(None, "gx", "gy", "gz"), P(None, "gx", "gy", "gz"), P()),
        out_specs=(P(None, "gx", "gy", "gz"), P(None, "gx", "gy", "gz")),
        check_vma=False,
    )
```

profile of v0, /device:TPU:2, one launch (start us, length us, event | category | flops | bytes accessed | tf_op | source)
XLA Modules:
  0.0 119.1 jit_solution(16818710644719364818)
XLA Ops:
  0.7 1.2 %reduce_sum.19 = f32[4,16,128]{2,1,0:T(8,128)S(1)} reduce(f32[19,4,16,128]{3,2,1,0:T(8,128)} %param.4, f32[]{:T(128)} %constant.95.clone.1), dimensions={0}, to_apply=%region_1.2 | reduce | flops 147456 | bytes 655364 | tf_op jit(solution)/shard_map/reduce_sum | solution.py:154
  1.9 2.3 %collective-permute-start.3 = (f32[4,1,128]{2,1,0:T(1,128)S(1)}, f32[4,1,128]{2,1,0:T(1,128)S(1)}, u32[]{:S(2)}, u32[]{:S(2)}) collective-permute-start(f32[4,1,128]{2,1,0:T(1,128)S(1)} %get-tuple-element.108), channel_id=1, source_target_pairs={{2,0},{4,2},{6,4},{0,6},{3,1},{5,3},{7,5},{1,7},{10,8},{12,10},{14... | collective-permute-start | bytes 6152 | tf_op jit(solution)/shard_map/ppermute | solution.py:42
  4.2 5.8 %collective-permute-start.1 = (f32[1,1,16,128]{3,2,1,0:T(8,128)S(1)}, f32[1,1,16,128]{3,2,1,0:T(8,128)S(1)}, u32[]{:S(2)}, u32[]{:S(2)}) collective-permute-start(f32[1,1,16,128]{3,2,1,0:T(8,128)S(1)} %get-tuple-element.114), channel_id=1, source_target_pairs={{8,0},{16,8},{24,16},{32,24},{40,32},{48,40},{56,48},{64,56},{72,6... | collective-permute-start | bytes 24584 | tf_op jit(solution)/shard_map/ppermute | solution.py:42
  10.8 0.1 pad.67.clone
  10.8 0.1 pad.60.clone
  10.9 1.1 reduce_sum.18
  12.1 0.1 fusion.109
  12.2 4.5 %collective-permute-start.5 = (f32[4,18,1]{2,1,0:T(8,128)S(1)}, f32[4,18,1]{2,1,0:T(8,128)S(1)}, u32[]{:S(2)}, u32[]{:S(2)}) collective-permute-start(f32[4,18,1]{2,1,0:T(8,128)S(1)} %get-tuple-element.106), channel_id=1, source_target_pairs={{1,0},{0,1},{3,2},{2,3},{5,4},{4,5},{7,6},{6,7},{9,8},{8,9},{11,10... | collective-permute-start | bytes 872 | tf_op jit(solution)/shard_map/ppermute | solution.py:42
  16.7 1.4 %collective-permute-start.4 = (f32[4,18,1]{2,1,0:T(8,128)S(1)}, f32[4,18,1]{2,1,0:T(8,128)S(1)}, u32[]{:S(2)}, u32[]{:S(2)}) collective-permute-start(f32[4,18,1]{2,1,0:T(8,128)S(1)} %get-tuple-element.107), channel_id=1, source_target_pairs={{0,1},{1,0},{2,3},{3,2},{4,5},{5,4},{6,7},{7,6},{8,9},{9,8},{10,11... | collective-permute-start | bytes 872 | tf_op jit(solution)/shard_map/ppermute | solution.py:40
  18.1 13.2 %all-gather = f32[1,1,64,128]{3,2,1,0:T(8,128)S(1)} all-gather(f32[1,1,16,128]{3,2,1,0:T(8,128)S(1)} %collective-permute-done), channel_id=2, replica_groups=mesh['gx'=32,'gy'=4,'gz'=2] {'gy'}, dimensions={2}, use_global_device_ids=true | all-gather | bytes 40960 | tf_op jit(solution)/shard_map/all_gather | solution.py:118
  31.3 11.9 %all-gather.1 = f32[1,1,64,128]{3,2,1,0:T(8,128)S(1)} all-gather(f32[1,1,16,128]{3,2,1,0:T(8,128)S(1)} %collective-permute-done.1), channel_id=3, replica_groups=mesh['gx'=32,'gy'=4,'gz'=2] {'gy'}, dimensions={2}, use_global_device_ids=true | all-gather | bytes 40960 | tf_op jit(solution)/shard_map/all_gather | solution.py:119
  43.3 1.4 %bitcast_subtract_fusion.16 = (f32[4,16,128]{2,1,0:T(8,128)S(1)}, f32[4,16,128]{2,1,0:T(8,128)S(1)}, f32[4,16,128]{2,1,0:T(8,128)S(1)}, f32[4,16,128]{2,1,0:T(8,...) fusion(f32[4,16,128]{2,1,0:T(8,128)S(1)} %reduce_sum.19, ...), kind=kLoop, calls=%fused_computation.190 | loop fusion | flops 2064384 | bytes 1512000 | tf_op jit(solution)/shard_map/sub | solution.py:103
  45.3 0.1 constant_dynamic-update-slice_fusion
  45.4 0.1 collective-permute-start.7
  45.5 0.5 collective-permute-start.6
  46.0 0.8 copy.371
  47.4 6.0 %collective-permute-done.6 = f32[10,1,16,128]{3,2,1,0:T(8,128)S(1)} collective-permute-done((f32[10,1,16,128]{3,2,1,0:T(8,128)S(1)}, f32[10,1,16,128]{3,2,1,0:T(8,128)S(1)}, u32[]{:S(2)}, u32[]{:S(2)}) %collective-permute-start.6) | collective-permute-done | bytes 81952 | tf_op jit(solution)/shard_map/ppermute | solution.py:40
  53.4 0.1 copy.282
  53.5 12.4 %all-gather.2 = f32[10,1,64,128]{3,1,0,2:T(1,128)S(1)} all-gather(f32[10,1,16,128]{3,1,0,2:T(1,128)S(1)} %copy.282), channel_id=4, replica_groups=mesh['gx'=32,'gy'=4,'gz'=2] {'gy'}, dimensions={2}, use_global_device_ids=true | all-gather | bytes 409600 | tf_op jit(solution)/shard_map/all_gather | solution.py:118
  65.9 0.1 copy.284
  66.0 12.4 %all-gather.3 = f32[10,1,64,128]{3,1,0,2:T(1,128)S(1)} all-gather(f32[10,1,16,128]{3,1,0,2:T(1,128)S(1)} %copy.284), channel_id=5, replica_groups=mesh['gx'=32,'gy'=4,'gz'=2] {'gy'}, dimensions={2}, use_global_device_ids=true | all-gather | bytes 409600 | tf_op jit(solution)/shard_map/all_gather | solution.py:119
  78.5 0.1 maximum_bitcast_fusion.2
  78.6 0.1 maximum_bitcast_fusion.1
  78.7 0.2 fusion
  78.9 0.1 collective-permute-start.8
  79.0 2.3 %collective-permute-start.9 = (f32[38,6,1,128]{3,0,2,1:T(8,128)S(1)}, f32[38,6,1,128]{3,0,2,1:T(8,128)S(1)}, u32[]{:S(2)}, u32[]{:S(2)}) collective-permute-start(f32[38,6,1,128]{3,0,2,1:T(8,128)S(1)} %copy.290), channel_id=1, source_target_pairs={{2,0},{4,2},{6,4},{0,6},{3,1},{5,3},{7,5},{1,7},{10,8},{12,10},{14... | collective-permute-start | bytes 350216 | tf_op jit(solution)/shard_map/ppermute | solution.py:42
  81.3 2.6 %collective-permute-done.8 = f32[38,6,1,128]{3,0,2,1:T(8,128)S(1)} collective-permute-done((f32[38,6,1,128]{3,0,2,1:T(8,128)S(1)}, f32[38,6,1,128]{3,0,2,1:T(8,128)S(1)}, u32[]{:S(2)}, u32[]{:S(2)}) %collective-permute-start.8) | collective-permute-done | bytes 116768 | tf_op jit(solution)/shard_map/ppermute | solution.py:40
  83.9 0.1 copy.289
  84.0 0.7 collective-permute-done.9
  84.8 0.1 copy.291
  84.9 0.5 pad_maximum_fusion
  85.4 3.2 %fusion.105 = (f32[38,6,18,1]{3,2,1,0:T(8,128)}, f32[38,6,18,1]{3,2,1,0:T(8,128)}) fusion(f32[38,6,18,128]{3,2,1,0:T(8,128)S(1)} %pad_maximum_fusion), kind=kLoop, calls=%fused_computation.399 | loop fusion | bytes 65664 | tf_op jit(solution)/shard_map/slice | solution.py:36
  88.6 3.0 %copy.294 = f32[38,6,18,1]{0,2,3,1:T(8,128)S(1)} copy(f32[38,6,18,1]{3,2,1,0:T(8,128)} %get-tuple-element.53) | data formatting | bytes 32832 | tf_op jit(solution)/shard_map/slice | solution.py:37
  91.7 4.6 %collective-permute-start.10 = (f32[38,6,18,1]{0,2,3,1:T(8,128)S(1)}, f32[38,6,18,1]{0,2,3,1:T(8,128)S(1)}, u32[]{:S(2)}, u32[]{:S(2)}) collective-permute-start(f32[38,6,18,1]{0,2,3,1:T(8,128)S(1)} %copy.294), channel_id=1, source_target_pairs={{0,1},{1,0},{2,3},{3,2},{4,5},{5,4},{6,7},{7,6},{8,9},{9,8},{10,11... | collective-permute-start | bytes 49256 | tf_op jit(solution)/shard_map/ppermute | solution.py:40
  96.2 3.0 %copy.296 = f32[38,6,18,1]{0,2,3,1:T(8,128)S(1)} copy(f32[38,6,18,1]{3,2,1,0:T(8,128)} %get-tuple-element.52) | data formatting | bytes 32832 | tf_op jit(solution)/shard_map/slice | solution.py:36
  99.3 1.5 %collective-permute-start.11 = (f32[38,6,18,1]{0,2,3,1:T(8,128)S(1)}, f32[38,6,18,1]{0,2,3,1:T(8,128)S(1)}, u32[]{:S(2)}, u32[]{:S(2)}) collective-permute-start(f32[38,6,18,1]{0,2,3,1:T(8,128)S(1)} %copy.296), channel_id=1, source_target_pairs={{1,0},{0,1},{3,2},{2,3},{5,4},{4,5},{7,6},{6,7},{9,8},{8,9},{11,10... | collective-permute-start | bytes 49256 | tf_op jit(solution)/shard_map/ppermute | solution.py:42
  100.8 2.8 %copy.295 = f32[38,6,18,1]{3,2,1,0:T(8,128)} copy(f32[38,6,18,1]{0,2,3,1:T(8,128)S(1)} %collective-permute-done.10) | data formatting | bytes 32832 | tf_op jit(solution)/shard_map/ppermute | solution.py:40
  103.5 0.9 constant_dynamic-update-slice_fusion.91
  104.4 3.2 %collective-permute-done.11 = f32[38,6,18,1]{0,2,3,1:T(8,128)S(1)} collective-permute-done((f32[38,6,18,1]{0,2,3,1:T(8,128)S(1)}, f32[38,6,18,1]{0,2,3,1:T(8,128)S(1)}, u32[]{:S(2)}, u32[]{:S(2)}) %collective-permute-start.11) | collective-permute-done | bytes 16448 | tf_op jit(solution)/shard_map/ppermute | solution.py:42
  107.6 2.8 %copy.297 = f32[38,6,18,1]{3,2,1,0:T(8,128)} copy(f32[38,6,18,1]{0,2,3,1:T(8,128)S(1)} %collective-permute-done.11) | data formatting | bytes 32832 | tf_op jit(solution)/shard_map/ppermute | solution.py:42
  110.4 0.9 constant_dynamic-update-slice_fusion.90
  111.4 1.7 %copy-done.1 = f32[38,6,18,1]{3,2,1,0:T(8,128)S(1)} copy-done((f32[38,6,18,1]{3,2,1,0:T(8,128)S(1)}, f32[38,6,18,1]{3,2,1,0:T(8,128)}, u32[]{:S(2)}) %copy-start.1) | copy-done | bytes 16440
  113.1 0.1 constant_dynamic-update-slice_fusion.86
  113.2 1.7 %copy-done = f32[38,6,18,1]{3,2,1,0:T(8,128)S(1)} copy-done((f32[38,6,18,1]{3,2,1,0:T(8,128)S(1)}, f32[38,6,18,1]{3,2,1,0:T(8,128)}, u32[]{:S(2)}) %copy-start) | copy-done | bytes 16440
  114.9 0.1 constant_dynamic-update-slice_fusion.85
  115.0 0.1 constant_dynamic-update-slice_fusion.82
  115.1 0.1 constant_dynamic-update-slice_fusion.81
  115.2 1.0 copy-done.5
  116.2 0.1 constant_dynamic-update-slice_fusion.80
  116.2 0.1 constant_dynamic-update-slice_fusion.79
  116.4 0.1 constant_dynamic-update-slice_fusion.72
  116.4 0.1 constant_dynamic-update-slice_fusion.71
  116.6 0.1 constant_dynamic-update-slice_fusion.78
  116.7 0.1 constant_dynamic-update-slice_fusion.67
  116.8 0.1 constant_dynamic-update-slice_fusion.66
  116.9 0.1 constant_dynamic-update-slice_fusion.77
  117.0 0.1 constant_dynamic-update-slice_fusion.63
  117.1 0.7 copy-done.4
  117.8 0.1 constant_dynamic-update-slice_fusion.62
  117.9 0.1 constant_dynamic-update-slice_fusion.61
  117.9 0.1 constant_dynamic-update-slice_fusion.60
  118.1 0.1 constant_dynamic-update-slice_fusion.59
  118.1 0.1 constant_dynamic-update-slice_fusion.58
  118.3 0.8 copy-done.6
  (97 shorter events, 1.2 us)
Async XLA Ops:
  0.6 44.3 %copy-start.3 = (f32[19,4,16,128]{3,2,1,0:T(8,128)S(1)}, f32[19,4,16,128]{3,2,1,0:T(8,128)}, u32[]{:S(2)}) copy-start(f32[19,4,16,128]{3,2,1,0:T(8,128)} %param.4) | copy-start | bytes 1867780
  0.6 44.1 %copy-start.2 = (f32[19,4,16,128]{3,2,1,0:T(8,128)S(1)}, f32[19,4,16,128]{3,2,1,0:T(8,128)}, u32[]{:S(2)}) copy-start(f32[19,4,16,128]{3,2,1,0:T(8,128)} %param.3) | copy-start | bytes 1867780
  1.9 10.2 %collective-permute-start.3 = (f32[4,1,128]{2,1,0:T(1,128)S(1)}, f32[4,1,128]{2,1,0:T(1,128)S(1)}, u32[]{:S(2)}, u32[]{:S(2)}) collective-permute-start(f32[4,1,128]{2,1,0:T(1,128)S(1)} %get-tuple-element.108), channel_id=1, source_target_pairs={{2,0},{4,2},{6,4},{0,6},{3,1},{5,3},{7,5},{1,7},{10,8},{12,10},{14... | collective-permute-start | bytes 6152 | tf_op jit(solution)/shard_map/ppermute | solution.py:42
  4.2 7.9 %collective-permute-start.2 = (f32[4,1,128]{2,1,0:T(1,128)S(1)}, f32[4,1,128]{2,1,0:T(1,128)S(1)}, u32[]{:S(2)}, u32[]{:S(2)}) collective-permute-start(f32[4,1,128]{2,1,0:T(1,128)S(1)} %get-tuple-element.109), channel_id=1, source_target_pairs={{0,2},{2,4},{4,6},{6,0},{1,3},{3,5},{5,7},{7,1},{8,10},{10,12},{12... | collective-permute-start | bytes 6152 | tf_op jit(solution)/shard_map/ppermute | solution.py:40
  4.2 27.1 %collective-permute-start.1 = (f32[1,1,16,128]{3,2,1,0:T(8,128)S(1)}, f32[1,1,16,128]{3,2,1,0:T(8,128)S(1)}, u32[]{:S(2)}, u32[]{:S(2)}) collective-permute-start(f32[1,1,16,128]{3,2,1,0:T(8,128)S(1)} %get-tuple-element.114), channel_id=1, source_target_pairs={{8,0},{16,8},{24,16},{32,24},{40,32},{48,40},{56,48},{64,56},{72,6... | collective-permute-start | bytes 24584 | tf_op jit(solution)/shard_map/ppermute | solution.py:42
  10.0 8.1 %collective-permute-start = (f32[1,1,16,128]{3,2,1,0:T(8,128)S(1)}, f32[1,1,16,128]{3,2,1,0:T(8,128)S(1)}, u32[]{:S(2)}, u32[]{:S(2)}) collective-permute-start(f32[1,1,16,128]{3,2,1,0:T(8,128)S(1)} %get-tuple-element.115), channel_id=1, source_target_pairs={{0,8},{8,16},{16,24},{24,32},{32,40},{40,48},{48,56},{56,64},{64,7... | collective-permute-start | bytes 24584 | tf_op jit(solution)/shard_map/ppermute | solution.py:40
  12.2 31.1 %collective-permute-start.5 = (f32[4,18,1]{2,1,0:T(8,128)S(1)}, f32[4,18,1]{2,1,0:T(8,128)S(1)}, u32[]{:S(2)}, u32[]{:S(2)}) collective-permute-start(f32[4,18,1]{2,1,0:T(8,128)S(1)} %get-tuple-element.106), channel_id=1, source_target_pairs={{1,0},{0,1},{3,2},{2,3},{5,4},{4,5},{7,6},{6,7},{9,8},{8,9},{11,10... | collective-permute-start | bytes 872 | tf_op jit(solution)/shard_map/ppermute | solution.py:42
  16.7 26.6 %collective-permute-start.4 = (f32[4,18,1]{2,1,0:T(8,128)S(1)}, f32[4,18,1]{2,1,0:T(8,128)S(1)}, u32[]{:S(2)}, u32[]{:S(2)}) collective-permute-start(f32[4,18,1]{2,1,0:T(8,128)S(1)} %get-tuple-element.107), channel_id=1, source_target_pairs={{0,1},{1,0},{2,3},{3,2},{4,5},{5,4},{6,7},{7,6},{8,9},{9,8},{10,11... | collective-permute-start | bytes 872 | tf_op jit(solution)/shard_map/ppermute | solution.py:40
  45.4 20.5 %collective-permute-start.7 = (f32[10,1,16,128]{3,2,1,0:T(8,128)S(1)}, f32[10,1,16,128]{3,2,1,0:T(8,128)S(1)}, u32[]{:S(2)}, u32[]{:S(2)}) collective-permute-start(f32[10,1,16,128]{3,2,1,0:T(8,128)S(1)} %get-tuple-element.92), channel_id=1, source_target_pairs={{8,0},{16,8},{24,16},{32,24},{40,32},{48,40},{56,48},{64,56},{72,6... | collective-permute-start | bytes 245768 | tf_op jit(solution)/shard_map/ppermute | solution.py:42
  45.5 7.9 %collective-permute-start.6 = (f32[10,1,16,128]{3,2,1,0:T(8,128)S(1)}, f32[10,1,16,128]{3,2,1,0:T(8,128)S(1)}, u32[]{:S(2)}, u32[]{:S(2)}) collective-permute-start(f32[10,1,16,128]{3,2,1,0:T(8,128)S(1)} %get-tuple-element.93), channel_id=1, source_target_pairs={{0,8},{8,16},{16,24},{24,32},{32,40},{40,48},{48,56},{56,64},{64,7... | collective-permute-start | bytes 245768 | tf_op jit(solution)/shard_map/ppermute | solution.py:40
  78.9 5.0 %collective-permute-start.8 = (f32[38,6,1,128]{3,0,2,1:T(8,128)S(1)}, f32[38,6,1,128]{3,0,2,1:T(8,128)S(1)}, u32[]{:S(2)}, u32[]{:S(2)}) collective-permute-start(f32[38,6,1,128]{3,0,2,1:T(8,128)S(1)} %copy.288), channel_id=1, source_target_pairs={{0,2},{2,4},{4,6},{6,0},{1,3},{3,5},{5,7},{7,1},{8,10},{10,12},{12... | collective-permute-start | bytes 350216 | tf_op jit(solution)/shard_map/ppermute | solution.py:40
  79.0 5.7 %collective-permute-start.9 = (f32[38,6,1,128]{3,0,2,1:T(8,128)S(1)}, f32[38,6,1,128]{3,0,2,1:T(8,128)S(1)}, u32[]{:S(2)}, u32[]{:S(2)}) collective-permute-start(f32[38,6,1,128]{3,0,2,1:T(8,128)S(1)} %copy.290), channel_id=1, source_target_pairs={{2,0},{4,2},{6,4},{0,6},{3,1},{5,3},{7,5},{1,7},{10,8},{12,10},{14... | collective-permute-start | bytes 350216 | tf_op jit(solution)/shard_map/ppermute | solution.py:42
  91.7 9.1 %collective-permute-start.10 = (f32[38,6,18,1]{0,2,3,1:T(8,128)S(1)}, f32[38,6,18,1]{0,2,3,1:T(8,128)S(1)}, u32[]{:S(2)}, u32[]{:S(2)}) collective-permute-start(f32[38,6,18,1]{0,2,3,1:T(8,128)S(1)} %copy.294), channel_id=1, source_target_pairs={{0,1},{1,0},{2,3},{3,2},{4,5},{5,4},{6,7},{7,6},{8,9},{9,8},{10,11... | collective-permute-start | bytes 49256 | tf_op jit(solution)/shard_map/ppermute | solution.py:40
  99.3 8.3 %collective-permute-start.11 = (f32[38,6,18,1]{0,2,3,1:T(8,128)S(1)}, f32[38,6,18,1]{0,2,3,1:T(8,128)S(1)}, u32[]{:S(2)}, u32[]{:S(2)}) collective-permute-start(f32[38,6,18,1]{0,2,3,1:T(8,128)S(1)} %copy.296), channel_id=1, source_target_pairs={{1,0},{0,1},{3,2},{2,3},{5,4},{4,5},{7,6},{6,7},{9,8},{8,9},{11,10... | collective-permute-start | bytes 49256 | tf_op jit(solution)/shard_map/ppermute | solution.py:42
  111.3 1.8 %copy-start.1 = (f32[38,6,18,1]{3,2,1,0:T(8,128)S(1)}, f32[38,6,18,1]{3,2,1,0:T(8,128)}, u32[]{:S(2)}) copy-start(f32[38,6,18,1]{3,2,1,0:T(8,128)} %copy.297) | copy-start | bytes 49252
  113.1 1.8 %copy-start = (f32[38,6,18,1]{3,2,1,0:T(8,128)S(1)}, f32[38,6,18,1]{3,2,1,0:T(8,128)}, u32[]{:S(2)}) copy-start(f32[38,6,18,1]{3,2,1,0:T(8,128)} %copy.295) | copy-start | bytes 49252
  115.1 1.1 copy-start.5
  116.9 0.8 copy-start.4
  118.2 0.8 copy-start.6
where the time goes:
time: 121 us; the launch traced here: 119 us
  blocking collectives  49.9 us (41%)
  starting transfers between devices  23.1 us (19%)
  local copies, waits for them, and re-layouts  22.6 us (19%)
  waiting for transfers between devices  12.5 us (10%)
  other arithmetic  8.9 us (7%)
  between operations  2.13 us (2%)
    all_gather x2, blocking collectives, sliding(): lax.all_gather(below, 'gy', axis=1, tiled=True)  25.6 us
    all_gather x2, blocking collectives, sliding(): lax.all_gather(above, 'gy', axis=1, tiled=True)  24.3 us
    ppermute x6, starting transfers between devices, with_halo(): lax.ppermute(head, axis, [((i + 1) % count, i) for i in range(count)])  16.5 us
    ppermute x6, waiting for transfers between devices, with_halo(): lax.ppermute(tail, axis, [(i, (i + 1) % count) for i in range(count)])  8.57 us
    unnamed x27, local copies, waits for them, and re-layouts  6.9 us
    ppermute x6, starting transfers between devices, with_halo(): lax.ppermute(tail, axis, [(i, (i + 1) % count) for i in range(count)])  6.59 us
    slice x7, local copies, waits for them, and re-layouts, with_halo(): head = lax.slice_in_dim(cells, 0, width, axis=dim)  6.39 us
    ppermute x6, waiting for transfers between devices, with_halo(): lax.ppermute(head, axis, [((i + 1) % count, i) for i in range(count)])  3.93 us
  transfers between devices with their start and end apart: 12, of which 4 were waited for; matrix products, arithmetic and copies ran while one was open for 8% of the time, Pallas kernels for 0%

commit v1 on v0

v1 whole, which is shorter than its diff:
```python
import jax
import jax.numpy as jnp
from jax import lax
from jax.sharding import PartitionSpec as P

VELOCITIES = [
    (0, 0, 0),
    (1, 0, 0),
    (1, 1, 0),
    (1, -1, 0),
    (1, 0, 1),
    (1, 0, -1),
    (-1, 0, 0),
    (-1, -1, 0),
    (-1, 1, 0),
    (-1, 0, -1),
    (-1, 0, 1),
    (0, 1, 0),
    (0, -1, 0),
    (0, 0, 1),
    (0, 0, -1),
    (0, 1, 1),
    (0, -1, -1),
    (0, 1, -1),
    (0, -1, 1),
]
BULK_COEF = 0.5
STIFFNESS = 0.5
TAU_FLUID = 0.8
TAU_ORDER = 0.9
SHIFT_MIN = 33
SHIFT_MAX = 47
AXES = ("gx", "gy", "gz")


def lattice_weight(number):
    steps_sq = sum((abs(comp) for comp in VELOCITIES[number]))
    if steps_sq == 0:
        return 1.0 / 3.0
    if steps_sq == 1:
        return 1.0 / 18.0
    return 1.0 / 36.0


def along(number, values, base):
    result = jnp.zeros_like(base)
    for axis_id in range(3):
        comp = VELOCITIES[number][axis_id]
        if comp != 0:
            result = result + comp * values[axis_id]
    return result


def collide(f_pop, g_pop, order_field, laplace, slopes):
    density = jnp.sum(f_pop, axis=0)
    chemical = (
        BULK_COEF * (order_field * order_field * order_field - order_field) - STIFFNESS * laplace
    )
    forces = [chemical * slope for slope in slopes]
    moments = []
    for axis_id in range(3):
        moment = jnp.zeros_like(density)
        for number in range(19):
            comp = VELOCITIES[number][axis_id]
            if comp != 0:
                moment = moment + comp * f_pop[number]
        moments.append(moment)
    flows = [(moments[axis_id] + 0.5 * forces[axis_id]) / density for axis_id in range(3)]
    speed_sq = flows[0] * flows[0] + flows[1] * flows[1] + flows[2] * flows[2]
    flow_force = flows[0] * forces[0] + flows[1] * forces[1] + flows[2] * forces[2]
    f_posts = []
    g_eqs = []
    for number in range(19):
        weight = lattice_weight(number)
        proj_flow = along(number, flows, density)
        proj_force = along(number, forces, density)
        shape_term = 3.0 * proj_flow + 4.5 * proj_flow * proj_flow - 1.5 * speed_sq
        f_eq = weight * density * (1.0 + shape_term)
        source = (
            (1.0 - 0.5 / TAU_FLUID)
            * weight
            * (3.0 * (proj_force - flow_force) + 9.0 * proj_flow * proj_force)
        )
        f_posts.append(f_pop[number] - (f_pop[number] - f_eq) / TAU_FLUID + source)
        g_eqs.append(weight * (3.0 * chemical + order_field * shape_term))
    rest_eq = order_field
    for number in range(1, 19):
        rest_eq = rest_eq - g_eqs[number]
    g_eqs[0] = rest_eq
    g_posts = [g_pop[number] - (g_pop[number] - g_eqs[number]) / TAU_ORDER for number in range(19)]
    return (jnp.stack(f_posts), jnp.stack(g_posts))


def exchange(sends):
    sizes = [lax.axis_size(a) for a in AXES]
    groups = {}
    order = []
    for index, (value, offset) in enumerate(sends):
        key = (tuple(o % n for o, n in zip(offset, sizes)), value.shape[1:])
        if key not in groups:
            groups[key] = []
            order.append(key)
        groups[key].append(index)
    results = [None] * len(sends)
    for key in order:
        members = groups[key]
        offset = key[0]
        pairs = []
        for i in range(sizes[0]):
            for j in range(sizes[1]):
                for k in range(sizes[2]):
                    src = (i * sizes[1] + j) * sizes[2] + k
                    ti, tj, tk = [(c + o) % n for c, o, n in zip((i, j, k), offset, sizes)]
                    pairs.append((src, (ti * sizes[1] + tj) * sizes[2] + tk))
        payload = [sends[m][0] for m in members]
        joined = payload[0] if len(payload) == 1 else jnp.concatenate(payload, axis=0)
        got = lax.ppermute(joined, AXES, pairs)
        start = 0
        for m in members:
            count = sends[m][0].shape[0]
            results[m] = got[start : start + count]
            start += count
    return results


def local(f_pop, g_pop, displacement):
    shift = displacement[0]
    nx, ny, nz = (f_pop.shape[1], f_pop.shape[2], f_pop.shape[3])
    q = SHIFT_MIN // ny
    assert SHIFT_MAX // ny == q and SHIFT_MIN % ny != 0
    rem = shift - q * ny

    phi = jnp.sum(g_pop, axis=0)
    pa, pb, pc, pd, pym, pyp, pzm, pzp = exchange(
        [
            (phi[-1:], (1, q + 1, 0)),
            (phi[-1:], (1, q, 0)),
            (phi[:1], (-1, -q, 0)),
            (phi[:1], (-1, -q - 1, 0)),
            (phi[:, -1:], (0, 1, 0)),
            (phi[:, :1], (0, -1, 0)),
            (jnp.transpose(phi[:, :, -1:], (2, 0, 1)), (0, 0, 1)),
            (jnp.transpose(phi[:, :, :1], (2, 0, 1)), (0, 0, -1)),
        ]
    )
    low = lax.dynamic_slice_in_dim(jnp.concatenate([pa, pb], axis=1), ny - rem, ny, 1)
    high = lax.dynamic_slice_in_dim(jnp.concatenate([pc, pd], axis=1), rem, ny, 1)
    neigh_xm = jnp.concatenate([low, phi[:-1]], axis=0)
    neigh_xp = jnp.concatenate([phi[1:], high], axis=0)
    neigh_ym = jnp.concatenate([pym, phi[:, :-1]], axis=1)
    neigh_yp = jnp.concatenate([phi[:, 1:], pyp], axis=1)
    neigh_zm = jnp.concatenate([jnp.transpose(pzm, (1, 2, 0)), phi[:, :, :-1]], axis=2)
    neigh_zp = jnp.concatenate([phi[:, :, 1:], jnp.transpose(pzp, (1, 2, 0))], axis=2)
    laplace = neigh_xm + neigh_xp + neigh_ym + neigh_yp + neigh_zm + neigh_zp - 6.0 * phi
    slopes = [0.5 * (neigh_xp - neigh_xm), 0.5 * (neigh_yp - neigh_ym), 0.5 * (neigh_zp - neigh_zm)]
    f_post, g_post = collide(f_pop, g_pop, phi, laplace, slopes)
    post = jnp.concatenate([f_post, g_post], axis=0)

    vel = [VELOCITIES[n % 19] for n in range(38)]

    def pick(cond):
        return [n for n in range(38) if cond(vel[n])]

    x_up = pick(lambda c: c[0] == 1)
    x_dn = pick(lambda c: c[0] == -1)
    y_up = pick(lambda c: c[1] == 1)
    y_dn = pick(lambda c: c[1] == -1)
    z_up = pick(lambda c: c[2] == 1)
    z_dn = pick(lambda c: c[2] == -1)
    xz = {(cx, cz): pick(lambda c, cx=cx, cz=cz: c[0] == cx and c[2] == cz) for cx in (1, -1) for cz in (1, -1)}
    yz = {(cy, cz): pick(lambda c, cy=cy, cz=cz: c[1] == cy and c[2] == cz) for cy in (1, -1) for cz in (1, -1)}

    def rows(idx):
        return jnp.stack([post[n] for n in idx])

    last_x = rows(x_up)[:, -1]
    first_x = rows(x_dn)[:, 0]
    sends = [
        (last_x, (1, q + 1, 0)),
        (last_x, (1, q, 0)),
        (first_x, (-1, -q, 0)),
        (first_x, (-1, -q - 1, 0)),
        (rows(y_up)[:, :, -1], (0, 1, 0)),
        (rows(y_dn)[:, :, 0], (0, -1, 0)),
        (rows(z_up)[:, :, :, -1], (0, 0, 1)),
        (rows(z_dn)[:, :, :, 0], (0, 0, -1)),
    ]
    xz_keys = []
    for (cx, cz), idx in xz.items():
        plane = rows(idx)[:, -1 if cx == 1 else 0, :, -1 if cz == 1 else 0]
        for dy in ((q + 1, q) if cx == 1 else (-q, -q - 1)):
            sends.append((plane, (cx, dy, cz)))
            xz_keys.append((cx, cz, dy))
    yz_keys = []
    for (cy, cz), idx in yz.items():
        line = rows(idx)[:, :, -1 if cy == 1 else 0, -1 if cz == 1 else 0]
        sends.append((line, (0, cy, cz)))
        yz_keys.append((cy, cz))
    got = exchange(sends)
    xa, xb, xc, xd, hy_m, hy_p, hz_m, hz_p = got[:8]
    xz_got = dict(zip(xz_keys, got[8 : 8 + len(xz_keys)]))
    yz_got = dict(zip(yz_keys, got[8 + len(xz_keys) :]))

    win_low = lax.dynamic_slice_in_dim(jnp.concatenate([xa, xb], axis=1), ny - rem - 1, ny + 2, 1)
    win_high = lax.dynamic_slice_in_dim(jnp.concatenate([xc, xd], axis=1), rem - 1, ny + 2, 1)
    xz_win = {}
    for (cx, cz) in xz:
        if cx == 1:
            both = jnp.concatenate([xz_got[(cx, cz, q + 1)], xz_got[(cx, cz, q)]], axis=1)
            xz_win[(cx, cz)] = lax.dynamic_slice_in_dim(both, ny - rem, ny, 1)
        else:
            both = jnp.concatenate([xz_got[(cx, cz, -q)], xz_got[(cx, cz, -q - 1)]], axis=1)
            xz_win[(cx, cz)] = lax.dynamic_slice_in_dim(both, rem, ny, 1)

    def shift_yz(t, cy, cz, ym, yp, zm, zp, corner):
        if cz == 1:
            t = jnp.concatenate([zm, t[:, :, :-1]], axis=2)
        elif cz == -1:
            t = jnp.concatenate([t[:, :, 1:], zp], axis=2)
        if cy != 0:
            edge = ym if cy == 1 else yp
            if cz == 1:
                edge = jnp.concatenate([corner, edge[:, :, :-1]], axis=2)
            elif cz == -1:
                edge = jnp.concatenate([edge[:, :, 1:], corner], axis=2)
            if cy == 1:
                t = jnp.concatenate([edge, t[:, :-1]], axis=1)
            else:
                t = jnp.concatenate([t[:, 1:], edge], axis=1)
        return t

    results = []
    for n in range(38):
        cx, cy, cz = vel[n]
        ym = yp = zm = zp = corner = None
        if cy == 1:
            ym = hy_m[y_up.index(n)][:, None, :]
        if cy == -1:
            yp = hy_p[y_dn.index(n)][:, None, :]
        if cz == 1:
            zm = hz_m[z_up.index(n)][:, :, None]
        if cz == -1:
            zp = hz_p[z_dn.index(n)][:, :, None]
        if cy != 0 and cz != 0:
            corner = yz_got[(cy, cz)][yz[(cy, cz)].index(n)][:, None, None]
        if cx == 0:
            results.append(shift_yz(post[n], cy, cz, ym, yp, zm, zp, corner))
            continue
        sl = slice(0, nx - 1) if cx == 1 else slice(1, nx)
        inner = shift_yz(
            post[n][sl],
            cy,
            cz,
            None if ym is None else ym[sl],
            None if yp is None else yp[sl],
            None if zm is None else zm[sl],
            None if zp is None else zp[sl],
            corner,
        )
        if cx == 1:
            win = win_low[x_up.index(n)]
        else:
            win = win_high[x_dn.index(n)]
        plane = win[1 - cy : 1 - cy + ny]
        if cz == 1:
            col = xz_win[(cx, cz)][xz[(cx, cz)].index(n)]
            plane = jnp.concatenate([col[:, None], plane[:, :-1]], axis=1)
        elif cz == -1:
            col = xz_win[(cx, cz)][xz[(cx, cz)].index(n)]
            plane = jnp.concatenate([plane[:, 1:], col[:, None]], axis=1)
        if cx == 1:
            results.append(jnp.concatenate([plane[None], inner], axis=0))
        else:
            results.append(jnp.concatenate([inner, plane[None]], axis=0))
    f_new = jnp.stack(results[:19])
    g_new = jnp.stack(results[19:])
    return (f_new, g_new)


def solution(mesh):
    return jax.shard_map(
        local,
        mesh=mesh,
        in_specs=(P(None, "gx", "gy", "gz"), P(None, "gx", "gy", "gz"), P()),
        out_specs=(P(None, "gx", "gy", "gz"), P(None, "gx", "gy", "gz")),
        check_vma=False,
    )
```

time: 121 us -> 116 us (0.959)
  blocking collectives: 49.9 us -> 0 us
  starting transfers between devices: 23.1 us -> 55.1 us
  waiting for transfers between devices: 12.5 us -> 19 us
  other arithmetic: 8.9 us -> 14.8 us
  local copies, waits for them, and re-layouts: 22.6 us -> 23.9 us
    all_gather x4 -> x0, blocking collectives: 49.9 us -> none  [the longest x2 25.6 us: sliding(): lax.all_gather(below, 'gy', axis=1, tiled=True)]
    ppermute x12 -> x20, starting transfers between devices: 23.1 us -> 55.1 us  [exchange(): got = lax.ppermute(joined, AXES, pairs)]
    unnamed x27 -> x101, local copies, waits for them, and re-layouts: 6.9 us -> 13.5 us
    ppermute x12 -> x20, waiting for transfers between devices: 12.5 us -> 19 us  [exchange(): got = lax.ppermute(joined, AXES, pairs)]
    ppermute x6 -> x0, local copies, waits for them, and re-layouts: 5.98 us -> none  [the longest x3 3.01 us: with_halo(): lax.ppermute(head, axis, [((i + 1) % count, i) for i in range(count)])]
    slice x17 -> x50, local copies, waits for them, and re-layouts: 9.48 us -> 4.48 us  [the longest x2 0.94 us: local(): rows(y_up)[:, :, -1]]
    another operation x3 -> x39, local copies, waits for them, and re-layouts: 0.01 us -> 3.9 us  [the longest x2 1.24 us: rows(): return jnp.stack([post[n] for n in idx])]
    unnamed x56 -> x49, other arithmetic: 3.92 us -> 6.83 us
  transfers between devices with their start and end apart: 12 -> 20, of which waited for: 4 -> 7; matrix products, arithmetic and copies ran while one was open for 8% -> 13% of each run, Pallas kernels for 0% -> 0%
where the time goes in v1:
time: 116 us; the launch traced here: 115 us
  starting transfers between devices  55.1 us (48%)
  local copies, waits for them, and re-layouts  23.9 us (21%)
  waiting for transfers between devices  19 us (16%)
  other arithmetic  14.8 us (13%)
  between operations  2 us (2%)
    ppermute x20, starting transfers between devices, exchange(): got = lax.ppermute(joined, AXES, pairs)  55.1 us
    ppermute x20, waiting for transfers between devices, exchange(): got = lax.ppermute(joined, AXES, pairs)  19 us
    unnamed x101, local copies, waits for them, and re-layouts  13.5 us
    unnamed x49, other arithmetic  6.83 us
  transfers between devices with their start and end apart: 20, of which 7 were waited for; matrix products, arithmetic and copies ran while one was open for 13% of the time, Pallas kernels for 0%

profile of v1, /device:TPU:2, one launch (start us, length us, event | category | flops | bytes accessed | tf_op | source)
XLA Modules:
  0.0 114.8 jit_solution(9285755671021983926)
XLA Ops:
  0.6 1.2 %reduce_sum.24 = f32[4,16,128]{2,1,0:T(8,128)S(1)} reduce(f32[19,4,16,128]{3,2,1,0:T(8,128)} %param.4, f32[]{:T(128)} %constant.79.clone.1), dimensions={0}, to_apply=%region_1.0 | reduce | flops 147456 | bytes 655364 | tf_op jit(solution)/shard_map/reduce_sum | solution.py:133
  1.8 7.5 %collective-permute-start.3 = (f32[1,16,128]{2,1,0:T(8,128)S(1)}, f32[1,16,128]{2,1,0:T(8,128)S(1)}, u32[]{:S(2)}, u32[]{:S(2)}) collective-permute-start(f32[1,16,128]{2,1,0:T(8,128)S(1)} %get-tuple-element.316), channel_id=1, source_target_pairs={{0,250},{1,251},{2,252},{3,253},{4,254},{5,255},{6,248},{7,249},{8... | collective-permute-start | bytes 24584 | tf_op jit(solution)/shard_map/ppermute | solution.py:117
  9.4 1.4 %collective-permute-start.2 = (f32[1,16,128]{2,1,0:T(8,128)S(1)}, f32[1,16,128]{2,1,0:T(8,128)S(1)}, u32[]{:S(2)}, u32[]{:S(2)}) collective-permute-start(f32[1,16,128]{2,1,0:T(8,128)S(1)} %get-tuple-element.316), channel_id=1, source_target_pairs={{0,252},{1,253},{2,254},{3,255},{4,248},{5,249},{6,250},{7,251},{8... | collective-permute-start | bytes 24584 | tf_op jit(solution)/shard_map/ppermute | solution.py:117
  10.7 1.9 %collective-permute-start.1 = (f32[1,16,128]{2,1,0:T(8,128)S(1)}, f32[1,16,128]{2,1,0:T(8,128)S(1)}, u32[]{:S(2)}, u32[]{:S(2)}) collective-permute-start(f32[1,16,128]{2,1,0:T(8,128)S(1)} %get-tuple-element.317), channel_id=1, source_target_pairs={{0,12},{1,13},{2,14},{3,15},{4,8},{5,9},{6,10},{7,11},{8,20},{9,21... | collective-permute-start | bytes 24584 | tf_op jit(solution)/shard_map/ppermute | solution.py:117
  12.8 4.6 %collective-permute-start.6 = (f32[2,4,16]{2,1,0:T(4,128)S(1)}, f32[2,4,16]{2,1,0:T(4,128)S(1)}, u32[]{:S(2)}, u32[]{:S(2)}) collective-permute-start(f32[2,4,16]{2,1,0:T(4,128)S(1)} %pad_maximum_fusion.29), channel_id=1, source_target_pairs={{0,1},{1,0},{2,3},{3,2},{4,5},{5,4},{6,7},{7,6},{8,9},{9,8},{10,11... | collective-permute-start | bytes 1544 | tf_op jit(solution)/shard_map/ppermute | solution.py:117
  17.5 0.7 slice_bitcast_fusion.26
  18.3 0.4 copy-done.1
  18.7 0.7 slice_bitcast_fusion.7
  20.1 0.2 collective-permute-done.6
  20.4 1.2 %collective-permute-start.5 = (f32[4,1,128]{2,0,1:T(4,128)S(1)}, f32[4,1,128]{2,0,1:T(4,128)S(1)}, u32[]{:S(2)}, u32[]{:S(2)}) collective-permute-start(f32[4,1,128]{2,0,1:T(4,128)S(1)} %bitcast.1679), channel_id=1, source_target_pairs={{0,6},{1,7},{2,0},{3,1},{4,2},{5,3},{6,4},{7,5},{8,14},{9,15},{10,... | collective-permute-start | bytes 6152 | tf_op jit(solution)/shard_map/ppermute | solution.py:117
  22.0 0.9 collective-permute-start.4
  23.0 1.0 collective-permute-done.5
  24.0 1.6 %collective-permute-done.4 = f32[4,1,128]{2,1,0:T(1,128)S(1)} collective-permute-done((f32[4,1,128]{2,1,0:T(1,128)S(1)}, f32[4,1,128]{2,1,0:T(1,128)S(1)}, u32[]{:S(2)}, u32[]{:S(2)}) %collective-permute-start.4) | collective-permute-done | bytes 2080 | tf_op jit(solution)/shard_map/ppermute | solution.py:117
  25.7 0.7 multiply_subtract_fusion.2
  26.4 0.8 multiply_subtract_fusion.3
  27.2 0.6 fusion.303
  28.0 1.0 constant_dynamic-update-slice_fusion.97
  29.0 0.6 constant_dynamic-update-slice_fusion.78
  29.7 0.7 constant_dynamic-update-slice_fusion.57
  30.5 0.6 constant_dynamic-update-slice_fusion.28
  31.3 0.7 constant_dynamic-update-slice_fusion.46
  32.1 0.6 constant_dynamic-update-slice_fusion.26
  32.7 0.6 constant_dynamic-update-slice_fusion.25
  33.3 0.6 constant_dynamic-update-slice_fusion.24
  33.9 0.6 constant_dynamic-update-slice_fusion.23
  34.8 1.5 %collective-permute-start.12 = (f32[4,16]{1,0:T(4,128)S(1)}, f32[4,16]{1,0:T(4,128)S(1)}, u32[]{:S(2)}, u32[]{:S(2)}) collective-permute-start(f32[4,16]{1,0:T(4,128)S(1)} %pad_maximum_fusion.30), channel_id=1, source_target_pairs={{0,13},{1,12},{2,15},{3,14},{4,9},{5,8},{6,11},{7,10},{8,21},{9,20... | collective-permute-start | bytes 776 | tf_op jit(solution)/shard_map/ppermute | solution.py:117
  36.4 4.8 %collective-permute-start.11 = (f32[4,16]{1,0:T(4,128)S(1)}, f32[4,16]{1,0:T(4,128)S(1)}, u32[]{:S(2)}, u32[]{:S(2)}) collective-permute-start(f32[4,16]{1,0:T(4,128)S(1)} %pad_maximum_fusion.30), channel_id=1, source_target_pairs={{0,15},{1,14},{2,9},{3,8},{4,11},{5,10},{6,13},{7,12},{8,23},{9,22... | collective-permute-start | bytes 776 | tf_op jit(solution)/shard_map/ppermute | solution.py:117
  41.1 1.1 collective-permute-start.8
  42.2 2.8 %collective-permute-start.7 = (f32[10,16,128]{2,1,0:T(8,128)S(1)}, f32[10,16,128]{2,1,0:T(8,128)}, u32[]{:S(2)}, u32[]{:S(2)}) collective-permute-start(f32[10,16,128]{2,1,0:T(8,128)S(1)} %slice_bitcast_fusion.1), channel_id=1, source_target_pairs={{0,14},{1,15},{2,8},{3,9},{4,10},{5,11},{6,12},{7,13},{8,22},{9,23... | collective-permute-start | bytes 245768 | tf_op jit(solution)/shard_map/ppermute | solution.py:117
  45.2 0.7 constant_dynamic-update-slice_fusion.22
  46.0 0.6 copy-done.37
  46.7 0.6 constant_dynamic-update-slice_fusion.21
  47.4 0.6 constant_dynamic-update-slice_fusion.11
  48.3 0.6 constant_dynamic-update-slice_fusion.20
  49.0 0.9 slice.1204
  49.9 0.6 constant_dynamic-update-slice_fusion.10
  50.5 0.9 slice.1187
  51.6 0.3 copy.899
  51.9 0.3 copy.915
  52.4 6.6 %collective-permute-start.18 = (f32[4,4]{1,0:T(4,128)S(1)}, f32[4,4]{1,0:T(4,128)S(1)}, u32[]{:S(2)}, u32[]{:S(2)}) collective-permute-start(f32[4,4]{1,0:T(4,128)S(1)} %pad_maximum_fusion.32), channel_id=1, source_target_pairs={{0,3},{1,2},{2,5},{3,4},{4,7},{5,6},{6,1},{7,0},{8,11},{9,10},{10,... | collective-permute-start | bytes 200 | tf_op jit(solution)/shard_map/ppermute | solution.py:117
  59.4 0.6 copy-done.29
  60.1 0.7 copy-done.15
  60.9 0.7 copy-done.31
  61.7 0.7 copy-done.13
  62.5 0.7 copy-done.11
  63.4 0.6 copy-done.25
  64.2 0.6 copy-done.9
  65.0 0.6 copy-done.2
  65.7 0.7 copy-done.4
  66.5 0.2 fusion.174
  66.6 1.4 %collective-permute-start.19 = (f32[4,4]{1,0:T(4,128)S(1)}, f32[4,4]{1,0:T(4,128)S(1)}, u32[]{:S(2)}, u32[]{:S(2)}) collective-permute-start(f32[4,4]{1,0:T(4,128)S(1)} %pad_maximum_fusion.34), channel_id=1, source_target_pairs={{0,7},{1,6},{2,1},{3,0},{4,3},{5,2},{6,5},{7,4},{8,15},{9,14},{10,... | collective-permute-start | bytes 200 | tf_op jit(solution)/shard_map/ppermute | solution.py:117
  68.4 6.7 %collective-permute-done.19 = f32[4,4]{1,0:T(4,128)S(1)} collective-permute-done((f32[4,4]{1,0:T(4,128)S(1)}, f32[4,4]{1,0:T(4,128)S(1)}, u32[]{:S(2)}, u32[]{:S(2)}) %collective-permute-start.19) | collective-permute-done | bytes 96 | tf_op jit(solution)/shard_map/ppermute | solution.py:117
  75.5 7.4 %collective-permute-start.16 = (f32[4,16]{1,0:T(4,128)S(1)}, f32[4,16]{1,0:T(4,128)S(1)}, u32[]{:S(2)}, u32[]{:S(2)}) collective-permute-start(f32[4,16]{1,0:T(4,128)S(1)} %pad_maximum_fusion.31), channel_id=1, source_target_pairs={{0,253},{1,252},{2,255},{3,254},{4,249},{5,248},{6,251},{7,250},{8... | collective-permute-start | bytes 776 | tf_op jit(solution)/shard_map/ppermute | solution.py:117
  83.3 8.7 %collective-permute-start.14 = (f32[10,16,128]{2,1,0:T(8,128)S(1)}, f32[10,16,128]{2,1,0:T(8,128)S(1)}, u32[]{:S(2)}, u32[]{:S(2)}) collective-permute-start(f32[10,16,128]{2,1,0:T(8,128)S(1)} %slice_bitcast_fusion), channel_id=1, source_target_pairs={{0,252},{1,253},{2,254},{3,255},{4,248},{5,249},{6,250},{7,251},{8... | collective-permute-start | bytes 245768 | tf_op jit(solution)/shard_map/ppermute | solution.py:117
  92.0 2.2 %collective-permute-start.13 = (f32[20,4,16]{2,1,0:T(4,128)S(1)}, f32[20,4,16]{2,1,0:T(4,128)S(1)}, u32[]{:S(2)}, u32[]{:S(2)}) collective-permute-start(f32[20,4,16]{2,1,0:T(4,128)S(1)} %pad_maximum_fusion), channel_id=1, source_target_pairs={{0,1},{1,0},{2,3},{3,2},{4,5},{5,4},{6,7},{7,6},{8,9},{9,8},{10,11... | collective-permute-start | bytes 15368 | tf_op jit(solution)/shard_map/ppermute | solution.py:117
  95.1 4.9 %collective-permute-done.13 = f32[20,4,16]{2,1,0:T(4,128)S(1)} collective-permute-done((f32[20,4,16]{2,1,0:T(4,128)S(1)}, f32[20,4,16]{2,1,0:T(4,128)S(1)}, u32[]{:S(2)}, u32[]{:S(2)}) %collective-permute-start.13) | collective-permute-done | bytes 5152 | tf_op jit(solution)/shard_map/ppermute | solution.py:117
  101.8 2.0 %collective-permute-done.9 = f32[10,4,128]{2,1,0:T(4,128)S(1)} collective-permute-done((f32[10,4,128]{2,1,0:T(4,128)S(1)}, f32[10,4,128]{2,1,0:T(4,128)S(1)}, u32[]{:S(2)}, u32[]{:S(2)}) %collective-permute-start.9) | collective-permute-done | bytes 20512 | tf_op jit(solution)/shard_map/ppermute | solution.py:117
  103.8 1.1 collective-permute-start.10
  105.1 2.5 %collective-permute-done.10 = f32[10,4,128]{2,1,0:T(4,128)S(1)} collective-permute-done((f32[10,4,128]{2,1,0:T(4,128)S(1)}, f32[10,4,128]{2,1,0:T(4,128)S(1)}, u32[]{:S(2)}, u32[]{:S(2)}) %collective-permute-start.10) | collective-permute-done | bytes 20512 | tf_op jit(solution)/shard_map/ppermute | solution.py:117
  108.2 1.0 fusion.1
  110.3 0.7 copy-done.36
  111.2 0.7 copy-done.35
  113.5 0.5 copy-done.39
  114.0 0.8 copy-done.41
  (286 shorter events, 11.4 us)
Async XLA Ops:
  0.6 16.8 %copy-start = (f32[19,4,16,128]{3,2,1,0:T(8,128)S(1)}, f32[19,4,16,128]{3,2,1,0:T(8,128)}, u32[]{:S(2)}) copy-start(f32[19,4,16,128]{3,2,1,0:T(8,128)} %param.3) | copy-start | bytes 1867780
  1.8 20.1 %collective-permute-start.3 = (f32[1,16,128]{2,1,0:T(8,128)S(1)}, f32[1,16,128]{2,1,0:T(8,128)S(1)}, u32[]{:S(2)}, u32[]{:S(2)}) collective-permute-start(f32[1,16,128]{2,1,0:T(8,128)S(1)} %get-tuple-element.316), channel_id=1, source_target_pairs={{0,250},{1,251},{2,252},{3,253},{4,254},{5,255},{6,248},{7,249},{8... | collective-permute-start | bytes 24584 | tf_op jit(solution)/shard_map/ppermute | solution.py:117
  9.4 13.5 %collective-permute-start.2 = (f32[1,16,128]{2,1,0:T(8,128)S(1)}, f32[1,16,128]{2,1,0:T(8,128)S(1)}, u32[]{:S(2)}, u32[]{:S(2)}) collective-permute-start(f32[1,16,128]{2,1,0:T(8,128)S(1)} %get-tuple-element.316), channel_id=1, source_target_pairs={{0,252},{1,253},{2,254},{3,255},{4,248},{5,249},{6,250},{7,251},{8... | collective-permute-start | bytes 24584 | tf_op jit(solution)/shard_map/ppermute | solution.py:117
  10.7 12.2 %collective-permute-start.1 = (f32[1,16,128]{2,1,0:T(8,128)S(1)}, f32[1,16,128]{2,1,0:T(8,128)S(1)}, u32[]{:S(2)}, u32[]{:S(2)}) collective-permute-start(f32[1,16,128]{2,1,0:T(8,128)S(1)} %get-tuple-element.317), channel_id=1, source_target_pairs={{0,12},{1,13},{2,14},{3,15},{4,8},{5,9},{6,10},{7,11},{8,20},{9,21... | collective-permute-start | bytes 24584 | tf_op jit(solution)/shard_map/ppermute | solution.py:117
  12.6 10.3 %collective-permute-start = (f32[1,16,128]{2,1,0:T(8,128)S(1)}, f32[1,16,128]{2,1,0:T(8,128)S(1)}, u32[]{:S(2)}, u32[]{:S(2)}) collective-permute-start(f32[1,16,128]{2,1,0:T(8,128)S(1)} %get-tuple-element.317), channel_id=1, source_target_pairs={{0,14},{1,15},{2,8},{3,9},{4,10},{5,11},{6,12},{7,13},{8,22},{9,23... | collective-permute-start | bytes 24584 | tf_op jit(solution)/shard_map/ppermute | solution.py:117
  12.8 7.6 %collective-permute-start.6 = (f32[2,4,16]{2,1,0:T(4,128)S(1)}, f32[2,4,16]{2,1,0:T(4,128)S(1)}, u32[]{:S(2)}, u32[]{:S(2)}) collective-permute-start(f32[2,4,16]{2,1,0:T(4,128)S(1)} %pad_maximum_fusion.29), channel_id=1, source_target_pairs={{0,1},{1,0},{2,3},{3,2},{4,5},{5,4},{6,7},{7,6},{8,9},{9,8},{10,11... | collective-permute-start | bytes 1544 | tf_op jit(solution)/shard_map/ppermute | solution.py:117
  17.5 1.2 %copy-start.1 = (f32[19,4,16,128]{3,2,1,0:T(8,128)S(1)}, f32[19,4,16,128]{3,2,1,0:T(8,128)}, u32[]{:S(2)}) copy-start(f32[19,4,16,128]{3,2,1,0:T(8,128)} %param.4) | copy-start | bytes 1867780
  20.4 3.6 %collective-permute-start.5 = (f32[4,1,128]{2,0,1:T(4,128)S(1)}, f32[4,1,128]{2,0,1:T(4,128)S(1)}, u32[]{:S(2)}, u32[]{:S(2)}) collective-permute-start(f32[4,1,128]{2,0,1:T(4,128)S(1)} %bitcast.1679), channel_id=1, source_target_pairs={{0,6},{1,7},{2,0},{3,1},{4,2},{5,3},{6,4},{7,5},{8,14},{9,15},{10,... | collective-permute-start | bytes 6152 | tf_op jit(solution)/shard_map/ppermute | solution.py:117
  22.0 3.7 %collective-permute-start.4 = (f32[4,1,128]{2,1,0:T(1,128)S(1)}, f32[4,1,128]{2,1,0:T(1,128)S(1)}, u32[]{:S(2)}, u32[]{:S(2)}) collective-permute-start(f32[4,1,128]{2,1,0:T(1,128)S(1)} %get-tuple-element.315), channel_id=1, source_target_pairs={{0,2},{1,3},{2,4},{3,5},{4,6},{5,7},{6,0},{7,1},{8,10},{9,11},{10,... | collective-permute-start | bytes 6152 | tf_op jit(solution)/shard_map/ppermute | solution.py:117
  34.8 40.7 %collective-permute-start.12 = (f32[4,16]{1,0:T(4,128)S(1)}, f32[4,16]{1,0:T(4,128)S(1)}, u32[]{:S(2)}, u32[]{:S(2)}) collective-permute-start(f32[4,16]{1,0:T(4,128)S(1)} %pad_maximum_fusion.30), channel_id=1, source_target_pairs={{0,13},{1,12},{2,15},{3,14},{4,9},{5,8},{6,11},{7,10},{8,21},{9,20... | collective-permute-start | bytes 776 | tf_op jit(solution)/shard_map/ppermute | solution.py:117
  36.4 46.6 %collective-permute-start.11 = (f32[4,16]{1,0:T(4,128)S(1)}, f32[4,16]{1,0:T(4,128)S(1)}, u32[]{:S(2)}, u32[]{:S(2)}) collective-permute-start(f32[4,16]{1,0:T(4,128)S(1)} %pad_maximum_fusion.30), channel_id=1, source_target_pairs={{0,15},{1,14},{2,9},{3,8},{4,11},{5,10},{6,13},{7,12},{8,23},{9,22... | collective-permute-start | bytes 776 | tf_op jit(solution)/shard_map/ppermute | solution.py:117
  41.1 67.1 %collective-permute-start.8 = (f32[10,16,128]{2,1,0:T(8,128)S(1)}, f32[10,16,128]{2,1,0:T(8,128)}, u32[]{:S(2)}, u32[]{:S(2)}) collective-permute-start(f32[10,16,128]{2,1,0:T(8,128)S(1)} %slice_bitcast_fusion.1), channel_id=1, source_target_pairs={{0,12},{1,13},{2,14},{3,15},{4,8},{5,9},{6,10},{7,11},{8,20},{9,21... | collective-permute-start | bytes 245768 | tf_op jit(solution)/shard_map/ppermute | solution.py:117
  42.2 66.0 %collective-permute-start.7 = (f32[10,16,128]{2,1,0:T(8,128)S(1)}, f32[10,16,128]{2,1,0:T(8,128)}, u32[]{:S(2)}, u32[]{:S(2)}) collective-permute-start(f32[10,16,128]{2,1,0:T(8,128)S(1)} %slice_bitcast_fusion.1), channel_id=1, source_target_pairs={{0,14},{1,15},{2,8},{3,9},{4,10},{5,11},{6,12},{7,13},{8,22},{9,23... | collective-permute-start | bytes 245768 | tf_op jit(solution)/shard_map/ppermute | solution.py:117
  45.9 0.7 copy-start.37
  47.4 0.8 copy-start.7
  47.4 0.8 copy-start.8
  52.4 14.2 %collective-permute-start.18 = (f32[4,4]{1,0:T(4,128)S(1)}, f32[4,4]{1,0:T(4,128)S(1)}, u32[]{:S(2)}, u32[]{:S(2)}) collective-permute-start(f32[4,4]{1,0:T(4,128)S(1)} %pad_maximum_fusion.32), channel_id=1, source_target_pairs={{0,3},{1,2},{2,5},{3,4},{4,7},{5,6},{6,1},{7,0},{8,11},{9,10},{10,... | collective-permute-start | bytes 200 | tf_op jit(solution)/shard_map/ppermute | solution.py:117
  59.3 0.8 copy-start.29
  59.3 0.8 copy-start.30
  60.0 0.8 copy-start.15
  60.1 0.8 copy-start.16
  60.1 0.8 copy-start.23
  60.1 0.8 copy-start.24
  60.9 0.8 copy-start.31
  60.9 0.8 copy-start.32
  60.9 0.8 copy-start.33
  60.9 0.8 copy-start.34
  61.7 0.8 copy-start.13
  61.7 0.8 copy-start.14
  61.7 0.8 copy-start.21
  61.7 0.8 copy-start.22
  62.5 0.8 copy-start.11
  62.5 0.8 copy-start.12
  62.5 0.8 copy-start.19
  62.5 0.8 copy-start.20
  63.3 0.8 copy-start.25
  63.3 0.8 copy-start.26
  63.3 0.8 copy-start.27
  63.3 0.8 copy-start.28
  64.1 0.8 copy-start.9
  64.1 0.8 copy-start.10
  64.1 0.8 copy-start.17
  64.1 0.8 copy-start.18
  64.9 0.8 copy-start.2
  64.9 0.8 copy-start.3
  64.9 0.8 copy-start.6
  65.7 0.8 copy-start.4
  65.7 0.8 copy-start.5
  66.6 8.5 %collective-permute-start.19 = (f32[4,4]{1,0:T(4,128)S(1)}, f32[4,4]{1,0:T(4,128)S(1)}, u32[]{:S(2)}, u32[]{:S(2)}) collective-permute-start(f32[4,4]{1,0:T(4,128)S(1)} %pad_maximum_fusion.34), channel_id=1, source_target_pairs={{0,7},{1,6},{2,1},{3,0},{4,3},{5,2},{6,5},{7,4},{8,15},{9,14},{10,... | collective-permute-start | bytes 200 | tf_op jit(solution)/shard_map/ppermute | solution.py:117
  75.1 8.2 %collective-permute-start.17 = (f32[4,16]{1,0:T(4,128)S(1)}, f32[4,16]{1,0:T(4,128)S(1)}, u32[]{:S(2)}, u32[]{:S(2)}) collective-permute-start(f32[4,16]{1,0:T(4,128)S(1)} %pad_maximum_fusion.31), channel_id=1, source_target_pairs={{0,251},{1,250},{2,253},{3,252},{4,255},{5,254},{6,249},{7,248},{8... | collective-permute-start | bytes 776 | tf_op jit(solution)/shard_map/ppermute | solution.py:117
  75.5 16.5 %collective-permute-start.16 = (f32[4,16]{1,0:T(4,128)S(1)}, f32[4,16]{1,0:T(4,128)S(1)}, u32[]{:S(2)}, u32[]{:S(2)}) collective-permute-start(f32[4,16]{1,0:T(4,128)S(1)} %pad_maximum_fusion.31), channel_id=1, source_target_pairs={{0,253},{1,252},{2,255},{3,254},{4,249},{5,248},{6,251},{7,250},{8... | collective-permute-start | bytes 776 | tf_op jit(solution)/shard_map/ppermute | solution.py:117
  82.9 26.5 %collective-permute-start.15 = (f32[10,16,128]{2,1,0:T(8,128)S(1)}, f32[10,16,128]{2,1,0:T(8,128)S(1)}, u32[]{:S(2)}, u32[]{:S(2)}) collective-permute-start(f32[10,16,128]{2,1,0:T(8,128)S(1)} %slice_bitcast_fusion), channel_id=1, source_target_pairs={{0,250},{1,251},{2,252},{3,253},{4,254},{5,255},{6,248},{7,249},{8... | collective-permute-start | bytes 245768 | tf_op jit(solution)/shard_map/ppermute | solution.py:117
  83.3 26.1 %collective-permute-start.14 = (f32[10,16,128]{2,1,0:T(8,128)S(1)}, f32[10,16,128]{2,1,0:T(8,128)S(1)}, u32[]{:S(2)}, u32[]{:S(2)}) collective-permute-start(f32[10,16,128]{2,1,0:T(8,128)S(1)} %slice_bitcast_fusion), channel_id=1, source_target_pairs={{0,252},{1,253},{2,254},{3,255},{4,248},{5,249},{6,250},{7,251},{8... | collective-permute-start | bytes 245768 | tf_op jit(solution)/shard_map/ppermute | solution.py:117
  92.0 8.0 %collective-permute-start.13 = (f32[20,4,16]{2,1,0:T(4,128)S(1)}, f32[20,4,16]{2,1,0:T(4,128)S(1)}, u32[]{:S(2)}, u32[]{:S(2)}) collective-permute-start(f32[20,4,16]{2,1,0:T(4,128)S(1)} %pad_maximum_fusion), channel_id=1, source_target_pairs={{0,1},{1,0},{2,3},{3,2},{4,5},{5,4},{6,7},{7,6},{8,9},{9,8},{10,11... | collective-permute-start | bytes 15368 | tf_op jit(solution)/shard_map/ppermute | solution.py:117
  100.0 3.8 %collective-permute-start.9 = (f32[10,4,128]{2,1,0:T(4,128)S(1)}, f32[10,4,128]{2,1,0:T(4,128)S(1)}, u32[]{:S(2)}, u32[]{:S(2)}) collective-permute-start(f32[10,4,128]{2,1,0:T(4,128)S(1)} %bitcast.1653), channel_id=1, source_target_pairs={{0,2},{1,3},{2,4},{3,5},{4,6},{5,7},{6,0},{7,1},{8,10},{9,11},{10,... | collective-permute-start | bytes 61448 | tf_op jit(solution)/shard_map/ppermute | solution.py:117
  103.8 3.8 %collective-permute-start.10 = (f32[10,4,128]{2,1,0:T(4,128)S(1)}, f32[10,4,128]{2,1,0:T(4,128)S(1)}, u32[]{:S(2)}, u32[]{:S(2)}) collective-permute-start(f32[10,4,128]{2,1,0:T(4,128)S(1)} %bitcast.1652), channel_id=1, source_target_pairs={{0,6},{1,7},{2,0},{3,1},{4,2},{5,3},{6,4},{7,5},{8,14},{9,15},{10,... | collective-permute-start | bytes 61448 | tf_op jit(solution)/shard_map/ppermute | solution.py:117
  107.7 2.5 %copy-start.40 = (f32[19,4,16,128]{3,2,1,0:T(8,128)S(1)}, f32[19,4,16,128]{3,2,1,0:T(8,128)}, u32[]{:S(2)}) copy-start(f32[19,4,16,128]{3,2,1,0:T(8,128)} %constant_dynamic-update-slice_fusion.78) | copy-start | bytes 1867780
  108.2 2.1 %copy-start.38 = (f32[19,4,16,128]{3,2,1,0:T(8,128)S(1)}, f32[19,4,16,128]{3,2,1,0:T(8,128)}, u32[]{:S(2)}) copy-start(f32[19,4,16,128]{3,2,1,0:T(8,128)} %get-tuple-element.8) | copy-start | bytes 1867780
  110.2 0.8 copy-start.36
  111.1 0.7 copy-start.35
  113.1 0.8 copy-start.39
  114.0 0.8 copy-start.41

commit v2 on v1

--- a/solution.py
+++ b/solution.py
@@ -158,8 +158,8 @@
 
     vel = [VELOCITIES[n % 19] for n in range(38)]
 
-    def pick(cond):
-        return [n for n in range(38) if cond(vel[n])]
+    def pick(cond, among=range(38)):
+        return [n for n in among if cond(vel[n])]
 
     x_up = pick(lambda c: c[0] == 1)
     x_dn = pick(lambda c: c[0] == -1)
@@ -167,50 +167,58 @@
     y_dn = pick(lambda c: c[1] == -1)
     z_up = pick(lambda c: c[2] == 1)
     z_dn = pick(lambda c: c[2] == -1)
-    xz = {(cx, cz): pick(lambda c, cx=cx, cz=cz: c[0] == cx and c[2] == cz) for cx in (1, -1) for cz in (1, -1)}
-    yz = {(cy, cz): pick(lambda c, cy=cy, cz=cz: c[1] == cy and c[2] == cz) for cy in (1, -1) for cz in (1, -1)}
+    xz_up = pick(lambda c: c[2] != 0, x_up)
+    xz_dn = pick(lambda c: c[2] != 0, x_dn)
+    yz_up = pick(lambda c: c[2] != 0, y_up)
+    yz_dn = pick(lambda c: c[2] != 0, y_dn)
 
     def rows(idx):
         return jnp.stack([post[n] for n in idx])
 
-    last_x = rows(x_up)[:, -1]
-    first_x = rows(x_dn)[:, 0]
-    sends = [
-        (last_x, (1, q + 1, 0)),
-        (last_x, (1, q, 0)),
-        (first_x, (-1, -q, 0)),
-        (first_x, (-1, -q - 1, 0)),
-        (rows(y_up)[:, :, -1], (0, 1, 0)),
-        (rows(y_dn)[:, :, 0], (0, -1, 0)),
-        (rows(z_up)[:, :, :, -1], (0, 0, 1)),
-        (rows(z_dn)[:, :, :, 0], (0, 0, -1)),
-    ]
-    xz_keys = []
-    for (cx, cz), idx in xz.items():
-        plane = rows(idx)[:, -1 if cx == 1 else 0, :, -1 if cz == 1 else 0]
-        for dy in ((q + 1, q) if cx == 1 else (-q, -q - 1)):
-            sends.append((plane, (cx, dy, cz)))
-            xz_keys.append((cx, cz, dy))
-    yz_keys = []
-    for (cy, cz), idx in yz.items():
-        line = rows(idx)[:, :, -1 if cy == 1 else 0, -1 if cz == 1 else 0]
-        sends.append((line, (0, cy, cz)))
-        yz_keys.append((cy, cz))
-    got = exchange(sends)
-    xa, xb, xc, xd, hy_m, hy_p, hz_m, hz_p = got[:8]
-    xz_got = dict(zip(xz_keys, got[8 : 8 + len(xz_keys)]))
-    yz_got = dict(zip(yz_keys, got[8 + len(xz_keys) :]))
-
-    win_low = lax.dynamic_slice_in_dim(jnp.concatenate([xa, xb], axis=1), ny - rem - 1, ny + 2, 1)
-    win_high = lax.dynamic_slice_in_dim(jnp.concatenate([xc, xd], axis=1), rem - 1, ny + 2, 1)
-    xz_win = {}
-    for (cx, cz) in xz:
-        if cx == 1:
-            both = jnp.concatenate([xz_got[(cx, cz, q + 1)], xz_got[(cx, cz, q)]], axis=1)
-            xz_win[(cx, cz)] = lax.dynamic_slice_in_dim(both, ny - rem, ny, 1)
-        else:
-            both = jnp.concatenate([xz_got[(cx, cz, -q)], xz_got[(cx, cz, -q - 1)]], axis=1)
-            xz_win[(cx, cz)] = lax.dynamic_slice_in_dim(both, rem, ny, 1)
+    hz_m, hz_p = exchange(
+        [(rows(z_up)[:, :, :, -1], (0, 0, 1)), (rows(z_dn)[:, :, :, 0], (0, 0, -1))]
+    )
+
+    def zhalo(n):
+        return hz_m[z_up.index(n)] if vel[n][2] == 1 else hz_p[z_dn.index(n)]
+
+    def lanes(a):
+        return jnp.pad(a, ((0, 0), (0, nz - a.shape[1])))
+
+    def packed(face, extra):
+        return jnp.concatenate([face.reshape(-1, nz), lanes(jnp.stack(extra))], axis=0)
+
+    send_up = packed(rows(x_up)[:, -1], [zhalo(n)[-1] for n in xz_up])
+    send_dn = packed(rows(x_dn)[:, 0], [zhalo(n)[0] for n in xz_dn])
+    send_yu = packed(rows(y_up)[:, :, -1], [zhalo(n)[:, -1] for n in yz_up])
+    send_yd = packed(rows(y_dn)[:, :, 0], [zhalo(n)[:, 0] for n in yz_dn])
+    xa, xb, xc, xd, hy_m, hy_p = exchange(
+        [
+            (send_up, (1, q + 1, 0)),
+            (send_up, (1, q, 0)),
+            (send_dn, (-1, -q, 0)),
+            (send_dn, (-1, -q - 1, 0)),
+            (send_yu, (0, 1, 0)),
+            (send_yd, (0, -1, 0)),
+        ]
+    )
+
+    def unpack_x(got, count):
+        return got[: count * ny].reshape(count, ny, nz), got[count * ny :, :ny]
+
+    def unpack_y(got, count):
+        return got[: count * nx].reshape(count, nx, nz), got[count * nx :, :nx]
+
+    pa2, ca = unpack_x(xa, len(x_up))
+    pb2, cb = unpack_x(xb, len(x_up))
+    pc2, cc = unpack_x(xc, len(x_dn))
+    pd2, cd = unpack_x(xd, len(x_dn))
+    hy_m, cy_m = unpack_y(hy_m, len(y_up))
+    hy_p, cy_p = unpack_y(hy_p, len(y_dn))
+    win_low = lax.dynamic_slice_in_dim(jnp.concatenate([pa2, pb2], axis=1), ny - rem - 1, ny + 2, 1)
+    win_high = lax.dynamic_slice_in_dim(jnp.concatenate([pc2, pd2], axis=1), rem - 1, ny + 2, 1)
+    xzw_low = lax.dynamic_slice_in_dim(jnp.concatenate([ca, cb], axis=1), ny - rem, ny, 1)
+    xzw_high = lax.dynamic_slice_in_dim(jnp.concatenate([cc, cd], axis=1), rem, ny, 1)
 
     def shift_yz(t, cy, cz, ym, yp, zm, zp, corner):
         if cz == 1:
@@ -241,8 +249,10 @@
             zm = hz_m[z_up.index(n)][:, :, None]
         if cz == -1:
             zp = hz_p[z_dn.index(n)][:, :, None]
-        if cy != 0 and cz != 0:
-            corner = yz_got[(cy, cz)][yz[(cy, cz)].index(n)][:, None, None]
+        if cy == 1 and cz != 0:
+            corner = cy_m[yz_up.index(n)][:, None, None]
+        if cy == -1 and cz != 0:
+            corner = cy_p[yz_dn.index(n)][:, None, None]
         if cx == 0:
             results.append(shift_yz(post[n], cy, cz, ym, yp, zm, zp, corner))
             continue
@@ -262,11 +272,11 @@
         else:
             win = win_high[x_dn.index(n)]
         plane = win[1 - cy : 1 - cy + ny]
+        if cz != 0:
+            col = xzw_low[xz_up.index(n)] if cx == 1 else xzw_high[xz_dn.index(n)]
         if cz == 1:
-            col = xz_win[(cx, cz)][xz[(cx, cz)].index(n)]
             plane = jnp.concatenate([col[:, None], plane[:, :-1]], axis=1)
         elif cz == -1:
-            col = xz_win[(cx, cz)][xz[(cx, cz)].index(n)]
             plane = jnp.concatenate([plane[:, 1:], col[:, None]], axis=1)
         if cx == 1:
             results.append(jnp.concatenate([plane[None], inner], axis=0))

time: 116 us -> 87.7 us (0.76)
  the two profiles are of different devices: /device:TPU:2 before, /device:TPU:1 now
where the time goes in v2:
time: 87.7 us; the launch traced here: 87.1 us
  starting transfers between devices  37.1 us (42%)
  other arithmetic  23 us (26%)
  local copies, waits for them, and re-layouts  17.4 us (20%)
  waiting for transfers between devices  7.29 us (8%)
  between operations  2.21 us (3%)
    ppermute x14, starting transfers between devices, exchange(): got = lax.ppermute(joined, AXES, pairs)  37.1 us
    unnamed x54, other arithmetic  16.8 us
    unnamed x46, local copies, waits for them, and re-layouts  7.4 us
    ppermute x14, waiting for transfers between devices, exchange(): got = lax.ppermute(joined, AXES, pairs)  7.29 us
  transfers between devices with their start and end apart: 14, of which 3 were waited for; matrix products, arithmetic and copies ran while one was open for 15% of the time, Pallas kernels for 0%

profile of v2, /device:TPU:1, one launch (start us, length us, event | category | flops | bytes accessed | tf_op | source)
XLA Modules:
  0.0 87.1 jit_solution(3115722582969948616)
XLA Ops:
  0.6 1.2 %reduce_sum.24 = f32[4,16,128]{2,1,0:T(8,128)S(1)} reduce(f32[19,4,16,128]{3,2,1,0:T(8,128)} %param.4, f32[]{:T(128)} %constant.80.clone.1), dimensions={0}, to_apply=%region_1.0 | reduce | flops 147456 | bytes 655364 | tf_op jit(solution)/shard_map/reduce_sum | solution.py:133
  1.8 4.9 %collective-permute-start = (f32[1,16,128]{2,1,0:T(8,128)S(1)}, f32[1,16,128]{2,1,0:T(8,128)S(1)}, u32[]{:S(2)}, u32[]{:S(2)}) collective-permute-start(f32[1,16,128]{2,1,0:T(8,128)S(1)} %get-tuple-element.321), channel_id=1, source_target_pairs={{0,14},{1,15},{2,8},{3,9},{4,10},{5,11},{6,12},{7,13},{8,22},{9,23... | collective-permute-start | bytes 24584 | tf_op jit(solution)/shard_map/ppermute | solution.py:117
  6.8 0.4 collective-permute-start.1
  7.1 2.9 %collective-permute-start.2 = (f32[1,16,128]{2,1,0:T(8,128)S(1)}, f32[1,16,128]{2,1,0:T(8,128)S(1)}, u32[]{:S(2)}, u32[]{:S(2)}) collective-permute-start(f32[1,16,128]{2,1,0:T(8,128)S(1)} %get-tuple-element.320), channel_id=1, source_target_pairs={{0,252},{1,253},{2,254},{3,255},{4,248},{5,249},{6,250},{7,251},{8... | collective-permute-start | bytes 24584 | tf_op jit(solution)/shard_map/ppermute | solution.py:117
  10.0 2.7 %collective-permute-start.3 = (f32[1,16,128]{2,1,0:T(8,128)S(1)}, f32[1,16,128]{2,1,0:T(8,128)S(1)}, u32[]{:S(2)}, u32[]{:S(2)}) collective-permute-start(f32[1,16,128]{2,1,0:T(8,128)S(1)} %get-tuple-element.320), channel_id=1, source_target_pairs={{0,250},{1,251},{2,252},{3,253},{4,254},{5,255},{6,248},{7,249},{8... | collective-permute-start | bytes 24584 | tf_op jit(solution)/shard_map/ppermute | solution.py:117
  12.9 6.9 %collective-permute-start.6 = (f32[2,4,16]{2,1,0:T(4,128)S(1)}, f32[2,4,16]{2,1,0:T(4,128)S(1)}, u32[]{:S(2)}, u32[]{:S(2)}) collective-permute-start(f32[2,4,16]{2,1,0:T(4,128)S(1)} %pad_maximum_fusion.25), channel_id=1, source_target_pairs={{0,1},{1,0},{2,3},{3,2},{4,5},{5,4},{6,7},{7,6},{8,9},{9,8},{10,11... | collective-permute-start | bytes 1544 | tf_op jit(solution)/shard_map/ppermute | solution.py:117
  20.8 3.6 %collective-permute-start.5 = (f32[4,1,128]{2,1,0:T(1,128)S(1)}, f32[4,1,128]{2,1,0:T(1,128)S(1)}, u32[]{:S(2)}, u32[]{:S(2)}) collective-permute-start(f32[4,1,128]{2,1,0:T(1,128)S(1)} %get-tuple-element.318), channel_id=1, source_target_pairs={{0,6},{1,7},{2,0},{3,1},{4,2},{5,3},{6,4},{7,5},{8,14},{9,15},{10,... | collective-permute-start | bytes 6152 | tf_op jit(solution)/shard_map/ppermute | solution.py:117
  25.2 3.4 %collective-permute-done.4 = f32[4,1,128]{2,1,0:T(1,128)S(1)} collective-permute-done((f32[4,1,128]{2,1,0:T(1,128)S(1)}, f32[4,1,128]{2,1,0:T(1,128)S(1)}, u32[]{:S(2)}, u32[]{:S(2)}) %collective-permute-start.4) | collective-permute-done | bytes 2080 | tf_op jit(solution)/shard_map/ppermute | solution.py:117
  28.6 0.3 constant_dynamic-update-slice_fusion.97
  29.0 0.7 constant_dynamic-update-slice_fusion.58
  29.7 0.7 constant_dynamic-update-slice_fusion.57
  30.5 0.7 constant_dynamic-update-slice_fusion.55
  31.3 0.7 copy-done.12
  32.3 0.7 copy-done.13
  33.0 0.7 copy-done.15
  34.0 0.9 %copy.529 = f32[10,4,16,1]{2,1,0,3:T(4,128)} copy(f32[10,4,16,1]{3,2,0,1:T(8,128)S(1)} %slice.1307) | data formatting | bytes 5120 | tf_op jit(solution)/shard_map/slice | solution.py:179
  35.0 0.3 copy.544
  35.3 0.4 copy-done.11
  35.7 5.4 %collective-permute-start.7 = (f32[20,4,16]{2,1,0:T(4,128)S(1)}, f32[20,4,16]{2,1,0:T(4,128)S(1)}, u32[]{:S(2)}, u32[]{:S(2)}) collective-permute-start(f32[20,4,16]{2,1,0:T(4,128)S(1)} %pad_maximum_fusion.2), channel_id=1, source_target_pairs={{0,1},{1,0},{2,3},{3,2},{4,5},{5,4},{6,7},{7,6},{8,9},{9,8},{10,11... | collective-permute-start | bytes 15368 | tf_op jit(solution)/shard_map/ppermute | solution.py:117
  41.1 0.6 constant_dynamic-update-slice_fusion.54
  41.7 0.6 constant_dynamic-update-slice_fusion.53
  42.4 0.6 constant_dynamic-update-slice_fusion.52
  43.0 0.6 slice_bitcast_fusion
  43.6 0.6 slice_bitcast_fusion.9
  44.3 0.3 copy-done.14
  44.9 0.2 multiply_subtract_fusion.3
  45.4 0.7 copy-done.9
  46.2 0.2 fusion.62
  46.5 0.7 copy-done.7
  47.5 0.6 copy-done.5
  48.3 0.6 copy-done.3
  49.0 0.7 copy-done.2
  49.8 0.9 %slice.1344 = f32[10,4,1,128]{3,2,0,1:T(1,128)S(1)} slice(f32[10,4,16,128]{3,2,0,1:T(8,128)} %copy-done.16), slice={[0:10], [0:4], [0:1], [0:128]} | slice | bytes 40960 | tf_op jit(solution)/shard_map/slice | solution.py:194
  50.7 0.9 %slice.1323 = f32[10,4,1,128]{3,2,0,1:T(1,128)S(1)} slice(f32[10,4,16,128]{3,2,0,1:T(8,128)} %copy-done.15), slice={[0:10], [0:4], [15:16], [0:128]} | slice | bytes 40960 | tf_op jit(solution)/shard_map/slice | solution.py:193
  51.7 0.9 %slice.1378 = f32[10,1,16,128]{3,2,1,0:T(8,128)S(1)} slice(f32[10,4,16,128]{3,2,1,0:T(8,128)} %get-tuple-element.122), slice={[0:10], [0:1], [0:16], [0:128]} | slice | bytes 163840 | tf_op jit(solution)/shard_map/slice | solution.py:192
  52.6 1.6 %collective-permute-start.12 = (f32[164,128]{1,0:T(8,128)S(1)}, f32[164,128]{1,0:T(8,128)S(1)}, u32[]{:S(2)}, u32[]{:S(2)}) collective-permute-start(f32[164,128]{1,0:T(8,128)S(1)} %pad_maximum_fusion.1), channel_id=1, source_target_pairs={{0,252},{1,253},{2,254},{3,255},{4,248},{5,249},{6,250},{7,251},{8... | collective-permute-start | bytes 251912 | tf_op jit(solution)/shard_map/ppermute | solution.py:117
  54.2 0.5 collective-permute-start.13
  54.8 3.4 %collective-permute-start.8 = (f32[164,128]{1,0:T(8,128)S(1)}, f32[164,128]{1,0:T(8,128)S(1)}, u32[]{:S(2)}, u32[]{:S(2)}) collective-permute-start(f32[164,128]{1,0:T(8,128)S(1)} %pad_maximum_fusion), channel_id=1, source_target_pairs={{0,14},{1,15},{2,8},{3,9},{4,10},{5,11},{6,12},{7,13},{8,22},{9,23... | collective-permute-start | bytes 251912 | tf_op jit(solution)/shard_map/ppermute | solution.py:117
  58.2 1.6 %collective-permute-start.9 = (f32[164,128]{1,0:T(8,128)S(1)}, f32[164,128]{1,0:T(8,128)S(1)}, u32[]{:S(2)}, u32[]{:S(2)}) collective-permute-start(f32[164,128]{1,0:T(8,128)S(1)} %pad_maximum_fusion), channel_id=1, source_target_pairs={{0,12},{1,13},{2,14},{3,15},{4,8},{5,9},{6,10},{7,11},{8,20},{9,21... | collective-permute-start | bytes 251912 | tf_op jit(solution)/shard_map/ppermute | solution.py:117
  60.3 3.0 %collective-permute-start.11 = (f32[44,128]{1,0:T(8,128)S(1)}, f32[44,128]{1,0:T(8,128)S(1)}, u32[]{:S(2)}, u32[]{:S(2)}) collective-permute-start(f32[44,128]{1,0:T(8,128)S(1)} %pad_maximum_fusion.24), channel_id=1, source_target_pairs={{0,6},{1,7},{2,0},{3,1},{4,2},{5,3},{6,4},{7,5},{8,14},{9,15},{10,... | collective-permute-start | bytes 67592 | tf_op jit(solution)/shard_map/ppermute | solution.py:117
  63.3 0.2 slice_reduce_fusion.8
  63.5 0.2 slice_reduce_fusion.7
  63.7 0.2 slice_reduce_fusion.6
  63.9 0.2 slice_reduce_fusion.9
  66.2 3.7 %collective-permute-done.10 = f32[44,128]{1,0:T(8,128)S(1)} collective-permute-done((f32[44,128]{1,0:T(8,128)S(1)}, f32[44,128]{1,0:T(8,128)S(1)}, u32[]{:S(2)}, u32[]{:S(2)}) %collective-permute-start.10) | collective-permute-done | bytes 22560 | tf_op jit(solution)/shard_map/ppermute | solution.py:117
  73.5 0.9 %copy.643 = f32[19,4,16,128]{3,2,1,0:T(8,128)} copy(f32[19,4,16,128]{3,2,0,1:T(8,128)S(1)} %constant_dynamic-update-slice_fusion.79) | data formatting | bytes 1245184
  75.2 0.6 constant_dynamic-update-slice_fusion.77
  75.8 0.6 constant_dynamic-update-slice_fusion.76
  76.4 0.6 constant_dynamic-update-slice_fusion.75
  77.0 0.7 constant_dynamic-update-slice_fusion.74
  77.7 0.7 constant_dynamic-update-slice_fusion.73
  78.4 0.6 constant_dynamic-update-slice_fusion.72
  79.1 0.6 constant_dynamic-update-slice_fusion.71
  79.7 0.6 constant_dynamic-update-slice_fusion.70
  80.3 0.7 constant_dynamic-update-slice_fusion.69
  81.0 0.7 constant_dynamic-update-slice_fusion.68
  81.7 0.6 constant_dynamic-update-slice_fusion.67
  82.3 0.6 constant_dynamic-update-slice_fusion.66
  82.9 0.7 constant_dynamic-update-slice_fusion.65
  83.6 0.7 constant_dynamic-update-slice_fusion.64
  84.3 0.7 constant_dynamic-update-slice_fusion.63
  85.0 0.7 constant_dynamic-update-slice_fusion.62
  85.7 0.7 constant_dynamic-update-slice_fusion.61
  86.4 0.7 constant_dynamic-update-slice_fusion.60
  (225 shorter events, 10.1 us)
Async XLA Ops:
  0.6 20.0 %copy-start = (f32[19,4,16,128]{3,2,1,0:T(8,128)S(1)}, f32[19,4,16,128]{3,2,1,0:T(8,128)}, u32[]{:S(2)}) copy-start(f32[19,4,16,128]{3,2,1,0:T(8,128)} %param.3) | copy-start | bytes 1867780
  1.8 23.0 %collective-permute-start = (f32[1,16,128]{2,1,0:T(8,128)S(1)}, f32[1,16,128]{2,1,0:T(8,128)S(1)}, u32[]{:S(2)}, u32[]{:S(2)}) collective-permute-start(f32[1,16,128]{2,1,0:T(8,128)S(1)} %get-tuple-element.321), channel_id=1, source_target_pairs={{0,14},{1,15},{2,8},{3,9},{4,10},{5,11},{6,12},{7,13},{8,22},{9,23... | collective-permute-start | bytes 24584 | tf_op jit(solution)/shard_map/ppermute | solution.py:117
  6.8 18.2 %collective-permute-start.1 = (f32[1,16,128]{2,1,0:T(8,128)S(1)}, f32[1,16,128]{2,1,0:T(8,128)S(1)}, u32[]{:S(2)}, u32[]{:S(2)}) collective-permute-start(f32[1,16,128]{2,1,0:T(8,128)S(1)} %get-tuple-element.321), channel_id=1, source_target_pairs={{0,12},{1,13},{2,14},{3,15},{4,8},{5,9},{6,10},{7,11},{8,20},{9,21... | collective-permute-start | bytes 24584 | tf_op jit(solution)/shard_map/ppermute | solution.py:117
  7.1 17.8 %collective-permute-start.2 = (f32[1,16,128]{2,1,0:T(8,128)S(1)}, f32[1,16,128]{2,1,0:T(8,128)S(1)}, u32[]{:S(2)}, u32[]{:S(2)}) collective-permute-start(f32[1,16,128]{2,1,0:T(8,128)S(1)} %get-tuple-element.320), channel_id=1, source_target_pairs={{0,252},{1,253},{2,254},{3,255},{4,248},{5,249},{6,250},{7,251},{8... | collective-permute-start | bytes 24584 | tf_op jit(solution)/shard_map/ppermute | solution.py:117
  10.0 15.0 %collective-permute-start.3 = (f32[1,16,128]{2,1,0:T(8,128)S(1)}, f32[1,16,128]{2,1,0:T(8,128)S(1)}, u32[]{:S(2)}, u32[]{:S(2)}) collective-permute-start(f32[1,16,128]{2,1,0:T(8,128)S(1)} %get-tuple-element.320), channel_id=1, source_target_pairs={{0,250},{1,251},{2,252},{3,253},{4,254},{5,255},{6,248},{7,249},{8... | collective-permute-start | bytes 24584 | tf_op jit(solution)/shard_map/ppermute | solution.py:117
  12.9 7.9 %collective-permute-start.6 = (f32[2,4,16]{2,1,0:T(4,128)S(1)}, f32[2,4,16]{2,1,0:T(4,128)S(1)}, u32[]{:S(2)}, u32[]{:S(2)}) collective-permute-start(f32[2,4,16]{2,1,0:T(4,128)S(1)} %pad_maximum_fusion.25), channel_id=1, source_target_pairs={{0,1},{1,0},{2,3},{3,2},{4,5},{5,4},{6,7},{7,6},{8,9},{9,8},{10,11... | collective-permute-start | bytes 1544 | tf_op jit(solution)/shard_map/ppermute | solution.py:117
  19.9 8.7 %copy-start.1 = (f32[19,4,16,128]{3,2,1,0:T(8,128)S(1)}, f32[19,4,16,128]{3,2,1,0:T(8,128)}, u32[]{:S(2)}) copy-start(f32[19,4,16,128]{3,2,1,0:T(8,128)} %param.4) | copy-start | bytes 1867780
  20.8 4.4 %collective-permute-start.5 = (f32[4,1,128]{2,1,0:T(1,128)S(1)}, f32[4,1,128]{2,1,0:T(1,128)S(1)}, u32[]{:S(2)}, u32[]{:S(2)}) collective-permute-start(f32[4,1,128]{2,1,0:T(1,128)S(1)} %get-tuple-element.318), channel_id=1, source_target_pairs={{0,6},{1,7},{2,0},{3,1},{4,2},{5,3},{6,4},{7,5},{8,14},{9,15},{10,... | collective-permute-start | bytes 6152 | tf_op jit(solution)/shard_map/ppermute | solution.py:117
  24.8 3.7 %collective-permute-start.4 = (f32[4,1,128]{2,1,0:T(1,128)S(1)}, f32[4,1,128]{2,1,0:T(1,128)S(1)}, u32[]{:S(2)}, u32[]{:S(2)}) collective-permute-start(f32[4,1,128]{2,1,0:T(1,128)S(1)} %get-tuple-element.319), channel_id=1, source_target_pairs={{0,2},{1,3},{2,4},{3,5},{4,6},{5,7},{6,0},{7,1},{8,10},{9,11},{10,... | collective-permute-start | bytes 6152 | tf_op jit(solution)/shard_map/ppermute | solution.py:117
  31.2 0.7 copy-start.12
  32.3 0.7 copy-start.13
  33.0 0.7 copy-start.15
  33.0 0.9 copy-start.16
  35.0 0.7 copy-start.11
  35.7 16.9 %collective-permute-start.7 = (f32[20,4,16]{2,1,0:T(4,128)S(1)}, f32[20,4,16]{2,1,0:T(4,128)S(1)}, u32[]{:S(2)}, u32[]{:S(2)}) collective-permute-start(f32[20,4,16]{2,1,0:T(4,128)S(1)} %pad_maximum_fusion.2), channel_id=1, source_target_pairs={{0,1},{1,0},{2,3},{3,2},{4,5},{5,4},{6,7},{7,6},{8,9},{9,8},{10,11... | collective-permute-start | bytes 15368 | tf_op jit(solution)/shard_map/ppermute | solution.py:117
  43.6 1.0 %copy-start.14 = (f32[10,4,16,128]{3,2,0,1:T(8,128)S(1)}, f32[10,4,16,128]{3,2,0,1:T(8,128)}, u32[]{:S(2)}) copy-start(f32[10,4,16,128]{3,2,0,1:T(8,128)} %copy-done.13) | copy-start | bytes 983044
  45.3 0.8 copy-start.9
  45.4 0.8 copy-start.10
  46.5 0.8 copy-start.7
  46.5 0.8 copy-start.8
  47.4 0.8 copy-start.5
  47.4 0.8 copy-start.6
  48.1 0.8 copy-start.3
  48.1 0.8 copy-start.4
  48.9 0.8 copy-start.2
  52.6 18.6 %collective-permute-start.12 = (f32[164,128]{1,0:T(8,128)S(1)}, f32[164,128]{1,0:T(8,128)S(1)}, u32[]{:S(2)}, u32[]{:S(2)}) collective-permute-start(f32[164,128]{1,0:T(8,128)S(1)} %pad_maximum_fusion.1), channel_id=1, source_target_pairs={{0,252},{1,253},{2,254},{3,255},{4,248},{5,249},{6,250},{7,251},{8... | collective-permute-start | bytes 251912 | tf_op jit(solution)/shard_map/ppermute | solution.py:117
  54.2 17.0 %collective-permute-start.13 = (f32[164,128]{1,0:T(8,128)S(1)}, f32[164,128]{1,0:T(8,128)S(1)}, u32[]{:S(2)}, u32[]{:S(2)}) collective-permute-start(f32[164,128]{1,0:T(8,128)S(1)} %pad_maximum_fusion.1), channel_id=1, source_target_pairs={{0,250},{1,251},{2,252},{3,253},{4,254},{5,255},{6,248},{7,249},{8... | collective-permute-start | bytes 251912 | tf_op jit(solution)/shard_map/ppermute | solution.py:117
  54.8 17.0 %collective-permute-start.8 = (f32[164,128]{1,0:T(8,128)S(1)}, f32[164,128]{1,0:T(8,128)S(1)}, u32[]{:S(2)}, u32[]{:S(2)}) collective-permute-start(f32[164,128]{1,0:T(8,128)S(1)} %pad_maximum_fusion), channel_id=1, source_target_pairs={{0,14},{1,15},{2,8},{3,9},{4,10},{5,11},{6,12},{7,13},{8,22},{9,23... | collective-permute-start | bytes 251912 | tf_op jit(solution)/shard_map/ppermute | solution.py:117
  58.2 13.6 %collective-permute-start.9 = (f32[164,128]{1,0:T(8,128)S(1)}, f32[164,128]{1,0:T(8,128)S(1)}, u32[]{:S(2)}, u32[]{:S(2)}) collective-permute-start(f32[164,128]{1,0:T(8,128)S(1)} %pad_maximum_fusion), channel_id=1, source_target_pairs={{0,12},{1,13},{2,14},{3,15},{4,8},{5,9},{6,10},{7,11},{8,20},{9,21... | collective-permute-start | bytes 251912 | tf_op jit(solution)/shard_map/ppermute | solution.py:117
  60.3 5.6 %collective-permute-start.11 = (f32[44,128]{1,0:T(8,128)S(1)}, f32[44,128]{1,0:T(8,128)S(1)}, u32[]{:S(2)}, u32[]{:S(2)}) collective-permute-start(f32[44,128]{1,0:T(8,128)S(1)} %pad_maximum_fusion.24), channel_id=1, source_target_pairs={{0,6},{1,7},{2,0},{3,1},{4,2},{5,3},{6,4},{7,5},{8,14},{9,15},{10,... | collective-permute-start | bytes 67592 | tf_op jit(solution)/shard_map/ppermute | solution.py:117
  65.9 4.0 %collective-permute-start.10 = (f32[44,128]{1,0:T(8,128)S(1)}, f32[44,128]{1,0:T(8,128)S(1)}, u32[]{:S(2)}, u32[]{:S(2)}) collective-permute-start(f32[44,128]{1,0:T(8,128)S(1)} %pad_maximum_fusion.23), channel_id=1, source_target_pairs={{0,2},{1,3},{2,4},{3,5},{4,6},{5,7},{6,0},{7,1},{8,10},{9,11},{10,... | collective-permute-start | bytes 67592 | tf_op jit(solution)/shard_map/ppermute | solution.py:117

commit v3 on v2

--- a/solution.py
+++ b/solution.py
@@ -2,6 +2,8 @@
 import jax.numpy as jnp
 from jax import lax
 from jax.sharding import PartitionSpec as P
+from jax.experimental import pallas as pl
+from jax.experimental.pallas import tpu as pltpu
 
 VELOCITIES = [
     (0, 0, 0),
@@ -31,6 +33,7 @@
 SHIFT_MIN = 33
 SHIFT_MAX = 47
 AXES = ("gx", "gy", "gz")
+INTERPRET = False
 
 
 def lattice_weight(number):
@@ -91,6 +94,95 @@
     return (jnp.stack(f_posts), jnp.stack(g_posts))
 
 
+def collide_lists(f_pop, g_pop, order_field, laplace, slopes):
+    density = f_pop[0]
+    for number in range(1, 19):
+        density = density + f_pop[number]
+    chemical = (
+        BULK_COEF * (order_field * order_field * order_field - order_field) - STIFFNESS * laplace
+    )
+    forces = [chemical * slope for slope in slopes]
+    moments = []
+    for axis_id in range(3):
+        moment = jnp.zeros_like(density)
+        for number in range(19):
+            comp = VELOCITIES[number][axis_id]
+            if comp != 0:
+                moment = moment + comp * f_pop[number]
+        moments.append(moment)
+    flows = [(moments[axis_id] + 0.5 * forces[axis_id]) / density for axis_id in range(3)]
+    speed_sq = flows[0] * flows[0] + flows[1] * flows[1] + flows[2] * flows[2]
+    flow_force = flows[0] * forces[0] + flows[1] * forces[1] + flows[2] * forces[2]
+    f_posts = []
+    g_eqs = []
+    for number in range(19):
+        weight = lattice_weight(number)
+        proj_flow = along(number, flows, density)
+        proj_force = along(number, forces, density)
+        shape_term = 3.0 * proj_flow + 4.5 * proj_flow * proj_flow - 1.5 * speed_sq
+        f_eq = weight * density * (1.0 + shape_term)
+        source = (
+            (1.0 - 0.5 / TAU_FLUID)
+            * weight
+            * (3.0 * (proj_force - flow_force) + 9.0 * proj_flow * proj_force)
+        )
+        f_posts.append(f_pop[number] - (f_pop[number] - f_eq) / TAU_FLUID + source)
+        g_eqs.append(weight * (3.0 * chemical + order_field * shape_term))
+    rest_eq = order_field
+    for number in range(1, 19):
+        rest_eq = rest_eq - g_eqs[number]
+    g_eqs[0] = rest_eq
+    g_posts = [g_pop[number] - (g_pop[number] - g_eqs[number]) / TAU_ORDER for number in range(19)]
+    return (f_posts, g_posts)
+
+
+def collide_kernel(f_ref, g_ref, nb_ref, post_ref):
+    pops = f_ref.shape[0]
+    for x in range(f_ref.shape[1]):
+        f_planes = [f_ref[n, x] for n in range(pops)]
+        g_planes = [g_ref[n, x] for n in range(pops)]
+        slopes = [nb_ref[2 + a, x] for a in range(3)]
+        f_posts, g_posts = collide_lists(f_planes, g_planes, nb_ref[0, x], nb_ref[1, x], slopes)
+        for n in range(pops):
+            post_ref[n, x] = f_posts[n]
+            post_ref[pops + n, x] = g_posts[n]
+
+
+def stream_kernel(post_ref, xlow_ref, xhigh_ref, hym_ref, hyp_ref, col_ref, f_ref, g_ref):
+    pops = f_ref.shape[0]
+    nx, ny, nz = f_ref.shape[1:]
+    row = lax.broadcasted_iota(jnp.int32, (ny, nz), 0)
+    lane = lax.broadcasted_iota(jnp.int32, (ny, nz), 1)
+    vel = [VELOCITIES[n % pops] for n in range(2 * pops)]
+    x_up = [n for n in range(2 * pops) if vel[n][0] == 1]
+    x_dn = [n for n in range(2 * pops) if vel[n][0] == -1]
+    y_up = [n for n in range(2 * pops) if vel[n][1] == 1]
+    y_dn = [n for n in range(2 * pops) if vel[n][1] == -1]
+    z_any = [n for n in range(2 * pops) if vel[n][2] != 0]
+    for n in range(2 * pops):
+        cx, cy, cz = vel[n]
+        out = f_ref if n < pops else g_ref
+        for x in range(nx):
+            src = x - cx
+            if src < 0:
+                tile = xlow_ref[x_up.index(n)]
+            elif src >= nx:
+                tile = xhigh_ref[x_dn.index(n)]
+            else:
+                tile = post_ref[n, src]
+                if cy == 1:
+                    edge = jnp.broadcast_to(hym_ref[y_up.index(n), pl.ds(src, 1), :], (ny, nz))
+                    tile = jnp.where(row == 0, edge, pltpu.roll(tile, 1, 0))
+                elif cy == -1:
+                    edge = jnp.broadcast_to(hyp_ref[y_dn.index(n), pl.ds(src, 1), :], (ny, nz))
+                    tile = jnp.where(row == ny - 1, edge, pltpu.roll(tile, ny - 1, 0))
+            if cz == 1:
+                tile = jnp.where(lane == 0, col_ref[z_any.index(n), x], pltpu.roll(tile, 1, 1))
+            elif cz == -1:
+                tile = jnp.where(lane == nz - 1, col_ref[z_any.index(n), x], pltpu.roll(tile, nz - 1, 1))
+            out[n % pops, x] = tile
+
+
 def exchange(sends):
     sizes = [lax.axis_size(a) for a in AXES]
     groups = {}
@@ -153,8 +245,12 @@
     neigh_zp = jnp.concatenate([phi[:, :, 1:], jnp.transpose(pzp, (1, 2, 0))], axis=2)
     laplace = neigh_xm + neigh_xp + neigh_ym + neigh_yp + neigh_zm + neigh_zp - 6.0 * phi
     slopes = [0.5 * (neigh_xp - neigh_xm), 0.5 * (neigh_yp - neigh_ym), 0.5 * (neigh_zp - neigh_zm)]
-    f_post, g_post = collide(f_pop, g_pop, phi, laplace, slopes)
-    post = jnp.concatenate([f_post, g_post], axis=0)
+    nb = jnp.stack([phi, laplace] + slopes)
+    post = pl.pallas_call(
+        collide_kernel,
+        out_shape=jax.ShapeDtypeStruct((2 * f_pop.shape[0], nx, ny, nz), jnp.float32),
+        interpret=INTERPRET,
+    )(f_pop, g_pop, nb)
 
     vel = [VELOCITIES[n % 19] for n in range(38)]
 
@@ -220,70 +316,38 @@
     xzw_low = lax.dynamic_slice_in_dim(jnp.concatenate([ca, cb], axis=1), ny - rem, ny, 1)
     xzw_high = lax.dynamic_slice_in_dim(jnp.concatenate([cc, cd], axis=1), rem, ny, 1)
 
-    def shift_yz(t, cy, cz, ym, yp, zm, zp, corner):
-        if cz == 1:
-            t = jnp.concatenate([zm, t[:, :, :-1]], axis=2)
-        elif cz == -1:
-            t = jnp.concatenate([t[:, :, 1:], zp], axis=2)
-        if cy != 0:
-            edge = ym if cy == 1 else yp
-            if cz == 1:
-                edge = jnp.concatenate([corner, edge[:, :, :-1]], axis=2)
-            elif cz == -1:
-                edge = jnp.concatenate([edge[:, :, 1:], corner], axis=2)
+    xlow = jnp.stack([win_low[a, 1 - vel[n][1] : 1 - vel[n][1] + ny] for a, n in enumerate(x_up)])
+    xhigh = jnp.stack([win_high[a, 1 - vel[n][1] : 1 - vel[n][1] + ny] for a, n in enumerate(x_dn)])
+    z_any = pick(lambda c: c[2] != 0)
+    cols = []
+    for n in z_any:
+        cx, cy, cz = vel[n]
+        per_x = []
+        for x in range(nx):
+            src_x = x - cx
+            if src_x < 0:
+                per_x.append(xzw_low[xz_up.index(n)])
+                continue
+            if src_x >= nx:
+                per_x.append(xzw_high[xz_dn.index(n)])
+                continue
+            line = zhalo(n)[src_x]
             if cy == 1:
-                t = jnp.concatenate([edge, t[:, :-1]], axis=1)
-            else:
-                t = jnp.concatenate([t[:, 1:], edge], axis=1)
-        return t
-
-    results = []
-    for n in range(38):
-        cx, cy, cz = vel[n]
-        ym = yp = zm = zp = corner = None
-        if cy == 1:
-            ym = hy_m[y_up.index(n)][:, None, :]
-        if cy == -1:
-            yp = hy_p[y_dn.index(n)][:, None, :]
-        if cz == 1:
-            zm = hz_m[z_up.index(n)][:, :, None]
-        if cz == -1:
-            zp = hz_p[z_dn.index(n)][:, :, None]
-        if cy == 1 and cz != 0:
-            corner = cy_m[yz_up.index(n)][:, None, None]
-        if cy == -1 and cz != 0:
-            corner = cy_p[yz_dn.index(n)][:, None, None]
-        if cx == 0:
-            results.append(shift_yz(post[n], cy, cz, ym, yp, zm, zp, corner))
-            continue
-        sl = slice(0, nx - 1) if cx == 1 else slice(1, nx)
-        inner = shift_yz(
-            post[n][sl],
-            cy,
-            cz,
-            None if ym is None else ym[sl],
-            None if yp is None else yp[sl],
-            None if zm is None else zm[sl],
-            None if zp is None else zp[sl],
-            corner,
-        )
-        if cx == 1:
-            win = win_low[x_up.index(n)]
-        else:
-            win = win_high[x_dn.index(n)]
-        plane = win[1 - cy : 1 - cy + ny]
-        if cz != 0:
-            col = xzw_low[xz_up.index(n)] if cx == 1 else xzw_high[xz_dn.index(n)]
-        if cz == 1:
-            plane = jnp.concatenate([col[:, None], plane[:, :-1]], axis=1)
-        elif cz == -1:
-            plane = jnp.concatenate([plane[:, 1:], col[:, None]], axis=1)
-        if cx == 1:
-            results.append(jnp.concatenate([plane[None], inner], axis=0))
-        else:
-            results.append(jnp.concatenate([inner, plane[None]], axis=0))
-    f_new = jnp.stack(results[:19])
-    g_new = jnp.stack(results[19:])
+                line = jnp.concatenate([cy_m[yz_up.index(n), src_x : src_x + 1], line[:-1]])
+            elif cy == -1:
+                line = jnp.concatenate([line[1:], cy_p[yz_dn.index(n), src_x : src_x + 1]])
+            per_x.append(line)
+        cols.append(jnp.stack(per_x))
+    cols = jnp.broadcast_to(jnp.stack(cols)[:, :, :, None], (len(z_any), nx, ny, nz))
+    pops = f_pop.shape[0]
+    f_new, g_new = pl.pallas_call(
+        stream_kernel,
+        out_shape=(
+            jax.ShapeDtypeStruct((pops, nx, ny, nz), jnp.float32),
+            jax.ShapeDtypeStruct((pops, nx, ny, nz), jnp.float32),
+        ),
+        interpret=INTERPRET,
+    )(post, xlow, xhigh, hy_m, hy_p, cols)
     return (f_new, g_new)
 
 

time: 87.7 us -> 86.1 us (0.982)
  local copies, waits for them, and re-layouts: 17.4 us -> 9.09 us
  Pallas kernels: 0 us -> 5.82 us
  waiting for transfers between devices: 7.29 us -> 5.03 us
  starting transfers between devices: 37.1 us -> 39.3 us
  other arithmetic: 23 us -> 24.4 us
    another operation x2 -> x34, other arithmetic: 0.78 us -> 22.4 us  [the longest x32 22.3 us: local(): cols.append(jnp.stack(per_x))]
    unnamed x54 -> x22, other arithmetic: 16.8 us -> 0.45 us
    pallas_call x0 -> x2, Pallas kernels: none -> 5.82 us  [the longest x1 3.03 us: local(): pl.pallas_call(collide_kernel, out_shape=jax.ShapeDtypeStruct((2 * f_pop....]
    unnamed x46 -> x36, local copies, waits for them, and re-layouts: 7.4 us -> 1.72 us
    another operation x33 -> x5, local copies, waits for them, and re-layouts: 2.64 us -> 0.04 us  [the longest x3 0.03 us: rows(): return jnp.stack([post[n] for n in idx])]
    ppermute x14, waiting for transfers between devices: 7.29 us -> 5.03 us  [exchange(): got = lax.ppermute(joined, AXES, pairs)]
    ppermute x14, starting transfers between devices: 37.1 us -> 39.3 us  [exchange(): got = lax.ppermute(joined, AXES, pairs)]
    squeeze x2 -> x0, other arithmetic: 1.27 us -> none  [collide(): g_pop[number] - (g_pop[number] - g_eqs[number]) / TAU_ORDER]
  transfers between devices with their start and end apart: 14 -> 14, of which waited for: 3 -> 4; matrix products, arithmetic and copies ran while one was open for 15% -> 32% of each run, Pallas kernels for 0% -> 0%
where the time goes in v3:
time: 86.1 us; the launch traced here: 85.6 us
  starting transfers between devices  39.3 us (46%)
  other arithmetic  24.4 us (28%)
  local copies, waits for them, and re-layouts  9.09 us (11%)
  Pallas kernels  5.82 us (7%)
  waiting for transfers between devices  5.03 us (6%)
  between operations  1.92 us (2%)
    ppermute x14, starting transfers between devices, exchange(): got = lax.ppermute(joined, AXES, pairs)  39.3 us
    another operation x32, other arithmetic, local(): cols.append(jnp.stack(per_x))  22.3 us
    ppermute x14, waiting for transfers between devices, exchange(): got = lax.ppermute(joined, AXES, pairs)  5.03 us
    pallas_call x1, Pallas kernels, local(): pl.pallas_call(collide_kernel, out_shape=jax.ShapeDtypeStruct((2 * f_pop....  3.03 us
    pallas_call x1, Pallas kernels, local(): pl.pallas_call(stream_kernel, out_shape=(jax.ShapeDtypeStruct((pops, nx,...  2.79 us
    unnamed x36, local copies, waits for them, and re-layouts  1.72 us
  transfers between devices with their start and end apart: 14, of which 4 were waited for; matrix products, arithmetic and copies ran while one was open for 32% of the time, Pallas kernels for 0%

profile of v3, /device:TPU:1, one launch (start us, length us, event | category | flops | bytes accessed | tf_op | source)
XLA Modules:
  0.0 85.6 jit_solution(7799832383261454792)
XLA Ops:
  0.6 1.1 %reduce_sum.9 = f32[4,16,128]{2,1,0:T(8,128)S(1)} reduce(f32[19,4,16,128]{3,2,1,0:T(8,128)} %g_ref.1, f32[]{:T(128)} %constant.17.clone.1), dimensions={0}, to_apply=%region_0.0 | reduce | flops 147456 | bytes 655364 | tf_op jit(solution)/shard_map/reduce_sum | solution.py:225
  1.8 4.9 %collective-permute-start = (f32[1,16,128]{2,1,0:T(8,128)S(1)}, f32[1,16,128]{2,1,0:T(8,128)S(1)}, u32[]{:S(2)}, u32[]{:S(2)}) collective-permute-start(f32[1,16,128]{2,1,0:T(8,128)S(1)} %get-tuple-element.132), channel_id=1, source_target_pairs={{0,14},{1,15},{2,8},{3,9},{4,10},{5,11},{6,12},{7,13},{8,22},{9,23... | collective-permute-start | bytes 24584 | tf_op jit(solution)/shard_map/ppermute | solution.py:209
  6.7 0.4 collective-permute-start.1
  7.1 2.9 %collective-permute-start.2 = (f32[1,16,128]{2,1,0:T(8,128)S(1)}, f32[1,16,128]{2,1,0:T(8,128)S(1)}, u32[]{:S(2)}, u32[]{:S(2)}) collective-permute-start(f32[1,16,128]{2,1,0:T(8,128)S(1)} %get-tuple-element.133), channel_id=1, source_target_pairs={{0,252},{1,253},{2,254},{3,255},{4,248},{5,249},{6,250},{7,251},{8... | collective-permute-start | bytes 24584 | tf_op jit(solution)/shard_map/ppermute | solution.py:209
  10.0 2.7 %collective-permute-start.3 = (f32[1,16,128]{2,1,0:T(8,128)S(1)}, f32[1,16,128]{2,1,0:T(8,128)S(1)}, u32[]{:S(2)}, u32[]{:S(2)}) collective-permute-start(f32[1,16,128]{2,1,0:T(8,128)S(1)} %get-tuple-element.133), channel_id=1, source_target_pairs={{0,250},{1,251},{2,252},{3,253},{4,254},{5,255},{6,248},{7,249},{8... | collective-permute-start | bytes 24584 | tf_op jit(solution)/shard_map/ppermute | solution.py:209
  12.9 6.9 %collective-permute-start.6 = (f32[2,4,16]{2,1,0:T(4,128)S(1)}, f32[2,4,16]{2,1,0:T(4,128)S(1)}, u32[]{:S(2)}, u32[]{:S(2)}) collective-permute-start(f32[2,4,16]{2,1,0:T(4,128)S(1)} %pad_maximum_fusion.13), channel_id=1, source_target_pairs={{0,1},{1,0},{2,3},{3,2},{4,5},{5,4},{6,7},{7,6},{8,9},{9,8},{10,11... | collective-permute-start | bytes 1544 | tf_op jit(solution)/shard_map/ppermute | solution.py:209
  20.5 0.2 collective-permute-done.6
  20.7 3.6 %collective-permute-start.5 = (f32[4,1,128]{2,1,0:T(1,128)S(1)}, f32[4,1,128]{2,1,0:T(1,128)S(1)}, u32[]{:S(2)}, u32[]{:S(2)}) collective-permute-start(f32[4,1,128]{2,1,0:T(1,128)S(1)} %get-tuple-element.129), channel_id=1, source_target_pairs={{0,6},{1,7},{2,0},{3,1},{4,2},{5,3},{6,4},{7,5},{8,14},{9,15},{10,... | collective-permute-start | bytes 6152 | tf_op jit(solution)/shard_map/ppermute | solution.py:209
  24.7 0.4 collective-permute-done.5
  25.1 3.2 %collective-permute-done.4 = f32[4,1,128]{2,1,0:T(1,128)S(1)} collective-permute-done((f32[4,1,128]{2,1,0:T(1,128)S(1)}, f32[4,1,128]{2,1,0:T(1,128)S(1)}, u32[]{:S(2)}, u32[]{:S(2)}) %collective-permute-start.4) | collective-permute-done | bytes 2080 | tf_op jit(solution)/shard_map/ppermute | solution.py:209
  28.5 0.7 copy-done.1
  29.1 3.0 %shard_map.50.post_ref = f32[38,4,16,128]{3,2,1,0:T(8,128)} custom-call(f32[19,4,16,128]{3,2,1,0:T(8,128)} %f_ref.1, f32[19,4,16,128]{3,2,1,0:T(8,128)} %g_ref.1, f32[5,4,16,128]{3,2,1,0:T(8,128)} %copy-done.1), custom_call_target="tpu_custom_call" | custom-call | tf_op jit(solution)/shard_map/pallas_call | solution.py:249
  32.2 0.9 %constant_dynamic-update-slice_fusion.56 = (f32[10,4,16,128]{3,2,1,0:T(8,128)S(1)}, f32[10,4,16,128]{3,2,1,0:T(8,128)S(1)}) fusion(f32[38,4,16,128]{3,2,1,0:T(8,128)} %shard_map.50.post_ref), kind=kLoop, calls=%fused_computation.62 | loop fusion | bytes 131072
  33.1 1.2 %fusion.7 = (f32[5,4,16,128]{3,2,1,0:T(8,128)S(1)}, f32[5,4,16,128]{3,2,1,0:T(8,128)S(1)}, f32[5,4,16,128]{3,2,1,0:T(8,128)S(1)}, f32[5,4,16,128]{3,2,1,0:T(8,128)S(1)}) fusion(f32[38,4,16,128]{3,2,1,0:T(8,128)} %shard_map.50.post_ref), kind=kLoop, calls=%fused_computation.285 | loop fusion | bytes 1310720 | tf_op jit(solution)/shard_map/slice | solution.py:272
  34.5 0.4 slice_reduce_fusion
  34.9 5.5 %collective-permute-start.7 = (f32[20,4,16]{2,1,0:T(4,128)S(1)}, f32[20,4,16]{2,1,0:T(4,128)S(1)}, u32[]{:S(2)}, u32[]{:S(2)}) collective-permute-start(f32[20,4,16]{2,1,0:T(4,128)S(1)} %pad_maximum_fusion.4), channel_id=1, source_target_pairs={{0,1},{1,0},{2,3},{3,2},{4,5},{5,4},{6,7},{7,6},{8,9},{9,8},{10,11... | collective-permute-start | bytes 15368 | tf_op jit(solution)/shard_map/ppermute | solution.py:209
  40.5 1.3 %collective-permute-done.7 = f32[20,4,16]{2,1,0:T(4,128)S(1)} collective-permute-done((f32[20,4,16]{2,1,0:T(4,128)S(1)}, f32[20,4,16]{2,1,0:T(4,128)S(1)}, u32[]{:S(2)}, u32[]{:S(2)}) %collective-permute-start.7) | collective-permute-done | bytes 5152 | tf_op jit(solution)/shard_map/ppermute | solution.py:209
  41.7 2.2 %collective-permute-start.10 = (f32[164,128]{1,0:T(8,128)S(1)}, f32[164,128]{1,0:T(8,128)S(1)}, u32[]{:S(2)}, u32[]{:S(2)}) collective-permute-start(f32[164,128]{1,0:T(8,128)S(1)} %pad_maximum_fusion.1), channel_id=1, source_target_pairs={{0,252},{1,253},{2,254},{3,255},{4,248},{5,249},{6,250},{7,251},{8... | collective-permute-start | bytes 251912 | tf_op jit(solution)/shard_map/ppermute | solution.py:209
  43.9 0.5 collective-permute-start.11
  44.5 3.4 %collective-permute-start.8 = (f32[164,128]{1,0:T(8,128)S(1)}, f32[164,128]{1,0:T(8,128)S(1)}, u32[]{:S(2)}, u32[]{:S(2)}) collective-permute-start(f32[164,128]{1,0:T(8,128)S(1)} %pad_maximum_fusion), channel_id=1, source_target_pairs={{0,14},{1,15},{2,8},{3,9},{4,10},{5,11},{6,12},{7,13},{8,22},{9,23... | collective-permute-start | bytes 251912 | tf_op jit(solution)/shard_map/ppermute | solution.py:209
  47.9 1.4 %collective-permute-start.9 = (f32[164,128]{1,0:T(8,128)S(1)}, f32[164,128]{1,0:T(8,128)S(1)}, u32[]{:S(2)}, u32[]{:S(2)}) collective-permute-start(f32[164,128]{1,0:T(8,128)S(1)} %pad_maximum_fusion), channel_id=1, source_target_pairs={{0,12},{1,13},{2,14},{3,15},{4,8},{5,9},{6,10},{7,11},{8,20},{9,21... | collective-permute-start | bytes 251912 | tf_op jit(solution)/shard_map/ppermute | solution.py:209
  49.8 3.0 %collective-permute-start.13 = (f32[44,128]{1,0:T(8,128)S(1)}, f32[44,128]{1,0:T(8,128)S(1)}, u32[]{:S(2)}, u32[]{:S(2)}) collective-permute-start(f32[44,128]{1,0:T(8,128)S(1)} %pad_maximum_fusion.12), channel_id=1, source_target_pairs={{0,6},{1,7},{2,0},{3,1},{4,2},{5,3},{6,4},{7,5},{8,14},{9,15},{10,... | collective-permute-start | bytes 67592 | tf_op jit(solution)/shard_map/ppermute | solution.py:209
  52.8 0.2 slice_reduce_fusion.11
  53.0 0.2 slice_reduce_fusion.10
  53.2 0.2 slice_reduce_fusion.9
  53.8 1.8 %collective-permute-start.12 = (f32[44,128]{1,0:T(8,128)S(1)}, f32[44,128]{1,0:T(8,128)S(1)}, u32[]{:S(2)}, u32[]{:S(2)}) collective-permute-start(f32[44,128]{1,0:T(8,128)S(1)} %pad_maximum_fusion.11), channel_id=1, source_target_pairs={{0,2},{1,3},{2,4},{3,5},{4,6},{5,7},{6,0},{7,1},{8,10},{9,11},{10,... | collective-permute-start | bytes 67592 | tf_op jit(solution)/shard_map/ppermute | solution.py:209
  55.6 0.7 fusion.10
  56.3 0.7 maximum_bitcast_fusion.48
  57.0 0.7 maximum_bitcast_fusion.49
  57.8 0.7 maximum_bitcast_fusion.50
  58.5 0.7 maximum_bitcast_fusion.51
  59.2 0.7 fusion.11
  59.9 0.7 maximum_bitcast_fusion.44
  60.6 0.6 maximum_bitcast_fusion.45
  61.3 0.8 maximum_bitcast_fusion.46
  62.0 0.7 maximum_bitcast_fusion.47
  62.7 0.7 maximum_bitcast_fusion.40
  63.4 0.7 maximum_bitcast_fusion.41
  64.1 0.6 maximum_bitcast_fusion.42
  64.8 0.6 maximum_bitcast_fusion.43
  65.4 0.7 maximum_bitcast_fusion.36
  66.1 0.7 maximum_bitcast_fusion.37
  66.8 0.6 maximum_bitcast_fusion.38
  67.4 0.7 maximum_bitcast_fusion.39
  68.2 0.7 maximum_bitcast_fusion.32
  68.9 0.7 maximum_bitcast_fusion.33
  69.6 0.7 maximum_bitcast_fusion.34
  70.3 0.7 maximum_bitcast_fusion.35
  70.9 0.7 maximum_bitcast_fusion.28
  71.7 0.7 maximum_bitcast_fusion.29
  72.4 0.7 maximum_bitcast_fusion.30
  73.1 0.7 maximum_bitcast_fusion.31
  73.8 0.7 maximum_bitcast_fusion.24
  74.5 0.7 maximum_bitcast_fusion.25
  75.2 0.7 maximum_bitcast_fusion.26
  76.0 0.6 maximum_bitcast_fusion.27
  76.6 0.8 maximum_bitcast_fusion.20
  77.3 0.6 maximum_bitcast_fusion.21
  78.0 0.7 maximum_bitcast_fusion.22
  78.7 0.6 slice.1635
  79.3 0.6 slice.1621
  79.9 0.7 maximum_bitcast_fusion.23
  81.7 1.1 %broadcast_in_dim.2.col_ref = f32[20,4,16,128]{3,2,1,0:T(8,128)} broadcast(f32[20,4,16]{2,1,0:T(4,128)S(1)} %constant_dynamic-update-slice_fusion.57), dimensions={0,1,2} | broadcast | bytes 660480 | tf_op jit(solution)/shard_map/broadcast_in_dim | solution.py:341
  82.8 2.8 %shard_map.51 = (f32[19,4,16,128]{3,2,1,0:T(8,128)}, f32[19,4,16,128]{3,2,1,0:T(8,128)}) custom-call(f32[38,4,16,128]{3,2,1,0:T(8,128)} %shard_map.50.post_ref, f32[10,16,128]{2,1,0:T(8,128)} %copy-done.3, f32[10,16,128]{2,1,0:T(8,128)} %copy-done.2, f32[10,4,128]{2,1,0:T(4,128)} %bitcast.417, f32[10,4,128]{2,1,0:T(4,128)} %bitcast.416, ...), custom_call_target="tpu_custom_call" | custom-call | tf_op jit(solution)/shard_map/pallas_call | solution.py:343
  (125 shorter events, 2.8 us)
Async XLA Ops:
  1.8 22.8 %collective-permute-start = (f32[1,16,128]{2,1,0:T(8,128)S(1)}, f32[1,16,128]{2,1,0:T(8,128)S(1)}, u32[]{:S(2)}, u32[]{:S(2)}) collective-permute-start(f32[1,16,128]{2,1,0:T(8,128)S(1)} %get-tuple-element.132), channel_id=1, source_target_pairs={{0,14},{1,15},{2,8},{3,9},{4,10},{5,11},{6,12},{7,13},{8,22},{9,23... | collective-permute-start | bytes 24584 | tf_op jit(solution)/shard_map/ppermute | solution.py:209
  6.7 17.9 %collective-permute-start.1 = (f32[1,16,128]{2,1,0:T(8,128)S(1)}, f32[1,16,128]{2,1,0:T(8,128)S(1)}, u32[]{:S(2)}, u32[]{:S(2)}) collective-permute-start(f32[1,16,128]{2,1,0:T(8,128)S(1)} %get-tuple-element.132), channel_id=1, source_target_pairs={{0,12},{1,13},{2,14},{3,15},{4,8},{5,9},{6,10},{7,11},{8,20},{9,21... | collective-permute-start | bytes 24584 | tf_op jit(solution)/shard_map/ppermute | solution.py:209
  7.1 17.6 %collective-permute-start.2 = (f32[1,16,128]{2,1,0:T(8,128)S(1)}, f32[1,16,128]{2,1,0:T(8,128)S(1)}, u32[]{:S(2)}, u32[]{:S(2)}) collective-permute-start(f32[1,16,128]{2,1,0:T(8,128)S(1)} %get-tuple-element.133), channel_id=1, source_target_pairs={{0,252},{1,253},{2,254},{3,255},{4,248},{5,249},{6,250},{7,251},{8... | collective-permute-start | bytes 24584 | tf_op jit(solution)/shard_map/ppermute | solution.py:209
  10.0 14.7 %collective-permute-start.3 = (f32[1,16,128]{2,1,0:T(8,128)S(1)}, f32[1,16,128]{2,1,0:T(8,128)S(1)}, u32[]{:S(2)}, u32[]{:S(2)}) collective-permute-start(f32[1,16,128]{2,1,0:T(8,128)S(1)} %get-tuple-element.133), channel_id=1, source_target_pairs={{0,250},{1,251},{2,252},{3,253},{4,254},{5,255},{6,248},{7,249},{8... | collective-permute-start | bytes 24584 | tf_op jit(solution)/shard_map/ppermute | solution.py:209
  12.9 7.9 %collective-permute-start.6 = (f32[2,4,16]{2,1,0:T(4,128)S(1)}, f32[2,4,16]{2,1,0:T(4,128)S(1)}, u32[]{:S(2)}, u32[]{:S(2)}) collective-permute-start(f32[2,4,16]{2,1,0:T(4,128)S(1)} %pad_maximum_fusion.13), channel_id=1, source_target_pairs={{0,1},{1,0},{2,3},{3,2},{4,5},{5,4},{6,7},{7,6},{8,9},{9,8},{10,11... | collective-permute-start | bytes 1544 | tf_op jit(solution)/shard_map/ppermute | solution.py:209
  20.7 4.3 %collective-permute-start.5 = (f32[4,1,128]{2,1,0:T(1,128)S(1)}, f32[4,1,128]{2,1,0:T(1,128)S(1)}, u32[]{:S(2)}, u32[]{:S(2)}) collective-permute-start(f32[4,1,128]{2,1,0:T(1,128)S(1)} %get-tuple-element.129), channel_id=1, source_target_pairs={{0,6},{1,7},{2,0},{3,1},{4,2},{5,3},{6,4},{7,5},{8,14},{9,15},{10,... | collective-permute-start | bytes 6152 | tf_op jit(solution)/shard_map/ppermute | solution.py:209
  24.5 3.7 %collective-permute-start.4 = (f32[4,1,128]{2,1,0:T(1,128)S(1)}, f32[4,1,128]{2,1,0:T(1,128)S(1)}, u32[]{:S(2)}, u32[]{:S(2)}) collective-permute-start(f32[4,1,128]{2,1,0:T(1,128)S(1)} %get-tuple-element.128), channel_id=1, source_target_pairs={{0,2},{1,3},{2,4},{3,5},{4,6},{5,7},{6,0},{7,1},{8,10},{9,11},{10,... | collective-permute-start | bytes 6152 | tf_op jit(solution)/shard_map/ppermute | solution.py:209
  28.5 0.7 copy-start.1
  32.2 2.1 %copy-start = (f32[38,4,16,128]{3,2,1,0:T(8,128)S(1)}, f32[38,4,16,128]{3,2,1,0:T(8,128)}, u32[]{:S(2)}) copy-start(f32[38,4,16,128]{3,2,1,0:T(8,128)} %shard_map.50.post_ref) | copy-start | bytes 3735556
  34.9 6.8 %collective-permute-start.7 = (f32[20,4,16]{2,1,0:T(4,128)S(1)}, f32[20,4,16]{2,1,0:T(4,128)S(1)}, u32[]{:S(2)}, u32[]{:S(2)}) collective-permute-start(f32[20,4,16]{2,1,0:T(4,128)S(1)} %pad_maximum_fusion.4), channel_id=1, source_target_pairs={{0,1},{1,0},{2,3},{3,2},{4,5},{5,4},{6,7},{7,6},{8,9},{9,8},{10,11... | collective-permute-start | bytes 15368 | tf_op jit(solution)/shard_map/ppermute | solution.py:209
  41.7 38.8 %collective-permute-start.10 = (f32[164,128]{1,0:T(8,128)S(1)}, f32[164,128]{1,0:T(8,128)S(1)}, u32[]{:S(2)}, u32[]{:S(2)}) collective-permute-start(f32[164,128]{1,0:T(8,128)S(1)} %pad_maximum_fusion.1), channel_id=1, source_target_pairs={{0,252},{1,253},{2,254},{3,255},{4,248},{5,249},{6,250},{7,251},{8... | collective-permute-start | bytes 251912 | tf_op jit(solution)/shard_map/ppermute | solution.py:209
  43.9 36.7 %collective-permute-start.11 = (f32[164,128]{1,0:T(8,128)S(1)}, f32[164,128]{1,0:T(8,128)S(1)}, u32[]{:S(2)}, u32[]{:S(2)}) collective-permute-start(f32[164,128]{1,0:T(8,128)S(1)} %pad_maximum_fusion.1), channel_id=1, source_target_pairs={{0,250},{1,251},{2,252},{3,253},{4,254},{5,255},{6,248},{7,249},{8... | collective-permute-start | bytes 251912 | tf_op jit(solution)/shard_map/ppermute | solution.py:209
  44.5 36.3 %collective-permute-start.8 = (f32[164,128]{1,0:T(8,128)S(1)}, f32[164,128]{1,0:T(8,128)S(1)}, u32[]{:S(2)}, u32[]{:S(2)}) collective-permute-start(f32[164,128]{1,0:T(8,128)S(1)} %pad_maximum_fusion), channel_id=1, source_target_pairs={{0,14},{1,15},{2,8},{3,9},{4,10},{5,11},{6,12},{7,13},{8,22},{9,23... | collective-permute-start | bytes 251912 | tf_op jit(solution)/shard_map/ppermute | solution.py:209
  47.9 32.9 %collective-permute-start.9 = (f32[164,128]{1,0:T(8,128)S(1)}, f32[164,128]{1,0:T(8,128)S(1)}, u32[]{:S(2)}, u32[]{:S(2)}) collective-permute-start(f32[164,128]{1,0:T(8,128)S(1)} %pad_maximum_fusion), channel_id=1, source_target_pairs={{0,12},{1,13},{2,14},{3,15},{4,8},{5,9},{6,10},{7,11},{8,20},{9,21... | collective-permute-start | bytes 251912 | tf_op jit(solution)/shard_map/ppermute | solution.py:209
  49.8 4.0 %collective-permute-start.13 = (f32[44,128]{1,0:T(8,128)S(1)}, f32[44,128]{1,0:T(8,128)S(1)}, u32[]{:S(2)}, u32[]{:S(2)}) collective-permute-start(f32[44,128]{1,0:T(8,128)S(1)} %pad_maximum_fusion.12), channel_id=1, source_target_pairs={{0,6},{1,7},{2,0},{3,1},{4,2},{5,3},{6,4},{7,5},{8,14},{9,15},{10,... | collective-permute-start | bytes 67592 | tf_op jit(solution)/shard_map/ppermute | solution.py:209
  53.8 5.4 %collective-permute-start.12 = (f32[44,128]{1,0:T(8,128)S(1)}, f32[44,128]{1,0:T(8,128)S(1)}, u32[]{:S(2)}, u32[]{:S(2)}) collective-permute-start(f32[44,128]{1,0:T(8,128)S(1)} %pad_maximum_fusion.11), channel_id=1, source_target_pairs={{0,2},{1,3},{2,4},{3,5},{4,6},{5,7},{6,0},{7,1},{8,10},{9,11},{10,... | collective-permute-start | bytes 67592 | tf_op jit(solution)/shard_map/ppermute | solution.py:209
  81.1 1.7 %copy-start.2 = (f32[10,16,128]{2,1,0:T(8,128)}, f32[10,16,128]{2,1,0:T(8,128)S(1)}, u32[]{:S(2)}) copy-start(f32[10,16,128]{2,1,0:T(8,128)S(1)} %constant_dynamic-update-slice_fusion.30.xhigh_ref) | copy-start | bytes 245764
  81.3 1.5 %copy-start.3 = (f32[10,16,128]{2,1,0:T(8,128)}, f32[10,16,128]{2,1,0:T(8,128)S(1)}, u32[]{:S(2)}) copy-start(f32[10,16,128]{2,1,0:T(8,128)S(1)} %constant_dynamic-update-slice_fusion.23.xlow_ref) | copy-start | bytes 245764

commit v4 on v3

--- a/solution.py
+++ b/solution.py
@@ -316,29 +316,38 @@
     xzw_low = lax.dynamic_slice_in_dim(jnp.concatenate([ca, cb], axis=1), ny - rem, ny, 1)
     xzw_high = lax.dynamic_slice_in_dim(jnp.concatenate([cc, cd], axis=1), rem, ny, 1)
 
-    xlow = jnp.stack([win_low[a, 1 - vel[n][1] : 1 - vel[n][1] + ny] for a, n in enumerate(x_up)])
-    xhigh = jnp.stack([win_high[a, 1 - vel[n][1] : 1 - vel[n][1] + ny] for a, n in enumerate(x_dn)])
+    def by_pop(idx, axis_id, shape):
+        return jnp.array([vel[n][axis_id] for n in idx], jnp.int32).reshape(shape)
+
+    def pick_y(win, idx):
+        cy = by_pop(idx, 1, (-1, 1, 1))
+        return jnp.where(cy == 1, win[:, :ny], jnp.where(cy == -1, win[:, 2:], win[:, 1 : ny + 1]))
+
+    xlow = pick_y(win_low, x_up)
+    xhigh = pick_y(win_high, x_dn)
     z_any = pick(lambda c: c[2] != 0)
-    cols = []
-    for n in z_any:
-        cx, cy, cz = vel[n]
-        per_x = []
-        for x in range(nx):
-            src_x = x - cx
-            if src_x < 0:
-                per_x.append(xzw_low[xz_up.index(n)])
-                continue
-            if src_x >= nx:
-                per_x.append(xzw_high[xz_dn.index(n)])
-                continue
-            line = zhalo(n)[src_x]
-            if cy == 1:
-                line = jnp.concatenate([cy_m[yz_up.index(n), src_x : src_x + 1], line[:-1]])
-            elif cy == -1:
-                line = jnp.concatenate([line[1:], cy_p[yz_dn.index(n), src_x : src_x + 1]])
-            per_x.append(line)
-        cols.append(jnp.stack(per_x))
-    cols = jnp.broadcast_to(jnp.stack(cols)[:, :, :, None], (len(z_any), nx, ny, nz))
+    zh = jnp.concatenate([hz_m, hz_p])[jnp.array([z_up.index(n) if vel[n][2] == 1 else len(z_up) + z_dn.index(n) for n in z_any])]
+
+    def spread(values, idx):
+        zero = jnp.zeros((1,) + values.shape[1:], values.dtype)
+        both = jnp.concatenate([values, zero])
+        return both[jnp.array([idx.index(n) if n in idx else len(idx) for n in z_any])]
+
+    corner_m = spread(cy_m, yz_up)[:, :, None]
+    corner_p = spread(cy_p, yz_dn)[:, :, None]
+    cy = by_pop(z_any, 1, (-1, 1, 1))
+    cx = by_pop(z_any, 0, (-1, 1, 1))
+    down = jnp.concatenate([corner_m, zh[:, :, :-1]], axis=2)
+    up = jnp.concatenate([zh[:, :, 1:], corner_p], axis=2)
+    zy = jnp.where(cy == 1, down, jnp.where(cy == -1, up, zh))
+    edge_low = spread(xzw_low, xz_up)[:, None]
+    edge_high = spread(xzw_high, xz_dn)[:, None]
+    cols = jnp.where(
+        cx == 1,
+        jnp.concatenate([edge_low, zy[:, :-1]], axis=1),
+        jnp.where(cx == -1, jnp.concatenate([zy[:, 1:], edge_high], axis=1), zy),
+    )
+    cols = jnp.broadcast_to(cols[:, :, :, None], (len(z_any), nx, ny, nz))
     pops = f_pop.shape[0]
     f_new, g_new = pl.pallas_call(
         stream_kernel,

time: 86.1 us -> 68.3 us (0.79)
  the two profiles are of different devices: /device:TPU:1 before, /device:TPU:2 now
where the time goes in v4:
time: 68.3 us; the launch traced here: 68.1 us
  starting transfers between devices  33.9 us (50%)
  waiting for transfers between devices  12.5 us (18%)
  local copies, waits for them, and re-layouts  11 us (16%)
  Pallas kernels  5.85 us (9%)
  other arithmetic  2.79 us (4%)
  between operations  2 us (3%)
    ppermute x14, starting transfers between devices, exchange(): got = lax.ppermute(joined, AXES, pairs)  33.9 us
    ppermute x14, waiting for transfers between devices, exchange(): got = lax.ppermute(joined, AXES, pairs)  12.5 us
    pallas_call x1, Pallas kernels, local(): pl.pallas_call(collide_kernel, out_shape=jax.ShapeDtypeStruct((2 * f_pop....  3.06 us
    pallas_call x1, Pallas kernels, local(): pl.pallas_call(stream_kernel, out_shape=(jax.ShapeDtypeStruct((pops, nx,...  2.79 us
    gather x4, local copies, waits for them, and re-layouts, spread(): both[jnp.array([idx.index(n) if n in idx else len(idx) for n in z_any])]  2.25 us
    unnamed x42, local copies, waits for them, and re-layouts  1.74 us
  transfers between devices with their start and end apart: 14, of which 6 were waited for; matrix products, arithmetic and copies ran while one was open for 9% of the time, Pallas kernels for 0%

profile of v4, /device:TPU:2, one launch (start us, length us, event | category | flops | bytes accessed | tf_op | source)
XLA Modules:
  0.0 68.1 jit_solution(5947286667921623561)
XLA Ops:
  0.6 0.0 copy-start.12
  0.6 0.0 copy-start.11
  0.7 0.0 copy-start.10
  0.7 0.0 copy-start.8
  0.7 1.1 %reduce_sum.9 = f32[4,16,128]{2,1,0:T(8,128)S(1)} reduce(f32[19,4,16,128]{3,2,1,0:T(8,128)} %g_ref.1, f32[]{:T(128)} %constant.23.clone.1), dimensions={0}, to_apply=%region_0.0 | reduce | flops 147456 | bytes 655364 | tf_op jit(solution)/shard_map/reduce_sum | solution.py:225
  1.8 0.1 collective-permute-start
  1.9 3.7 %collective-permute-start.1 = (f32[1,16,128]{2,1,0:T(8,128)S(1)}, f32[1,16,128]{2,1,0:T(8,128)S(1)}, u32[]{:S(2)}, u32[]{:S(2)}) collective-permute-start(f32[1,16,128]{2,1,0:T(8,128)S(1)} %get-tuple-element.64), channel_id=1, source_target_pairs={{0,12},{1,13},{2,14},{3,15},{4,8},{5,9},{6,10},{7,11},{8,20},{9,21... | collective-permute-start | bytes 24584 | tf_op jit(solution)/shard_map/ppermute | solution.py:209
  5.6 4.6 %collective-permute-start.2 = (f32[1,16,128]{2,1,0:T(8,128)S(1)}, f32[1,16,128]{2,1,0:T(8,128)S(1)}, u32[]{:S(2)}, u32[]{:S(2)}) collective-permute-start(f32[1,16,128]{2,1,0:T(8,128)S(1)} %get-tuple-element.65), channel_id=1, source_target_pairs={{0,252},{1,253},{2,254},{3,255},{4,248},{5,249},{6,250},{7,251},{8... | collective-permute-start | bytes 24584 | tf_op jit(solution)/shard_map/ppermute | solution.py:209
  10.2 2.5 %collective-permute-start.3 = (f32[1,16,128]{2,1,0:T(8,128)S(1)}, f32[1,16,128]{2,1,0:T(8,128)S(1)}, u32[]{:S(2)}, u32[]{:S(2)}) collective-permute-start(f32[1,16,128]{2,1,0:T(8,128)S(1)} %get-tuple-element.65), channel_id=1, source_target_pairs={{0,250},{1,251},{2,252},{3,253},{4,254},{5,255},{6,248},{7,249},{8... | collective-permute-start | bytes 24584 | tf_op jit(solution)/shard_map/ppermute | solution.py:209
  12.7 0.2 slice_reduce_fusion.3
  12.9 6.3 %collective-permute-start.6 = (f32[2,4,16]{2,1,0:T(4,128)S(1)}, f32[2,4,16]{2,1,0:T(4,128)S(1)}, u32[]{:S(2)}, u32[]{:S(2)}) collective-permute-start(f32[2,4,16]{2,1,0:T(4,128)S(1)} %pad_maximum_fusion.13), channel_id=1, source_target_pairs={{0,1},{1,0},{2,3},{3,2},{4,5},{5,4},{6,7},{7,6},{8,9},{9,8},{10,11... | collective-permute-start | bytes 1544 | tf_op jit(solution)/shard_map/ppermute | solution.py:209
  19.2 0.1 slice_bitcast_fusion.1
  20.1 0.7 collective-permute-done.6
  20.8 1.0 %collective-permute-start.5 = (f32[4,1,128]{2,1,0:T(1,128)S(1)}, f32[4,1,128]{2,1,0:T(1,128)S(1)}, u32[]{:S(2)}, u32[]{:S(2)}) collective-permute-start(f32[4,1,128]{2,1,0:T(1,128)S(1)} %get-tuple-element.61), channel_id=1, source_target_pairs={{0,6},{1,7},{2,0},{3,1},{4,2},{5,3},{6,4},{7,5},{8,14},{9,15},{10,... | collective-permute-start | bytes 6152 | tf_op jit(solution)/shard_map/ppermute | solution.py:209
  21.8 0.1 copy.44
  21.9 0.1 copy.45
  22.0 1.1 %collective-permute-start.4 = (f32[4,1,128]{2,1,0:T(1,128)S(1)}, f32[4,1,128]{2,1,0:T(1,128)S(1)}, u32[]{:S(2)}, u32[]{:S(2)}) collective-permute-start(f32[4,1,128]{2,1,0:T(1,128)S(1)} %get-tuple-element.60), channel_id=1, source_target_pairs={{0,2},{1,3},{2,4},{3,5},{4,6},{5,7},{6,0},{7,1},{8,10},{9,11},{10,... | collective-permute-start | bytes 6152 | tf_op jit(solution)/shard_map/ppermute | solution.py:209
  23.1 1.2 %collective-permute-done.5 = f32[4,1,128]{2,1,0:T(1,128)S(1)} collective-permute-done((f32[4,1,128]{2,1,0:T(1,128)S(1)}, f32[4,1,128]{2,1,0:T(1,128)S(1)}, u32[]{:S(2)}, u32[]{:S(2)}) %collective-permute-start.5) | collective-permute-done | bytes 2080 | tf_op jit(solution)/shard_map/ppermute | solution.py:209
  24.3 2.8 %collective-permute-done.4 = f32[4,1,128]{2,1,0:T(1,128)S(1)} collective-permute-done((f32[4,1,128]{2,1,0:T(1,128)S(1)}, f32[4,1,128]{2,1,0:T(1,128)S(1)}, u32[]{:S(2)}, u32[]{:S(2)}) %collective-permute-start.4) | collective-permute-done | bytes 2080 | tf_op jit(solution)/shard_map/ppermute | solution.py:209
  27.1 0.1 constant_dynamic-update-slice_fusion.3
  27.2 0.1 constant_dynamic-update-slice_fusion.nb_ref
  27.3 0.7 copy-done.1
  28.0 3.1 %shard_map.131.post_ref = f32[38,4,16,128]{3,2,1,0:T(8,128)} custom-call(f32[19,4,16,128]{3,2,1,0:T(8,128)} %f_ref.1, f32[19,4,16,128]{3,2,1,0:T(8,128)} %g_ref.1, f32[5,4,16,128]{3,2,1,0:T(8,128)} %copy-done.1), custom_call_target="tpu_custom_call" | custom-call | tf_op jit(solution)/shard_map/pallas_call | solution.py:249
  31.1 0.9 %constant_dynamic-update-slice_fusion.42 = (f32[10,4,16,128]{3,2,1,0:T(8,128)S(1)}, f32[10,4,16,128]{3,2,1,0:T(8,128)S(1)}) fusion(f32[38,4,16,128]{3,2,1,0:T(8,128)} %shard_map.131.post_ref), kind=kLoop, calls=%fused_computation.55 | loop fusion | bytes 131072
  31.9 1.2 %fusion.9 = (f32[5,4,16,128]{3,2,1,0:T(8,128)S(1)}, f32[5,4,16,128]{3,2,1,0:T(8,128)S(1)}, f32[5,4,16,128]{3,2,1,0:T(8,128)S(1)}, f32[5,4,16,128]{3,2,1,0:T(8,128)S(1)}) fusion(f32[38,4,16,128]{3,2,1,0:T(8,128)} %shard_map.131.post_ref), kind=kLoop, calls=%fused_computation.145 | loop fusion | bytes 1310720 | tf_op jit(solution)/shard_map/slice | solution.py:272
  33.4 0.4 slice_reduce_fusion
  33.8 0.0 copy-start.6
  33.8 6.0 %collective-permute-start.7 = (f32[20,4,16]{2,1,0:T(4,128)S(1)}, f32[20,4,16]{2,1,0:T(4,128)S(1)}, u32[]{:S(2)}, u32[]{:S(2)}) collective-permute-start(f32[20,4,16]{2,1,0:T(4,128)S(1)} %pad_maximum_fusion.4), channel_id=1, source_target_pairs={{0,1},{1,0},{2,3},{3,2},{4,5},{5,4},{6,7},{7,6},{8,9},{9,8},{10,11... | collective-permute-start | bytes 15368 | tf_op jit(solution)/shard_map/ppermute | solution.py:209
  39.9 1.8 %collective-permute-done.7 = f32[20,4,16]{2,1,0:T(4,128)S(1)} collective-permute-done((f32[20,4,16]{2,1,0:T(4,128)S(1)}, f32[20,4,16]{2,1,0:T(4,128)S(1)}, u32[]{:S(2)}, u32[]{:S(2)}) %collective-permute-start.7) | collective-permute-done | bytes 5152 | tf_op jit(solution)/shard_map/ppermute | solution.py:209
  41.8 0.1 collective-permute-start.10
  41.9 5.7 %collective-permute-start.11 = (f32[164,128]{1,0:T(8,128)S(1)}, f32[164,128]{1,0:T(8,128)S(1)}, u32[]{:S(2)}, u32[]{:S(2)}) collective-permute-start(f32[164,128]{1,0:T(8,128)S(1)} %pad_maximum_fusion.1), channel_id=1, source_target_pairs={{0,250},{1,251},{2,252},{3,253},{4,254},{5,255},{6,248},{7,249},{8... | collective-permute-start | bytes 251912 | tf_op jit(solution)/shard_map/ppermute | solution.py:209
  47.7 0.1 collective-permute-start.8
  47.8 0.1 slice_reduce_fusion.7
  47.9 0.1 slice_reduce_fusion.6
  48.0 0.1 slice_reduce_fusion.5
  48.1 0.1 slice_reduce_fusion.4
  48.3 0.6 collective-permute-start.13
  48.9 0.2 slice_reduce_fusion.11
  49.0 0.2 slice_reduce_fusion.10
  49.2 0.2 slice_reduce_fusion.9
  49.4 0.2 slice_reduce_fusion.8
  49.6 1.6 %collective-permute-start.12 = (f32[44,128]{1,0:T(8,128)S(1)}, f32[44,128]{1,0:T(8,128)S(1)}, u32[]{:S(2)}, u32[]{:S(2)}) collective-permute-start(f32[44,128]{1,0:T(8,128)S(1)} %pad_maximum_fusion.11), channel_id=1, source_target_pairs={{0,2},{1,3},{2,4},{3,5},{4,6},{5,7},{6,0},{7,1},{8,10},{9,11},{10,... | collective-permute-start | bytes 67592 | tf_op jit(solution)/shard_map/ppermute | solution.py:209
  51.2 0.6 gather_fusion.2
  51.8 0.1 fusion.11
  51.9 0.3 collective-permute-done.13
  52.2 0.6 collective-permute-start.9
  52.8 0.6 gather_fusion.3
  53.4 0.2 copy.50
  53.6 0.6 gather_fusion.1
  54.2 0.2 copy.48
  54.4 0.2 maximum_select_fusion
  54.6 0.6 slice.606
  55.2 0.6 slice.592
  55.9 0.1 pad_maximum_fusion.15
  55.9 0.1 constant_dynamic-slice_fusion
  56.0 0.6 gather_fusion.4
  56.6 5.8 %collective-permute-done.9 = f32[164,128]{1,0:T(8,128)S(1)} collective-permute-done((f32[164,128]{1,0:T(8,128)S(1)}, f32[164,128]{1,0:T(8,128)S(1)}, u32[]{:S(2)}, u32[]{:S(2)}) %collective-permute-start.9) | collective-permute-done | bytes 84000 | tf_op jit(solution)/shard_map/ppermute | solution.py:209
  62.4 0.1 pad_maximum_fusion.14
  62.5 0.1 constant_dynamic-slice_fusion.1
  62.6 0.6 gather_fusion
  63.3 0.8 %fusion.2 = (f32[10,16,128]{2,1,0:T(8,128)}, f32[10,16,128]{2,1,0:T(8,128)}) fusion(f32[10,18,128]{2,1,0:T(8,128)S(1)} %fusion, pred[10]{0:T(512)(128)(4,1)S(1)} %copy-done.5, pred[10]{0:T(512)(128)(4,1)S(1)} %copy-done.4, f32[10,18,128]{2,1,0:T(8,128)S(1)} %fusion.1), kind=kLoop, calls=%fused_computation.59 | loop fusion | flops 81920 | bytes 655380 | tf_op jit(solution)/shard_map/jit(_where)/select_n | solution.py:324
  64.1 0.1 maximum_select_fusion.2
  64.2 1.1 %broadcast_in_dim.90.col_ref = f32[20,4,16,128]{3,2,1,0:T(8,128)} broadcast(f32[20,4,16]{2,1,0:T(4,128)S(1)} %maximum_select_fusion.2), dimensions={0,1,2} | broadcast | bytes 660480 | tf_op jit(solution)/shard_map/broadcast_in_dim | solution.py:350
  65.3 2.8 %shard_map.132 = (f32[19,4,16,128]{3,2,1,0:T(8,128)}, f32[19,4,16,128]{3,2,1,0:T(8,128)}) custom-call(f32[38,4,16,128]{3,2,1,0:T(8,128)} %shard_map.131.post_ref, f32[10,16,128]{2,1,0:T(8,128)} %get-tuple-element.71.xlow_ref, f32[10,16,128]{2,1,0:T(8,128)} %get-tuple-element.70.xhigh_ref, f32[10,4,128]{2,1,0:T(4,128)} %bitcast.101, f32[10,4,128]{2,1,0:T(4,128)} %bitcast.100, ...), custom_call_target="tpu_custom_call" | custom-call | tf_op jit(solution)/shard_map/pallas_call | solution.py:352
  (93 shorter events, 0.7 us)
Async XLA Ops:
  0.6 19.3 %copy-start.12 = (s32[20]{0:T(128)S(1)}, s32[20]{0:T(128)}, u32[]{:S(2)}) copy-start(s32[20]{0:T(128)} %constant.116) | copy-start | bytes 244
  0.6 19.3 %copy-start.11 = (s32[20]{0:T(128)S(1)}, s32[20]{0:T(128)}, u32[]{:S(2)}) copy-start(s32[20]{0:T(128)} %constant.114) | copy-start | bytes 244
  0.7 19.3 %copy-start.10 = (s32[20]{0:T(128)S(1)}, s32[20]{0:T(128)}, u32[]{:S(2)}) copy-start(s32[20]{0:T(128)} %constant.115) | copy-start | bytes 244
  0.7 19.4 %copy-start.8 = (s32[20]{0:T(128)S(1)}, s32[20]{0:T(128)}, u32[]{:S(2)}) copy-start(s32[20]{0:T(128)} %constant.113) | copy-start | bytes 244
  0.7 19.4 %copy-start.9 = (s32[20]{0:T(128)S(1)}, s32[20]{0:T(128)}, u32[]{:S(2)}) copy-start(s32[20]{0:T(128)} %constant.117) | copy-start | bytes 244
  1.8 20.1 %collective-permute-start = (f32[1,16,128]{2,1,0:T(8,128)S(1)}, f32[1,16,128]{2,1,0:T(8,128)S(1)}, u32[]{:S(2)}, u32[]{:S(2)}) collective-permute-start(f32[1,16,128]{2,1,0:T(8,128)S(1)} %get-tuple-element.64), channel_id=1, source_target_pairs={{0,14},{1,15},{2,8},{3,9},{4,10},{5,11},{6,12},{7,13},{8,22},{9,23... | collective-permute-start | bytes 24584 | tf_op jit(solution)/shard_map/ppermute | solution.py:209
  1.9 21.1 %collective-permute-start.1 = (f32[1,16,128]{2,1,0:T(8,128)S(1)}, f32[1,16,128]{2,1,0:T(8,128)S(1)}, u32[]{:S(2)}, u32[]{:S(2)}) collective-permute-start(f32[1,16,128]{2,1,0:T(8,128)S(1)} %get-tuple-element.64), channel_id=1, source_target_pairs={{0,12},{1,13},{2,14},{3,15},{4,8},{5,9},{6,10},{7,11},{8,20},{9,21... | collective-permute-start | bytes 24584 | tf_op jit(solution)/shard_map/ppermute | solution.py:209
  5.6 17.5 %collective-permute-start.2 = (f32[1,16,128]{2,1,0:T(8,128)S(1)}, f32[1,16,128]{2,1,0:T(8,128)S(1)}, u32[]{:S(2)}, u32[]{:S(2)}) collective-permute-start(f32[1,16,128]{2,1,0:T(8,128)S(1)} %get-tuple-element.65), channel_id=1, source_target_pairs={{0,252},{1,253},{2,254},{3,255},{4,248},{5,249},{6,250},{7,251},{8... | collective-permute-start | bytes 24584 | tf_op jit(solution)/shard_map/ppermute | solution.py:209
  10.2 12.9 %collective-permute-start.3 = (f32[1,16,128]{2,1,0:T(8,128)S(1)}, f32[1,16,128]{2,1,0:T(8,128)S(1)}, u32[]{:S(2)}, u32[]{:S(2)}) collective-permute-start(f32[1,16,128]{2,1,0:T(8,128)S(1)} %get-tuple-element.65), channel_id=1, source_target_pairs={{0,250},{1,251},{2,252},{3,253},{4,254},{5,255},{6,248},{7,249},{8... | collective-permute-start | bytes 24584 | tf_op jit(solution)/shard_map/ppermute | solution.py:209
  12.9 7.9 %collective-permute-start.6 = (f32[2,4,16]{2,1,0:T(4,128)S(1)}, f32[2,4,16]{2,1,0:T(4,128)S(1)}, u32[]{:S(2)}, u32[]{:S(2)}) collective-permute-start(f32[2,4,16]{2,1,0:T(4,128)S(1)} %pad_maximum_fusion.13), channel_id=1, source_target_pairs={{0,1},{1,0},{2,3},{3,2},{4,5},{5,4},{6,7},{7,6},{8,9},{9,8},{10,11... | collective-permute-start | bytes 1544 | tf_op jit(solution)/shard_map/ppermute | solution.py:209
  20.8 3.6 %collective-permute-start.5 = (f32[4,1,128]{2,1,0:T(1,128)S(1)}, f32[4,1,128]{2,1,0:T(1,128)S(1)}, u32[]{:S(2)}, u32[]{:S(2)}) collective-permute-start(f32[4,1,128]{2,1,0:T(1,128)S(1)} %get-tuple-element.61), channel_id=1, source_target_pairs={{0,6},{1,7},{2,0},{3,1},{4,2},{5,3},{6,4},{7,5},{8,14},{9,15},{10,... | collective-permute-start | bytes 6152 | tf_op jit(solution)/shard_map/ppermute | solution.py:209
  22.0 5.1 %collective-permute-start.4 = (f32[4,1,128]{2,1,0:T(1,128)S(1)}, f32[4,1,128]{2,1,0:T(1,128)S(1)}, u32[]{:S(2)}, u32[]{:S(2)}) collective-permute-start(f32[4,1,128]{2,1,0:T(1,128)S(1)} %get-tuple-element.60), channel_id=1, source_target_pairs={{0,2},{1,3},{2,4},{3,5},{4,6},{5,7},{6,0},{7,1},{8,10},{9,11},{10,... | collective-permute-start | bytes 6152 | tf_op jit(solution)/shard_map/ppermute | solution.py:209
  27.3 0.7 copy-start.1
  31.1 2.1 %copy-start = (f32[38,4,16,128]{3,2,1,0:T(8,128)S(1)}, f32[38,4,16,128]{3,2,1,0:T(8,128)}, u32[]{:S(2)}) copy-start(f32[38,4,16,128]{3,2,1,0:T(8,128)} %shard_map.131.post_ref) | copy-start | bytes 3735556
  33.8 20.7 %copy-start.6 = (pred[20]{0:T(512)(128)(4,1)S(1)}, pred[20]{0:T(512)(128)(4,1)}, u32[]{:S(2)}) copy-start(pred[20]{0:T(512)(128)(4,1)} %constant.103) | copy-start | bytes 64
  33.8 20.6 %copy-start.7 = (pred[20]{0:T(512)(128)(4,1)S(1)}, pred[20]{0:T(512)(128)(4,1)}, u32[]{:S(2)}) copy-start(pred[20]{0:T(512)(128)(4,1)} %constant.94) | copy-start | bytes 64
  33.8 8.0 %collective-permute-start.7 = (f32[20,4,16]{2,1,0:T(4,128)S(1)}, f32[20,4,16]{2,1,0:T(4,128)S(1)}, u32[]{:S(2)}, u32[]{:S(2)}) collective-permute-start(f32[20,4,16]{2,1,0:T(4,128)S(1)} %pad_maximum_fusion.4), channel_id=1, source_target_pairs={{0,1},{1,0},{2,3},{3,2},{4,5},{5,4},{6,7},{7,6},{8,9},{9,8},{10,11... | collective-permute-start | bytes 15368 | tf_op jit(solution)/shard_map/ppermute | solution.py:209
  41.8 14.0 %collective-permute-start.10 = (f32[164,128]{1,0:T(8,128)S(1)}, f32[164,128]{1,0:T(8,128)S(1)}, u32[]{:S(2)}, u32[]{:S(2)}) collective-permute-start(f32[164,128]{1,0:T(8,128)S(1)} %pad_maximum_fusion.1), channel_id=1, source_target_pairs={{0,252},{1,253},{2,254},{3,255},{4,248},{5,249},{6,250},{7,251},{8... | collective-permute-start | bytes 251912 | tf_op jit(solution)/shard_map/ppermute | solution.py:209
  41.9 13.9 %collective-permute-start.11 = (f32[164,128]{1,0:T(8,128)S(1)}, f32[164,128]{1,0:T(8,128)S(1)}, u32[]{:S(2)}, u32[]{:S(2)}) collective-permute-start(f32[164,128]{1,0:T(8,128)S(1)} %pad_maximum_fusion.1), channel_id=1, source_target_pairs={{0,250},{1,251},{2,252},{3,253},{4,254},{5,255},{6,248},{7,249},{8... | collective-permute-start | bytes 251912 | tf_op jit(solution)/shard_map/ppermute | solution.py:209
  47.7 8.9 %collective-permute-start.8 = (f32[164,128]{1,0:T(8,128)S(1)}, f32[164,128]{1,0:T(8,128)S(1)}, u32[]{:S(2)}, u32[]{:S(2)}) collective-permute-start(f32[164,128]{1,0:T(8,128)S(1)} %pad_maximum_fusion), channel_id=1, source_target_pairs={{0,14},{1,15},{2,8},{3,9},{4,10},{5,11},{6,12},{7,13},{8,22},{9,23... | collective-permute-start | bytes 251912 | tf_op jit(solution)/shard_map/ppermute | solution.py:209
  48.3 3.9 %collective-permute-start.13 = (f32[44,128]{1,0:T(8,128)S(1)}, f32[44,128]{1,0:T(8,128)S(1)}, u32[]{:S(2)}, u32[]{:S(2)}) collective-permute-start(f32[44,128]{1,0:T(8,128)S(1)} %pad_maximum_fusion.12), channel_id=1, source_target_pairs={{0,6},{1,7},{2,0},{3,1},{4,2},{5,3},{6,4},{7,5},{8,14},{9,15},{10,... | collective-permute-start | bytes 67592 | tf_op jit(solution)/shard_map/ppermute | solution.py:209
  49.6 4.0 %collective-permute-start.12 = (f32[44,128]{1,0:T(8,128)S(1)}, f32[44,128]{1,0:T(8,128)S(1)}, u32[]{:S(2)}, u32[]{:S(2)}) collective-permute-start(f32[44,128]{1,0:T(8,128)S(1)} %pad_maximum_fusion.11), channel_id=1, source_target_pairs={{0,2},{1,3},{2,4},{3,5},{4,6},{5,7},{6,0},{7,1},{8,10},{9,11},{10,... | collective-permute-start | bytes 67592 | tf_op jit(solution)/shard_map/ppermute | solution.py:209
  51.9 11.4 %copy-start.4 = (pred[10]{0:T(512)(128)(4,1)S(1)}, pred[10]{0:T(512)(128)(4,1)}, u32[]{:S(2)}) copy-start(pred[10]{0:T(512)(128)(4,1)} %constant.85) | copy-start | bytes 34
  51.9 11.4 %copy-start.5 = (pred[10]{0:T(512)(128)(4,1)S(1)}, pred[10]{0:T(512)(128)(4,1)}, u32[]{:S(2)}) copy-start(pred[10]{0:T(512)(128)(4,1)} %constant.86) | copy-start | bytes 34
  52.2 10.2 %collective-permute-start.9 = (f32[164,128]{1,0:T(8,128)S(1)}, f32[164,128]{1,0:T(8,128)S(1)}, u32[]{:S(2)}, u32[]{:S(2)}) collective-permute-start(f32[164,128]{1,0:T(8,128)S(1)} %pad_maximum_fusion), channel_id=1, source_target_pairs={{0,12},{1,13},{2,14},{3,15},{4,8},{5,9},{6,10},{7,11},{8,20},{9,21... | collective-permute-start | bytes 251912 | tf_op jit(solution)/shard_map/ppermute | solution.py:209
  54.6 9.5 %copy-start.2 = (pred[20]{0:T(512)(128)(4,1)S(1)}, pred[20]{0:T(512)(128)(4,1)}, u32[]{:S(2)}) copy-start(pred[20]{0:T(512)(128)(4,1)} %constant.108) | copy-start | bytes 64
  54.6 9.5 %copy-start.3 = (pred[20]{0:T(512)(128)(4,1)S(1)}, pred[20]{0:T(512)(128)(4,1)}, u32[]{:S(2)}) copy-start(pred[20]{0:T(512)(128)(4,1)} %constant.89) | copy-start | bytes 64

commit v5 on v4

--- a/solution.py
+++ b/solution.py
@@ -223,26 +223,28 @@
     rem = shift - q * ny
 
     phi = jnp.sum(g_pop, axis=0)
-    pa, pb, pc, pd, pym, pyp, pzm, pzp = exchange(
+    up1, dn1, pzm, pzp = exchange(
         [
-            (phi[-1:], (1, q + 1, 0)),
-            (phi[-1:], (1, q, 0)),
-            (phi[:1], (-1, -q, 0)),
-            (phi[:1], (-1, -q - 1, 0)),
-            (phi[:, -1:], (0, 1, 0)),
-            (phi[:, :1], (0, -1, 0)),
-            (jnp.transpose(phi[:, :, -1:], (2, 0, 1)), (0, 0, 1)),
-            (jnp.transpose(phi[:, :, :1], (2, 0, 1)), (0, 0, -1)),
+            (jnp.concatenate([phi[:, -1], phi[-1]]), (0, 1, 0)),
+            (jnp.concatenate([phi[:, 0], phi[0]]), (0, -1, 0)),
+            (phi[:, :, -1][None], (0, 0, 1)),
+            (phi[:, :, 0][None], (0, 0, -1)),
         ]
     )
-    low = lax.dynamic_slice_in_dim(jnp.concatenate([pa, pb], axis=1), ny - rem, ny, 1)
-    high = lax.dynamic_slice_in_dim(jnp.concatenate([pc, pd], axis=1), rem, ny, 1)
+    low_pair, high_pair = exchange(
+        [
+            (jnp.concatenate([up1[nx:], phi[-1]]), (1, q, 0)),
+            (jnp.concatenate([phi[0], dn1[nx:]]), (-1, -q, 0)),
+        ]
+    )
+    low = lax.dynamic_slice_in_dim(low_pair, ny - rem, ny, 0)[None]
+    high = lax.dynamic_slice_in_dim(high_pair, rem, ny, 0)[None]
     neigh_xm = jnp.concatenate([low, phi[:-1]], axis=0)
     neigh_xp = jnp.concatenate([phi[1:], high], axis=0)
-    neigh_ym = jnp.concatenate([pym, phi[:, :-1]], axis=1)
-    neigh_yp = jnp.concatenate([phi[:, 1:], pyp], axis=1)
-    neigh_zm = jnp.concatenate([jnp.transpose(pzm, (1, 2, 0)), phi[:, :, :-1]], axis=2)
-    neigh_zp = jnp.concatenate([phi[:, :, 1:], jnp.transpose(pzp, (1, 2, 0))], axis=2)
+    neigh_ym = jnp.concatenate([up1[:nx][:, None], phi[:, :-1]], axis=1)
+    neigh_yp = jnp.concatenate([phi[:, 1:], dn1[:nx][:, None]], axis=1)
+    neigh_zm = jnp.concatenate([pzm[0][:, :, None], phi[:, :, :-1]], axis=2)
+    neigh_zp = jnp.concatenate([phi[:, :, 1:], pzp[0][:, :, None]], axis=2)
     laplace = neigh_xm + neigh_xp + neigh_ym + neigh_yp + neigh_zm + neigh_zp - 6.0 * phi
     slopes = [0.5 * (neigh_xp - neigh_xm), 0.5 * (neigh_yp - neigh_ym), 0.5 * (neigh_zp - neigh_zm)]
     nb = jnp.stack([phi, laplace] + slopes)
@@ -288,16 +290,22 @@
     send_dn = packed(rows(x_dn)[:, 0], [zhalo(n)[0] for n in xz_dn])
     send_yu = packed(rows(y_up)[:, :, -1], [zhalo(n)[:, -1] for n in yz_up])
     send_yd = packed(rows(y_dn)[:, :, 0], [zhalo(n)[:, 0] for n in yz_dn])
-    xa, xb, xc, xd, hy_m, hy_p = exchange(
+    n_yu, n_yd = send_yu.shape[0], send_yd.shape[0]
+    up2, dn2 = exchange(
         [
-            (send_up, (1, q + 1, 0)),
-            (send_up, (1, q, 0)),
-            (send_dn, (-1, -q, 0)),
-            (send_dn, (-1, -q - 1, 0)),
-            (send_yu, (0, 1, 0)),
-            (send_yd, (0, -1, 0)),
+            (jnp.concatenate([send_yu, send_up]), (0, 1, 0)),
+            (jnp.concatenate([send_yd, send_dn]), (0, -1, 0)),
         ]
     )
+    hy_m, hy_p = up2[:n_yu], dn2[:n_yd]
+    low2, high2 = exchange(
+        [
+            (jnp.concatenate([up2[n_yu:], send_up]), (1, q, 0)),
+            (jnp.concatenate([send_dn, dn2[n_yd:]]), (-1, -q, 0)),
+        ]
+    )
+    n_up, n_dn = send_up.shape[0], send_dn.shape[0]
+    xa, xb, xc, xd = low2[:n_up], low2[n_up:], high2[:n_dn], high2[n_dn:]
 
     def unpack_x(got, count):
         return got[: count * ny].reshape(count, ny, nz), got[count * ny :, :ny]

time: 68.3 us -> 67.4 us (0.987)
    ppermute x14 -> x10, starting transfers between devices: 33.9 us -> 33.3 us  [exchange(): got = lax.ppermute(joined, AXES, pairs)]
    ppermute x14 -> x10, waiting for transfers between devices: 12.5 us -> 12.2 us  [exchange(): got = lax.ppermute(joined, AXES, pairs)]
  transfers between devices with their start and end apart: 14 -> 10, of which waited for: 6 -> 6; matrix products, arithmetic and copies ran while one was open for 9% -> 9% of each run, Pallas kernels for 0% -> 0%
where the time goes in v5:
time: 67.4 us; the launch traced here: 67.2 us
  starting transfers between devices  33.3 us (49%)
  waiting for transfers between devices  12.2 us (18%)
  local copies, waits for them, and re-layouts  11 us (16%)
  Pallas kernels  5.85 us (9%)
  other arithmetic  2.8 us (4%)
  between operations  1.99 us (3%)
    ppermute x10, starting transfers between devices, exchange(): got = lax.ppermute(joined, AXES, pairs)  33.3 us
    ppermute x10, waiting for transfers between devices, exchange(): got = lax.ppermute(joined, AXES, pairs)  12.2 us
    pallas_call x1, Pallas kernels, local(): pl.pallas_call(collide_kernel, out_shape=jax.ShapeDtypeStruct((2 * f_pop....  3.06 us
    pallas_call x1, Pallas kernels, local(): pl.pallas_call(stream_kernel, out_shape=(jax.ShapeDtypeStruct((pops, nx,...  2.79 us
    gather x4, local copies, waits for them, and re-layouts, spread(): both[jnp.array([idx.index(n) if n in idx else len(idx) for n in z_any])]  2.25 us
    unnamed x42, local copies, waits for them, and re-layouts  1.74 us
  transfers between devices with their start and end apart: 10, of which 6 were waited for; matrix products, arithmetic and copies ran while one was open for 9% of the time, Pallas kernels for 0%

profile of v5, /device:TPU:2, one launch (start us, length us, event | category | flops | bytes accessed | tf_op | source)
XLA Modules:
  0.0 67.2 jit_solution(18142002709525375832)
XLA Ops:
  0.6 0.0 copy-start.12
  0.7 0.0 copy-start.10
  0.7 0.0 copy-start.8
  0.7 0.0 copy-start.9
  0.7 1.1 %reduce_sum.9 = f32[4,16,128]{2,1,0:T(8,128)S(1)} reduce(f32[19,4,16,128]{3,2,1,0:T(8,128)} %g_ref.1, f32[]{:T(128)} %constant.23.clone.1), dimensions={0}, to_apply=%region_0.0 | reduce | flops 147456 | bytes 655364 | tf_op jit(solution)/shard_map/reduce_sum | solution.py:225
  1.9 1.6 %collective-permute-start = (f32[20,128]{1,0:T(8,128)S(1)}, f32[20,128]{1,0:T(8,128)S(1)}, u32[]{:S(2)}, u32[]{:S(2)}) collective-permute-start(f32[20,128]{1,0:T(8,128)S(1)} %pad_maximum_fusion.15), channel_id=1, source_target_pairs={{0,2},{1,3},{2,4},{3,5},{4,6},{5,7},{6,0},{7,1},{8,10},{9,11},{10,... | collective-permute-start | bytes 30728 | tf_op jit(solution)/shard_map/ppermute | solution.py:209
  3.4 0.8 %collective-permute-start.2 = (f32[20,128]{1,0:T(8,128)S(1)}, f32[20,128]{1,0:T(8,128)S(1)}, u32[]{:S(2)}, u32[]{:S(2)}) collective-permute-start(f32[20,128]{1,0:T(8,128)S(1)} %pad_maximum_fusion.16), channel_id=1, source_target_pairs={{0,6},{1,7},{2,0},{3,1},{4,2},{5,3},{6,4},{7,5},{8,14},{9,15},{10,... | collective-permute-start | bytes 30728 | tf_op jit(solution)/shard_map/ppermute | solution.py:209
  4.3 0.2 slice_reduce_fusion.3
  4.5 7.0 %collective-permute-start.4 = (f32[2,4,16]{2,1,0:T(4,128)S(1)}, f32[2,4,16]{2,1,0:T(4,128)S(1)}, u32[]{:S(2)}, u32[]{:S(2)}) collective-permute-start(f32[2,4,16]{2,1,0:T(4,128)S(1)} %pad_maximum_fusion.17), channel_id=1, source_target_pairs={{0,1},{1,0},{2,3},{3,2},{4,5},{5,4},{6,7},{7,6},{8,9},{9,8},{10,11... | collective-permute-start | bytes 1544 | tf_op jit(solution)/shard_map/ppermute | solution.py:209
  11.4 0.1 slice_bitcast_fusion.1
  12.3 0.7 %collective-permute-done.4 = f32[2,4,16]{2,1,0:T(4,128)S(1)} collective-permute-done((f32[2,4,16]{2,1,0:T(4,128)S(1)}, f32[2,4,16]{2,1,0:T(4,128)S(1)}, u32[]{:S(2)}, u32[]{:S(2)}) %collective-permute-start.4) | collective-permute-done | bytes 544 | tf_op jit(solution)/shard_map/ppermute | solution.py:209
  13.0 0.1 copy.47
  13.1 0.1 copy.48
  13.2 0.2 collective-permute-start.1
  13.5 8.0 %collective-permute-start.3 = (f32[32,128]{1,0:T(8,128)S(1)}, f32[32,128]{1,0:T(8,128)S(1)}, u32[]{:S(2)}, u32[]{:S(2)}) collective-permute-start(f32[32,128]{1,0:T(8,128)S(1)} %pad_maximum_fusion.14), channel_id=1, source_target_pairs={{0,252},{1,253},{2,254},{3,255},{4,248},{5,249},{6,250},{7,251},{8... | collective-permute-start | bytes 49160 | tf_op jit(solution)/shard_map/ppermute | solution.py:209
  21.5 1.3 %collective-permute-done.1 = f32[32,128]{1,0:T(8,128)S(1)} collective-permute-done((f32[32,128]{1,0:T(8,128)S(1)}, f32[32,128]{1,0:T(8,128)S(1)}, u32[]{:S(2)}, u32[]{:S(2)}) %collective-permute-start.1) | collective-permute-done | bytes 16416 | tf_op jit(solution)/shard_map/ppermute | solution.py:209
  22.8 0.1 collective-permute-done.3
  22.9 0.1 constant_dynamic-update-slice_fusion.3
  23.0 0.1 constant_dynamic-update-slice_fusion.nb_ref
  23.1 0.7 copy-done.1
  23.8 3.1 %shard_map.131.post_ref = f32[38,4,16,128]{3,2,1,0:T(8,128)} custom-call(f32[19,4,16,128]{3,2,1,0:T(8,128)} %f_ref.1, f32[19,4,16,128]{3,2,1,0:T(8,128)} %g_ref.1, f32[5,4,16,128]{3,2,1,0:T(8,128)} %copy-done.1), custom_call_target="tpu_custom_call" | custom-call | tf_op jit(solution)/shard_map/pallas_call | solution.py:251
  26.9 0.9 %constant_dynamic-update-slice_fusion.42 = (f32[10,4,16,128]{3,2,1,0:T(8,128)S(1)}, f32[10,4,16,128]{3,2,1,0:T(8,128)S(1)}) fusion(f32[38,4,16,128]{3,2,1,0:T(8,128)} %shard_map.131.post_ref), kind=kLoop, calls=%fused_computation.59 | loop fusion | bytes 131072
  27.8 1.2 %fusion.5 = (f32[5,4,16,128]{3,2,1,0:T(8,128)S(1)}, f32[5,4,16,128]{3,2,1,0:T(8,128)S(1)}, f32[5,4,16,128]{3,2,1,0:T(8,128)S(1)}, f32[5,4,16,128]{3,2,1,0:T(8,128)S(1)}) fusion(f32[38,4,16,128]{3,2,1,0:T(8,128)} %shard_map.131.post_ref), kind=kLoop, calls=%fused_computation.145 | loop fusion | bytes 1310720 | tf_op jit(solution)/shard_map/slice | solution.py:274
  29.2 0.4 slice_reduce_fusion
  29.6 6.0 %collective-permute-start.5 = (f32[20,4,16]{2,1,0:T(4,128)S(1)}, f32[20,4,16]{2,1,0:T(4,128)S(1)}, u32[]{:S(2)}, u32[]{:S(2)}) collective-permute-start(f32[20,4,16]{2,1,0:T(4,128)S(1)} %pad_maximum_fusion.6), channel_id=1, source_target_pairs={{0,1},{1,0},{2,3},{3,2},{4,5},{5,4},{6,7},{7,6},{8,9},{9,8},{10,11... | collective-permute-start | bytes 15368 | tf_op jit(solution)/shard_map/ppermute | solution.py:209
  35.7 0.0 copy-start.6
  35.7 1.9 %collective-permute-done.5 = f32[20,4,16]{2,1,0:T(4,128)S(1)} collective-permute-done((f32[20,4,16]{2,1,0:T(4,128)S(1)}, f32[20,4,16]{2,1,0:T(4,128)S(1)}, u32[]{:S(2)}, u32[]{:S(2)}) %collective-permute-start.5) | collective-permute-done | bytes 5152 | tf_op jit(solution)/shard_map/ppermute | solution.py:209
  37.6 0.1 slice_reduce_fusion.7
  37.8 0.1 slice_reduce_fusion.6
  37.9 0.1 slice_reduce_fusion.5
  38.0 0.1 slice_reduce_fusion.4
  38.2 2.3 %collective-permute-start.8 = (f32[208,128]{1,0:T(8,128)S(1)}, f32[208,128]{1,0:T(8,128)S(1)}, u32[]{:S(2)}, u32[]{:S(2)}) collective-permute-start(f32[208,128]{1,0:T(8,128)S(1)} %pad_maximum_fusion.3), channel_id=1, source_target_pairs={{0,6},{1,7},{2,0},{3,1},{4,2},{5,3},{6,4},{7,5},{8,14},{9,15},{10,... | collective-permute-start | bytes 319496 | tf_op jit(solution)/shard_map/ppermute | solution.py:209
  40.4 0.2 slice_reduce_fusion.11
  40.6 0.2 slice_reduce_fusion.10
  40.8 0.2 slice_reduce_fusion.9
  41.0 0.2 slice_reduce_fusion.8
  41.2 0.1 collective-permute-start.6
  41.3 0.6 gather_fusion.2
  41.9 0.1 fusion.11
  42.0 1.0 %collective-permute-done.8 = f32[208,128]{1,0:T(8,128)S(1)} collective-permute-done((f32[208,128]{1,0:T(8,128)S(1)}, f32[208,128]{1,0:T(8,128)S(1)}, u32[]{:S(2)}, u32[]{:S(2)}) %collective-permute-start.8) | collective-permute-done | bytes 106528 | tf_op jit(solution)/shard_map/ppermute | solution.py:209
  43.0 7.3 %collective-permute-start.9 = (f32[328,128]{1,0:T(8,128)S(1)}, f32[328,128]{1,0:T(8,128)S(1)}, u32[]{:S(2)}, u32[]{:S(2)}) collective-permute-start(f32[328,128]{1,0:T(8,128)S(1)} %pad_maximum_fusion.1), channel_id=1, source_target_pairs={{0,252},{1,253},{2,254},{3,255},{4,248},{5,249},{6,250},{7,251},{8... | collective-permute-start | bytes 503816 | tf_op jit(solution)/shard_map/ppermute | solution.py:209
  50.3 0.0 copy-start.4
  50.4 0.0 copy-start.5
  50.4 0.1 collective-permute-start.7
  50.5 0.6 gather_fusion.1
  51.0 0.2 copy.51
  51.3 0.6 gather_fusion.3
  51.9 0.2 copy.53
  52.1 0.2 maximum_select_fusion
  52.3 0.0 copy-start.2
  52.3 0.0 copy-start.3
  52.3 0.6 slice.653
  52.9 0.6 slice.654
  53.5 0.1 pad_maximum_fusion.19
  53.6 0.1 constant_dynamic-slice_fusion
  53.7 0.6 gather_fusion.4
  54.3 7.3 %collective-permute-done.7 = f32[328,128]{1,0:T(8,128)S(1)} collective-permute-done((f32[328,128]{1,0:T(8,128)S(1)}, f32[328,128]{1,0:T(8,128)S(1)}, u32[]{:S(2)}, u32[]{:S(2)}) %collective-permute-start.7) | collective-permute-done | bytes 167968 | tf_op jit(solution)/shard_map/ppermute | solution.py:209
  61.5 0.1 pad_maximum_fusion.18
  61.6 0.1 constant_dynamic-slice_fusion.1
  61.7 0.6 gather_fusion
  62.4 0.8 %fusion.2 = (f32[10,16,128]{2,1,0:T(8,128)}, f32[10,16,128]{2,1,0:T(8,128)}) fusion(f32[10,18,128]{2,1,0:T(8,128)S(1)} %fusion, pred[10]{0:T(512)(128)(4,1)S(1)} %copy-done.5, pred[10]{0:T(512)(128)(4,1)S(1)} %copy-done.4, f32[10,18,128]{2,1,0:T(8,128)S(1)} %fusion.1), kind=kLoop, calls=%fused_computation.61 | loop fusion | flops 81920 | bytes 655380 | tf_op jit(solution)/shard_map/jit(_where)/select_n | solution.py:332
  63.2 0.1 maximum_select_fusion.2
  63.4 1.1 %broadcast_in_dim.94.col_ref = f32[20,4,16,128]{3,2,1,0:T(8,128)} broadcast(f32[20,4,16]{2,1,0:T(4,128)S(1)} %maximum_select_fusion.2), dimensions={0,1,2} | broadcast | bytes 660480 | tf_op jit(solution)/shard_map/broadcast_in_dim | solution.py:358
  64.4 2.8 %shard_map.132 = (f32[19,4,16,128]{3,2,1,0:T(8,128)}, f32[19,4,16,128]{3,2,1,0:T(8,128)}) custom-call(f32[38,4,16,128]{3,2,1,0:T(8,128)} %shard_map.131.post_ref, f32[10,16,128]{2,1,0:T(8,128)} %get-tuple-element.79.xlow_ref, f32[10,16,128]{2,1,0:T(8,128)} %get-tuple-element.78.xhigh_ref, f32[10,4,128]{2,1,0:T(4,128)} %bitcast.110, f32[10,4,128]{2,1,0:T(4,128)} %bitcast.111, ...), custom_call_target="tpu_custom_call" | custom-call | tf_op jit(solution)/shard_map/pallas_call | solution.py:360
  (91 shorter events, 0.7 us)
Async XLA Ops:
  0.6 11.6 %copy-start.12 = (s32[20]{0:T(128)S(1)}, s32[20]{0:T(128)}, u32[]{:S(2)}) copy-start(s32[20]{0:T(128)} %constant.114) | copy-start | bytes 244
  0.6 11.6 %copy-start.11 = (s32[20]{0:T(128)S(1)}, s32[20]{0:T(128)}, u32[]{:S(2)}) copy-start(s32[20]{0:T(128)} %constant.116) | copy-start | bytes 244
  0.7 11.6 %copy-start.10 = (s32[20]{0:T(128)S(1)}, s32[20]{0:T(128)}, u32[]{:S(2)}) copy-start(s32[20]{0:T(128)} %constant.115) | copy-start | bytes 244
  0.7 11.6 %copy-start.8 = (s32[20]{0:T(128)S(1)}, s32[20]{0:T(128)}, u32[]{:S(2)}) copy-start(s32[20]{0:T(128)} %constant.113) | copy-start | bytes 244
  0.7 11.6 %copy-start.9 = (s32[20]{0:T(128)S(1)}, s32[20]{0:T(128)}, u32[]{:S(2)}) copy-start(s32[20]{0:T(128)} %constant.117) | copy-start | bytes 244
  1.9 11.4 %collective-permute-start = (f32[20,128]{1,0:T(8,128)S(1)}, f32[20,128]{1,0:T(8,128)S(1)}, u32[]{:S(2)}, u32[]{:S(2)}) collective-permute-start(f32[20,128]{1,0:T(8,128)S(1)} %pad_maximum_fusion.15), channel_id=1, source_target_pairs={{0,2},{1,3},{2,4},{3,5},{4,6},{5,7},{6,0},{7,1},{8,10},{9,11},{10,... | collective-permute-start | bytes 30728 | tf_op jit(solution)/shard_map/ppermute | solution.py:209
  3.4 10.0 %collective-permute-start.2 = (f32[20,128]{1,0:T(8,128)S(1)}, f32[20,128]{1,0:T(8,128)S(1)}, u32[]{:S(2)}, u32[]{:S(2)}) collective-permute-start(f32[20,128]{1,0:T(8,128)S(1)} %pad_maximum_fusion.16), channel_id=1, source_target_pairs={{0,6},{1,7},{2,0},{3,1},{4,2},{5,3},{6,4},{7,5},{8,14},{9,15},{10,... | collective-permute-start | bytes 30728 | tf_op jit(solution)/shard_map/ppermute | solution.py:209
  4.5 8.5 %collective-permute-start.4 = (f32[2,4,16]{2,1,0:T(4,128)S(1)}, f32[2,4,16]{2,1,0:T(4,128)S(1)}, u32[]{:S(2)}, u32[]{:S(2)}) collective-permute-start(f32[2,4,16]{2,1,0:T(4,128)S(1)} %pad_maximum_fusion.17), channel_id=1, source_target_pairs={{0,1},{1,0},{2,3},{3,2},{4,5},{5,4},{6,7},{7,6},{8,9},{9,8},{10,11... | collective-permute-start | bytes 1544 | tf_op jit(solution)/shard_map/ppermute | solution.py:209
  13.2 9.6 %collective-permute-start.1 = (f32[32,128]{1,0:T(8,128)S(1)}, f32[32,128]{1,0:T(8,128)S(1)}, u32[]{:S(2)}, u32[]{:S(2)}) collective-permute-start(f32[32,128]{1,0:T(8,128)S(1)} %pad_maximum_fusion.13), channel_id=1, source_target_pairs={{0,12},{1,13},{2,14},{3,15},{4,8},{5,9},{6,10},{7,11},{8,20},{9,21... | collective-permute-start | bytes 49160 | tf_op jit(solution)/shard_map/ppermute | solution.py:209
  13.5 9.4 %collective-permute-start.3 = (f32[32,128]{1,0:T(8,128)S(1)}, f32[32,128]{1,0:T(8,128)S(1)}, u32[]{:S(2)}, u32[]{:S(2)}) collective-permute-start(f32[32,128]{1,0:T(8,128)S(1)} %pad_maximum_fusion.14), channel_id=1, source_target_pairs={{0,252},{1,253},{2,254},{3,255},{4,248},{5,249},{6,250},{7,251},{8... | collective-permute-start | bytes 49160 | tf_op jit(solution)/shard_map/ppermute | solution.py:209
  23.1 0.7 copy-start.1
  26.9 2.1 %copy-start = (f32[38,4,16,128]{3,2,1,0:T(8,128)S(1)}, f32[38,4,16,128]{3,2,1,0:T(8,128)}, u32[]{:S(2)}) copy-start(f32[38,4,16,128]{3,2,1,0:T(8,128)} %shard_map.131.post_ref) | copy-start | bytes 3735556
  29.6 8.0 %collective-permute-start.5 = (f32[20,4,16]{2,1,0:T(4,128)S(1)}, f32[20,4,16]{2,1,0:T(4,128)S(1)}, u32[]{:S(2)}, u32[]{:S(2)}) collective-permute-start(f32[20,4,16]{2,1,0:T(4,128)S(1)} %pad_maximum_fusion.6), channel_id=1, source_target_pairs={{0,1},{1,0},{2,3},{3,2},{4,5},{5,4},{6,7},{7,6},{8,9},{9,8},{10,11... | collective-permute-start | bytes 15368 | tf_op jit(solution)/shard_map/ppermute | solution.py:209
  35.7 16.4 %copy-start.6 = (pred[20]{0:T(512)(128)(4,1)S(1)}, pred[20]{0:T(512)(128)(4,1)}, u32[]{:S(2)}) copy-start(pred[20]{0:T(512)(128)(4,1)} %constant.103) | copy-start | bytes 64
  35.7 16.4 %copy-start.7 = (pred[20]{0:T(512)(128)(4,1)S(1)}, pred[20]{0:T(512)(128)(4,1)}, u32[]{:S(2)}) copy-start(pred[20]{0:T(512)(128)(4,1)} %constant.94) | copy-start | bytes 64
  38.2 4.8 %collective-permute-start.8 = (f32[208,128]{1,0:T(8,128)S(1)}, f32[208,128]{1,0:T(8,128)S(1)}, u32[]{:S(2)}, u32[]{:S(2)}) collective-permute-start(f32[208,128]{1,0:T(8,128)S(1)} %pad_maximum_fusion.3), channel_id=1, source_target_pairs={{0,6},{1,7},{2,0},{3,1},{4,2},{5,3},{6,4},{7,5},{8,14},{9,15},{10,... | collective-permute-start | bytes 319496 | tf_op jit(solution)/shard_map/ppermute | solution.py:209
  41.2 9.1 %collective-permute-start.6 = (f32[208,128]{1,0:T(8,128)S(1)}, f32[208,128]{1,0:T(8,128)S(1)}, u32[]{:S(2)}, u32[]{:S(2)}) collective-permute-start(f32[208,128]{1,0:T(8,128)S(1)} %pad_maximum_fusion.2), channel_id=1, source_target_pairs={{0,2},{1,3},{2,4},{3,5},{4,6},{5,7},{6,0},{7,1},{8,10},{9,11},{10,... | collective-permute-start | bytes 319496 | tf_op jit(solution)/shard_map/ppermute | solution.py:209
  43.0 10.5 %collective-permute-start.9 = (f32[328,128]{1,0:T(8,128)S(1)}, f32[328,128]{1,0:T(8,128)S(1)}, u32[]{:S(2)}, u32[]{:S(2)}) collective-permute-start(f32[328,128]{1,0:T(8,128)S(1)} %pad_maximum_fusion.1), channel_id=1, source_target_pairs={{0,252},{1,253},{2,254},{3,255},{4,248},{5,249},{6,250},{7,251},{8... | collective-permute-start | bytes 503816 | tf_op jit(solution)/shard_map/ppermute | solution.py:209
  50.3 12.1 %copy-start.4 = (pred[10]{0:T(512)(128)(4,1)S(1)}, pred[10]{0:T(512)(128)(4,1)}, u32[]{:S(2)}) copy-start(pred[10]{0:T(512)(128)(4,1)} %constant.85) | copy-start | bytes 34
  50.4 12.1 %copy-start.5 = (pred[10]{0:T(512)(128)(4,1)S(1)}, pred[10]{0:T(512)(128)(4,1)}, u32[]{:S(2)}) copy-start(pred[10]{0:T(512)(128)(4,1)} %constant.86) | copy-start | bytes 34
  50.4 11.2 %collective-permute-start.7 = (f32[328,128]{1,0:T(8,128)S(1)}, f32[328,128]{1,0:T(8,128)S(1)}, u32[]{:S(2)}, u32[]{:S(2)}) collective-permute-start(f32[328,128]{1,0:T(8,128)S(1)} %pad_maximum_fusion), channel_id=1, source_target_pairs={{0,12},{1,13},{2,14},{3,15},{4,8},{5,9},{6,10},{7,11},{8,20},{9,21... | collective-permute-start | bytes 503816 | tf_op jit(solution)/shard_map/ppermute | solution.py:209
  52.3 11.0 %copy-start.2 = (pred[20]{0:T(512)(128)(4,1)S(1)}, pred[20]{0:T(512)(128)(4,1)}, u32[]{:S(2)}) copy-start(pred[20]{0:T(512)(128)(4,1)} %constant.108) | copy-start | bytes 64
  52.3 11.0 %copy-start.3 = (pred[20]{0:T(512)(128)(4,1)S(1)}, pred[20]{0:T(512)(128)(4,1)}, u32[]{:S(2)}) copy-start(pred[20]{0:T(512)(128)(4,1)} %constant.89) | copy-start | bytes 64

commit v6 on v5

--- a/solution.py
+++ b/solution.py
@@ -290,22 +290,16 @@
     send_dn = packed(rows(x_dn)[:, 0], [zhalo(n)[0] for n in xz_dn])
     send_yu = packed(rows(y_up)[:, :, -1], [zhalo(n)[:, -1] for n in yz_up])
     send_yd = packed(rows(y_dn)[:, :, 0], [zhalo(n)[:, 0] for n in yz_dn])
-    n_yu, n_yd = send_yu.shape[0], send_yd.shape[0]
-    up2, dn2 = exchange(
+    xa, xb, xc, xd, hy_m, hy_p = exchange(
         [
-            (jnp.concatenate([send_yu, send_up]), (0, 1, 0)),
-            (jnp.concatenate([send_yd, send_dn]), (0, -1, 0)),
+            (send_up, (1, q + 1, 0)),
+            (send_up, (1, q, 0)),
+            (send_dn, (-1, -q, 0)),
+            (send_dn, (-1, -q - 1, 0)),
+            (send_yu, (0, 1, 0)),
+            (send_yd, (0, -1, 0)),
         ]
     )
-    hy_m, hy_p = up2[:n_yu], dn2[:n_yd]
-    low2, high2 = exchange(
-        [
-            (jnp.concatenate([up2[n_yu:], send_up]), (1, q, 0)),
-            (jnp.concatenate([send_dn, dn2[n_yd:]]), (-1, -q, 0)),
-        ]
-    )
-    n_up, n_dn = send_up.shape[0], send_dn.shape[0]
-    xa, xb, xc, xd = low2[:n_up], low2[n_up:], high2[:n_dn], high2[n_dn:]
 
     def unpack_x(got, count):
         return got[: count * ny].reshape(count, ny, nz), got[count * ny :, :ny]

time: 67.4 us -> 69.8 us (1.036)
  the two profiles are of different devices: /device:TPU:2 before, /device:TPU:6 now
where the time goes in v6:
time: 69.8 us; the launch traced here: 69.6 us
  starting transfers between devices  36 us (52%)
  waiting for transfers between devices  12 us (17%)
  local copies, waits for them, and re-layouts  11 us (16%)
  Pallas kernels  5.83 us (8%)
  other arithmetic  2.77 us (4%)
  between operations  1.99 us (3%)
    ppermute x12, starting transfers between devices, exchange(): got = lax.ppermute(joined, AXES, pairs)  36 us
    ppermute x12, waiting for transfers between devices, exchange(): got = lax.ppermute(joined, AXES, pairs)  12 us
    pallas_call x1, Pallas kernels, local(): pl.pallas_call(collide_kernel, out_shape=jax.ShapeDtypeStruct((2 * f_pop....  3.04 us
    pallas_call x1, Pallas kernels, local(): pl.pallas_call(stream_kernel, out_shape=(jax.ShapeDtypeStruct((pops, nx,...  2.79 us
    gather x4, local copies, waits for them, and re-layouts, spread(): both[jnp.array([idx.index(n) if n in idx else len(idx) for n in z_any])]  2.25 us
    unnamed x42, local copies, waits for them, and re-layouts  1.74 us
  transfers between devices with their start and end apart: 12, of which 6 were waited for; matrix products, arithmetic and copies ran while one was open for 9% of the time, Pallas kernels for 0%

profile of v6, /device:TPU:6, one launch (start us, length us, event | category | flops | bytes accessed | tf_op | source)
XLA Modules:
  0.0 69.6 jit_solution(18074179075884490957)
XLA Ops:
  0.6 0.0 copy-start.12
  0.6 0.0 copy-start.11
  0.7 0.0 copy-start.10
  0.7 0.0 copy-start.8
  0.7 0.0 copy-start.9
  0.7 1.1 %reduce_sum.9 = f32[4,16,128]{2,1,0:T(8,128)S(1)} reduce(f32[19,4,16,128]{3,2,1,0:T(8,128)} %g_ref.1, f32[]{:T(128)} %constant.23.clone.1), dimensions={0}, to_apply=%region_0.0 | reduce | flops 147456 | bytes 655364 | tf_op jit(solution)/shard_map/reduce_sum | solution.py:225
  1.9 2.3 %collective-permute-start = (f32[20,128]{1,0:T(8,128)S(1)}, f32[20,128]{1,0:T(8,128)S(1)}, u32[]{:S(2)}, u32[]{:S(2)}) collective-permute-start(f32[20,128]{1,0:T(8,128)S(1)} %pad_maximum_fusion.15), channel_id=1, source_target_pairs={{0,2},{1,3},{2,4},{3,5},{4,6},{5,7},{6,0},{7,1},{8,10},{9,11},{10,... | collective-permute-start | bytes 30728 | tf_op jit(solution)/shard_map/ppermute | solution.py:209
  4.1 0.2 slice_reduce_fusion.3
  4.3 7.1 %collective-permute-start.4 = (f32[2,4,16]{2,1,0:T(4,128)S(1)}, f32[2,4,16]{2,1,0:T(4,128)S(1)}, u32[]{:S(2)}, u32[]{:S(2)}) collective-permute-start(f32[2,4,16]{2,1,0:T(4,128)S(1)} %pad_maximum_fusion.17), channel_id=1, source_target_pairs={{0,1},{1,0},{2,3},{3,2},{4,5},{5,4},{6,7},{7,6},{8,9},{9,8},{10,11... | collective-permute-start | bytes 1544 | tf_op jit(solution)/shard_map/ppermute | solution.py:209
  11.4 0.1 slice_bitcast_fusion.1
  12.3 0.7 collective-permute-done.4
  13.0 0.1 copy.47
  13.1 0.1 copy.48
  13.2 0.1 collective-permute-start.1
  13.4 8.1 %collective-permute-start.3 = (f32[32,128]{1,0:T(8,128)S(1)}, f32[32,128]{1,0:T(8,128)S(1)}, u32[]{:S(2)}, u32[]{:S(2)}) collective-permute-start(f32[32,128]{1,0:T(8,128)S(1)} %pad_maximum_fusion.14), channel_id=1, source_target_pairs={{0,252},{1,253},{2,254},{3,255},{4,248},{5,249},{6,250},{7,251},{8... | collective-permute-start | bytes 49160 | tf_op jit(solution)/shard_map/ppermute | solution.py:209
  21.5 1.3 %collective-permute-done.1 = f32[32,128]{1,0:T(8,128)S(1)} collective-permute-done((f32[32,128]{1,0:T(8,128)S(1)}, f32[32,128]{1,0:T(8,128)S(1)}, u32[]{:S(2)}, u32[]{:S(2)}) %collective-permute-start.1) | collective-permute-done | bytes 16416 | tf_op jit(solution)/shard_map/ppermute | solution.py:209
  22.8 0.1 collective-permute-done.3
  22.9 0.1 constant_dynamic-update-slice_fusion.3
  23.0 0.1 constant_dynamic-update-slice_fusion.nb_ref
  23.1 0.7 copy-done.1
  23.8 3.0 %shard_map.131.post_ref = f32[38,4,16,128]{3,2,1,0:T(8,128)} custom-call(f32[19,4,16,128]{3,2,1,0:T(8,128)} %f_ref.1, f32[19,4,16,128]{3,2,1,0:T(8,128)} %g_ref.1, f32[5,4,16,128]{3,2,1,0:T(8,128)} %copy-done.1), custom_call_target="tpu_custom_call" | custom-call | tf_op jit(solution)/shard_map/pallas_call | solution.py:251
  26.8 0.9 %constant_dynamic-update-slice_fusion.42 = (f32[10,4,16,128]{3,2,1,0:T(8,128)S(1)}, f32[10,4,16,128]{3,2,1,0:T(8,128)S(1)}) fusion(f32[38,4,16,128]{3,2,1,0:T(8,128)} %shard_map.131.post_ref), kind=kLoop, calls=%fused_computation.55 | loop fusion | bytes 131072
  27.7 1.2 %fusion.5 = (f32[5,4,16,128]{3,2,1,0:T(8,128)S(1)}, f32[5,4,16,128]{3,2,1,0:T(8,128)S(1)}, f32[5,4,16,128]{3,2,1,0:T(8,128)S(1)}, f32[5,4,16,128]{3,2,1,0:T(8,128)S(1)}) fusion(f32[38,4,16,128]{3,2,1,0:T(8,128)} %shard_map.131.post_ref), kind=kLoop, calls=%fused_computation.145 | loop fusion | bytes 1310720 | tf_op jit(solution)/shard_map/slice | solution.py:274
  29.1 0.4 slice_reduce_fusion
  29.5 0.0 copy-start.6
  29.5 0.0 copy-start.7
  29.6 6.0 %collective-permute-start.5 = (f32[20,4,16]{2,1,0:T(4,128)S(1)}, f32[20,4,16]{2,1,0:T(4,128)S(1)}, u32[]{:S(2)}, u32[]{:S(2)}) collective-permute-start(f32[20,4,16]{2,1,0:T(4,128)S(1)} %pad_maximum_fusion.4), channel_id=1, source_target_pairs={{0,1},{1,0},{2,3},{3,2},{4,5},{5,4},{6,7},{7,6},{8,9},{9,8},{10,11... | collective-permute-start | bytes 15368 | tf_op jit(solution)/shard_map/ppermute | solution.py:209
  35.7 1.8 %collective-permute-done.5 = f32[20,4,16]{2,1,0:T(4,128)S(1)} collective-permute-done((f32[20,4,16]{2,1,0:T(4,128)S(1)}, f32[20,4,16]{2,1,0:T(4,128)S(1)}, u32[]{:S(2)}, u32[]{:S(2)}) %collective-permute-start.5) | collective-permute-done | bytes 5152 | tf_op jit(solution)/shard_map/ppermute | solution.py:209
  37.6 7.2 %collective-permute-start.8 = (f32[164,128]{1,0:T(8,128)S(1)}, f32[164,128]{1,0:T(8,128)S(1)}, u32[]{:S(2)}, u32[]{:S(2)}) collective-permute-start(f32[164,128]{1,0:T(8,128)S(1)} %pad_maximum_fusion.1), channel_id=1, source_target_pairs={{0,252},{1,253},{2,254},{3,255},{4,248},{5,249},{6,250},{7,251},{8... | collective-permute-start | bytes 251912 | tf_op jit(solution)/shard_map/ppermute | solution.py:209
  44.8 0.1 collective-permute-start.9
  44.9 1.8 %collective-permute-start.6 = (f32[164,128]{1,0:T(8,128)S(1)}, f32[164,128]{1,0:T(8,128)S(1)}, u32[]{:S(2)}, u32[]{:S(2)}) collective-permute-start(f32[164,128]{1,0:T(8,128)S(1)} %pad_maximum_fusion), channel_id=1, source_target_pairs={{0,14},{1,15},{2,8},{3,9},{4,10},{5,11},{6,12},{7,13},{8,22},{9,23... | collective-permute-start | bytes 251912 | tf_op jit(solution)/shard_map/ppermute | solution.py:209
  46.7 0.1 slice_reduce_fusion.7
  46.8 0.1 slice_reduce_fusion.6
  46.9 0.1 slice_reduce_fusion.5
  47.0 0.1 slice_reduce_fusion.4
  47.2 0.9 %collective-permute-start.11 = (f32[44,128]{1,0:T(8,128)S(1)}, f32[44,128]{1,0:T(8,128)S(1)}, u32[]{:S(2)}, u32[]{:S(2)}) collective-permute-start(f32[44,128]{1,0:T(8,128)S(1)} %pad_maximum_fusion.12), channel_id=1, source_target_pairs={{0,6},{1,7},{2,0},{3,1},{4,2},{5,3},{6,4},{7,5},{8,14},{9,15},{10,... | collective-permute-start | bytes 67592 | tf_op jit(solution)/shard_map/ppermute | solution.py:209
  48.1 0.2 slice_reduce_fusion.11
  48.3 0.2 slice_reduce_fusion.10
  48.5 0.2 slice_reduce_fusion.9
  48.6 0.2 slice_reduce_fusion.8
  48.9 2.5 %collective-permute-start.10 = (f32[44,128]{1,0:T(8,128)S(1)}, f32[44,128]{1,0:T(8,128)S(1)}, u32[]{:S(2)}, u32[]{:S(2)}) collective-permute-start(f32[44,128]{1,0:T(8,128)S(1)} %pad_maximum_fusion.11), channel_id=1, source_target_pairs={{0,2},{1,3},{2,4},{3,5},{4,6},{5,7},{6,0},{7,1},{8,10},{9,11},{10,... | collective-permute-start | bytes 67592 | tf_op jit(solution)/shard_map/ppermute | solution.py:209
  51.3 0.6 gather_fusion.2
  51.9 0.1 fusion.7
  52.0 0.0 copy-start.4
  52.0 1.6 %collective-permute-done.11 = f32[44,128]{1,0:T(8,128)S(1)} collective-permute-done((f32[44,128]{1,0:T(8,128)S(1)}, f32[44,128]{1,0:T(8,128)S(1)}, u32[]{:S(2)}, u32[]{:S(2)}) %collective-permute-start.11) | collective-permute-done | bytes 22560 | tf_op jit(solution)/shard_map/ppermute | solution.py:209
  53.7 0.6 gather_fusion.3
  54.2 0.2 copy.53
  54.5 0.6 gather_fusion.1
  55.0 0.2 copy.51
  55.3 0.2 maximum_select_fusion
  55.4 0.0 copy-start.2
  55.5 0.6 slice.626
  56.1 0.6 slice.612
  56.7 0.1 pad_maximum_fusion.19
  56.8 0.1 constant_dynamic-slice_fusion
  56.9 0.6 gather_fusion.4
  57.5 6.4 %collective-permute-done.7 = f32[164,128]{1,0:T(8,128)S(1)} collective-permute-done((f32[164,128]{1,0:T(8,128)S(1)}, f32[164,128]{1,0:T(8,128)S(1)}, u32[]{:S(2)}, u32[]{:S(2)}) %collective-permute-start.7) | collective-permute-done | bytes 84000 | tf_op jit(solution)/shard_map/ppermute | solution.py:209
  63.9 0.1 pad_maximum_fusion.18
  64.0 0.1 constant_dynamic-slice_fusion.1
  64.0 0.6 gather_fusion
  64.8 0.8 %fusion.2 = (f32[10,16,128]{2,1,0:T(8,128)}, f32[10,16,128]{2,1,0:T(8,128)}) fusion(f32[10,18,128]{2,1,0:T(8,128)S(1)} %fusion, pred[10]{0:T(512)(128)(4,1)S(1)} %copy-done.5, pred[10]{0:T(512)(128)(4,1)S(1)} %copy-done.4, f32[10,18,128]{2,1,0:T(8,128)S(1)} %fusion.1), kind=kLoop, calls=%fused_computation.59 | loop fusion | flops 81920 | bytes 655380 | tf_op jit(solution)/shard_map/jit(_where)/select_n | solution.py:326
  65.6 0.1 maximum_select_fusion.2
  65.7 1.1 %broadcast_in_dim.94.col_ref = f32[20,4,16,128]{3,2,1,0:T(8,128)} broadcast(f32[20,4,16]{2,1,0:T(4,128)S(1)} %maximum_select_fusion.2), dimensions={0,1,2} | broadcast | bytes 660480 | tf_op jit(solution)/shard_map/broadcast_in_dim | solution.py:352
  66.8 2.8 %shard_map.132 = (f32[19,4,16,128]{3,2,1,0:T(8,128)}, f32[19,4,16,128]{3,2,1,0:T(8,128)}) custom-call(f32[38,4,16,128]{3,2,1,0:T(8,128)} %shard_map.131.post_ref, f32[10,16,128]{2,1,0:T(8,128)} %get-tuple-element.71.xlow_ref, f32[10,16,128]{2,1,0:T(8,128)} %get-tuple-element.70.xhigh_ref, f32[10,4,128]{2,1,0:T(4,128)} %bitcast.109, f32[10,4,128]{2,1,0:T(4,128)} %bitcast.108, ...), custom_call_target="tpu_custom_call" | custom-call | tf_op jit(solution)/shard_map/pallas_call | solution.py:354
  (97 shorter events, 0.7 us)
Async XLA Ops:
  0.6 11.6 %copy-start.12 = (s32[20]{0:T(128)S(1)}, s32[20]{0:T(128)}, u32[]{:S(2)}) copy-start(s32[20]{0:T(128)} %constant.116) | copy-start | bytes 244
  0.6 11.6 %copy-start.11 = (s32[20]{0:T(128)S(1)}, s32[20]{0:T(128)}, u32[]{:S(2)}) copy-start(s32[20]{0:T(128)} %constant.114) | copy-start | bytes 244
  0.7 11.6 %copy-start.10 = (s32[20]{0:T(128)S(1)}, s32[20]{0:T(128)}, u32[]{:S(2)}) copy-start(s32[20]{0:T(128)} %constant.115) | copy-start | bytes 244
  0.7 11.6 %copy-start.8 = (s32[20]{0:T(128)S(1)}, s32[20]{0:T(128)}, u32[]{:S(2)}) copy-start(s32[20]{0:T(128)} %constant.113) | copy-start | bytes 244
  0.7 11.6 %copy-start.9 = (s32[20]{0:T(128)S(1)}, s32[20]{0:T(128)}, u32[]{:S(2)}) copy-start(s32[20]{0:T(128)} %constant.117) | copy-start | bytes 244
  1.9 11.4 %collective-permute-start = (f32[20,128]{1,0:T(8,128)S(1)}, f32[20,128]{1,0:T(8,128)S(1)}, u32[]{:S(2)}, u32[]{:S(2)}) collective-permute-start(f32[20,128]{1,0:T(8,128)S(1)} %pad_maximum_fusion.15), channel_id=1, source_target_pairs={{0,2},{1,3},{2,4},{3,5},{4,6},{5,7},{6,0},{7,1},{8,10},{9,11},{10,... | collective-permute-start | bytes 30728 | tf_op jit(solution)/shard_map/ppermute | solution.py:209
  4.1 9.2 %collective-permute-start.2 = (f32[20,128]{1,0:T(8,128)S(1)}, f32[20,128]{1,0:T(8,128)S(1)}, u32[]{:S(2)}, u32[]{:S(2)}) collective-permute-start(f32[20,128]{1,0:T(8,128)S(1)} %pad_maximum_fusion.16), channel_id=1, source_target_pairs={{0,6},{1,7},{2,0},{3,1},{4,2},{5,3},{6,4},{7,5},{8,14},{9,15},{10,... | collective-permute-start | bytes 30728 | tf_op jit(solution)/shard_map/ppermute | solution.py:209
  4.3 8.7 %collective-permute-start.4 = (f32[2,4,16]{2,1,0:T(4,128)S(1)}, f32[2,4,16]{2,1,0:T(4,128)S(1)}, u32[]{:S(2)}, u32[]{:S(2)}) collective-permute-start(f32[2,4,16]{2,1,0:T(4,128)S(1)} %pad_maximum_fusion.17), channel_id=1, source_target_pairs={{0,1},{1,0},{2,3},{3,2},{4,5},{5,4},{6,7},{7,6},{8,9},{9,8},{10,11... | collective-permute-start | bytes 1544 | tf_op jit(solution)/shard_map/ppermute | solution.py:209
  13.2 9.6 %collective-permute-start.1 = (f32[32,128]{1,0:T(8,128)S(1)}, f32[32,128]{1,0:T(8,128)S(1)}, u32[]{:S(2)}, u32[]{:S(2)}) collective-permute-start(f32[32,128]{1,0:T(8,128)S(1)} %pad_maximum_fusion.13), channel_id=1, source_target_pairs={{0,12},{1,13},{2,14},{3,15},{4,8},{5,9},{6,10},{7,11},{8,20},{9,21... | collective-permute-start | bytes 49160 | tf_op jit(solution)/shard_map/ppermute | solution.py:209
  13.4 9.5 %collective-permute-start.3 = (f32[32,128]{1,0:T(8,128)S(1)}, f32[32,128]{1,0:T(8,128)S(1)}, u32[]{:S(2)}, u32[]{:S(2)}) collective-permute-start(f32[32,128]{1,0:T(8,128)S(1)} %pad_maximum_fusion.14), channel_id=1, source_target_pairs={{0,252},{1,253},{2,254},{3,255},{4,248},{5,249},{6,250},{7,251},{8... | collective-permute-start | bytes 49160 | tf_op jit(solution)/shard_map/ppermute | solution.py:209
  23.1 0.7 copy-start.1
  26.8 2.1 %copy-start = (f32[38,4,16,128]{3,2,1,0:T(8,128)S(1)}, f32[38,4,16,128]{3,2,1,0:T(8,128)}, u32[]{:S(2)}) copy-start(f32[38,4,16,128]{3,2,1,0:T(8,128)} %shard_map.131.post_ref) | copy-start | bytes 3735556
  29.5 25.8 %copy-start.6 = (pred[20]{0:T(512)(128)(4,1)S(1)}, pred[20]{0:T(512)(128)(4,1)}, u32[]{:S(2)}) copy-start(pred[20]{0:T(512)(128)(4,1)} %constant.103) | copy-start | bytes 64
  29.5 25.7 %copy-start.7 = (pred[20]{0:T(512)(128)(4,1)S(1)}, pred[20]{0:T(512)(128)(4,1)}, u32[]{:S(2)}) copy-start(pred[20]{0:T(512)(128)(4,1)} %constant.94) | copy-start | bytes 64
  29.6 8.0 %collective-permute-start.5 = (f32[20,4,16]{2,1,0:T(4,128)S(1)}, f32[20,4,16]{2,1,0:T(4,128)S(1)}, u32[]{:S(2)}, u32[]{:S(2)}) collective-permute-start(f32[20,4,16]{2,1,0:T(4,128)S(1)} %pad_maximum_fusion.4), channel_id=1, source_target_pairs={{0,1},{1,0},{2,3},{3,2},{4,5},{5,4},{6,7},{7,6},{8,9},{9,8},{10,11... | collective-permute-start | bytes 15368 | tf_op jit(solution)/shard_map/ppermute | solution.py:209
  37.6 19.1 %collective-permute-start.8 = (f32[164,128]{1,0:T(8,128)S(1)}, f32[164,128]{1,0:T(8,128)S(1)}, u32[]{:S(2)}, u32[]{:S(2)}) collective-permute-start(f32[164,128]{1,0:T(8,128)S(1)} %pad_maximum_fusion.1), channel_id=1, source_target_pairs={{0,252},{1,253},{2,254},{3,255},{4,248},{5,249},{6,250},{7,251},{8... | collective-permute-start | bytes 251912 | tf_op jit(solution)/shard_map/ppermute | solution.py:209
  44.8 11.9 %collective-permute-start.9 = (f32[164,128]{1,0:T(8,128)S(1)}, f32[164,128]{1,0:T(8,128)S(1)}, u32[]{:S(2)}, u32[]{:S(2)}) collective-permute-start(f32[164,128]{1,0:T(8,128)S(1)} %pad_maximum_fusion.1), channel_id=1, source_target_pairs={{0,250},{1,251},{2,252},{3,253},{4,254},{5,255},{6,248},{7,249},{8... | collective-permute-start | bytes 251912 | tf_op jit(solution)/shard_map/ppermute | solution.py:209
  44.9 12.6 %collective-permute-start.6 = (f32[164,128]{1,0:T(8,128)S(1)}, f32[164,128]{1,0:T(8,128)S(1)}, u32[]{:S(2)}, u32[]{:S(2)}) collective-permute-start(f32[164,128]{1,0:T(8,128)S(1)} %pad_maximum_fusion), channel_id=1, source_target_pairs={{0,14},{1,15},{2,8},{3,9},{4,10},{5,11},{6,12},{7,13},{8,22},{9,23... | collective-permute-start | bytes 251912 | tf_op jit(solution)/shard_map/ppermute | solution.py:209
  47.2 6.5 %collective-permute-start.11 = (f32[44,128]{1,0:T(8,128)S(1)}, f32[44,128]{1,0:T(8,128)S(1)}, u32[]{:S(2)}, u32[]{:S(2)}) collective-permute-start(f32[44,128]{1,0:T(8,128)S(1)} %pad_maximum_fusion.12), channel_id=1, source_target_pairs={{0,6},{1,7},{2,0},{3,1},{4,2},{5,3},{6,4},{7,5},{8,14},{9,15},{10,... | collective-permute-start | bytes 67592 | tf_op jit(solution)/shard_map/ppermute | solution.py:209
  48.9 5.6 %collective-permute-start.10 = (f32[44,128]{1,0:T(8,128)S(1)}, f32[44,128]{1,0:T(8,128)S(1)}, u32[]{:S(2)}, u32[]{:S(2)}) collective-permute-start(f32[44,128]{1,0:T(8,128)S(1)} %pad_maximum_fusion.11), channel_id=1, source_target_pairs={{0,2},{1,3},{2,4},{3,5},{4,6},{5,7},{6,0},{7,1},{8,10},{9,11},{10,... | collective-permute-start | bytes 67592 | tf_op jit(solution)/shard_map/ppermute | solution.py:209
  52.0 12.8 %copy-start.4 = (pred[10]{0:T(512)(128)(4,1)S(1)}, pred[10]{0:T(512)(128)(4,1)}, u32[]{:S(2)}) copy-start(pred[10]{0:T(512)(128)(4,1)} %constant.85) | copy-start | bytes 34
  52.0 12.8 %copy-start.5 = (pred[10]{0:T(512)(128)(4,1)S(1)}, pred[10]{0:T(512)(128)(4,1)}, u32[]{:S(2)}) copy-start(pred[10]{0:T(512)(128)(4,1)} %constant.86) | copy-start | bytes 34
  53.7 10.2 %collective-permute-start.7 = (f32[164,128]{1,0:T(8,128)S(1)}, f32[164,128]{1,0:T(8,128)S(1)}, u32[]{:S(2)}, u32[]{:S(2)}) collective-permute-start(f32[164,128]{1,0:T(8,128)S(1)} %pad_maximum_fusion), channel_id=1, source_target_pairs={{0,12},{1,13},{2,14},{3,15},{4,8},{5,9},{6,10},{7,11},{8,20},{9,21... | collective-permute-start | bytes 251912 | tf_op jit(solution)/shard_map/ppermute | solution.py:209
  55.4 10.1 %copy-start.2 = (pred[20]{0:T(512)(128)(4,1)S(1)}, pred[20]{0:T(512)(128)(4,1)}, u32[]{:S(2)}) copy-start(pred[20]{0:T(512)(128)(4,1)} %constant.108) | copy-start | bytes 64
  55.5 10.1 %copy-start.3 = (pred[20]{0:T(512)(128)(4,1)S(1)}, pred[20]{0:T(512)(128)(4,1)}, u32[]{:S(2)}) copy-start(pred[20]{0:T(512)(128)(4,1)} %constant.89) | copy-start | bytes 64

commit v7 on v5

--- a/solution.py
+++ b/solution.py
@@ -298,31 +298,33 @@
         ]
     )
     hy_m, hy_p = up2[:n_yu], dn2[:n_yd]
+
+    def unpack_x(got, count):
+        return got[: count * ny].reshape(count, ny, nz), got[count * ny :, :ny]
+
+    def unpack_y(got, count):
+        return got[: count * nx].reshape(count, nx, nz), got[count * nx :, :nx]
+
+    def window(first, second, count, start):
+        pa, ca = unpack_x(first, count)
+        pb, cb = unpack_x(second, count)
+        planes = lax.dynamic_slice_in_dim(jnp.concatenate([pa, pb], axis=1), start - 1, ny + 2, 1)
+        cols = lax.dynamic_slice_in_dim(jnp.concatenate([ca, cb], axis=1), start, ny, 1)
+        return jnp.concatenate([planes.reshape(-1, nz), lanes(cols)], axis=0)
+
     low2, high2 = exchange(
         [
-            (jnp.concatenate([up2[n_yu:], send_up]), (1, q, 0)),
-            (jnp.concatenate([send_dn, dn2[n_yd:]]), (-1, -q, 0)),
+            (window(up2[n_yu:], send_up, len(x_up), ny - rem), (1, q, 0)),
+            (window(send_dn, dn2[n_yd:], len(x_dn), rem), (-1, -q, 0)),
         ]
     )
-    n_up, n_dn = send_up.shape[0], send_dn.shape[0]
-    xa, xb, xc, xd = low2[:n_up], low2[n_up:], high2[:n_dn], high2[n_dn:]
-
-    def unpack_x(got, count):
-        return got[: count * ny].reshape(count, ny, nz), got[count * ny :, :ny]
-
-    def unpack_y(got, count):
-        return got[: count * nx].reshape(count, nx, nz), got[count * nx :, :nx]
-
-    pa2, ca = unpack_x(xa, len(x_up))
-    pb2, cb = unpack_x(xb, len(x_up))
-    pc2, cc = unpack_x(xc, len(x_dn))
-    pd2, cd = unpack_x(xd, len(x_dn))
     hy_m, cy_m = unpack_y(hy_m, len(y_up))
     hy_p, cy_p = unpack_y(hy_p, len(y_dn))
-    win_low = lax.dynamic_slice_in_dim(jnp.concatenate([pa2, pb2], axis=1), ny - rem - 1, ny + 2, 1)
-    win_high = lax.dynamic_slice_in_dim(jnp.concatenate([pc2, pd2], axis=1), rem - 1, ny + 2, 1)
-    xzw_low = lax.dynamic_slice_in_dim(jnp.concatenate([ca, cb], axis=1), ny - rem, ny, 1)
-    xzw_high = lax.dynamic_slice_in_dim(jnp.concatenate([cc, cd], axis=1), rem, ny, 1)
+    n_lo, n_hi = len(x_up) * (ny + 2), len(x_dn) * (ny + 2)
+    win_low = low2[:n_lo].reshape(len(x_up), ny + 2, nz)
+    win_high = high2[:n_hi].reshape(len(x_dn), ny + 2, nz)
+    xzw_low = low2[n_lo:, :ny]
+    xzw_high = high2[n_hi:, :ny]
 
     def by_pop(idx, axis_id, shape):
         return jnp.array([vel[n][axis_id] for n in idx], jnp.int32).reshape(shape)

time: 67.4 us -> 66.3 us (0.984)
  the two profiles are of different devices: /device:TPU:2 before, /device:TPU:251 now
where the time goes in v7:
time: 66.3 us; the launch traced here: 66.1 us
  waiting for transfers between devices  30.1 us (45%)
  starting transfers between devices  14.3 us (22%)
  local copies, waits for them, and re-layouts  11.1 us (17%)
  Pallas kernels  5.82 us (9%)
  other arithmetic  2.79 us (4%)
  between operations  2.03 us (3%)
    ppermute x10, waiting for transfers between devices, exchange(): got = lax.ppermute(joined, AXES, pairs)  30.1 us
    ppermute x10, starting transfers between devices, exchange(): got = lax.ppermute(joined, AXES, pairs)  14.3 us
    pallas_call x1, Pallas kernels, local(): pl.pallas_call(collide_kernel, out_shape=jax.ShapeDtypeStruct((2 * f_pop....  3.03 us
    pallas_call x1, Pallas kernels, local(): pl.pallas_call(stream_kernel, out_shape=(jax.ShapeDtypeStruct((pops, nx,...  2.79 us
    gather x4, local copies, waits for them, and re-layouts, spread(): both[jnp.array([idx.index(n) if n in idx else len(idx) for n in z_any])]  2.25 us
    unnamed x42, local copies, waits for them, and re-layouts  1.74 us
  transfers between devices with their start and end apart: 10, of which 7 were waited for; matrix products, arithmetic and copies ran while one was open for 7% of the time, Pallas kernels for 0%

profile of v7, /device:TPU:251, one launch (start us, length us, event | category | flops | bytes accessed | tf_op | source)
XLA Modules:
  0.0 66.1 jit_solution(4045355843179236686)
XLA Ops:
  0.6 0.0 copy-start.12
  0.6 0.0 copy-start.11
  0.7 0.0 copy-start.10
  0.7 0.0 copy-start.9
  0.7 1.1 %reduce_sum.9 = f32[4,16,128]{2,1,0:T(8,128)S(1)} reduce(f32[19,4,16,128]{3,2,1,0:T(8,128)} %g_ref.1, f32[]{:T(128)} %constant.23.clone.1), dimensions={0}, to_apply=%region_0.0 | reduce | flops 147456 | bytes 655364 | tf_op jit(solution)/shard_map/reduce_sum | solution.py:225
  1.9 1.3 %collective-permute-start = (f32[20,128]{1,0:T(8,128)S(1)}, f32[20,128]{1,0:T(8,128)S(1)}, u32[]{:S(2)}, u32[]{:S(2)}) collective-permute-start(f32[20,128]{1,0:T(8,128)S(1)} %pad_maximum_fusion.13), channel_id=1, source_target_pairs={{0,2},{1,3},{2,4},{3,5},{4,6},{5,7},{6,0},{7,1},{8,10},{9,11},{10,... | collective-permute-start | bytes 30728 | tf_op jit(solution)/shard_map/ppermute | solution.py:209
  3.2 0.3 collective-permute-start.2
  3.4 0.2 slice_reduce_fusion.3
  3.6 1.2 %collective-permute-start.4 = (f32[2,4,16]{2,1,0:T(4,128)S(1)}, f32[2,4,16]{2,1,0:T(4,128)S(1)}, u32[]{:S(2)}, u32[]{:S(2)}) collective-permute-start(f32[2,4,16]{2,1,0:T(4,128)S(1)} %pad_maximum_fusion.15), channel_id=1, source_target_pairs={{0,1},{1,0},{2,3},{3,2},{4,5},{5,4},{6,7},{7,6},{8,9},{9,8},{10,11... | collective-permute-start | bytes 1544 | tf_op jit(solution)/shard_map/ppermute | solution.py:209
  4.8 0.1 slice_bitcast_fusion.1
  5.8 4.3 %collective-permute-done.4 = f32[2,4,16]{2,1,0:T(4,128)S(1)} collective-permute-done((f32[2,4,16]{2,1,0:T(4,128)S(1)}, f32[2,4,16]{2,1,0:T(4,128)S(1)}, u32[]{:S(2)}, u32[]{:S(2)}) %collective-permute-start.4) | collective-permute-done | bytes 544 | tf_op jit(solution)/shard_map/ppermute | solution.py:209
  10.0 0.1 copy.47
  10.1 0.1 copy.48
  10.3 5.2 %collective-permute-start.1 = (f32[32,128]{1,0:T(8,128)S(1)}, f32[32,128]{1,0:T(8,128)S(1)}, u32[]{:S(2)}, u32[]{:S(2)}) collective-permute-start(f32[32,128]{1,0:T(8,128)S(1)} %pad_maximum_fusion.11), channel_id=1, source_target_pairs={{0,12},{1,13},{2,14},{3,15},{4,8},{5,9},{6,10},{7,11},{8,20},{9,21... | collective-permute-start | bytes 49160 | tf_op jit(solution)/shard_map/ppermute | solution.py:209
  15.5 0.1 collective-permute-start.3
  15.6 0.7 %collective-permute-done.1 = f32[32,128]{1,0:T(8,128)S(1)} collective-permute-done((f32[32,128]{1,0:T(8,128)S(1)}, f32[32,128]{1,0:T(8,128)S(1)}, u32[]{:S(2)}, u32[]{:S(2)}) %collective-permute-start.1) | collective-permute-done | bytes 16416 | tf_op jit(solution)/shard_map/ppermute | solution.py:209
  16.3 8.7 %collective-permute-done.3 = f32[32,128]{1,0:T(8,128)S(1)} collective-permute-done((f32[32,128]{1,0:T(8,128)S(1)}, f32[32,128]{1,0:T(8,128)S(1)}, u32[]{:S(2)}, u32[]{:S(2)}) %collective-permute-start.3) | collective-permute-done | bytes 16416 | tf_op jit(solution)/shard_map/ppermute | solution.py:209
  25.0 0.1 constant_dynamic-update-slice_fusion.3
  25.2 0.1 constant_dynamic-update-slice_fusion.nb_ref
  25.3 0.7 copy-done.1
  25.9 3.0 %shard_map.131.post_ref = f32[38,4,16,128]{3,2,1,0:T(8,128)} custom-call(f32[19,4,16,128]{3,2,1,0:T(8,128)} %f_ref.1, f32[19,4,16,128]{3,2,1,0:T(8,128)} %g_ref.1, f32[5,4,16,128]{3,2,1,0:T(8,128)} %copy-done.1), custom_call_target="tpu_custom_call" | custom-call | tf_op jit(solution)/shard_map/pallas_call | solution.py:251
  29.0 0.9 %constant_dynamic-update-slice_fusion.42 = (f32[10,4,16,128]{3,2,1,0:T(8,128)S(1)}, f32[10,4,16,128]{3,2,1,0:T(8,128)S(1)}) fusion(f32[38,4,16,128]{3,2,1,0:T(8,128)} %shard_map.131.post_ref), kind=kLoop, calls=%fused_computation.60 | loop fusion | bytes 131072
  29.8 1.2 %fusion.5 = (f32[5,4,16,128]{3,2,1,0:T(8,128)S(1)}, f32[5,4,16,128]{3,2,1,0:T(8,128)S(1)}, f32[5,4,16,128]{3,2,1,0:T(8,128)S(1)}, f32[5,4,16,128]{3,2,1,0:T(8,128)S(1)}) fusion(f32[38,4,16,128]{3,2,1,0:T(8,128)} %shard_map.131.post_ref), kind=kLoop, calls=%fused_computation.146 | loop fusion | bytes 1310720 | tf_op jit(solution)/shard_map/slice | solution.py:274
  31.3 0.4 slice_reduce_fusion
  31.7 0.1 collective-permute-start.5
  31.9 6.7 %collective-permute-done.5 = f32[20,4,16]{2,1,0:T(4,128)S(1)} collective-permute-done((f32[20,4,16]{2,1,0:T(4,128)S(1)}, f32[20,4,16]{2,1,0:T(4,128)S(1)}, u32[]{:S(2)}, u32[]{:S(2)}) %collective-permute-start.5) | collective-permute-done | bytes 5152 | tf_op jit(solution)/shard_map/ppermute | solution.py:209
  38.6 0.2 slice_reduce_fusion.11
  38.8 0.2 slice_reduce_fusion.10
  38.9 0.2 slice_reduce_fusion.9
  39.1 0.2 slice_reduce_fusion.8
  39.4 0.9 %collective-permute-start.6 = (f32[208,128]{1,0:T(8,128)S(1)}, f32[208,128]{1,0:T(8,128)S(1)}, u32[]{:S(2)}, u32[]{:S(2)}) collective-permute-start(f32[208,128]{1,0:T(8,128)S(1)} %pad_maximum_fusion), channel_id=1, source_target_pairs={{0,2},{1,3},{2,4},{3,5},{4,6},{5,7},{6,0},{7,1},{8,10},{9,11},{10,... | collective-permute-start | bytes 319496 | tf_op jit(solution)/shard_map/ppermute | solution.py:209
  40.3 0.1 slice_reduce_fusion.7
  40.4 0.1 slice_reduce_fusion.6
  40.5 0.1 slice_reduce_fusion.5
  40.6 0.1 slice_reduce_fusion.4
  40.8 0.0 copy-start.6
  40.8 0.0 copy-start.7
  40.8 0.7 %collective-permute-start.8 = (f32[208,128]{1,0:T(8,128)S(1)}, f32[208,128]{1,0:T(8,128)S(1)}, u32[]{:S(2)}, u32[]{:S(2)}) collective-permute-start(f32[208,128]{1,0:T(8,128)S(1)} %pad_maximum_fusion.1), channel_id=1, source_target_pairs={{0,6},{1,7},{2,0},{3,1},{4,2},{5,3},{6,4},{7,5},{8,14},{9,15},{10,... | collective-permute-start | bytes 319496 | tf_op jit(solution)/shard_map/ppermute | solution.py:209
  41.5 0.6 gather_fusion.2
  42.1 0.1 fusion.7
  42.2 0.8 %collective-permute-done.6 = f32[208,128]{1,0:T(8,128)S(1)} collective-permute-done((f32[208,128]{1,0:T(8,128)S(1)}, f32[208,128]{1,0:T(8,128)S(1)}, u32[]{:S(2)}, u32[]{:S(2)}) %collective-permute-start.6) | collective-permute-done | bytes 106528 | tf_op jit(solution)/shard_map/ppermute | solution.py:209
  43.0 0.6 gather_fusion.1
  43.6 0.2 copy.51
  43.8 0.6 collective-permute-done.8
  44.5 0.6 gather_fusion.3
  45.0 0.2 copy.53
  45.3 0.0 copy-start.4
  45.3 0.0 copy-start.5
  45.4 0.1 maximum_maximum_fusion
  45.4 0.1 constant_dynamic-slice_fusion.1
  45.5 4.5 %collective-permute-start.7 = (f32[184,128]{1,0:T(8,128)S(1)}, f32[184,128]{1,0:T(8,128)S(1)}, u32[]{:S(2)}, u32[]{:S(2)}) collective-permute-start(f32[184,128]{1,0:T(8,128)S(1)} %select_maximum_fusion.1), channel_id=1, source_target_pairs={{0,12},{1,13},{2,14},{3,15},{4,8},{5,9},{6,10},{7,11},{8,20},{9,21... | collective-permute-start | bytes 282632 | tf_op jit(solution)/shard_map/ppermute | solution.py:209
  50.1 0.1 pad_maximum_fusion.16
  50.2 0.1 constant_dynamic-slice_fusion
  50.3 0.1 collective-permute-start.9
  50.4 0.2 maximum_select_fusion
  50.6 0.6 slice.641
  51.2 0.6 slice.642
  51.8 0.6 gather_fusion
  52.4 8.3 %collective-permute-done.9 = f32[184,128]{1,0:T(8,128)S(1)} collective-permute-done((f32[184,128]{1,0:T(8,128)S(1)}, f32[184,128]{1,0:T(8,128)S(1)}, u32[]{:S(2)}, u32[]{:S(2)}) %collective-permute-start.9) | collective-permute-done | bytes 94240 | tf_op jit(solution)/shard_map/ppermute | solution.py:209
  60.7 0.6 gather_fusion.4
  61.4 0.8 %fusion.2 = (f32[10,16,128]{2,1,0:T(8,128)}, f32[10,16,128]{2,1,0:T(8,128)}) fusion(f32[10,18,128]{2,1,0:T(8,128)S(1)} %reshape.494, pred[10]{0:T(512)(128)(4,1)S(1)} %copy-done.5, pred[10]{0:T(512)(128)(4,1)S(1)} %copy-done.4, f32[10,18,128]{2,1,0:T(8,128)S(1)} %reshape.491), kind=kLoop, calls=%fused_computation.62 | loop fusion | flops 81920 | bytes 655380 | tf_op jit(solution)/shard_map/jit(_where)/select_n | solution.py:334
  62.1 0.1 maximum_select_fusion.2
  62.2 1.1 %broadcast_in_dim.94.col_ref = f32[20,4,16,128]{3,2,1,0:T(8,128)} broadcast(f32[20,4,16]{2,1,0:T(4,128)S(1)} %maximum_select_fusion.2), dimensions={0,1,2} | broadcast | bytes 660480 | tf_op jit(solution)/shard_map/broadcast_in_dim | solution.py:360
  63.3 2.8 %shard_map.132 = (f32[19,4,16,128]{3,2,1,0:T(8,128)}, f32[19,4,16,128]{3,2,1,0:T(8,128)}) custom-call(f32[38,4,16,128]{3,2,1,0:T(8,128)} %shard_map.131.post_ref, f32[10,16,128]{2,1,0:T(8,128)} %get-tuple-element.71.xlow_ref, f32[10,16,128]{2,1,0:T(8,128)} %get-tuple-element.70.xhigh_ref, f32[10,4,128]{2,1,0:T(4,128)} %bitcast.112, f32[10,4,128]{2,1,0:T(4,128)} %bitcast.113, ...), custom_call_target="tpu_custom_call" | custom-call | tf_op jit(solution)/shard_map/pallas_call | solution.py:362
  (96 shorter events, 0.7 us)
Async XLA Ops:
  0.6 5.0 %copy-start.12 = (s32[20]{0:T(128)S(1)}, s32[20]{0:T(128)}, u32[]{:S(2)}) copy-start(s32[20]{0:T(128)} %constant.118) | copy-start | bytes 244
  0.6 5.0 %copy-start.11 = (s32[20]{0:T(128)S(1)}, s32[20]{0:T(128)}, u32[]{:S(2)}) copy-start(s32[20]{0:T(128)} %constant.120) | copy-start | bytes 244
  0.7 5.0 %copy-start.10 = (s32[20]{0:T(128)S(1)}, s32[20]{0:T(128)}, u32[]{:S(2)}) copy-start(s32[20]{0:T(128)} %constant.119) | copy-start | bytes 244
  0.7 5.0 %copy-start.9 = (s32[20]{0:T(128)S(1)}, s32[20]{0:T(128)}, u32[]{:S(2)}) copy-start(s32[20]{0:T(128)} %constant.117) | copy-start | bytes 244
  0.7 5.0 %copy-start.8 = (s32[20]{0:T(128)S(1)}, s32[20]{0:T(128)}, u32[]{:S(2)}) copy-start(s32[20]{0:T(128)} %constant.121) | copy-start | bytes 244
  1.9 8.4 %collective-permute-start = (f32[20,128]{1,0:T(8,128)S(1)}, f32[20,128]{1,0:T(8,128)S(1)}, u32[]{:S(2)}, u32[]{:S(2)}) collective-permute-start(f32[20,128]{1,0:T(8,128)S(1)} %pad_maximum_fusion.13), channel_id=1, source_target_pairs={{0,2},{1,3},{2,4},{3,5},{4,6},{5,7},{6,0},{7,1},{8,10},{9,11},{10,... | collective-permute-start | bytes 30728 | tf_op jit(solution)/shard_map/ppermute | solution.py:209
  3.2 12.3 %collective-permute-start.2 = (f32[20,128]{1,0:T(8,128)S(1)}, f32[20,128]{1,0:T(8,128)S(1)}, u32[]{:S(2)}, u32[]{:S(2)}) collective-permute-start(f32[20,128]{1,0:T(8,128)S(1)} %pad_maximum_fusion.14), channel_id=1, source_target_pairs={{0,6},{1,7},{2,0},{3,1},{4,2},{5,3},{6,4},{7,5},{8,14},{9,15},{10,... | collective-permute-start | bytes 30728 | tf_op jit(solution)/shard_map/ppermute | solution.py:209
  3.6 6.5 %collective-permute-start.4 = (f32[2,4,16]{2,1,0:T(4,128)S(1)}, f32[2,4,16]{2,1,0:T(4,128)S(1)}, u32[]{:S(2)}, u32[]{:S(2)}) collective-permute-start(f32[2,4,16]{2,1,0:T(4,128)S(1)} %pad_maximum_fusion.15), channel_id=1, source_target_pairs={{0,1},{1,0},{2,3},{3,2},{4,5},{5,4},{6,7},{7,6},{8,9},{9,8},{10,11... | collective-permute-start | bytes 1544 | tf_op jit(solution)/shard_map/ppermute | solution.py:209
  10.3 6.1 %collective-permute-start.1 = (f32[32,128]{1,0:T(8,128)S(1)}, f32[32,128]{1,0:T(8,128)S(1)}, u32[]{:S(2)}, u32[]{:S(2)}) collective-permute-start(f32[32,128]{1,0:T(8,128)S(1)} %pad_maximum_fusion.11), channel_id=1, source_target_pairs={{0,12},{1,13},{2,14},{3,15},{4,8},{5,9},{6,10},{7,11},{8,20},{9,21... | collective-permute-start | bytes 49160 | tf_op jit(solution)/shard_map/ppermute | solution.py:209
  15.5 9.6 %collective-permute-start.3 = (f32[32,128]{1,0:T(8,128)S(1)}, f32[32,128]{1,0:T(8,128)S(1)}, u32[]{:S(2)}, u32[]{:S(2)}) collective-permute-start(f32[32,128]{1,0:T(8,128)S(1)} %pad_maximum_fusion.12), channel_id=1, source_target_pairs={{0,252},{1,253},{2,254},{3,255},{4,248},{5,249},{6,250},{7,251},{8... | collective-permute-start | bytes 49160 | tf_op jit(solution)/shard_map/ppermute | solution.py:209
  25.2 0.7 %copy-start.1 = (f32[5,4,16,128]{3,2,1,0:T(8,128)}, f32[5,4,16,128]{3,2,1,0:T(8,128)S(1)}, u32[]{:S(2)}) copy-start(f32[5,4,16,128]{3,2,1,0:T(8,128)S(1)} %constant_dynamic-update-slice_fusion.nb_ref) | copy-start | bytes 491524
  28.9 2.1 %copy-start = (f32[38,4,16,128]{3,2,1,0:T(8,128)S(1)}, f32[38,4,16,128]{3,2,1,0:T(8,128)}, u32[]{:S(2)}) copy-start(f32[38,4,16,128]{3,2,1,0:T(8,128)} %shard_map.131.post_ref) | copy-start | bytes 3735556
  31.7 6.8 %collective-permute-start.5 = (f32[20,4,16]{2,1,0:T(4,128)S(1)}, f32[20,4,16]{2,1,0:T(4,128)S(1)}, u32[]{:S(2)}, u32[]{:S(2)}) collective-permute-start(f32[20,4,16]{2,1,0:T(4,128)S(1)} %pad_maximum_fusion.4), channel_id=1, source_target_pairs={{0,1},{1,0},{2,3},{3,2},{4,5},{5,4},{6,7},{7,6},{8,9},{9,8},{10,11... | collective-permute-start | bytes 15368 | tf_op jit(solution)/shard_map/ppermute | solution.py:209
  39.4 3.6 %collective-permute-start.6 = (f32[208,128]{1,0:T(8,128)S(1)}, f32[208,128]{1,0:T(8,128)S(1)}, u32[]{:S(2)}, u32[]{:S(2)}) collective-permute-start(f32[208,128]{1,0:T(8,128)S(1)} %pad_maximum_fusion), channel_id=1, source_target_pairs={{0,2},{1,3},{2,4},{3,5},{4,6},{5,7},{6,0},{7,1},{8,10},{9,11},{10,... | collective-permute-start | bytes 319496 | tf_op jit(solution)/shard_map/ppermute | solution.py:209
  40.8 9.6 %copy-start.6 = (pred[20]{0:T(512)(128)(4,1)S(1)}, pred[20]{0:T(512)(128)(4,1)}, u32[]{:S(2)}) copy-start(pred[20]{0:T(512)(128)(4,1)} %constant.107) | copy-start | bytes 64
  40.8 9.6 %copy-start.7 = (pred[20]{0:T(512)(128)(4,1)S(1)}, pred[20]{0:T(512)(128)(4,1)}, u32[]{:S(2)}) copy-start(pred[20]{0:T(512)(128)(4,1)} %constant.98) | copy-start | bytes 64
  40.8 3.6 %collective-permute-start.8 = (f32[208,128]{1,0:T(8,128)S(1)}, f32[208,128]{1,0:T(8,128)S(1)}, u32[]{:S(2)}, u32[]{:S(2)}) collective-permute-start(f32[208,128]{1,0:T(8,128)S(1)} %pad_maximum_fusion.1), channel_id=1, source_target_pairs={{0,6},{1,7},{2,0},{3,1},{4,2},{5,3},{6,4},{7,5},{8,14},{9,15},{10,... | collective-permute-start | bytes 319496 | tf_op jit(solution)/shard_map/ppermute | solution.py:209
  45.3 16.0 %copy-start.4 = (pred[10]{0:T(512)(128)(4,1)S(1)}, pred[10]{0:T(512)(128)(4,1)}, u32[]{:S(2)}) copy-start(pred[10]{0:T(512)(128)(4,1)} %constant.89) | copy-start | bytes 34
  45.3 16.0 %copy-start.5 = (pred[10]{0:T(512)(128)(4,1)S(1)}, pred[10]{0:T(512)(128)(4,1)}, u32[]{:S(2)}) copy-start(pred[10]{0:T(512)(128)(4,1)} %constant.90) | copy-start | bytes 34
  45.5 6.3 %collective-permute-start.7 = (f32[184,128]{1,0:T(8,128)S(1)}, f32[184,128]{1,0:T(8,128)S(1)}, u32[]{:S(2)}, u32[]{:S(2)}) collective-permute-start(f32[184,128]{1,0:T(8,128)S(1)} %select_maximum_fusion.1), channel_id=1, source_target_pairs={{0,12},{1,13},{2,14},{3,15},{4,8},{5,9},{6,10},{7,11},{8,20},{9,21... | collective-permute-start | bytes 282632 | tf_op jit(solution)/shard_map/ppermute | solution.py:209
  50.0 12.1 %copy-start.2 = (pred[20]{0:T(512)(128)(4,1)S(1)}, pred[20]{0:T(512)(128)(4,1)}, u32[]{:S(2)}) copy-start(pred[20]{0:T(512)(128)(4,1)} %constant.112) | copy-start | bytes 64
  50.1 12.1 %copy-start.3 = (pred[20]{0:T(512)(128)(4,1)S(1)}, pred[20]{0:T(512)(128)(4,1)}, u32[]{:S(2)}) copy-start(pred[20]{0:T(512)(128)(4,1)} %constant.93) | copy-start | bytes 64
  50.3 10.4 %collective-permute-start.9 = (f32[184,128]{1,0:T(8,128)S(1)}, f32[184,128]{1,0:T(8,128)S(1)}, u32[]{:S(2)}, u32[]{:S(2)}) collective-permute-start(f32[184,128]{1,0:T(8,128)S(1)} %select_maximum_fusion), channel_id=1, source_target_pairs={{0,252},{1,253},{2,254},{3,255},{4,248},{5,249},{6,250},{7,251},{8... | collective-permute-start | bytes 282632 | tf_op jit(solution)/shard_map/ppermute | solution.py:209

commit v8 on v5

--- a/solution.py
+++ b/solution.py
@@ -176,9 +176,9 @@
                 elif cy == -1:
                     edge = jnp.broadcast_to(hyp_ref[y_dn.index(n), pl.ds(src, 1), :], (ny, nz))
                     tile = jnp.where(row == ny - 1, edge, pltpu.roll(tile, ny - 1, 0))
-            if cz == 1:
+            if 0 <= src < nx and cz == 1:
                 tile = jnp.where(lane == 0, col_ref[z_any.index(n), x], pltpu.roll(tile, 1, 1))
-            elif cz == -1:
+            elif 0 <= src < nx and cz == -1:
                 tile = jnp.where(lane == nz - 1, col_ref[z_any.index(n), x], pltpu.roll(tile, nz - 1, 1))
             out[n % pops, x] = tile
 
@@ -298,31 +298,12 @@
         ]
     )
     hy_m, hy_p = up2[:n_yu], dn2[:n_yd]
-    low2, high2 = exchange(
-        [
-            (jnp.concatenate([up2[n_yu:], send_up]), (1, q, 0)),
-            (jnp.concatenate([send_dn, dn2[n_yd:]]), (-1, -q, 0)),
-        ]
-    )
-    n_up, n_dn = send_up.shape[0], send_dn.shape[0]
-    xa, xb, xc, xd = low2[:n_up], low2[n_up:], high2[:n_dn], high2[n_dn:]
 
     def unpack_x(got, count):
         return got[: count * ny].reshape(count, ny, nz), got[count * ny :, :ny]
 
     def unpack_y(got, count):
         return got[: count * nx].reshape(count, nx, nz), got[count * nx :, :nx]
-
-    pa2, ca = unpack_x(xa, len(x_up))
-    pb2, cb = unpack_x(xb, len(x_up))
-    pc2, cc = unpack_x(xc, len(x_dn))
-    pd2, cd = unpack_x(xd, len(x_dn))
-    hy_m, cy_m = unpack_y(hy_m, len(y_up))
-    hy_p, cy_p = unpack_y(hy_p, len(y_dn))
-    win_low = lax.dynamic_slice_in_dim(jnp.concatenate([pa2, pb2], axis=1), ny - rem - 1, ny + 2, 1)
-    win_high = lax.dynamic_slice_in_dim(jnp.concatenate([pc2, pd2], axis=1), rem - 1, ny + 2, 1)
-    xzw_low = lax.dynamic_slice_in_dim(jnp.concatenate([ca, cb], axis=1), ny - rem, ny, 1)
-    xzw_high = lax.dynamic_slice_in_dim(jnp.concatenate([cc, cd], axis=1), rem, ny, 1)
 
     def by_pop(idx, axis_id, shape):
         return jnp.array([vel[n][axis_id] for n in idx], jnp.int32).reshape(shape)
@@ -331,8 +312,37 @@
         cy = by_pop(idx, 1, (-1, 1, 1))
         return jnp.where(cy == 1, win[:, :ny], jnp.where(cy == -1, win[:, 2:], win[:, 1 : ny + 1]))
 
-    xlow = pick_y(win_low, x_up)
-    xhigh = pick_y(win_high, x_dn)
+    def shift_z(planes, idx, edge_cols, edge_idx):
+        cz = by_pop(idx, 2, (-1, 1, 1))
+        zero = jnp.zeros((1, ny), planes.dtype)
+        col = jnp.concatenate([edge_cols, zero])[
+            jnp.array([edge_idx.index(n) if n in edge_idx else len(edge_idx) for n in idx])
+        ][:, :, None]
+        return jnp.where(
+            cz == 1,
+            jnp.concatenate([col, planes[:, :, :-1]], axis=2),
+            jnp.where(cz == -1, jnp.concatenate([planes[:, :, 1:], col], axis=2), planes),
+        )
+
+    def window(first, second, idx, edge_idx, start):
+        count = len(idx)
+        pa, ca = unpack_x(first, count)
+        pb, cb = unpack_x(second, count)
+        planes = lax.dynamic_slice_in_dim(jnp.concatenate([pa, pb], axis=1), start - 1, ny + 2, 1)
+        cols = lax.dynamic_slice_in_dim(jnp.concatenate([ca, cb], axis=1), start, ny, 1)
+        return shift_z(pick_y(planes, idx), idx, cols, edge_idx).reshape(-1, nz)
+
+    low2, high2 = exchange(
+        [
+            (window(up2[n_yu:], send_up, x_up, xz_up, ny - rem), (1, q, 0)),
+            (window(send_dn, dn2[n_yd:], x_dn, xz_dn, rem), (-1, -q, 0)),
+        ]
+    )
+    hy_m, cy_m = unpack_y(hy_m, len(y_up))
+    hy_p, cy_p = unpack_y(hy_p, len(y_dn))
+
+    xlow = low2.reshape(len(x_up), ny, nz)
+    xhigh = high2.reshape(len(x_dn), ny, nz)
     z_any = pick(lambda c: c[2] != 0)
     zh = jnp.concatenate([hz_m, hz_p])[jnp.array([z_up.index(n) if vel[n][2] == 1 else len(z_up) + z_dn.index(n) for n in z_any])]
 
@@ -348,8 +358,8 @@
     down = jnp.concatenate([corner_m, zh[:, :, :-1]], axis=2)
     up = jnp.concatenate([zh[:, :, 1:], corner_p], axis=2)
     zy = jnp.where(cy == 1, down, jnp.where(cy == -1, up, zh))
-    edge_low = spread(xzw_low, xz_up)[:, None]
-    edge_high = spread(xzw_high, xz_dn)[:, None]
+    edge_low = jnp.zeros((len(z_any), 1, ny), jnp.float32)
+    edge_high = edge_low
     cols = jnp.where(
         cx == 1,
         jnp.concatenate([edge_low, zy[:, :-1]], axis=1),

time: 67.4 us -> 66.6 us (0.988)
  the two profiles are of different devices: /device:TPU:2 before, /device:TPU:251 now
where the time goes in v8:
time: 66.6 us; the launch traced here: 66.4 us
  waiting for transfers between devices  30.7 us (46%)
  starting transfers between devices  14.3 us (21%)
  local copies, waits for them, and re-layouts  11.4 us (17%)
  Pallas kernels  5.84 us (9%)
  other arithmetic  2.26 us (3%)
  between operations  1.99 us (3%)
    ppermute x10, waiting for transfers between devices, exchange(): got = lax.ppermute(joined, AXES, pairs)  30.7 us
    ppermute x10, starting transfers between devices, exchange(): got = lax.ppermute(joined, AXES, pairs)  14.3 us
    pallas_call x1, Pallas kernels, local(): pl.pallas_call(collide_kernel, out_shape=jax.ShapeDtypeStruct((2 * f_pop....  3.06 us
    pallas_call x1, Pallas kernels, local(): pl.pallas_call(stream_kernel, out_shape=(jax.ShapeDtypeStruct((pops, nx,...  2.78 us
    unnamed x48, local copies, waits for them, and re-layouts  1.75 us
  transfers between devices with their start and end apart: 10, of which 8 were waited for; matrix products, arithmetic and copies ran while one was open for 6% of the time, Pallas kernels for 0%

profile of v8, /device:TPU:251, one launch (start us, length us, event | category | flops | bytes accessed | tf_op | source)
XLA Modules:
  0.0 66.4 jit_solution(1718359996375786978)
XLA Ops:
  0.6 0.0 copy-start.15
  0.6 0.0 copy-start.14
  0.7 0.0 copy-start.13
  0.7 1.1 %reduce_sum.9 = f32[4,16,128]{2,1,0:T(8,128)S(1)} reduce(f32[19,4,16,128]{3,2,1,0:T(8,128)} %g_ref.1, f32[]{:T(128)} %constant.24.clone.1), dimensions={0}, to_apply=%region_0.0 | reduce | flops 147456 | bytes 655364 | tf_op jit(solution)/shard_map/reduce_sum | solution.py:225
  1.9 1.3 %collective-permute-start = (f32[20,128]{1,0:T(8,128)S(1)}, f32[20,128]{1,0:T(8,128)S(1)}, u32[]{:S(2)}, u32[]{:S(2)}) collective-permute-start(f32[20,128]{1,0:T(8,128)S(1)} %pad_maximum_fusion.13), channel_id=1, source_target_pairs={{0,2},{1,3},{2,4},{3,5},{4,6},{5,7},{6,0},{7,1},{8,10},{9,11},{10,... | collective-permute-start | bytes 30728 | tf_op jit(solution)/shard_map/ppermute | solution.py:209
  3.1 0.3 collective-permute-start.2
  3.4 0.2 slice_reduce_fusion.3
  3.6 1.2 %collective-permute-start.4 = (f32[2,4,16]{2,1,0:T(4,128)S(1)}, f32[2,4,16]{2,1,0:T(4,128)S(1)}, u32[]{:S(2)}, u32[]{:S(2)}) collective-permute-start(f32[2,4,16]{2,1,0:T(4,128)S(1)} %pad_maximum_fusion.15), channel_id=1, source_target_pairs={{0,1},{1,0},{2,3},{3,2},{4,5},{5,4},{6,7},{7,6},{8,9},{9,8},{10,11... | collective-permute-start | bytes 1544 | tf_op jit(solution)/shard_map/ppermute | solution.py:209
  4.8 0.1 slice_bitcast_fusion.1
  5.7 4.3 %collective-permute-done.4 = f32[2,4,16]{2,1,0:T(4,128)S(1)} collective-permute-done((f32[2,4,16]{2,1,0:T(4,128)S(1)}, f32[2,4,16]{2,1,0:T(4,128)S(1)}, u32[]{:S(2)}, u32[]{:S(2)}) %collective-permute-start.4) | collective-permute-done | bytes 544 | tf_op jit(solution)/shard_map/ppermute | solution.py:209
  10.0 0.1 copy.53
  10.1 0.1 copy.54
  10.2 5.2 %collective-permute-start.1 = (f32[32,128]{1,0:T(8,128)S(1)}, f32[32,128]{1,0:T(8,128)S(1)}, u32[]{:S(2)}, u32[]{:S(2)}) collective-permute-start(f32[32,128]{1,0:T(8,128)S(1)} %pad_maximum_fusion.11), channel_id=1, source_target_pairs={{0,12},{1,13},{2,14},{3,15},{4,8},{5,9},{6,10},{7,11},{8,20},{9,21... | collective-permute-start | bytes 49160 | tf_op jit(solution)/shard_map/ppermute | solution.py:209
  15.4 0.1 collective-permute-start.3
  15.6 0.7 %collective-permute-done.1 = f32[32,128]{1,0:T(8,128)S(1)} collective-permute-done((f32[32,128]{1,0:T(8,128)S(1)}, f32[32,128]{1,0:T(8,128)S(1)}, u32[]{:S(2)}, u32[]{:S(2)}) %collective-permute-start.1) | collective-permute-done | bytes 16416 | tf_op jit(solution)/shard_map/ppermute | solution.py:209
  16.3 8.7 %collective-permute-done.3 = f32[32,128]{1,0:T(8,128)S(1)} collective-permute-done((f32[32,128]{1,0:T(8,128)S(1)}, f32[32,128]{1,0:T(8,128)S(1)}, u32[]{:S(2)}, u32[]{:S(2)}) %collective-permute-start.3) | collective-permute-done | bytes 16416 | tf_op jit(solution)/shard_map/ppermute | solution.py:209
  25.0 0.1 constant_dynamic-update-slice_fusion.3
  25.1 0.1 constant_dynamic-update-slice_fusion.nb_ref
  25.2 0.7 copy-done.1
  25.9 3.1 %shard_map.149.post_ref = f32[38,4,16,128]{3,2,1,0:T(8,128)} custom-call(f32[19,4,16,128]{3,2,1,0:T(8,128)} %f_ref.1, f32[19,4,16,128]{3,2,1,0:T(8,128)} %g_ref.1, f32[5,4,16,128]{3,2,1,0:T(8,128)} %copy-done.1), custom_call_target="tpu_custom_call" | custom-call | tf_op jit(solution)/shard_map/pallas_call | solution.py:251
  29.0 0.9 %constant_dynamic-update-slice_fusion.42 = (f32[10,4,16,128]{3,2,1,0:T(8,128)S(1)}, f32[10,4,16,128]{3,2,1,0:T(8,128)S(1)}) fusion(f32[38,4,16,128]{3,2,1,0:T(8,128)} %shard_map.149.post_ref), kind=kLoop, calls=%fused_computation.57 | loop fusion | bytes 131072
  29.8 1.2 %fusion.5 = (f32[5,4,16,128]{3,2,1,0:T(8,128)S(1)}, f32[5,4,16,128]{3,2,1,0:T(8,128)S(1)}, f32[5,4,16,128]{3,2,1,0:T(8,128)S(1)}, f32[5,4,16,128]{3,2,1,0:T(8,128)S(1)}) fusion(f32[38,4,16,128]{3,2,1,0:T(8,128)} %shard_map.149.post_ref), kind=kLoop, calls=%fused_computation.145 | loop fusion | bytes 1310720 | tf_op jit(solution)/shard_map/slice | solution.py:274
  31.3 0.4 slice_reduce_fusion
  31.8 0.1 collective-permute-start.5
  31.9 6.7 %collective-permute-done.5 = f32[20,4,16]{2,1,0:T(4,128)S(1)} collective-permute-done((f32[20,4,16]{2,1,0:T(4,128)S(1)}, f32[20,4,16]{2,1,0:T(4,128)S(1)}, u32[]{:S(2)}, u32[]{:S(2)}) %collective-permute-start.5) | collective-permute-done | bytes 5152 | tf_op jit(solution)/shard_map/ppermute | solution.py:209
  38.6 0.2 slice_reduce_fusion.11
  38.8 0.2 slice_reduce_fusion.10
  39.0 0.2 slice_reduce_fusion.9
  39.2 0.2 slice_reduce_fusion.8
  39.4 0.9 %collective-permute-start.6 = (f32[208,128]{1,0:T(8,128)S(1)}, f32[208,128]{1,0:T(8,128)S(1)}, u32[]{:S(2)}, u32[]{:S(2)}) collective-permute-start(f32[208,128]{1,0:T(8,128)S(1)} %pad_maximum_fusion), channel_id=1, source_target_pairs={{0,2},{1,3},{2,4},{3,5},{4,6},{5,7},{6,0},{7,1},{8,10},{9,11},{10,... | collective-permute-start | bytes 319496 | tf_op jit(solution)/shard_map/ppermute | solution.py:209
  40.3 0.1 slice_reduce_fusion.7
  40.4 0.1 slice_reduce_fusion.6
  40.5 0.1 slice_reduce_fusion.5
  40.6 0.1 slice_reduce_fusion.4
  40.8 0.7 %collective-permute-start.8 = (f32[208,128]{1,0:T(8,128)S(1)}, f32[208,128]{1,0:T(8,128)S(1)}, u32[]{:S(2)}, u32[]{:S(2)}) collective-permute-start(f32[208,128]{1,0:T(8,128)S(1)} %pad_maximum_fusion.1), channel_id=1, source_target_pairs={{0,6},{1,7},{2,0},{3,1},{4,2},{5,3},{6,4},{7,5},{8,14},{9,15},{10,... | collective-permute-start | bytes 319496 | tf_op jit(solution)/shard_map/ppermute | solution.py:209
  41.6 0.6 gather_fusion.3
  42.2 0.1 fusion.9
  42.3 0.8 %collective-permute-done.6 = f32[208,128]{1,0:T(8,128)S(1)} collective-permute-done((f32[208,128]{1,0:T(8,128)S(1)}, f32[208,128]{1,0:T(8,128)S(1)}, u32[]{:S(2)}, u32[]{:S(2)}) %collective-permute-start.6) | collective-permute-done | bytes 106528 | tf_op jit(solution)/shard_map/ppermute | solution.py:209
  43.1 0.6 gather_fusion.2
  43.6 0.2 copy.62
  43.9 0.6 collective-permute-done.8
  44.5 0.6 gather_fusion.4
  45.1 0.2 copy.64
  45.3 0.2 maximum_select_fusion.4
  45.5 0.1 maximum_maximum_fusion
  45.6 0.1 constant_dynamic-slice_fusion.1
  45.6 0.6 gather_fusion
  46.2 0.1 copy.57
  46.4 0.1 pad_maximum_fusion.16
  46.5 0.1 constant_dynamic-slice_fusion
  46.5 0.6 gather_fusion.1
  47.1 0.1 copy.59
  47.4 0.1 fusion.2
  47.5 0.1 fusion.6
  47.6 0.1 fusion.7
  47.7 0.2 maximum_select_fusion.2
  47.9 4.5 %collective-permute-start.7 = (f32[160,128]{1,0:T(8,128)S(1)}, f32[160,128]{1,0:T(8,128)S(1)}, u32[]{:S(2)}, u32[]{:S(2)}) collective-permute-start(f32[160,128]{1,0:T(8,128)S(1)} %bitcast.120), channel_id=1, source_target_pairs={{0,12},{1,13},{2,14},{3,15},{4,8},{5,9},{6,10},{7,11},{8,20},{9,21... | collective-permute-start | bytes 245768 | tf_op jit(solution)/shard_map/ppermute | solution.py:209
  52.4 0.1 select_select_fusion
  52.5 0.6 slice.643
  53.1 0.6 slice.644
  53.7 0.1 collective-permute-done.7
  53.9 8.7 %collective-permute-done.9 = f32[160,128]{1,0:T(8,128)S(1)} collective-permute-done((f32[160,128]{1,0:T(8,128)S(1)}, f32[160,128]{1,0:T(8,128)S(1)}, u32[]{:S(2)}, u32[]{:S(2)}) %collective-permute-start.9) | collective-permute-done | bytes 81952 | tf_op jit(solution)/shard_map/ppermute | solution.py:209
  62.6 1.1 %broadcast_in_dim.125.col_ref = f32[20,4,16,128]{3,2,1,0:T(8,128)} broadcast(f32[20,4,16]{2,1,0:T(4,128)S(1)} %select_select_fusion), dimensions={0,1,2} | broadcast | bytes 660480 | tf_op jit(solution)/shard_map/broadcast_in_dim | solution.py:368
  63.6 2.8 %shard_map.150 = (f32[19,4,16,128]{3,2,1,0:T(8,128)}, f32[19,4,16,128]{3,2,1,0:T(8,128)}) custom-call(f32[38,4,16,128]{3,2,1,0:T(8,128)} %shard_map.149.post_ref, f32[10,16,128]{2,1,0:T(8,128)} %bitcast.117, f32[10,16,128]{2,1,0:T(8,128)} %bitcast.118, f32[10,4,128]{2,1,0:T(4,128)} %bitcast.115, f32[10,4,128]{2,1,0:T(4,128)} %bitcast.116, ...), custom_call_target="tpu_custom_call" | custom-call | tf_op jit(solution)/shard_map/pallas_call | solution.py:370
  (96 shorter events, 0.7 us)
Async XLA Ops:
  0.6 5.0 %copy-start.15 = (s32[20]{0:T(128)S(1)}, s32[20]{0:T(128)}, u32[]{:S(2)}) copy-start(s32[20]{0:T(128)} %constant.125) | copy-start | bytes 244
  0.6 5.0 %copy-start.14 = (s32[20]{0:T(128)S(1)}, s32[20]{0:T(128)}, u32[]{:S(2)}) copy-start(s32[20]{0:T(128)} %constant.127) | copy-start | bytes 244
  0.7 5.0 %copy-start.13 = (s32[20]{0:T(128)S(1)}, s32[20]{0:T(128)}, u32[]{:S(2)}) copy-start(s32[20]{0:T(128)} %constant.126) | copy-start | bytes 244
  0.7 5.0 %copy-start.12 = (s32[10]{0:T(128)S(1)}, s32[10]{0:T(128)}, u32[]{:S(2)}) copy-start(s32[10]{0:T(128)} %constant.123) | copy-start | bytes 124
  1.9 8.4 %collective-permute-start = (f32[20,128]{1,0:T(8,128)S(1)}, f32[20,128]{1,0:T(8,128)S(1)}, u32[]{:S(2)}, u32[]{:S(2)}) collective-permute-start(f32[20,128]{1,0:T(8,128)S(1)} %pad_maximum_fusion.13), channel_id=1, source_target_pairs={{0,2},{1,3},{2,4},{3,5},{4,6},{5,7},{6,0},{7,1},{8,10},{9,11},{10,... | collective-permute-start | bytes 30728 | tf_op jit(solution)/shard_map/ppermute | solution.py:209
  3.1 12.3 %collective-permute-start.2 = (f32[20,128]{1,0:T(8,128)S(1)}, f32[20,128]{1,0:T(8,128)S(1)}, u32[]{:S(2)}, u32[]{:S(2)}) collective-permute-start(f32[20,128]{1,0:T(8,128)S(1)} %pad_maximum_fusion.14), channel_id=1, source_target_pairs={{0,6},{1,7},{2,0},{3,1},{4,2},{5,3},{6,4},{7,5},{8,14},{9,15},{10,... | collective-permute-start | bytes 30728 | tf_op jit(solution)/shard_map/ppermute | solution.py:209
  3.6 6.5 %collective-permute-start.4 = (f32[2,4,16]{2,1,0:T(4,128)S(1)}, f32[2,4,16]{2,1,0:T(4,128)S(1)}, u32[]{:S(2)}, u32[]{:S(2)}) collective-permute-start(f32[2,4,16]{2,1,0:T(4,128)S(1)} %pad_maximum_fusion.15), channel_id=1, source_target_pairs={{0,1},{1,0},{2,3},{3,2},{4,5},{5,4},{6,7},{7,6},{8,9},{9,8},{10,11... | collective-permute-start | bytes 1544 | tf_op jit(solution)/shard_map/ppermute | solution.py:209
  10.2 6.1 %collective-permute-start.1 = (f32[32,128]{1,0:T(8,128)S(1)}, f32[32,128]{1,0:T(8,128)S(1)}, u32[]{:S(2)}, u32[]{:S(2)}) collective-permute-start(f32[32,128]{1,0:T(8,128)S(1)} %pad_maximum_fusion.11), channel_id=1, source_target_pairs={{0,12},{1,13},{2,14},{3,15},{4,8},{5,9},{6,10},{7,11},{8,20},{9,21... | collective-permute-start | bytes 49160 | tf_op jit(solution)/shard_map/ppermute | solution.py:209
  15.4 9.6 %collective-permute-start.3 = (f32[32,128]{1,0:T(8,128)S(1)}, f32[32,128]{1,0:T(8,128)S(1)}, u32[]{:S(2)}, u32[]{:S(2)}) collective-permute-start(f32[32,128]{1,0:T(8,128)S(1)} %pad_maximum_fusion.12), channel_id=1, source_target_pairs={{0,252},{1,253},{2,254},{3,255},{4,248},{5,249},{6,250},{7,251},{8... | collective-permute-start | bytes 49160 | tf_op jit(solution)/shard_map/ppermute | solution.py:209
  25.2 0.7 %copy-start.1 = (f32[5,4,16,128]{3,2,1,0:T(8,128)}, f32[5,4,16,128]{3,2,1,0:T(8,128)S(1)}, u32[]{:S(2)}) copy-start(f32[5,4,16,128]{3,2,1,0:T(8,128)S(1)} %constant_dynamic-update-slice_fusion.nb_ref) | copy-start | bytes 491524
  29.0 2.1 %copy-start = (f32[38,4,16,128]{3,2,1,0:T(8,128)S(1)}, f32[38,4,16,128]{3,2,1,0:T(8,128)}, u32[]{:S(2)}) copy-start(f32[38,4,16,128]{3,2,1,0:T(8,128)} %shard_map.149.post_ref) | copy-start | bytes 3735556
  31.7 13.6 %copy-start.10 = (pred[20]{0:T(512)(128)(4,1)S(1)}, pred[20]{0:T(512)(128)(4,1)}, u32[]{:S(2)}) copy-start(pred[20]{0:T(512)(128)(4,1)} %constant.108) | copy-start | bytes 64
  31.7 13.6 %copy-start.11 = (pred[20]{0:T(512)(128)(4,1)S(1)}, pred[20]{0:T(512)(128)(4,1)}, u32[]{:S(2)}) copy-start(pred[20]{0:T(512)(128)(4,1)} %constant.117) | copy-start | bytes 64
  31.8 6.8 %collective-permute-start.5 = (f32[20,4,16]{2,1,0:T(4,128)S(1)}, f32[20,4,16]{2,1,0:T(4,128)S(1)}, u32[]{:S(2)}, u32[]{:S(2)}) collective-permute-start(f32[20,4,16]{2,1,0:T(4,128)S(1)} %pad_maximum_fusion.4), channel_id=1, source_target_pairs={{0,1},{1,0},{2,3},{3,2},{4,5},{5,4},{6,7},{7,6},{8,9},{9,8},{10,11... | collective-permute-start | bytes 15368 | tf_op jit(solution)/shard_map/ppermute | solution.py:209
  39.4 3.6 %collective-permute-start.6 = (f32[208,128]{1,0:T(8,128)S(1)}, f32[208,128]{1,0:T(8,128)S(1)}, u32[]{:S(2)}, u32[]{:S(2)}) collective-permute-start(f32[208,128]{1,0:T(8,128)S(1)} %pad_maximum_fusion), channel_id=1, source_target_pairs={{0,2},{1,3},{2,4},{3,5},{4,6},{5,7},{6,0},{7,1},{8,10},{9,11},{10,... | collective-permute-start | bytes 319496 | tf_op jit(solution)/shard_map/ppermute | solution.py:209
  40.8 6.6 %copy-start.8 = (pred[10]{0:T(512)(128)(4,1)S(1)}, pred[10]{0:T(512)(128)(4,1)}, u32[]{:S(2)}) copy-start(pred[10]{0:T(512)(128)(4,1)} %constant.100) | copy-start | bytes 34
  40.8 6.6 %copy-start.9 = (pred[10]{0:T(512)(128)(4,1)S(1)}, pred[10]{0:T(512)(128)(4,1)}, u32[]{:S(2)}) copy-start(pred[10]{0:T(512)(128)(4,1)} %constant.101) | copy-start | bytes 34
  40.8 3.6 %collective-permute-start.8 = (f32[208,128]{1,0:T(8,128)S(1)}, f32[208,128]{1,0:T(8,128)S(1)}, u32[]{:S(2)}, u32[]{:S(2)}) collective-permute-start(f32[208,128]{1,0:T(8,128)S(1)} %pad_maximum_fusion.1), channel_id=1, source_target_pairs={{0,6},{1,7},{2,0},{3,1},{4,2},{5,3},{6,4},{7,5},{8,14},{9,15},{10,... | collective-permute-start | bytes 319496 | tf_op jit(solution)/shard_map/ppermute | solution.py:209
  46.2 1.5 %copy-start.6 = (pred[10]{0:T(512)(128)(4,1)S(1)}, pred[10]{0:T(512)(128)(4,1)}, u32[]{:S(2)}) copy-start(pred[10]{0:T(512)(128)(4,1)} %constant.102) | copy-start | bytes 34
  46.2 1.5 %copy-start.7 = (pred[10]{0:T(512)(128)(4,1)S(1)}, pred[10]{0:T(512)(128)(4,1)}, u32[]{:S(2)}) copy-start(pred[10]{0:T(512)(128)(4,1)} %constant.95) | copy-start | bytes 34
  47.3 5.1 %copy-start.4 = (pred[20]{0:T(512)(128)(4,1)S(1)}, pred[20]{0:T(512)(128)(4,1)}, u32[]{:S(2)}) copy-start(pred[20]{0:T(512)(128)(4,1)} %constant.107) | copy-start | bytes 64
  47.3 5.1 %copy-start.5 = (pred[20]{0:T(512)(128)(4,1)S(1)}, pred[20]{0:T(512)(128)(4,1)}, u32[]{:S(2)}) copy-start(pred[20]{0:T(512)(128)(4,1)} %constant.122) | copy-start | bytes 64
  47.9 6.0 %collective-permute-start.7 = (f32[160,128]{1,0:T(8,128)S(1)}, f32[160,128]{1,0:T(8,128)S(1)}, u32[]{:S(2)}, u32[]{:S(2)}) collective-permute-start(f32[160,128]{1,0:T(8,128)S(1)} %bitcast.120), channel_id=1, source_target_pairs={{0,12},{1,13},{2,14},{3,15},{4,8},{5,9},{6,10},{7,11},{8,20},{9,21... | collective-permute-start | bytes 245768 | tf_op jit(solution)/shard_map/ppermute | solution.py:209
  52.4 10.2 %collective-permute-start.9 = (f32[160,128]{1,0:T(8,128)S(1)}, f32[160,128]{1,0:T(8,128)S(1)}, u32[]{:S(2)}, u32[]{:S(2)}) collective-permute-start(f32[160,128]{1,0:T(8,128)S(1)} %bitcast.119), channel_id=1, source_target_pairs={{0,252},{1,253},{2,254},{3,255},{4,248},{5,249},{6,250},{7,251},{8... | collective-permute-start | bytes 245768 | tf_op jit(solution)/shard_map/ppermute | solution.py:209
  53.9 9.8 %copy-start.2 = (f32[160,128]{1,0:T(8,128)}, f32[160,128]{1,0:T(8,128)S(1)}, u32[]{:S(2)}) copy-start(f32[160,128]{1,0:T(8,128)S(1)} %collective-permute-done.7) | copy-start | bytes 245764
  62.6 1.1 %copy-start.3 = (f32[160,128]{1,0:T(8,128)}, f32[160,128]{1,0:T(8,128)S(1)}, u32[]{:S(2)}) copy-start(f32[160,128]{1,0:T(8,128)S(1)} %collective-permute-done.9) | copy-start | bytes 245764

commit v9 on v8

--- a/solution.py
+++ b/solution.py
@@ -136,16 +136,41 @@
     return (f_posts, g_posts)
 
 
-def collide_kernel(f_ref, g_ref, nb_ref, post_ref):
+def pop_groups(pops):
+    vel = [VELOCITIES[n % pops] for n in range(2 * pops)]
+    groups = {
+        name: [n for n in range(2 * pops) if vel[n][axis_id] == sign]
+        for name, axis_id, sign in (
+            ("x_up", 0, 1), ("x_dn", 0, -1), ("y_up", 1, 1), ("y_dn", 1, -1), ("z_up", 2, 1), ("z_dn", 2, -1)
+        )
+    }
+    order = groups["z_up"] + groups["z_dn"] + [n for n in range(2 * pops) if vel[n][2] == 0]
+    slot = {n: i for i, n in enumerate(order)}
+    return vel, groups, slot
+
+
+def collide_kernel(f_ref, g_ref, nb_ref, post_ref, xu_ref, xd_ref, yu_ref, yd_ref):
     pops = f_ref.shape[0]
-    for x in range(f_ref.shape[1]):
+    nx, ny = f_ref.shape[1], f_ref.shape[2]
+    vel, groups, slot = pop_groups(pops)
+    for x in range(nx):
         f_planes = [f_ref[n, x] for n in range(pops)]
         g_planes = [g_ref[n, x] for n in range(pops)]
         slopes = [nb_ref[2 + a, x] for a in range(3)]
         f_posts, g_posts = collide_lists(f_planes, g_planes, nb_ref[0, x], nb_ref[1, x], slopes)
-        for n in range(pops):
-            post_ref[n, x] = f_posts[n]
-            post_ref[pops + n, x] = g_posts[n]
+        planes = f_posts + g_posts
+        for n in range(2 * pops):
+            post_ref[slot[n], x] = planes[n]
+        if x == nx - 1:
+            for k, n in enumerate(groups["x_up"]):
+                xu_ref[k] = planes[n]
+        if x == 0:
+            for k, n in enumerate(groups["x_dn"]):
+                xd_ref[k] = planes[n]
+        for k, n in enumerate(groups["y_up"]):
+            yu_ref[k, pl.ds(x, 1), :] = planes[n][ny - 1 : ny, :]
+        for k, n in enumerate(groups["y_dn"]):
+            yd_ref[k, pl.ds(x, 1), :] = planes[n][0:1, :]
 
 
 def stream_kernel(post_ref, xlow_ref, xhigh_ref, hym_ref, hyp_ref, col_ref, f_ref, g_ref):
@@ -169,7 +194,7 @@
             elif src >= nx:
                 tile = xhigh_ref[x_dn.index(n)]
             else:
-                tile = post_ref[n, src]
+                tile = post_ref[pop_groups(pops)[2][n], src]
                 if cy == 1:
                     edge = jnp.broadcast_to(hym_ref[y_up.index(n), pl.ds(src, 1), :], (ny, nz))
                     tile = jnp.where(row == 0, edge, pltpu.roll(tile, 1, 0))
@@ -248,9 +273,18 @@
     laplace = neigh_xm + neigh_xp + neigh_ym + neigh_yp + neigh_zm + neigh_zp - 6.0 * phi
     slopes = [0.5 * (neigh_xp - neigh_xm), 0.5 * (neigh_yp - neigh_ym), 0.5 * (neigh_zp - neigh_zm)]
     nb = jnp.stack([phi, laplace] + slopes)
-    post = pl.pallas_call(
+    pops = f_pop.shape[0]
+    _, groups, slot = pop_groups(pops)
+    n_xu, n_xd, n_yu, n_yd = (len(groups[k]) for k in ("x_up", "x_dn", "y_up", "y_dn"))
+    post, face_xu, face_xd, face_yu, face_yd = pl.pallas_call(
         collide_kernel,
-        out_shape=jax.ShapeDtypeStruct((2 * f_pop.shape[0], nx, ny, nz), jnp.float32),
+        out_shape=(
+            jax.ShapeDtypeStruct((2 * pops, nx, ny, nz), jnp.float32),
+            jax.ShapeDtypeStruct((n_xu, ny, nz), jnp.float32),
+            jax.ShapeDtypeStruct((n_xd, ny, nz), jnp.float32),
+            jax.ShapeDtypeStruct((n_yu, nx, nz), jnp.float32),
+            jax.ShapeDtypeStruct((n_yd, nx, nz), jnp.float32),
+        ),
         interpret=INTERPRET,
     )(f_pop, g_pop, nb)
 
@@ -270,11 +304,11 @@
     yz_up = pick(lambda c: c[2] != 0, y_up)
     yz_dn = pick(lambda c: c[2] != 0, y_dn)
 
-    def rows(idx):
-        return jnp.stack([post[n] for n in idx])
-
     hz_m, hz_p = exchange(
-        [(rows(z_up)[:, :, :, -1], (0, 0, 1)), (rows(z_dn)[:, :, :, 0], (0, 0, -1))]
+        [
+            (post[: len(z_up), :, :, -1], (0, 0, 1)),
+            (post[len(z_up) : len(z_up) + len(z_dn), :, :, 0], (0, 0, -1)),
+        ]
     )
 
     def zhalo(n):
@@ -286,10 +320,10 @@
     def packed(face, extra):
         return jnp.concatenate([face.reshape(-1, nz), lanes(jnp.stack(extra))], axis=0)
 
-    send_up = packed(rows(x_up)[:, -1], [zhalo(n)[-1] for n in xz_up])
-    send_dn = packed(rows(x_dn)[:, 0], [zhalo(n)[0] for n in xz_dn])
-    send_yu = packed(rows(y_up)[:, :, -1], [zhalo(n)[:, -1] for n in yz_up])
-    send_yd = packed(rows(y_dn)[:, :, 0], [zhalo(n)[:, 0] for n in yz_dn])
+    send_up = packed(face_xu, [zhalo(n)[-1] for n in xz_up])
+    send_dn = packed(face_xd, [zhalo(n)[0] for n in xz_dn])
+    send_yu = packed(face_yu, [zhalo(n)[:, -1] for n in yz_up])
+    send_yd = packed(face_yd, [zhalo(n)[:, 0] for n in yz_dn])
     n_yu, n_yd = send_yu.shape[0], send_yd.shape[0]
     up2, dn2 = exchange(
         [

time: 66.6 us -> 65.2 us (0.979)
  the two profiles are of different devices: /device:TPU:251 before, /device:TPU:2 now
where the time goes in v9:
time: 65.2 us; the launch traced here: 64.9 us
  starting transfers between devices  31.5 us (48%)
  waiting for transfers between devices  12.7 us (19%)
  local copies, waits for them, and re-layouts  10 us (15%)
  Pallas kernels  5.83 us (9%)
  other arithmetic  3.14 us (5%)
  between operations  1.79 us (3%)
    ppermute x10, starting transfers between devices, exchange(): got = lax.ppermute(joined, AXES, pairs)  31.5 us
    ppermute x10, waiting for transfers between devices, exchange(): got = lax.ppermute(joined, AXES, pairs)  12.7 us
    pallas_call x1, Pallas kernels, local(): pl.pallas_call(collide_kernel, out_shape=(jax.ShapeDtypeStruct((2 * pops,...  3.05 us
    pallas_call x1, Pallas kernels, local(): pl.pallas_call(stream_kernel, out_shape=(jax.ShapeDtypeStruct((pops, nx,...  2.78 us
    slice x1, local copies, waits for them, and re-layouts, local(): post[:len(z_up), :, :, -1]  1.51 us
  transfers between devices with their start and end apart: 10, of which 7 were waited for; matrix products, arithmetic and copies ran while one was open for 6% of the time, Pallas kernels for 0%

profile of v9, /device:TPU:2, one launch (start us, length us, event | category | flops | bytes accessed | tf_op | source)
XLA Modules:
  0.0 64.9 jit_solution(7305432838048239146)
XLA Ops:
  0.6 0.0 copy-start.17
  0.6 0.0 copy-start.16
  0.7 0.0 copy-start.15
  0.7 1.1 %reduce_sum.9 = f32[4,16,128]{2,1,0:T(8,128)S(1)} reduce(f32[19,4,16,128]{3,2,1,0:T(8,128)} %g_ref.1, f32[]{:T(128)} %constant.24.clone.1), dimensions={0}, to_apply=%region_0.0 | reduce | flops 147456 | bytes 655364 | tf_op jit(solution)/shard_map/reduce_sum | solution.py:250
  1.8 0.2 slice_reduce_fusion.3
  2.0 7.3 %collective-permute-start.4 = (f32[2,4,16]{2,1,0:T(4,128)S(1)}, f32[2,4,16]{2,1,0:T(4,128)S(1)}, u32[]{:S(2)}, u32[]{:S(2)}) collective-permute-start(f32[2,4,16]{2,1,0:T(4,128)S(1)} %pad_maximum_fusion.13), channel_id=1, source_target_pairs={{0,1},{1,0},{2,3},{3,2},{4,5},{5,4},{6,7},{7,6},{8,9},{9,8},{10,11... | collective-permute-start | bytes 1544 | tf_op jit(solution)/shard_map/ppermute | solution.py:234
  9.3 0.6 collective-permute-start.2
  9.9 1.5 %collective-permute-start = (f32[20,128]{1,0:T(8,128)S(1)}, f32[20,128]{1,0:T(8,128)S(1)}, u32[]{:S(2)}, u32[]{:S(2)}) collective-permute-start(f32[20,128]{1,0:T(8,128)S(1)} %pad_maximum_fusion.11), channel_id=1, source_target_pairs={{0,2},{1,3},{2,4},{3,5},{4,6},{5,7},{6,0},{7,1},{8,10},{9,11},{10,... | collective-permute-start | bytes 30728 | tf_op jit(solution)/shard_map/ppermute | solution.py:234
  11.4 0.1 slice_bitcast_fusion.1
  12.2 0.1 copy.42
  12.3 0.1 copy.43
  12.4 1.9 %collective-permute-done = f32[20,128]{1,0:T(8,128)S(1)} collective-permute-done((f32[20,128]{1,0:T(8,128)S(1)}, f32[20,128]{1,0:T(8,128)S(1)}, u32[]{:S(2)}, u32[]{:S(2)}) %collective-permute-start) | collective-permute-done | bytes 10272 | tf_op jit(solution)/shard_map/ppermute | solution.py:234
  14.3 0.1 collective-permute-start.1
  14.5 8.0 %collective-permute-start.3 = (f32[32,128]{1,0:T(8,128)S(1)}, f32[32,128]{1,0:T(8,128)S(1)}, u32[]{:S(2)}, u32[]{:S(2)}) collective-permute-start(f32[32,128]{1,0:T(8,128)S(1)} %pad_maximum_fusion.10), channel_id=1, source_target_pairs={{0,252},{1,253},{2,254},{3,255},{4,248},{5,249},{6,250},{7,251},{8... | collective-permute-start | bytes 49160 | tf_op jit(solution)/shard_map/ppermute | solution.py:234
  22.5 1.3 %collective-permute-done.1 = f32[32,128]{1,0:T(8,128)S(1)} collective-permute-done((f32[32,128]{1,0:T(8,128)S(1)}, f32[32,128]{1,0:T(8,128)S(1)}, u32[]{:S(2)}, u32[]{:S(2)}) %collective-permute-start.1) | collective-permute-done | bytes 16416 | tf_op jit(solution)/shard_map/ppermute | solution.py:234
  23.8 0.1 collective-permute-done.3
  23.9 0.1 fusion.5
  24.0 0.0 copy-start.14
  24.1 0.1 multiply_dynamic-update-slice_fusion.nb_ref
  24.2 0.7 %copy-done.2 = f32[5,4,16,128]{3,2,1,0:T(8,128)} copy-done((f32[5,4,16,128]{3,2,1,0:T(8,128)}, f32[5,4,16,128]{3,2,1,0:T(8,128)S(1)}, u32[]{:S(2)}) %copy-start.2) | copy-done | bytes 163864
  24.8 3.0 %shard_map.149 = (f32[38,4,16,128]{3,2,1,0:T(8,128)}, f32[10,16,128]{2,1,0:T(8,128)}, f32[10,16,128]{2,1,0:T(8,128)}, f32[10,4,128]{2,1,0:T(4,128)}, f32[10,4,128]{2,1,0:T(4,128)}) custom-call(f32[19,4,16,128]{3,2,1,0:T(8,128)} %f_ref.1, f32[19,4,16,128]{3,2,1,0:T(8,128)} %g_ref.1, f32[5,4,16,128]{3,2,1,0:T(8,128)} %copy-done.2), custom_call_target="tpu_custom_call" | custom-call | tf_op jit(solution)/shard_map/pallas_call | solution.py:279
  27.9 0.0 copy-start.12
  27.9 0.0 copy-start.13
  27.9 1.5 %slice_reduce_fusion.1 = (f32[10,4,16]{2,1,0:T(4,128)S(1)}, f32[10,4,16]{2,1,0:T(4,128)S(1)}) fusion(f32[38,4,16,128]{3,2,1,0:T(8,128)} %get-tuple-element.7.post_ref), kind=kLoop, calls=%fused_computation.6 | loop fusion | bytes 10240 | tf_op jit(solution)/shard_map/slice | solution.py:309
  29.5 2.8 %collective-permute-start.5 = (f32[20,4,16]{2,1,0:T(4,128)S(1)}, f32[20,4,16]{2,1,0:T(4,128)S(1)}, u32[]{:S(2)}, u32[]{:S(2)}) collective-permute-start(f32[20,4,16]{2,1,0:T(4,128)S(1)} %pad_maximum_fusion.2), channel_id=1, source_target_pairs={{0,1},{1,0},{2,3},{3,2},{4,5},{5,4},{6,7},{7,6},{8,9},{9,8},{10,11... | collective-permute-start | bytes 15368 | tf_op jit(solution)/shard_map/ppermute | solution.py:234
  32.3 5.5 %collective-permute-done.5 = f32[20,4,16]{2,1,0:T(4,128)S(1)} collective-permute-done((f32[20,4,16]{2,1,0:T(4,128)S(1)}, f32[20,4,16]{2,1,0:T(4,128)S(1)}, u32[]{:S(2)}, u32[]{:S(2)}) %collective-permute-start.5) | collective-permute-done | bytes 5152 | tf_op jit(solution)/shard_map/ppermute | solution.py:234
  37.8 0.6 gather_fusion.3
  38.4 0.1 fusion.9
  38.5 0.1 slice_reduce_fusion.6
  38.7 0.2 slice_reduce_fusion.4
  38.9 0.9 %pad_maximum_fusion.1 = f32[208,128]{1,0:T(8,128)S(1)} fusion(f32[4,128]{1,0:T(4,128)S(1)} %select_maximum_fusion, f32[160,128]{1,0:T(8,128)} %bitcast.105, f32[4,128]{1,0:T(4,128)S(1)} %select_maximum_fusion.3, f32[40,128]{1,0:T(8,128)} %bitcast.119), kind=kLoop, calls=%fused_computation.14 | loop fusion | flops 79872 | bytes 212992 | tf_op jit(solution)/shard_map/concatenate | solution.py:331
  39.8 2.9 %collective-permute-start.8 = (f32[208,128]{1,0:T(8,128)S(1)}, f32[208,128]{1,0:T(8,128)S(1)}, u32[]{:S(2)}, u32[]{:S(2)}) collective-permute-start(f32[208,128]{1,0:T(8,128)S(1)} %pad_maximum_fusion.1), channel_id=1, source_target_pairs={{0,6},{1,7},{2,0},{3,1},{4,2},{5,3},{6,4},{7,5},{8,14},{9,15},{10,... | collective-permute-start | bytes 319496 | tf_op jit(solution)/shard_map/ppermute | solution.py:234
  42.7 0.2 slice_reduce_fusion.8
  43.0 0.2 slice_reduce_fusion.10
  43.3 0.1 collective-permute-start.6
  43.3 1.7 %collective-permute-done.8 = f32[208,128]{1,0:T(8,128)S(1)} collective-permute-done((f32[208,128]{1,0:T(8,128)S(1)}, f32[208,128]{1,0:T(8,128)S(1)}, u32[]{:S(2)}, u32[]{:S(2)}) %collective-permute-start.8) | collective-permute-done | bytes 106528 | tf_op jit(solution)/shard_map/ppermute | solution.py:234
  45.0 0.1 pad_maximum_fusion.14
  45.1 0.1 constant_dynamic-slice_fusion
  45.2 0.6 gather_fusion.4
  45.8 0.2 copy.51
  46.0 0.6 gather_fusion.1
  46.6 0.1 copy.46
  46.7 1.3 %collective-permute-done.6 = f32[208,128]{1,0:T(8,128)S(1)} collective-permute-done((f32[208,128]{1,0:T(8,128)S(1)}, f32[208,128]{1,0:T(8,128)S(1)}, u32[]{:S(2)}, u32[]{:S(2)}) %collective-permute-start.6) | collective-permute-done | bytes 106528 | tf_op jit(solution)/shard_map/ppermute | solution.py:234
  48.1 0.1 maximum_maximum_fusion
  48.1 0.1 constant_dynamic-slice_fusion.1
  48.2 0.6 gather_fusion
  48.8 0.6 gather_fusion.2
  49.3 0.2 copy.49
  49.6 0.1 copy.44
  49.7 0.2 maximum_select_fusion.4
  50.1 0.1 fusion.2
  50.2 0.1 fusion.6
  50.3 0.1 fusion.7
  50.4 0.1 copy-done.8
  50.5 0.0 copy-done.9
  50.6 0.2 maximum_select_fusion.2
  50.7 0.1 collective-permute-start.7
  50.8 8.0 %collective-permute-start.9 = (f32[160,128]{1,0:T(8,128)S(1)}, f32[160,128]{1,0:T(8,128)S(1)}, u32[]{:S(2)}, u32[]{:S(2)}) collective-permute-start(f32[160,128]{1,0:T(8,128)S(1)} %bitcast.112), channel_id=1, source_target_pairs={{0,252},{1,253},{2,254},{3,255},{4,248},{5,249},{6,250},{7,251},{8... | collective-permute-start | bytes 245768 | tf_op jit(solution)/shard_map/ppermute | solution.py:234
  58.9 0.1 select_select_fusion
  59.0 0.6 slice.406
  59.6 0.6 slice.405
  60.2 0.8 %collective-permute-done.7 = f32[160,128]{1,0:T(8,128)S(1)} collective-permute-done((f32[160,128]{1,0:T(8,128)S(1)}, f32[160,128]{1,0:T(8,128)S(1)}, u32[]{:S(2)}, u32[]{:S(2)}) %collective-permute-start.7) | collective-permute-done | bytes 81952 | tf_op jit(solution)/shard_map/ppermute | solution.py:234
  61.0 1.1 %broadcast_in_dim.125.col_ref = f32[20,4,16,128]{3,2,1,0:T(8,128)} broadcast(f32[20,4,16]{2,1,0:T(4,128)S(1)} %select_select_fusion), dimensions={0,1,2} | broadcast | bytes 660480 | tf_op jit(solution)/shard_map/broadcast_in_dim | solution.py:402
  62.1 2.8 %shard_map.150 = (f32[19,4,16,128]{3,2,1,0:T(8,128)}, f32[19,4,16,128]{3,2,1,0:T(8,128)}) custom-call(f32[38,4,16,128]{3,2,1,0:T(8,128)} %get-tuple-element.7.post_ref, f32[10,16,128]{2,1,0:T(8,128)} %bitcast.110, f32[10,16,128]{2,1,0:T(8,128)} %bitcast.111, f32[10,4,128]{2,1,0:T(4,128)} %bitcast.109, f32[10,4,128]{2,1,0:T(4,128)} %bitcast.108, ...), custom_call_target="tpu_custom_call" | custom-call | tf_op jit(solution)/shard_map/pallas_call | solution.py:404
  (74 shorter events, 0.5 us)
Async XLA Ops:
  0.6 11.5 %copy-start.17 = (s32[10]{0:T(128)S(1)}, s32[10]{0:T(128)}, u32[]{:S(2)}) copy-start(s32[10]{0:T(128)} %constant.123) | copy-start | bytes 124
  0.6 11.5 %copy-start.16 = (s32[20]{0:T(128)S(1)}, s32[20]{0:T(128)}, u32[]{:S(2)}) copy-start(s32[20]{0:T(128)} %constant.125) | copy-start | bytes 244
  0.7 11.5 %copy-start.15 = (s32[20]{0:T(128)S(1)}, s32[20]{0:T(128)}, u32[]{:S(2)}) copy-start(s32[20]{0:T(128)} %constant.126) | copy-start | bytes 244
  2.0 10.2 %collective-permute-start.4 = (f32[2,4,16]{2,1,0:T(4,128)S(1)}, f32[2,4,16]{2,1,0:T(4,128)S(1)}, u32[]{:S(2)}, u32[]{:S(2)}) collective-permute-start(f32[2,4,16]{2,1,0:T(4,128)S(1)} %pad_maximum_fusion.13), channel_id=1, source_target_pairs={{0,1},{1,0},{2,3},{3,2},{4,5},{5,4},{6,7},{7,6},{8,9},{9,8},{10,11... | collective-permute-start | bytes 1544 | tf_op jit(solution)/shard_map/ppermute | solution.py:234
  9.3 5.2 %collective-permute-start.2 = (f32[20,128]{1,0:T(8,128)S(1)}, f32[20,128]{1,0:T(8,128)S(1)}, u32[]{:S(2)}, u32[]{:S(2)}) collective-permute-start(f32[20,128]{1,0:T(8,128)S(1)} %pad_maximum_fusion.12), channel_id=1, source_target_pairs={{0,6},{1,7},{2,0},{3,1},{4,2},{5,3},{6,4},{7,5},{8,14},{9,15},{10,... | collective-permute-start | bytes 30728 | tf_op jit(solution)/shard_map/ppermute | solution.py:234
  9.9 4.4 %collective-permute-start = (f32[20,128]{1,0:T(8,128)S(1)}, f32[20,128]{1,0:T(8,128)S(1)}, u32[]{:S(2)}, u32[]{:S(2)}) collective-permute-start(f32[20,128]{1,0:T(8,128)S(1)} %pad_maximum_fusion.11), channel_id=1, source_target_pairs={{0,2},{1,3},{2,4},{3,5},{4,6},{5,7},{6,0},{7,1},{8,10},{9,11},{10,... | collective-permute-start | bytes 30728 | tf_op jit(solution)/shard_map/ppermute | solution.py:234
  14.3 9.5 %collective-permute-start.1 = (f32[32,128]{1,0:T(8,128)S(1)}, f32[32,128]{1,0:T(8,128)S(1)}, u32[]{:S(2)}, u32[]{:S(2)}) collective-permute-start(f32[32,128]{1,0:T(8,128)S(1)} %pad_maximum_fusion.9), channel_id=1, source_target_pairs={{0,12},{1,13},{2,14},{3,15},{4,8},{5,9},{6,10},{7,11},{8,20},{9,21... | collective-permute-start | bytes 49160 | tf_op jit(solution)/shard_map/ppermute | solution.py:234
  14.5 9.4 %collective-permute-start.3 = (f32[32,128]{1,0:T(8,128)S(1)}, f32[32,128]{1,0:T(8,128)S(1)}, u32[]{:S(2)}, u32[]{:S(2)}) collective-permute-start(f32[32,128]{1,0:T(8,128)S(1)} %pad_maximum_fusion.10), channel_id=1, source_target_pairs={{0,252},{1,253},{2,254},{3,255},{4,248},{5,249},{6,250},{7,251},{8... | collective-permute-start | bytes 49160 | tf_op jit(solution)/shard_map/ppermute | solution.py:234
  24.0 8.3 %copy-start.14 = (s32[20]{0:T(128)S(1)}, s32[20]{0:T(128)}, u32[]{:S(2)}) copy-start(s32[20]{0:T(128)} %constant.127) | copy-start | bytes 244
  24.2 0.7 %copy-start.2 = (f32[5,4,16,128]{3,2,1,0:T(8,128)}, f32[5,4,16,128]{3,2,1,0:T(8,128)S(1)}, u32[]{:S(2)}) copy-start(f32[5,4,16,128]{3,2,1,0:T(8,128)S(1)} %multiply_dynamic-update-slice_fusion.nb_ref) | copy-start | bytes 491524
  27.9 15.3 %copy-start = (f32[10,16,128]{2,1,0:T(8,128)S(1)}, f32[10,16,128]{2,1,0:T(8,128)}, u32[]{:S(2)}) copy-start(f32[10,16,128]{2,1,0:T(8,128)} %get-tuple-element.9) | copy-start | bytes 245764
  27.9 15.3 %copy-start.5 = (f32[10,4,128]{2,1,0:T(4,128)S(1)}, f32[10,4,128]{2,1,0:T(4,128)}, u32[]{:S(2)}) copy-start(f32[10,4,128]{2,1,0:T(4,128)} %get-tuple-element.8) | copy-start | bytes 61444
  27.9 21.8 %copy-start.12 = (pred[20]{0:T(512)(128)(4,1)S(1)}, pred[20]{0:T(512)(128)(4,1)}, u32[]{:S(2)}) copy-start(pred[20]{0:T(512)(128)(4,1)} %constant.117) | copy-start | bytes 64
  27.9 21.8 %copy-start.13 = (pred[20]{0:T(512)(128)(4,1)S(1)}, pred[20]{0:T(512)(128)(4,1)}, u32[]{:S(2)}) copy-start(pred[20]{0:T(512)(128)(4,1)} %constant.108) | copy-start | bytes 64
  29.4 20.5 %copy-start.1 = (f32[10,16,128]{2,1,0:T(8,128)S(1)}, f32[10,16,128]{2,1,0:T(8,128)}, u32[]{:S(2)}) copy-start(f32[10,16,128]{2,1,0:T(8,128)} %get-tuple-element.11) | copy-start | bytes 245764
  29.5 8.4 %collective-permute-start.5 = (f32[20,4,16]{2,1,0:T(4,128)S(1)}, f32[20,4,16]{2,1,0:T(4,128)S(1)}, u32[]{:S(2)}, u32[]{:S(2)}) collective-permute-start(f32[20,4,16]{2,1,0:T(4,128)S(1)} %pad_maximum_fusion.2), channel_id=1, source_target_pairs={{0,1},{1,0},{2,3},{3,2},{4,5},{5,4},{6,7},{7,6},{8,9},{9,8},{10,11... | collective-permute-start | bytes 15368 | tf_op jit(solution)/shard_map/ppermute | solution.py:234
  38.9 11.2 %copy-start.10 = (pred[10]{0:T(512)(128)(4,1)S(1)}, pred[10]{0:T(512)(128)(4,1)}, u32[]{:S(2)}) copy-start(pred[10]{0:T(512)(128)(4,1)} %constant.101) | copy-start | bytes 34
  38.9 11.2 %copy-start.11 = (pred[10]{0:T(512)(128)(4,1)S(1)}, pred[10]{0:T(512)(128)(4,1)}, u32[]{:S(2)}) copy-start(pred[10]{0:T(512)(128)(4,1)} %constant.100) | copy-start | bytes 34
  39.8 5.2 %collective-permute-start.8 = (f32[208,128]{1,0:T(8,128)S(1)}, f32[208,128]{1,0:T(8,128)S(1)}, u32[]{:S(2)}, u32[]{:S(2)}) collective-permute-start(f32[208,128]{1,0:T(8,128)S(1)} %pad_maximum_fusion.1), channel_id=1, source_target_pairs={{0,6},{1,7},{2,0},{3,1},{4,2},{5,3},{6,4},{7,5},{8,14},{9,15},{10,... | collective-permute-start | bytes 319496 | tf_op jit(solution)/shard_map/ppermute | solution.py:234
  43.3 4.8 %collective-permute-start.6 = (f32[208,128]{1,0:T(8,128)S(1)}, f32[208,128]{1,0:T(8,128)S(1)}, u32[]{:S(2)}, u32[]{:S(2)}) collective-permute-start(f32[208,128]{1,0:T(8,128)S(1)} %pad_maximum_fusion), channel_id=1, source_target_pairs={{0,2},{1,3},{2,4},{3,5},{4,6},{5,7},{6,0},{7,1},{8,10},{9,11},{10,... | collective-permute-start | bytes 319496 | tf_op jit(solution)/shard_map/ppermute | solution.py:234
  49.9 0.7 %copy-start.8 = (pred[10]{0:T(512)(128)(4,1)S(1)}, pred[10]{0:T(512)(128)(4,1)}, u32[]{:S(2)}) copy-start(pred[10]{0:T(512)(128)(4,1)} %constant.102) | copy-start | bytes 34
  49.9 0.7 %copy-start.9 = (pred[10]{0:T(512)(128)(4,1)S(1)}, pred[10]{0:T(512)(128)(4,1)}, u32[]{:S(2)}) copy-start(pred[10]{0:T(512)(128)(4,1)} %constant.95) | copy-start | bytes 34
  50.0 8.9 %copy-start.6 = (pred[20]{0:T(512)(128)(4,1)S(1)}, pred[20]{0:T(512)(128)(4,1)}, u32[]{:S(2)}) copy-start(pred[20]{0:T(512)(128)(4,1)} %constant.122) | copy-start | bytes 64
  50.0 8.8 %copy-start.7 = (pred[20]{0:T(512)(128)(4,1)S(1)}, pred[20]{0:T(512)(128)(4,1)}, u32[]{:S(2)}) copy-start(pred[20]{0:T(512)(128)(4,1)} %constant.107) | copy-start | bytes 64
  50.7 10.3 %collective-permute-start.7 = (f32[160,128]{1,0:T(8,128)S(1)}, f32[160,128]{1,0:T(8,128)S(1)}, u32[]{:S(2)}, u32[]{:S(2)}) collective-permute-start(f32[160,128]{1,0:T(8,128)S(1)} %bitcast.113), channel_id=1, source_target_pairs={{0,12},{1,13},{2,14},{3,15},{4,8},{5,9},{6,10},{7,11},{8,20},{9,21... | collective-permute-start | bytes 245768 | tf_op jit(solution)/shard_map/ppermute | solution.py:234
  50.8 10.2 %collective-permute-start.9 = (f32[160,128]{1,0:T(8,128)S(1)}, f32[160,128]{1,0:T(8,128)S(1)}, u32[]{:S(2)}, u32[]{:S(2)}) collective-permute-start(f32[160,128]{1,0:T(8,128)S(1)} %bitcast.112), channel_id=1, source_target_pairs={{0,252},{1,253},{2,254},{3,255},{4,248},{5,249},{6,250},{7,251},{8... | collective-permute-start | bytes 245768 | tf_op jit(solution)/shard_map/ppermute | solution.py:234
  61.0 1.1 %copy-start.3 = (f32[160,128]{1,0:T(8,128)}, f32[160,128]{1,0:T(8,128)S(1)}, u32[]{:S(2)}) copy-start(f32[160,128]{1,0:T(8,128)S(1)} %collective-permute-done.7) | copy-start | bytes 245764
  61.0 1.1 %copy-start.4 = (f32[160,128]{1,0:T(8,128)}, f32[160,128]{1,0:T(8,128)S(1)}, u32[]{:S(2)}) copy-start(f32[160,128]{1,0:T(8,128)S(1)} %collective-permute-done.9) | copy-start | bytes 245764

commit v10 on v9

--- a/solution.py
+++ b/solution.py
@@ -196,10 +196,10 @@
             else:
                 tile = post_ref[pop_groups(pops)[2][n], src]
                 if cy == 1:
-                    edge = jnp.broadcast_to(hym_ref[y_up.index(n), pl.ds(src, 1), :], (ny, nz))
+                    edge = jnp.broadcast_to(hym_ref[pl.ds(y_up.index(n) * nx + src, 1), :], (ny, nz))
                     tile = jnp.where(row == 0, edge, pltpu.roll(tile, 1, 0))
                 elif cy == -1:
-                    edge = jnp.broadcast_to(hyp_ref[y_dn.index(n), pl.ds(src, 1), :], (ny, nz))
+                    edge = jnp.broadcast_to(hyp_ref[pl.ds(y_dn.index(n) * nx + src, 1), :], (ny, nz))
                     tile = jnp.where(row == ny - 1, edge, pltpu.roll(tile, ny - 1, 0))
             if 0 <= src < nx and cz == 1:
                 tile = jnp.where(lane == 0, col_ref[z_any.index(n), x], pltpu.roll(tile, 1, 1))
@@ -408,7 +408,7 @@
             jax.ShapeDtypeStruct((pops, nx, ny, nz), jnp.float32),
         ),
         interpret=INTERPRET,
-    )(post, xlow, xhigh, hy_m, hy_p, cols)
+    )(post, xlow, xhigh, up2, dn2, cols)
     return (f_new, g_new)
 
 

time: 65.2 us -> 65.3 us (level)
  local copies, waits for them, and re-layouts: 10 us -> 8.78 us
  waiting for transfers between devices: 12.7 us -> 13.9 us
    slice x4 -> x2, local copies, waits for them, and re-layouts: 1.21 us -> 0.01 us  [unpack_y(): return (got[:count * nx].reshape(count, nx, nz), got[count * nx:, :nx])]
    ppermute x10, waiting for transfers between devices: 12.7 us -> 13.9 us  [exchange(): got = lax.ppermute(joined, AXES, pairs)]
  transfers between devices with their start and end apart: 10 -> 10, of which waited for: 7 -> 7; matrix products, arithmetic and copies ran while one was open for 6% -> 4% of each run, Pallas kernels for 0% -> 0%
where the time goes in v10:
time: 65.3 us; the launch traced here: 64.9 us
  starting transfers between devices  31.5 us (48%)
  waiting for transfers between devices  13.9 us (21%)
  local copies, waits for them, and re-layouts  8.78 us (13%)
  Pallas kernels  5.87 us (9%)
  other arithmetic  3.13 us (5%)
  between operations  1.82 us (3%)
    ppermute x10, starting transfers between devices, exchange(): got = lax.ppermute(joined, AXES, pairs)  31.5 us
    ppermute x10, waiting for transfers between devices, exchange(): got = lax.ppermute(joined, AXES, pairs)  13.9 us
    pallas_call x1, Pallas kernels, local(): pl.pallas_call(collide_kernel, out_shape=(jax.ShapeDtypeStruct((2 * pops,...  3.04 us
    pallas_call x1, Pallas kernels, local(): pl.pallas_call(stream_kernel, out_shape=(jax.ShapeDtypeStruct((pops, nx,...  2.83 us
    slice x1, local copies, waits for them, and re-layouts, local(): post[:len(z_up), :, :, -1]  1.51 us
  transfers between devices with their start and end apart: 10, of which 7 were waited for; matrix products, arithmetic and copies ran while one was open for 4% of the time, Pallas kernels for 0%

profile of v10, /device:TPU:2, one launch (start us, length us, event | category | flops | bytes accessed | tf_op | source)
XLA Modules:
  0.0 64.9 jit_solution(10230737322209271712)
XLA Ops:
  0.6 0.0 copy-start.19
  0.6 0.0 copy-start.18
  0.7 0.0 copy-start.17
  0.7 1.1 %reduce_sum.9 = f32[4,16,128]{2,1,0:T(8,128)S(1)} reduce(f32[19,4,16,128]{3,2,1,0:T(8,128)} %g_ref.1, f32[]{:T(128)} %constant.24.clone.1), dimensions={0}, to_apply=%region_0.0 | reduce | flops 147456 | bytes 655364 | tf_op jit(solution)/shard_map/reduce_sum | solution.py:250
  1.8 0.2 slice_reduce_fusion.3
  2.0 7.3 %collective-permute-start.4 = (f32[2,4,16]{2,1,0:T(4,128)S(1)}, f32[2,4,16]{2,1,0:T(4,128)S(1)}, u32[]{:S(2)}, u32[]{:S(2)}) collective-permute-start(f32[2,4,16]{2,1,0:T(4,128)S(1)} %pad_maximum_fusion.13), channel_id=1, source_target_pairs={{0,1},{1,0},{2,3},{3,2},{4,5},{5,4},{6,7},{7,6},{8,9},{9,8},{10,11... | collective-permute-start | bytes 1544 | tf_op jit(solution)/shard_map/ppermute | solution.py:234
  9.3 0.6 collective-permute-start.2
  9.9 1.5 %collective-permute-start = (f32[20,128]{1,0:T(8,128)S(1)}, f32[20,128]{1,0:T(8,128)S(1)}, u32[]{:S(2)}, u32[]{:S(2)}) collective-permute-start(f32[20,128]{1,0:T(8,128)S(1)} %pad_maximum_fusion.11), channel_id=1, source_target_pairs={{0,2},{1,3},{2,4},{3,5},{4,6},{5,7},{6,0},{7,1},{8,10},{9,11},{10,... | collective-permute-start | bytes 30728 | tf_op jit(solution)/shard_map/ppermute | solution.py:234
  11.4 0.1 slice_bitcast_fusion.1
  12.2 0.1 copy.42
  12.3 0.1 copy.43
  12.4 1.9 %collective-permute-done = f32[20,128]{1,0:T(8,128)S(1)} collective-permute-done((f32[20,128]{1,0:T(8,128)S(1)}, f32[20,128]{1,0:T(8,128)S(1)}, u32[]{:S(2)}, u32[]{:S(2)}) %collective-permute-start) | collective-permute-done | bytes 10272 | tf_op jit(solution)/shard_map/ppermute | solution.py:234
  14.3 0.1 collective-permute-start.1
  14.5 8.0 %collective-permute-start.3 = (f32[32,128]{1,0:T(8,128)S(1)}, f32[32,128]{1,0:T(8,128)S(1)}, u32[]{:S(2)}, u32[]{:S(2)}) collective-permute-start(f32[32,128]{1,0:T(8,128)S(1)} %pad_maximum_fusion.10), channel_id=1, source_target_pairs={{0,252},{1,253},{2,254},{3,255},{4,248},{5,249},{6,250},{7,251},{8... | collective-permute-start | bytes 49160 | tf_op jit(solution)/shard_map/ppermute | solution.py:234
  22.5 1.3 %collective-permute-done.1 = f32[32,128]{1,0:T(8,128)S(1)} collective-permute-done((f32[32,128]{1,0:T(8,128)S(1)}, f32[32,128]{1,0:T(8,128)S(1)}, u32[]{:S(2)}, u32[]{:S(2)}) %collective-permute-start.1) | collective-permute-done | bytes 16416 | tf_op jit(solution)/shard_map/ppermute | solution.py:234
  23.8 0.1 collective-permute-done.3
  23.9 0.1 fusion.5
  24.0 0.0 copy-start.16
  24.1 0.1 multiply_dynamic-update-slice_fusion.nb_ref
  24.2 0.7 %copy-done.4 = f32[5,4,16,128]{3,2,1,0:T(8,128)} copy-done((f32[5,4,16,128]{3,2,1,0:T(8,128)}, f32[5,4,16,128]{3,2,1,0:T(8,128)S(1)}, u32[]{:S(2)}) %copy-start.4) | copy-done | bytes 163864
  24.8 3.0 %shard_map.149 = (f32[38,4,16,128]{3,2,1,0:T(8,128)}, f32[10,16,128]{2,1,0:T(8,128)}, f32[10,16,128]{2,1,0:T(8,128)}, f32[10,4,128]{2,1,0:T(4,128)}, f32[10,4,128]{2,1,0:T(4,128)}) custom-call(f32[19,4,16,128]{3,2,1,0:T(8,128)} %f_ref.1, f32[19,4,16,128]{3,2,1,0:T(8,128)} %g_ref.1, f32[5,4,16,128]{3,2,1,0:T(8,128)} %copy-done.4), custom_call_target="tpu_custom_call" | custom-call | tf_op jit(solution)/shard_map/pallas_call | solution.py:279
  27.9 0.0 copy-start.14
  27.9 0.0 copy-start.15
  27.9 1.5 %slice_reduce_fusion.1 = (f32[10,4,16]{2,1,0:T(4,128)S(1)}, f32[10,4,16]{2,1,0:T(4,128)S(1)}) fusion(f32[38,4,16,128]{3,2,1,0:T(8,128)} %get-tuple-element.7.post_ref), kind=kLoop, calls=%fused_computation.6 | loop fusion | bytes 10240 | tf_op jit(solution)/shard_map/slice | solution.py:309
  29.4 2.8 %collective-permute-start.5 = (f32[20,4,16]{2,1,0:T(4,128)S(1)}, f32[20,4,16]{2,1,0:T(4,128)S(1)}, u32[]{:S(2)}, u32[]{:S(2)}) collective-permute-start(f32[20,4,16]{2,1,0:T(4,128)S(1)} %pad_maximum_fusion.2), channel_id=1, source_target_pairs={{0,1},{1,0},{2,3},{3,2},{4,5},{5,4},{6,7},{7,6},{8,9},{9,8},{10,11... | collective-permute-start | bytes 15368 | tf_op jit(solution)/shard_map/ppermute | solution.py:234
  32.3 5.5 %collective-permute-done.5 = f32[20,4,16]{2,1,0:T(4,128)S(1)} collective-permute-done((f32[20,4,16]{2,1,0:T(4,128)S(1)}, f32[20,4,16]{2,1,0:T(4,128)S(1)}, u32[]{:S(2)}, u32[]{:S(2)}) %collective-permute-start.5) | collective-permute-done | bytes 5152 | tf_op jit(solution)/shard_map/ppermute | solution.py:234
  37.8 0.6 gather_fusion.3
  38.4 0.1 fusion.9
  38.5 0.1 slice_reduce_fusion.6
  38.7 0.2 slice_reduce_fusion.4
  38.9 0.0 copy-start.13
  38.9 0.9 %pad_maximum_fusion.1 = f32[208,128]{1,0:T(8,128)S(1)} fusion(f32[4,128]{1,0:T(4,128)S(1)} %select_maximum_fusion, f32[160,128]{1,0:T(8,128)} %bitcast.103, f32[4,128]{1,0:T(4,128)S(1)} %select_maximum_fusion.3, f32[40,128]{1,0:T(8,128)} %bitcast.115), kind=kLoop, calls=%fused_computation.14 | loop fusion | flops 79872 | bytes 212992 | tf_op jit(solution)/shard_map/concatenate | solution.py:331
  39.8 2.9 %collective-permute-start.8 = (f32[208,128]{1,0:T(8,128)S(1)}, f32[208,128]{1,0:T(8,128)S(1)}, u32[]{:S(2)}, u32[]{:S(2)}) collective-permute-start(f32[208,128]{1,0:T(8,128)S(1)} %pad_maximum_fusion.1), channel_id=1, source_target_pairs={{0,6},{1,7},{2,0},{3,1},{4,2},{5,3},{6,4},{7,5},{8,14},{9,15},{10,... | collective-permute-start | bytes 319496 | tf_op jit(solution)/shard_map/ppermute | solution.py:234
  42.7 0.2 slice_reduce_fusion.8
  42.9 0.2 slice_reduce_fusion.10
  43.2 0.1 collective-permute-start.6
  43.3 1.7 %collective-permute-done.8.hyp_ref = f32[208,128]{1,0:T(8,128)S(1)} collective-permute-done((f32[208,128]{1,0:T(8,128)S(1)}, f32[208,128]{1,0:T(8,128)S(1)}, u32[]{:S(2)}, u32[]{:S(2)}) %collective-permute-start.8) | collective-permute-done | bytes 106528 | tf_op jit(solution)/shard_map/ppermute | solution.py:234
  45.0 0.1 pad_maximum_fusion.14
  45.1 0.1 constant_dynamic-slice_fusion
  45.2 0.6 gather_fusion.4
  45.8 0.2 copy.51
  46.0 0.6 gather_fusion.1
  46.6 0.1 copy.46
  46.7 1.3 %collective-permute-done.6.hym_ref = f32[208,128]{1,0:T(8,128)S(1)} collective-permute-done((f32[208,128]{1,0:T(8,128)S(1)}, f32[208,128]{1,0:T(8,128)S(1)}, u32[]{:S(2)}, u32[]{:S(2)}) %collective-permute-start.6) | collective-permute-done | bytes 106528 | tf_op jit(solution)/shard_map/ppermute | solution.py:234
  48.1 0.1 maximum_maximum_fusion
  48.1 0.1 constant_dynamic-slice_fusion.1
  48.2 0.6 gather_fusion
  48.8 0.6 gather_fusion.2
  49.3 0.2 copy.49
  49.6 0.1 copy.44
  49.7 0.2 maximum_select_fusion.4
  49.9 0.0 copy-start.10
  50.1 0.1 fusion.2
  50.2 0.1 fusion.6
  50.3 0.1 fusion.7
  50.4 0.1 copy-done.10
  50.5 0.0 copy-done.11
  50.6 0.2 maximum_select_fusion.2
  50.7 0.1 collective-permute-start.7
  50.8 8.0 %collective-permute-start.9 = (f32[160,128]{1,0:T(8,128)S(1)}, f32[160,128]{1,0:T(8,128)S(1)}, u32[]{:S(2)}, u32[]{:S(2)}) collective-permute-start(f32[160,128]{1,0:T(8,128)S(1)} %bitcast.108), channel_id=1, source_target_pairs={{0,252},{1,253},{2,254},{3,255},{4,248},{5,249},{6,250},{7,251},{8... | collective-permute-start | bytes 245768 | tf_op jit(solution)/shard_map/ppermute | solution.py:234
  58.9 0.1 select_select_fusion
  59.0 2.0 %collective-permute-done.7 = f32[160,128]{1,0:T(8,128)S(1)} collective-permute-done((f32[160,128]{1,0:T(8,128)S(1)}, f32[160,128]{1,0:T(8,128)S(1)}, u32[]{:S(2)}, u32[]{:S(2)}) %collective-permute-start.7) | collective-permute-done | bytes 81952 | tf_op jit(solution)/shard_map/ppermute | solution.py:234
  61.0 1.1 %broadcast_in_dim.125.col_ref = f32[20,4,16,128]{3,2,1,0:T(8,128)} broadcast(f32[20,4,16]{2,1,0:T(4,128)S(1)} %select_select_fusion), dimensions={0,1,2} | broadcast | bytes 660480 | tf_op jit(solution)/shard_map/broadcast_in_dim | solution.py:402
  62.1 2.8 %shard_map.150 = (f32[19,4,16,128]{3,2,1,0:T(8,128)}, f32[19,4,16,128]{3,2,1,0:T(8,128)}) custom-call(f32[38,4,16,128]{3,2,1,0:T(8,128)} %get-tuple-element.7.post_ref, f32[10,16,128]{2,1,0:T(8,128)} %bitcast.106, f32[10,16,128]{2,1,0:T(8,128)} %bitcast.107, f32[208,128]{1,0:T(8,128)} %copy-done.1, f32[208,128]{1,0:T(8,128)} %copy-done, ...), custom_call_target="tpu_custom_call" | custom-call | tf_op jit(solution)/shard_map/pallas_call | solution.py:404
  (76 shorter events, 0.5 us)
Async XLA Ops:
  0.6 11.5 %copy-start.19 = (s32[10]{0:T(128)S(1)}, s32[10]{0:T(128)}, u32[]{:S(2)}) copy-start(s32[10]{0:T(128)} %constant.123) | copy-start | bytes 124
  0.6 11.5 %copy-start.18 = (s32[20]{0:T(128)S(1)}, s32[20]{0:T(128)}, u32[]{:S(2)}) copy-start(s32[20]{0:T(128)} %constant.125) | copy-start | bytes 244
  0.7 11.5 %copy-start.17 = (s32[20]{0:T(128)S(1)}, s32[20]{0:T(128)}, u32[]{:S(2)}) copy-start(s32[20]{0:T(128)} %constant.126) | copy-start | bytes 244
  2.0 10.2 %collective-permute-start.4 = (f32[2,4,16]{2,1,0:T(4,128)S(1)}, f32[2,4,16]{2,1,0:T(4,128)S(1)}, u32[]{:S(2)}, u32[]{:S(2)}) collective-permute-start(f32[2,4,16]{2,1,0:T(4,128)S(1)} %pad_maximum_fusion.13), channel_id=1, source_target_pairs={{0,1},{1,0},{2,3},{3,2},{4,5},{5,4},{6,7},{7,6},{8,9},{9,8},{10,11... | collective-permute-start | bytes 1544 | tf_op jit(solution)/shard_map/ppermute | solution.py:234
  9.3 5.2 %collective-permute-start.2 = (f32[20,128]{1,0:T(8,128)S(1)}, f32[20,128]{1,0:T(8,128)S(1)}, u32[]{:S(2)}, u32[]{:S(2)}) collective-permute-start(f32[20,128]{1,0:T(8,128)S(1)} %pad_maximum_fusion.12), channel_id=1, source_target_pairs={{0,6},{1,7},{2,0},{3,1},{4,2},{5,3},{6,4},{7,5},{8,14},{9,15},{10,... | collective-permute-start | bytes 30728 | tf_op jit(solution)/shard_map/ppermute | solution.py:234
  9.9 4.4 %collective-permute-start = (f32[20,128]{1,0:T(8,128)S(1)}, f32[20,128]{1,0:T(8,128)S(1)}, u32[]{:S(2)}, u32[]{:S(2)}) collective-permute-start(f32[20,128]{1,0:T(8,128)S(1)} %pad_maximum_fusion.11), channel_id=1, source_target_pairs={{0,2},{1,3},{2,4},{3,5},{4,6},{5,7},{6,0},{7,1},{8,10},{9,11},{10,... | collective-permute-start | bytes 30728 | tf_op jit(solution)/shard_map/ppermute | solution.py:234
  14.3 9.5 %collective-permute-start.1 = (f32[32,128]{1,0:T(8,128)S(1)}, f32[32,128]{1,0:T(8,128)S(1)}, u32[]{:S(2)}, u32[]{:S(2)}) collective-permute-start(f32[32,128]{1,0:T(8,128)S(1)} %pad_maximum_fusion.9), channel_id=1, source_target_pairs={{0,12},{1,13},{2,14},{3,15},{4,8},{5,9},{6,10},{7,11},{8,20},{9,21... | collective-permute-start | bytes 49160 | tf_op jit(solution)/shard_map/ppermute | solution.py:234
  14.5 9.4 %collective-permute-start.3 = (f32[32,128]{1,0:T(8,128)S(1)}, f32[32,128]{1,0:T(8,128)S(1)}, u32[]{:S(2)}, u32[]{:S(2)}) collective-permute-start(f32[32,128]{1,0:T(8,128)S(1)} %pad_maximum_fusion.10), channel_id=1, source_target_pairs={{0,252},{1,253},{2,254},{3,255},{4,248},{5,249},{6,250},{7,251},{8... | collective-permute-start | bytes 49160 | tf_op jit(solution)/shard_map/ppermute | solution.py:234
  24.0 8.2 %copy-start.16 = (s32[20]{0:T(128)S(1)}, s32[20]{0:T(128)}, u32[]{:S(2)}) copy-start(s32[20]{0:T(128)} %constant.127) | copy-start | bytes 244
  24.2 0.7 %copy-start.4 = (f32[5,4,16,128]{3,2,1,0:T(8,128)}, f32[5,4,16,128]{3,2,1,0:T(8,128)S(1)}, u32[]{:S(2)}) copy-start(f32[5,4,16,128]{3,2,1,0:T(8,128)S(1)} %multiply_dynamic-update-slice_fusion.nb_ref) | copy-start | bytes 491524
  27.9 15.3 %copy-start.2 = (f32[10,16,128]{2,1,0:T(8,128)S(1)}, f32[10,16,128]{2,1,0:T(8,128)}, u32[]{:S(2)}) copy-start(f32[10,16,128]{2,1,0:T(8,128)} %get-tuple-element.9) | copy-start | bytes 245764
  27.9 15.3 %copy-start.7 = (f32[10,4,128]{2,1,0:T(4,128)S(1)}, f32[10,4,128]{2,1,0:T(4,128)}, u32[]{:S(2)}) copy-start(f32[10,4,128]{2,1,0:T(4,128)} %get-tuple-element.8) | copy-start | bytes 61444
  27.9 21.8 %copy-start.14 = (pred[20]{0:T(512)(128)(4,1)S(1)}, pred[20]{0:T(512)(128)(4,1)}, u32[]{:S(2)}) copy-start(pred[20]{0:T(512)(128)(4,1)} %constant.117) | copy-start | bytes 64
  27.9 21.8 %copy-start.15 = (pred[20]{0:T(512)(128)(4,1)S(1)}, pred[20]{0:T(512)(128)(4,1)}, u32[]{:S(2)}) copy-start(pred[20]{0:T(512)(128)(4,1)} %constant.108) | copy-start | bytes 64
  29.4 20.5 %copy-start.3 = (f32[10,16,128]{2,1,0:T(8,128)S(1)}, f32[10,16,128]{2,1,0:T(8,128)}, u32[]{:S(2)}) copy-start(f32[10,16,128]{2,1,0:T(8,128)} %get-tuple-element.11) | copy-start | bytes 245764
  29.4 8.4 %collective-permute-start.5 = (f32[20,4,16]{2,1,0:T(4,128)S(1)}, f32[20,4,16]{2,1,0:T(4,128)S(1)}, u32[]{:S(2)}, u32[]{:S(2)}) collective-permute-start(f32[20,4,16]{2,1,0:T(4,128)S(1)} %pad_maximum_fusion.2), channel_id=1, source_target_pairs={{0,1},{1,0},{2,3},{3,2},{4,5},{5,4},{6,7},{7,6},{8,9},{9,8},{10,11... | collective-permute-start | bytes 15368 | tf_op jit(solution)/shard_map/ppermute | solution.py:234
  38.9 11.2 %copy-start.12 = (pred[10]{0:T(512)(128)(4,1)S(1)}, pred[10]{0:T(512)(128)(4,1)}, u32[]{:S(2)}) copy-start(pred[10]{0:T(512)(128)(4,1)} %constant.101) | copy-start | bytes 34
  38.9 11.2 %copy-start.13 = (pred[10]{0:T(512)(128)(4,1)S(1)}, pred[10]{0:T(512)(128)(4,1)}, u32[]{:S(2)}) copy-start(pred[10]{0:T(512)(128)(4,1)} %constant.100) | copy-start | bytes 34
  39.8 5.2 %collective-permute-start.8 = (f32[208,128]{1,0:T(8,128)S(1)}, f32[208,128]{1,0:T(8,128)S(1)}, u32[]{:S(2)}, u32[]{:S(2)}) collective-permute-start(f32[208,128]{1,0:T(8,128)S(1)} %pad_maximum_fusion.1), channel_id=1, source_target_pairs={{0,6},{1,7},{2,0},{3,1},{4,2},{5,3},{6,4},{7,5},{8,14},{9,15},{10,... | collective-permute-start | bytes 319496 | tf_op jit(solution)/shard_map/ppermute | solution.py:234
  43.2 4.8 %collective-permute-start.6 = (f32[208,128]{1,0:T(8,128)S(1)}, f32[208,128]{1,0:T(8,128)S(1)}, u32[]{:S(2)}, u32[]{:S(2)}) collective-permute-start(f32[208,128]{1,0:T(8,128)S(1)} %pad_maximum_fusion), channel_id=1, source_target_pairs={{0,2},{1,3},{2,4},{3,5},{4,6},{5,7},{6,0},{7,1},{8,10},{9,11},{10,... | collective-permute-start | bytes 319496 | tf_op jit(solution)/shard_map/ppermute | solution.py:234
  45.0 5.2 %copy-start = (f32[208,128]{1,0:T(8,128)}, f32[208,128]{1,0:T(8,128)S(1)}, u32[]{:S(2)}) copy-start(f32[208,128]{1,0:T(8,128)S(1)} %collective-permute-done.8.hyp_ref) | copy-start | bytes 319492
  48.0 2.3 %copy-start.1 = (f32[208,128]{1,0:T(8,128)}, f32[208,128]{1,0:T(8,128)S(1)}, u32[]{:S(2)}) copy-start(f32[208,128]{1,0:T(8,128)S(1)} %collective-permute-done.6.hym_ref) | copy-start | bytes 319492
  49.9 0.7 %copy-start.10 = (pred[10]{0:T(512)(128)(4,1)S(1)}, pred[10]{0:T(512)(128)(4,1)}, u32[]{:S(2)}) copy-start(pred[10]{0:T(512)(128)(4,1)} %constant.102) | copy-start | bytes 34
  49.9 0.7 %copy-start.11 = (pred[10]{0:T(512)(128)(4,1)S(1)}, pred[10]{0:T(512)(128)(4,1)}, u32[]{:S(2)}) copy-start(pred[10]{0:T(512)(128)(4,1)} %constant.95) | copy-start | bytes 34
  50.0 8.9 %copy-start.8 = (pred[20]{0:T(512)(128)(4,1)S(1)}, pred[20]{0:T(512)(128)(4,1)}, u32[]{:S(2)}) copy-start(pred[20]{0:T(512)(128)(4,1)} %constant.122) | copy-start | bytes 64
  50.0 8.8 %copy-start.9 = (pred[20]{0:T(512)(128)(4,1)S(1)}, pred[20]{0:T(512)(128)(4,1)}, u32[]{:S(2)}) copy-start(pred[20]{0:T(512)(128)(4,1)} %constant.107) | copy-start | bytes 64
  50.7 10.3 %collective-permute-start.7 = (f32[160,128]{1,0:T(8,128)S(1)}, f32[160,128]{1,0:T(8,128)S(1)}, u32[]{:S(2)}, u32[]{:S(2)}) collective-permute-start(f32[160,128]{1,0:T(8,128)S(1)} %bitcast.109), channel_id=1, source_target_pairs={{0,12},{1,13},{2,14},{3,15},{4,8},{5,9},{6,10},{7,11},{8,20},{9,21... | collective-permute-start | bytes 245768 | tf_op jit(solution)/shard_map/ppermute | solution.py:234
  50.8 10.2 %collective-permute-start.9 = (f32[160,128]{1,0:T(8,128)S(1)}, f32[160,128]{1,0:T(8,128)S(1)}, u32[]{:S(2)}, u32[]{:S(2)}) collective-permute-start(f32[160,128]{1,0:T(8,128)S(1)} %bitcast.108), channel_id=1, source_target_pairs={{0,252},{1,253},{2,254},{3,255},{4,248},{5,249},{6,250},{7,251},{8... | collective-permute-start | bytes 245768 | tf_op jit(solution)/shard_map/ppermute | solution.py:234
  61.0 1.1 %copy-start.5 = (f32[160,128]{1,0:T(8,128)}, f32[160,128]{1,0:T(8,128)S(1)}, u32[]{:S(2)}) copy-start(f32[160,128]{1,0:T(8,128)S(1)} %collective-permute-done.7) | copy-start | bytes 245764
  61.0 1.1 %copy-start.6 = (f32[160,128]{1,0:T(8,128)}, f32[160,128]{1,0:T(8,128)S(1)}, u32[]{:S(2)}) copy-start(f32[160,128]{1,0:T(8,128)S(1)} %collective-permute-done.9) | copy-start | bytes 245764

commit v11 on v10

--- a/solution.py
+++ b/solution.py
@@ -248,18 +248,20 @@
     rem = shift - q * ny
 
     phi = jnp.sum(g_pop, axis=0)
+    face_x_last = jnp.sum(g_pop[:, -1], axis=0)
+    face_x_first = jnp.sum(g_pop[:, 0], axis=0)
     up1, dn1, pzm, pzp = exchange(
         [
-            (jnp.concatenate([phi[:, -1], phi[-1]]), (0, 1, 0)),
-            (jnp.concatenate([phi[:, 0], phi[0]]), (0, -1, 0)),
-            (phi[:, :, -1][None], (0, 0, 1)),
-            (phi[:, :, 0][None], (0, 0, -1)),
+            (jnp.concatenate([jnp.sum(g_pop[:, :, -1], axis=0), face_x_last]), (0, 1, 0)),
+            (jnp.concatenate([jnp.sum(g_pop[:, :, 0], axis=0), face_x_first]), (0, -1, 0)),
+            (jnp.sum(g_pop[:, :, :, -1], axis=0)[None], (0, 0, 1)),
+            (jnp.sum(g_pop[:, :, :, 0], axis=0)[None], (0, 0, -1)),
         ]
     )
     low_pair, high_pair = exchange(
         [
-            (jnp.concatenate([up1[nx:], phi[-1]]), (1, q, 0)),
-            (jnp.concatenate([phi[0], dn1[nx:]]), (-1, -q, 0)),
+            (jnp.concatenate([up1[nx:], face_x_last]), (1, q, 0)),
+            (jnp.concatenate([face_x_first, dn1[nx:]]), (-1, -q, 0)),
         ]
     )
     low = lax.dynamic_slice_in_dim(low_pair, ny - rem, ny, 0)[None]

time: 65.3 us -> 65.8 us (level)
  other arithmetic: 3.13 us -> 3.86 us
    reduce_sum x0 -> x3, other arithmetic: none -> 1.81 us  [the longest x1 1.72 us: local(): jnp.sum(g_pop[:, :, :, -1], axis=0)[None]]
    reduce_sum x1, other arithmetic: 1.13 us -> 0.04 us  [local(): phi = jnp.sum(g_pop, axis=0)]
where the time goes in v11:
time: 65.8 us; the launch traced here: 65.5 us
  starting transfers between devices  31.5 us (48%)
  waiting for transfers between devices  13.8 us (21%)
  local copies, waits for them, and re-layouts  8.64 us (13%)
  Pallas kernels  5.85 us (9%)
  other arithmetic  3.86 us (6%)
  between operations  1.85 us (3%)
    ppermute x10, starting transfers between devices, exchange(): got = lax.ppermute(joined, AXES, pairs)  31.5 us
    ppermute x10, waiting for transfers between devices, exchange(): got = lax.ppermute(joined, AXES, pairs)  13.8 us
    pallas_call x1, Pallas kernels, local(): pl.pallas_call(collide_kernel, out_shape=(jax.ShapeDtypeStruct((2 * pops,...  3.02 us
    pallas_call x1, Pallas kernels, local(): pl.pallas_call(stream_kernel, out_shape=(jax.ShapeDtypeStruct((pops, nx,...  2.83 us
    reduce_sum x1, other arithmetic, local(): jnp.sum(g_pop[:, :, :, -1], axis=0)[None]  1.72 us
    slice x1, local copies, waits for them, and re-layouts, local(): post[:len(z_up), :, :, -1]  1.51 us
  transfers between devices with their start and end apart: 10, of which 7 were waited for; matrix products, arithmetic and copies ran while one was open for 4% of the time, Pallas kernels for 0%

profile of v11, /device:TPU:2, one launch (start us, length us, event | category | flops | bytes accessed | tf_op | source)
XLA Modules:
  0.0 65.5 jit_solution(8175880606110797167)
XLA Ops:
  0.6 0.0 copy-start.20
  0.6 0.0 copy-start.19
  0.7 0.0 copy-start.18
  0.7 1.7 %slice_reduce_fusion.1 = (f32[4,16]{1,0:T(4,128)S(1)}, f32[4,16]{1,0:T(4,128)S(1)}) fusion(f32[19,4,16,128]{3,2,1,0:T(8,128)} %g_ref.1), kind=kLoop, calls=%fused_computation.6 | loop fusion | flops 2304 | bytes 10240 | tf_op jit(solution)/shard_map/reduce_sum | solution.py:257
  2.4 7.3 %collective-permute-start.4 = (f32[2,4,16]{2,1,0:T(4,128)S(1)}, f32[2,4,16]{2,1,0:T(4,128)S(1)}, u32[]{:S(2)}, u32[]{:S(2)}) collective-permute-start(f32[2,4,16]{2,1,0:T(4,128)S(1)} %pad_maximum_fusion.13), channel_id=1, source_target_pairs={{0,1},{1,0},{2,3},{3,2},{4,5},{5,4},{6,7},{7,6},{8,9},{9,8},{10,11... | collective-permute-start | bytes 1544 | tf_op jit(solution)/shard_map/ppermute | solution.py:234
  9.7 0.1 slice_reduce_fusion.7
  9.8 0.6 collective-permute-start.2
  10.4 1.5 %collective-permute-start = (f32[20,128]{1,0:T(8,128)S(1)}, f32[20,128]{1,0:T(8,128)S(1)}, u32[]{:S(2)}, u32[]{:S(2)}) collective-permute-start(f32[20,128]{1,0:T(8,128)S(1)} %pad_maximum_fusion.11), channel_id=1, source_target_pairs={{0,2},{1,3},{2,4},{3,5},{4,6},{5,7},{6,0},{7,1},{8,10},{9,11},{10,... | collective-permute-start | bytes 30728 | tf_op jit(solution)/shard_map/ppermute | solution.py:234
  12.0 0.1 slice_bitcast_fusion.1
  12.8 0.1 copy.33
  12.9 0.1 copy.34
  13.0 1.8 %collective-permute-done = f32[20,128]{1,0:T(8,128)S(1)} collective-permute-done((f32[20,128]{1,0:T(8,128)S(1)}, f32[20,128]{1,0:T(8,128)S(1)}, u32[]{:S(2)}, u32[]{:S(2)}) %collective-permute-start) | collective-permute-done | bytes 10272 | tf_op jit(solution)/shard_map/ppermute | solution.py:234
  14.9 0.2 collective-permute-start.1
  15.1 7.9 %collective-permute-start.3 = (f32[32,128]{1,0:T(8,128)S(1)}, f32[32,128]{1,0:T(8,128)S(1)}, u32[]{:S(2)}, u32[]{:S(2)}) collective-permute-start(f32[32,128]{1,0:T(8,128)S(1)} %pad_maximum_fusion.10), channel_id=1, source_target_pairs={{0,252},{1,253},{2,254},{3,255},{4,248},{5,249},{6,250},{7,251},{8... | collective-permute-start | bytes 49160 | tf_op jit(solution)/shard_map/ppermute | solution.py:234
  23.0 1.3 %collective-permute-done.1 = f32[32,128]{1,0:T(8,128)S(1)} collective-permute-done((f32[32,128]{1,0:T(8,128)S(1)}, f32[32,128]{1,0:T(8,128)S(1)}, u32[]{:S(2)}, u32[]{:S(2)}) %collective-permute-start.1) | collective-permute-done | bytes 16416 | tf_op jit(solution)/shard_map/ppermute | solution.py:234
  24.4 0.1 collective-permute-done.3
  24.5 0.1 fusion.5
  24.6 0.0 copy-start.17
  24.6 0.1 multiply_dynamic-update-slice_fusion.nb_ref
  24.7 0.7 %copy-done.5 = f32[5,4,16,128]{3,2,1,0:T(8,128)} copy-done((f32[5,4,16,128]{3,2,1,0:T(8,128)}, f32[5,4,16,128]{3,2,1,0:T(8,128)S(1)}, u32[]{:S(2)}) %copy-start.5) | copy-done | bytes 163864
  25.4 3.0 %shard_map.149 = (f32[38,4,16,128]{3,2,1,0:T(8,128)}, f32[10,16,128]{2,1,0:T(8,128)}, f32[10,16,128]{2,1,0:T(8,128)}, f32[10,4,128]{2,1,0:T(4,128)}, f32[10,4,128]{2,1,0:T(4,128)}) custom-call(f32[19,4,16,128]{3,2,1,0:T(8,128)} %f_ref.1, f32[19,4,16,128]{3,2,1,0:T(8,128)} %g_ref.1, f32[5,4,16,128]{3,2,1,0:T(8,128)} %copy-done.5), custom_call_target="tpu_custom_call" | custom-call | tf_op jit(solution)/shard_map/pallas_call | solution.py:281
  28.4 0.0 copy-start.15
  28.4 0.0 copy-start.16
  28.4 1.5 %slice_reduce_fusion.3 = (f32[10,4,16]{2,1,0:T(4,128)S(1)}, f32[10,4,16]{2,1,0:T(4,128)S(1)}) fusion(f32[38,4,16,128]{3,2,1,0:T(8,128)} %get-tuple-element.7.post_ref), kind=kLoop, calls=%fused_computation.8 | loop fusion | bytes 10240 | tf_op jit(solution)/shard_map/slice | solution.py:311
  30.0 2.7 %collective-permute-start.5 = (f32[20,4,16]{2,1,0:T(4,128)S(1)}, f32[20,4,16]{2,1,0:T(4,128)S(1)}, u32[]{:S(2)}, u32[]{:S(2)}) collective-permute-start(f32[20,4,16]{2,1,0:T(4,128)S(1)} %pad_maximum_fusion.2), channel_id=1, source_target_pairs={{0,1},{1,0},{2,3},{3,2},{4,5},{5,4},{6,7},{7,6},{8,9},{9,8},{10,11... | collective-permute-start | bytes 15368 | tf_op jit(solution)/shard_map/ppermute | solution.py:234
  32.7 5.5 %collective-permute-done.5 = f32[20,4,16]{2,1,0:T(4,128)S(1)} collective-permute-done((f32[20,4,16]{2,1,0:T(4,128)S(1)}, f32[20,4,16]{2,1,0:T(4,128)S(1)}, u32[]{:S(2)}, u32[]{:S(2)}) %collective-permute-start.5) | collective-permute-done | bytes 5152 | tf_op jit(solution)/shard_map/ppermute | solution.py:234
  38.3 0.6 gather_fusion.3
  38.8 0.1 fusion.9
  38.9 0.1 slice_reduce_fusion.10
  39.1 0.2 slice_reduce_fusion.8
  39.3 0.0 copy-start.13
  39.3 0.9 %pad_maximum_fusion.1 = f32[208,128]{1,0:T(8,128)S(1)} fusion(f32[4,128]{1,0:T(4,128)S(1)} %select_maximum_fusion, f32[160,128]{1,0:T(8,128)} %bitcast.91, f32[4,128]{1,0:T(4,128)S(1)} %select_maximum_fusion.3, f32[40,128]{1,0:T(8,128)} %bitcast.103), kind=kLoop, calls=%fused_computation.18 | loop fusion | flops 79872 | bytes 212992 | tf_op jit(solution)/shard_map/concatenate | solution.py:333
  40.2 3.0 %collective-permute-start.8 = (f32[208,128]{1,0:T(8,128)S(1)}, f32[208,128]{1,0:T(8,128)S(1)}, u32[]{:S(2)}, u32[]{:S(2)}) collective-permute-start(f32[208,128]{1,0:T(8,128)S(1)} %pad_maximum_fusion.1), channel_id=1, source_target_pairs={{0,6},{1,7},{2,0},{3,1},{4,2},{5,3},{6,4},{7,5},{8,14},{9,15},{10,... | collective-permute-start | bytes 319496 | tf_op jit(solution)/shard_map/ppermute | solution.py:234
  43.3 0.2 slice_reduce_fusion.12
  43.5 0.2 slice_reduce_fusion.14
  43.8 0.1 collective-permute-start.6
  43.9 1.7 %collective-permute-done.8.hyp_ref = f32[208,128]{1,0:T(8,128)S(1)} collective-permute-done((f32[208,128]{1,0:T(8,128)S(1)}, f32[208,128]{1,0:T(8,128)S(1)}, u32[]{:S(2)}, u32[]{:S(2)}) %collective-permute-start.8) | collective-permute-done | bytes 106528 | tf_op jit(solution)/shard_map/ppermute | solution.py:234
  45.6 0.1 pad_maximum_fusion.14
  45.7 0.1 constant_dynamic-slice_fusion
  45.7 0.6 gather_fusion.4
  46.3 0.2 copy.42
  46.5 0.6 gather_fusion.1
  47.1 0.1 copy.37
  47.2 1.3 %collective-permute-done.6.hym_ref = f32[208,128]{1,0:T(8,128)S(1)} collective-permute-done((f32[208,128]{1,0:T(8,128)S(1)}, f32[208,128]{1,0:T(8,128)S(1)}, u32[]{:S(2)}, u32[]{:S(2)}) %collective-permute-start.6) | collective-permute-done | bytes 106528 | tf_op jit(solution)/shard_map/ppermute | solution.py:234
  48.6 0.1 maximum_maximum_fusion
  48.7 0.1 constant_dynamic-slice_fusion.1
  48.7 0.6 gather_fusion
  49.3 0.6 gather_fusion.2
  49.9 0.2 copy.40
  50.1 0.1 copy.35
  50.2 0.2 maximum_select_fusion.4
  50.4 0.0 copy-start.11
  50.6 0.1 fusion.2
  50.8 0.1 fusion.6
  50.8 0.1 fusion.7
  50.9 0.1 copy-done.11
  51.1 0.0 copy-done.12
  51.1 0.2 maximum_select_fusion.2
  51.3 0.1 collective-permute-start.7
  51.4 8.0 %collective-permute-start.9 = (f32[160,128]{1,0:T(8,128)S(1)}, f32[160,128]{1,0:T(8,128)S(1)}, u32[]{:S(2)}, u32[]{:S(2)}) collective-permute-start(f32[160,128]{1,0:T(8,128)S(1)} %bitcast.96), channel_id=1, source_target_pairs={{0,252},{1,253},{2,254},{3,255},{4,248},{5,249},{6,250},{7,251},{8... | collective-permute-start | bytes 245768 | tf_op jit(solution)/shard_map/ppermute | solution.py:234
  59.4 0.1 select_select_fusion
  59.5 2.0 %collective-permute-done.7 = f32[160,128]{1,0:T(8,128)S(1)} collective-permute-done((f32[160,128]{1,0:T(8,128)S(1)}, f32[160,128]{1,0:T(8,128)S(1)}, u32[]{:S(2)}, u32[]{:S(2)}) %collective-permute-start.7) | collective-permute-done | bytes 81952 | tf_op jit(solution)/shard_map/ppermute | solution.py:234
  61.5 1.1 %broadcast_in_dim.133.col_ref = f32[20,4,16,128]{3,2,1,0:T(8,128)} broadcast(f32[20,4,16]{2,1,0:T(4,128)S(1)} %select_select_fusion), dimensions={0,1,2} | broadcast | bytes 660480 | tf_op jit(solution)/shard_map/broadcast_in_dim | solution.py:404
  62.6 2.8 %shard_map.150 = (f32[19,4,16,128]{3,2,1,0:T(8,128)}, f32[19,4,16,128]{3,2,1,0:T(8,128)}) custom-call(f32[38,4,16,128]{3,2,1,0:T(8,128)} %get-tuple-element.7.post_ref, f32[10,16,128]{2,1,0:T(8,128)} %bitcast.94, f32[10,16,128]{2,1,0:T(8,128)} %bitcast.95, f32[208,128]{1,0:T(8,128)} %copy-done.2, f32[208,128]{1,0:T(8,128)} %copy-done.1, ...), custom_call_target="tpu_custom_call" | custom-call | tf_op jit(solution)/shard_map/pallas_call | solution.py:406
  (78 shorter events, 0.5 us)
Async XLA Ops:
  0.6 12.1 %copy-start.20 = (s32[10]{0:T(128)S(1)}, s32[10]{0:T(128)}, u32[]{:S(2)}) copy-start(s32[10]{0:T(128)} %constant.123) | copy-start | bytes 124
  0.6 12.1 %copy-start.19 = (s32[20]{0:T(128)S(1)}, s32[20]{0:T(128)}, u32[]{:S(2)}) copy-start(s32[20]{0:T(128)} %constant.125) | copy-start | bytes 244
  0.7 12.1 %copy-start.18 = (s32[20]{0:T(128)S(1)}, s32[20]{0:T(128)}, u32[]{:S(2)}) copy-start(s32[20]{0:T(128)} %constant.126) | copy-start | bytes 244
  0.7 9.0 %copy-start = (f32[19,4,16,128]{3,2,1,0:T(8,128)S(1)}, f32[19,4,16,128]{3,2,1,0:T(8,128)}, u32[]{:S(2)}) copy-start(f32[19,4,16,128]{3,2,1,0:T(8,128)} %g_ref.1) | copy-start | bytes 1867780
  2.4 10.4 %collective-permute-start.4 = (f32[2,4,16]{2,1,0:T(4,128)S(1)}, f32[2,4,16]{2,1,0:T(4,128)S(1)}, u32[]{:S(2)}, u32[]{:S(2)}) collective-permute-start(f32[2,4,16]{2,1,0:T(4,128)S(1)} %pad_maximum_fusion.13), channel_id=1, source_target_pairs={{0,1},{1,0},{2,3},{3,2},{4,5},{5,4},{6,7},{7,6},{8,9},{9,8},{10,11... | collective-permute-start | bytes 1544 | tf_op jit(solution)/shard_map/ppermute | solution.py:234
  9.8 5.3 %collective-permute-start.2 = (f32[20,128]{1,0:T(8,128)S(1)}, f32[20,128]{1,0:T(8,128)S(1)}, u32[]{:S(2)}, u32[]{:S(2)}) collective-permute-start(f32[20,128]{1,0:T(8,128)S(1)} %pad_maximum_fusion.12), channel_id=1, source_target_pairs={{0,6},{1,7},{2,0},{3,1},{4,2},{5,3},{6,4},{7,5},{8,14},{9,15},{10,... | collective-permute-start | bytes 30728 | tf_op jit(solution)/shard_map/ppermute | solution.py:234
  10.4 4.4 %collective-permute-start = (f32[20,128]{1,0:T(8,128)S(1)}, f32[20,128]{1,0:T(8,128)S(1)}, u32[]{:S(2)}, u32[]{:S(2)}) collective-permute-start(f32[20,128]{1,0:T(8,128)S(1)} %pad_maximum_fusion.11), channel_id=1, source_target_pairs={{0,2},{1,3},{2,4},{3,5},{4,6},{5,7},{6,0},{7,1},{8,10},{9,11},{10,... | collective-permute-start | bytes 30728 | tf_op jit(solution)/shard_map/ppermute | solution.py:234
  14.9 9.5 %collective-permute-start.1 = (f32[32,128]{1,0:T(8,128)S(1)}, f32[32,128]{1,0:T(8,128)S(1)}, u32[]{:S(2)}, u32[]{:S(2)}) collective-permute-start(f32[32,128]{1,0:T(8,128)S(1)} %pad_maximum_fusion.9), channel_id=1, source_target_pairs={{0,12},{1,13},{2,14},{3,15},{4,8},{5,9},{6,10},{7,11},{8,20},{9,21... | collective-permute-start | bytes 49160 | tf_op jit(solution)/shard_map/ppermute | solution.py:234
  15.1 9.4 %collective-permute-start.3 = (f32[32,128]{1,0:T(8,128)S(1)}, f32[32,128]{1,0:T(8,128)S(1)}, u32[]{:S(2)}, u32[]{:S(2)}) collective-permute-start(f32[32,128]{1,0:T(8,128)S(1)} %pad_maximum_fusion.10), channel_id=1, source_target_pairs={{0,252},{1,253},{2,254},{3,255},{4,248},{5,249},{6,250},{7,251},{8... | collective-permute-start | bytes 49160 | tf_op jit(solution)/shard_map/ppermute | solution.py:234
  24.6 8.1 %copy-start.17 = (s32[20]{0:T(128)S(1)}, s32[20]{0:T(128)}, u32[]{:S(2)}) copy-start(s32[20]{0:T(128)} %constant.127) | copy-start | bytes 244
  24.7 0.7 %copy-start.5 = (f32[5,4,16,128]{3,2,1,0:T(8,128)}, f32[5,4,16,128]{3,2,1,0:T(8,128)S(1)}, u32[]{:S(2)}) copy-start(f32[5,4,16,128]{3,2,1,0:T(8,128)S(1)} %multiply_dynamic-update-slice_fusion.nb_ref) | copy-start | bytes 491524
  28.4 15.3 %copy-start.3 = (f32[10,16,128]{2,1,0:T(8,128)S(1)}, f32[10,16,128]{2,1,0:T(8,128)}, u32[]{:S(2)}) copy-start(f32[10,16,128]{2,1,0:T(8,128)} %get-tuple-element.9) | copy-start | bytes 245764
  28.4 15.3 %copy-start.8 = (f32[10,4,128]{2,1,0:T(4,128)S(1)}, f32[10,4,128]{2,1,0:T(4,128)}, u32[]{:S(2)}) copy-start(f32[10,4,128]{2,1,0:T(4,128)} %get-tuple-element.8) | copy-start | bytes 61444
  28.4 21.8 %copy-start.15 = (pred[20]{0:T(512)(128)(4,1)S(1)}, pred[20]{0:T(512)(128)(4,1)}, u32[]{:S(2)}) copy-start(pred[20]{0:T(512)(128)(4,1)} %constant.117) | copy-start | bytes 64
  28.4 21.8 %copy-start.16 = (pred[20]{0:T(512)(128)(4,1)S(1)}, pred[20]{0:T(512)(128)(4,1)}, u32[]{:S(2)}) copy-start(pred[20]{0:T(512)(128)(4,1)} %constant.108) | copy-start | bytes 64
  29.9 20.5 %copy-start.4 = (f32[10,16,128]{2,1,0:T(8,128)S(1)}, f32[10,16,128]{2,1,0:T(8,128)}, u32[]{:S(2)}) copy-start(f32[10,16,128]{2,1,0:T(8,128)} %get-tuple-element.11) | copy-start | bytes 245764
  30.0 8.3 %collective-permute-start.5 = (f32[20,4,16]{2,1,0:T(4,128)S(1)}, f32[20,4,16]{2,1,0:T(4,128)S(1)}, u32[]{:S(2)}, u32[]{:S(2)}) collective-permute-start(f32[20,4,16]{2,1,0:T(4,128)S(1)} %pad_maximum_fusion.2), channel_id=1, source_target_pairs={{0,1},{1,0},{2,3},{3,2},{4,5},{5,4},{6,7},{7,6},{8,9},{9,8},{10,11... | collective-permute-start | bytes 15368 | tf_op jit(solution)/shard_map/ppermute | solution.py:234
  39.3 11.3 %copy-start.13 = (pred[10]{0:T(512)(128)(4,1)S(1)}, pred[10]{0:T(512)(128)(4,1)}, u32[]{:S(2)}) copy-start(pred[10]{0:T(512)(128)(4,1)} %constant.101) | copy-start | bytes 34
  39.3 11.3 %copy-start.14 = (pred[10]{0:T(512)(128)(4,1)S(1)}, pred[10]{0:T(512)(128)(4,1)}, u32[]{:S(2)}) copy-start(pred[10]{0:T(512)(128)(4,1)} %constant.100) | copy-start | bytes 34
  40.2 5.3 %collective-permute-start.8 = (f32[208,128]{1,0:T(8,128)S(1)}, f32[208,128]{1,0:T(8,128)S(1)}, u32[]{:S(2)}, u32[]{:S(2)}) collective-permute-start(f32[208,128]{1,0:T(8,128)S(1)} %pad_maximum_fusion.1), channel_id=1, source_target_pairs={{0,6},{1,7},{2,0},{3,1},{4,2},{5,3},{6,4},{7,5},{8,14},{9,15},{10,... | collective-permute-start | bytes 319496 | tf_op jit(solution)/shard_map/ppermute | solution.py:234
  43.8 4.8 %collective-permute-start.6 = (f32[208,128]{1,0:T(8,128)S(1)}, f32[208,128]{1,0:T(8,128)S(1)}, u32[]{:S(2)}, u32[]{:S(2)}) collective-permute-start(f32[208,128]{1,0:T(8,128)S(1)} %pad_maximum_fusion), channel_id=1, source_target_pairs={{0,2},{1,3},{2,4},{3,5},{4,6},{5,7},{6,0},{7,1},{8,10},{9,11},{10,... | collective-permute-start | bytes 319496 | tf_op jit(solution)/shard_map/ppermute | solution.py:234
  45.6 5.2 %copy-start.1 = (f32[208,128]{1,0:T(8,128)}, f32[208,128]{1,0:T(8,128)S(1)}, u32[]{:S(2)}) copy-start(f32[208,128]{1,0:T(8,128)S(1)} %collective-permute-done.8.hyp_ref) | copy-start | bytes 319492
  48.6 2.3 %copy-start.2 = (f32[208,128]{1,0:T(8,128)}, f32[208,128]{1,0:T(8,128)S(1)}, u32[]{:S(2)}) copy-start(f32[208,128]{1,0:T(8,128)S(1)} %collective-permute-done.6.hym_ref) | copy-start | bytes 319492
  50.4 0.7 %copy-start.11 = (pred[10]{0:T(512)(128)(4,1)S(1)}, pred[10]{0:T(512)(128)(4,1)}, u32[]{:S(2)}) copy-start(pred[10]{0:T(512)(128)(4,1)} %constant.102) | copy-start | bytes 34
  50.4 0.7 %copy-start.12 = (pred[10]{0:T(512)(128)(4,1)S(1)}, pred[10]{0:T(512)(128)(4,1)}, u32[]{:S(2)}) copy-start(pred[10]{0:T(512)(128)(4,1)} %constant.95) | copy-start | bytes 34
  50.5 8.9 %copy-start.9 = (pred[20]{0:T(512)(128)(4,1)S(1)}, pred[20]{0:T(512)(128)(4,1)}, u32[]{:S(2)}) copy-start(pred[20]{0:T(512)(128)(4,1)} %constant.122) | copy-start | bytes 64
  50.6 8.8 %copy-start.10 = (pred[20]{0:T(512)(128)(4,1)S(1)}, pred[20]{0:T(512)(128)(4,1)}, u32[]{:S(2)}) copy-start(pred[20]{0:T(512)(128)(4,1)} %constant.107) | copy-start | bytes 64
  51.3 10.3 %collective-permute-start.7 = (f32[160,128]{1,0:T(8,128)S(1)}, f32[160,128]{1,0:T(8,128)S(1)}, u32[]{:S(2)}, u32[]{:S(2)}) collective-permute-start(f32[160,128]{1,0:T(8,128)S(1)} %bitcast.97), channel_id=1, source_target_pairs={{0,12},{1,13},{2,14},{3,15},{4,8},{5,9},{6,10},{7,11},{8,20},{9,21... | collective-permute-start | bytes 245768 | tf_op jit(solution)/shard_map/ppermute | solution.py:234
  51.4 10.2 %collective-permute-start.9 = (f32[160,128]{1,0:T(8,128)S(1)}, f32[160,128]{1,0:T(8,128)S(1)}, u32[]{:S(2)}, u32[]{:S(2)}) collective-permute-start(f32[160,128]{1,0:T(8,128)S(1)} %bitcast.96), channel_id=1, source_target_pairs={{0,252},{1,253},{2,254},{3,255},{4,248},{5,249},{6,250},{7,251},{8... | collective-permute-start | bytes 245768 | tf_op jit(solution)/shard_map/ppermute | solution.py:234
  61.5 1.1 %copy-start.6 = (f32[160,128]{1,0:T(8,128)}, f32[160,128]{1,0:T(8,128)S(1)}, u32[]{:S(2)}) copy-start(f32[160,128]{1,0:T(8,128)S(1)} %collective-permute-done.7) | copy-start | bytes 245764
  61.5 1.1 %copy-start.7 = (f32[160,128]{1,0:T(8,128)}, f32[160,128]{1,0:T(8,128)S(1)}, u32[]{:S(2)}) copy-start(f32[160,128]{1,0:T(8,128)S(1)} %collective-permute-done.9) | copy-start | bytes 245764

commit v12 on v10

--- a/solution.py
+++ b/solution.py
@@ -304,13 +304,6 @@
     yz_up = pick(lambda c: c[2] != 0, y_up)
     yz_dn = pick(lambda c: c[2] != 0, y_dn)
 
-    hz_m, hz_p = exchange(
-        [
-            (post[: len(z_up), :, :, -1], (0, 0, 1)),
-            (post[len(z_up) : len(z_up) + len(z_dn), :, :, 0], (0, 0, -1)),
-        ]
-    )
-
     def zhalo(n):
         return hz_m[z_up.index(n)] if vel[n][2] == 1 else hz_p[z_dn.index(n)]
 
@@ -320,18 +313,40 @@
     def packed(face, extra):
         return jnp.concatenate([face.reshape(-1, nz), lanes(jnp.stack(extra))], axis=0)
 
+    sends = [
+        (post[: len(z_up), :, :, -1], (0, 0, 1)),
+        (post[len(z_up) : len(z_up) + len(z_dn), :, :, 0], (0, 0, -1)),
+        (jnp.concatenate([face_yu.reshape(-1, nz), face_xu.reshape(-1, nz)]), (0, 1, 0)),
+        (jnp.concatenate([face_yd.reshape(-1, nz), face_xd.reshape(-1, nz)]), (0, -1, 0)),
+    ]
+    diag_keys = []
+    for dy in (1, -1):
+        for dz in (1, -1):
+            ypops = [n for n in (yz_up if dy == 1 else yz_dn) if vel[n][2] == dz]
+            xpops = [n for n in (xz_up if dy == 1 else xz_dn) if vel[n][2] == dz]
+            yrow, xrow, zl = (ny - 1, nx - 1, nz - 1 if dz == 1 else 0) if dy == 1 else (0, 0, nz - 1 if dz == 1 else 0)
+            ys = post[jnp.array([slot[n] for n in ypops]), :, yrow, zl]
+            xs = post[jnp.array([slot[n] for n in xpops]), xrow, :, zl]
+            sends.append((jnp.concatenate([lanes(ys), lanes(xs)]), (0, dy, dz)))
+            diag_keys.append((dy, dz, ypops, xpops))
+    got = exchange(sends)
+    hz_m, hz_p, up2, dn2 = got[:4]
+    diag = dict(((dy, dz), (g, yp, xp)) for (dy, dz, yp, xp), g in zip(diag_keys, got[4:]))
+
+    def edge_rows(dy, idx, kind):
+        rows = []
+        for n in idx:
+            g, yp, xp = diag[(dy, vel[n][2])]
+            rows.append(g[yp.index(n)][:nx] if kind == "y" else g[len(yp) + xp.index(n)][:ny])
+        return jnp.stack(rows)
+
+    cy_m = edge_rows(1, yz_up, "y")
+    cy_p = edge_rows(-1, yz_dn, "y")
+    n_face_u, n_face_d = face_yu.shape[0] * nx, face_yd.shape[0] * nx
     send_up = packed(face_xu, [zhalo(n)[-1] for n in xz_up])
     send_dn = packed(face_xd, [zhalo(n)[0] for n in xz_dn])
-    send_yu = packed(face_yu, [zhalo(n)[:, -1] for n in yz_up])
-    send_yd = packed(face_yd, [zhalo(n)[:, 0] for n in yz_dn])
-    n_yu, n_yd = send_yu.shape[0], send_yd.shape[0]
-    up2, dn2 = exchange(
-        [
-            (jnp.concatenate([send_yu, send_up]), (0, 1, 0)),
-            (jnp.concatenate([send_yd, send_dn]), (0, -1, 0)),
-        ]
-    )
-    hy_m, hy_p = up2[:n_yu], dn2[:n_yd]
+    from_up = jnp.concatenate([up2[n_face_u:], lanes(edge_rows(1, xz_up, "x"))])
+    from_dn = jnp.concatenate([dn2[n_face_d:], lanes(edge_rows(-1, xz_dn, "x"))])
 
     def unpack_x(got, count):
         return got[: count * ny].reshape(count, ny, nz), got[count * ny :, :ny]
@@ -368,12 +383,10 @@
 
     low2, high2 = exchange(
         [
-            (window(up2[n_yu:], send_up, x_up, xz_up, ny - rem), (1, q, 0)),
-            (window(send_dn, dn2[n_yd:], x_dn, xz_dn, rem), (-1, -q, 0)),
+            (window(from_up, send_up, x_up, xz_up, ny - rem), (1, q, 0)),
+            (window(send_dn, from_dn, x_dn, xz_dn, rem), (-1, -q, 0)),
         ]
     )
-    hy_m, cy_m = unpack_y(hy_m, len(y_up))
-    hy_p, cy_p = unpack_y(hy_p, len(y_dn))
 
     xlow = low2.reshape(len(x_up), ny, nz)
     xhigh = high2.reshape(len(x_dn), ny, nz)

time: 65.3 us -> 109 us (1.67)
  the two profiles are of different devices: /device:TPU:2 before, /device:TPU:123 now
where the time goes in v12:
time: 109 us; the launch traced here: 108 us
  local copies, waits for them, and re-layouts  45 us (41%)
  starting transfers between devices  26.1 us (24%)
  waiting for transfers between devices  25.4 us (23%)
  Pallas kernels  5.88 us (5%)
  other arithmetic  4.12 us (4%)
  between operations  1.78 us (2%)
    ppermute x12, starting transfers between devices, exchange(): got = lax.ppermute(joined, AXES, pairs)  26.1 us
    pallas_call x2, local copies, waits for them, and re-layouts, local(): pl.pallas_call(collide_kernel, out_shape=(jax.ShapeDtypeStruct((2 * pops,...  25.7 us
    ppermute x12, waiting for transfers between devices, exchange(): got = lax.ppermute(joined, AXES, pairs)  25.4 us
    gather x4, local copies, waits for them, and re-layouts, local(): ys = post[jnp.array([slot[n] for n in ypops]), :, yrow, zl]  5.81 us
    gather x4, local copies, waits for them, and re-layouts, local(): xs = post[jnp.array([slot[n] for n in xpops]), xrow, :, zl]  5.57 us
    pallas_call x1, Pallas kernels, local(): pl.pallas_call(collide_kernel, out_shape=(jax.ShapeDtypeStruct((2 * pops,...  3.05 us
    pallas_call x1, Pallas kernels, local(): pl.pallas_call(stream_kernel, out_shape=(jax.ShapeDtypeStruct((pops, nx,...  2.83 us
  transfers between devices with their start and end apart: 12, of which 6 were waited for; matrix products, arithmetic and copies ran while one was open for 17% of the time, Pallas kernels for 0%

profile of v12, /device:TPU:123, one launch (start us, length us, event | category | flops | bytes accessed | tf_op | source)
XLA Modules:
  0.0 108.2 jit_solution(13371333023152637120)
XLA Ops:
  0.6 1.1 %reduce_sum.9 = f32[4,16,128]{2,1,0:T(8,128)S(1)} reduce(f32[19,4,16,128]{3,2,1,0:T(8,128)} %g_ref.1, f32[]{:T(128)} %constant.35.clone.1), dimensions={0}, to_apply=%region_0.0 | reduce | flops 147456 | bytes 655364 | tf_op jit(solution)/shard_map/reduce_sum | solution.py:250
  1.8 0.2 slice_reduce_fusion.3
  1.9 4.3 %collective-permute-start.4 = (f32[2,4,16]{2,1,0:T(4,128)S(1)}, f32[2,4,16]{2,1,0:T(4,128)S(1)}, u32[]{:S(2)}, u32[]{:S(2)}) collective-permute-start(f32[2,4,16]{2,1,0:T(4,128)S(1)} %pad_maximum_fusion.13), channel_id=1, source_target_pairs={{0,1},{1,0},{2,3},{3,2},{4,5},{5,4},{6,7},{7,6},{8,9},{9,8},{10,11... | collective-permute-start | bytes 1544 | tf_op jit(solution)/shard_map/ppermute | solution.py:234
  6.2 0.3 collective-permute-start.2
  6.6 1.2 %collective-permute-start = (f32[20,128]{1,0:T(8,128)S(1)}, f32[20,128]{1,0:T(8,128)S(1)}, u32[]{:S(2)}, u32[]{:S(2)}) collective-permute-start(f32[20,128]{1,0:T(8,128)S(1)} %pad_maximum_fusion.11), channel_id=1, source_target_pairs={{0,2},{1,3},{2,4},{3,5},{4,6},{5,7},{6,0},{7,1},{8,10},{9,11},{10,... | collective-permute-start | bytes 30728 | tf_op jit(solution)/shard_map/ppermute | solution.py:234
  7.8 0.1 slice_bitcast_fusion.1
  8.6 0.7 pad_clamp_fusion.3
  9.2 0.7 pad_clamp_fusion.1
  9.9 0.7 pad_clamp_fusion
  10.6 0.1 copy.66
  10.7 0.1 copy.67
  10.8 5.5 %collective-permute-start.1 = (f32[32,128]{1,0:T(8,128)S(1)}, f32[32,128]{1,0:T(8,128)S(1)}, u32[]{:S(2)}, u32[]{:S(2)}) collective-permute-start(f32[32,128]{1,0:T(8,128)S(1)} %pad_maximum_fusion.9), channel_id=1, source_target_pairs={{0,12},{1,13},{2,14},{3,15},{4,8},{5,9},{6,10},{7,11},{8,20},{9,21... | collective-permute-start | bytes 49160 | tf_op jit(solution)/shard_map/ppermute | solution.py:234
  16.3 0.1 collective-permute-start.3
  16.4 0.7 collective-permute-done.1
  17.2 8.7 %collective-permute-done.3 = f32[32,128]{1,0:T(8,128)S(1)} collective-permute-done((f32[32,128]{1,0:T(8,128)S(1)}, f32[32,128]{1,0:T(8,128)S(1)}, u32[]{:S(2)}, u32[]{:S(2)}) %collective-permute-start.3) | collective-permute-done | bytes 16416 | tf_op jit(solution)/shard_map/ppermute | solution.py:234
  25.9 0.1 fusion.5
  26.0 0.1 multiply_dynamic-update-slice_fusion.nb_ref
  26.1 0.7 copy-done.5
  26.8 3.1 %shard_map.221 = (f32[38,4,16,128]{3,2,1,0:T(8,128)}, f32[10,16,128]{2,1,0:T(8,128)}, f32[10,16,128]{2,1,0:T(8,128)}, f32[10,4,128]{2,1,0:T(4,128)}, f32[10,4,128]{2,1,0:T(4,128)}) custom-call(f32[19,4,16,128]{3,2,1,0:T(8,128)} %f_ref.1, f32[19,4,16,128]{3,2,1,0:T(8,128)} %g_ref.1, f32[5,4,16,128]{3,2,1,0:T(8,128)} %copy-done.5), custom_call_target="tpu_custom_call" | custom-call | tf_op jit(solution)/shard_map/pallas_call | solution.py:279
  29.8 1.6 %slice_reduce_fusion.1 = (f32[10,4,16]{2,1,0:T(4,128)S(1)}, f32[10,4,16]{2,1,0:T(4,128)S(1)}) fusion(f32[38,4,16,128]{3,2,1,0:T(8,128)} %get-tuple-element.7.post_ref), kind=kLoop, calls=%fused_computation.14 | loop fusion | bytes 10240 | tf_op jit(solution)/shard_map/slice | solution.py:317
  31.4 6.5 %copy.69 = f32[38,4,16,128]{2,3,1,0:T(8,128)} copy(f32[38,4,16,128]{3,2,1,0:T(8,128)} %get-tuple-element.7.post_ref) | data formatting | bytes 2490368 | tf_op jit(solution)/shard_map/pallas_call | solution.py:279
  37.9 0.0 copy-start.16
  37.9 0.0 copy-start.15
  38.0 0.0 copy-start.14
  38.0 0.0 copy-start.13
  38.1 19.2 %copy.68 = f32[38,4,16,128]{1,3,2,0:T(8,128)} copy(f32[38,4,16,128]{3,2,1,0:T(8,128)S(1)} %copy-done) | data formatting | bytes 2490368 | tf_op jit(solution)/shard_map/pallas_call | solution.py:279
  57.3 1.2 %collective-permute-start.6 = (f32[20,4,16]{2,1,0:T(4,128)S(1)}, f32[20,4,16]{2,1,0:T(4,128)S(1)}, u32[]{:S(2)}, u32[]{:S(2)}) collective-permute-start(f32[20,4,16]{2,1,0:T(4,128)S(1)} %pad_maximum_fusion.2), channel_id=1, source_target_pairs={{0,1},{1,0},{2,3},{3,2},{4,5},{5,4},{6,7},{7,6},{8,9},{9,8},{10,11... | collective-permute-start | bytes 15368 | tf_op jit(solution)/shard_map/ppermute | solution.py:234
  58.5 0.1 collective-permute-start.7
  58.7 1.5 %collective-permute-start.10 = (f32[200,128]{1,0:T(8,128)S(1)}, f32[200,128]{1,0:T(8,128)S(1)}, u32[]{:S(2)}, u32[]{:S(2)}) collective-permute-start(f32[200,128]{1,0:T(8,128)S(1)} %pad_maximum_fusion.1), channel_id=1, source_target_pairs={{0,6},{1,7},{2,0},{3,1},{4,2},{5,3},{6,4},{7,5},{8,14},{9,15},{10,... | collective-permute-start | bytes 307208 | tf_op jit(solution)/shard_map/ppermute | solution.py:234
  60.2 1.3 %gather_fusion.1 = f32[2,16]{1,0:T(2,128)S(1)} fusion(f32[38,4,16,128]{2,3,1,0:T(8,128)} %copy.69, s32[2]{0:T(128)S(1)} %fusion.11), kind=kCustom, calls=%fused_computation.1 | custom fusion | bytes 280 | tf_op jit(solution)/shard_map/gather | solution.py:329
  61.5 1.4 %gather_fusion.8 = f32[2,16]{1,0:T(2,128)S(1)} fusion(f32[38,4,16,128]{2,3,1,0:T(8,128)} %copy.69, s32[2]{0:T(128)S(1)} %copy-done.16), kind=kCustom, calls=%fused_computation.8 | custom fusion | bytes 280 | tf_op jit(solution)/shard_map/gather | solution.py:329
  62.9 1.4 %gather_fusion.6 = f32[2,16]{1,0:T(2,128)S(1)} fusion(f32[38,4,16,128]{2,3,1,0:T(8,128)} %copy.69, s32[2]{0:T(128)S(1)} %copy-done.15), kind=kCustom, calls=%fused_computation.6 | custom fusion | bytes 280 | tf_op jit(solution)/shard_map/gather | solution.py:329
  64.3 1.4 %gather_fusion.3 = f32[2,16]{1,0:T(2,128)S(1)} fusion(f32[38,4,16,128]{2,3,1,0:T(8,128)} %copy.69, s32[2]{0:T(128)S(1)} %copy-done.14), kind=kCustom, calls=%fused_computation.3 | custom fusion | bytes 280 | tf_op jit(solution)/shard_map/gather | solution.py:329
  65.8 1.5 %gather_fusion.7 = f32[2,4]{1,0:T(2,128)S(1)} fusion(f32[38,4,16,128]{1,3,2,0:T(8,128)} %copy.68, s32[2]{0:T(128)S(1)} %copy-done.13), kind=kCustom, calls=%fused_computation.7 | custom fusion | bytes 88 | tf_op jit(solution)/shard_map/gather | solution.py:328
  67.2 1.5 %gather_fusion.5 = f32[2,4]{1,0:T(2,128)S(1)} fusion(f32[38,4,16,128]{1,3,2,0:T(8,128)} %copy.68, s32[2]{0:T(128)S(1)} %copy-done.12), kind=kCustom, calls=%fused_computation.5 | custom fusion | bytes 88 | tf_op jit(solution)/shard_map/gather | solution.py:328
  68.7 1.5 %gather_fusion.2 = f32[2,4]{1,0:T(2,128)S(1)} fusion(f32[38,4,16,128]{1,3,2,0:T(8,128)} %copy.68, s32[2]{0:T(128)S(1)} %copy-done.11), kind=kCustom, calls=%fused_computation.2 | custom fusion | bytes 88 | tf_op jit(solution)/shard_map/gather | solution.py:328
  70.1 1.5 %gather_fusion = f32[2,4]{1,0:T(2,128)S(1)} fusion(f32[38,4,16,128]{1,3,2,0:T(8,128)} %copy.68, s32[2]{0:T(128)S(1)} %copy-done.10), kind=kCustom, calls=%fused_computation | custom fusion | bytes 88 | tf_op jit(solution)/shard_map/gather | solution.py:328
  71.6 5.0 %collective-permute-start.5 = (f32[8,128]{1,0:T(8,128)S(1)}, f32[8,128]{1,0:T(8,128)S(1)}, u32[]{:S(2)}, u32[]{:S(2)}) collective-permute-start(f32[8,128]{1,0:T(8,128)S(1)} %select_maximum_fusion.3), channel_id=1, source_target_pairs={{0,3},{1,2},{2,5},{3,4},{4,7},{5,6},{6,1},{7,0},{8,11},{9,10},{10,... | collective-permute-start | bytes 12296 | tf_op jit(solution)/shard_map/ppermute | solution.py:234
  76.6 1.4 %collective-permute-start.9 = (f32[8,128]{1,0:T(8,128)S(1)}, f32[8,128]{1,0:T(8,128)S(1)}, u32[]{:S(2)}, u32[]{:S(2)}) collective-permute-start(f32[8,128]{1,0:T(8,128)S(1)} %select_maximum_fusion), channel_id=1, source_target_pairs={{0,7},{1,6},{2,1},{3,0},{4,3},{5,2},{6,5},{7,4},{8,15},{9,14},{10,... | collective-permute-start | bytes 12296 | tf_op jit(solution)/shard_map/ppermute | solution.py:234
  78.0 0.9 collective-permute-done.5
  78.9 5.0 %collective-permute-done.9 = f32[8,128]{1,0:T(8,128)S(1)} collective-permute-done((f32[8,128]{1,0:T(8,128)S(1)}, f32[8,128]{1,0:T(8,128)S(1)}, u32[]{:S(2)}, u32[]{:S(2)}) %collective-permute-start.9) | collective-permute-done | bytes 4128 | tf_op jit(solution)/shard_map/ppermute | solution.py:234
  84.0 0.6 gather_fusion.12
  84.6 0.2 copy.83
  84.8 0.6 gather_fusion.10
  85.4 0.2 copy.81
  85.6 0.6 gather_fusion.11
  86.2 0.1 fusion.15
  86.3 0.1 maximum_maximum_fusion
  86.4 0.1 constant_dynamic-slice_fusion
  86.5 0.2 maximum_select_fusion.4
  86.7 0.1 constant_dynamic-slice_fusion.1
  86.8 0.6 gather_fusion.4
  87.3 0.6 gather_fusion.9
  87.9 0.1 copy.72
  88.0 0.1 copy.78
  88.3 0.1 fusion.2
  88.4 0.1 fusion.12
  88.6 0.2 maximum_select_fusion.2
  88.7 5.4 %collective-permute-start.8 = (f32[160,128]{1,0:T(8,128)S(1)}, f32[160,128]{1,0:T(8,128)S(1)}, u32[]{:S(2)}, u32[]{:S(2)}) collective-permute-start(f32[160,128]{1,0:T(8,128)S(1)} %bitcast.85), channel_id=1, source_target_pairs={{0,12},{1,13},{2,14},{3,15},{4,8},{5,9},{6,10},{7,11},{8,20},{9,21... | collective-permute-start | bytes 245768 | tf_op jit(solution)/shard_map/ppermute | solution.py:234
  94.2 0.1 select_select_fusion
  94.3 1.4 %collective-permute-done.8 = f32[160,128]{1,0:T(8,128)S(1)} collective-permute-done((f32[160,128]{1,0:T(8,128)S(1)}, f32[160,128]{1,0:T(8,128)S(1)}, u32[]{:S(2)}, u32[]{:S(2)}) %collective-permute-start.8) | collective-permute-done | bytes 81952 | tf_op jit(solution)/shard_map/ppermute | solution.py:234
  95.6 8.7 %collective-permute-done.11 = f32[160,128]{1,0:T(8,128)S(1)} collective-permute-done((f32[160,128]{1,0:T(8,128)S(1)}, f32[160,128]{1,0:T(8,128)S(1)}, u32[]{:S(2)}, u32[]{:S(2)}) %collective-permute-start.11) | collective-permute-done | bytes 81952 | tf_op jit(solution)/shard_map/ppermute | solution.py:234
  104.3 1.1 broadcast_in_dim.157.col_ref
  105.4 2.8 %shard_map.222 = (f32[19,4,16,128]{3,2,1,0:T(8,128)}, f32[19,4,16,128]{3,2,1,0:T(8,128)}) custom-call(f32[38,4,16,128]{3,2,1,0:T(8,128)} %get-tuple-element.7.post_ref, f32[10,16,128]{2,1,0:T(8,128)} %bitcast.82, f32[10,16,128]{2,1,0:T(8,128)} %bitcast.83, f32[200,128]{1,0:T(8,128)} %copy-done.1, f32[200,128]{1,0:T(8,128)} %copy-done.2, ...), custom_call_target="tpu_custom_call" | custom-call | tf_op jit(solution)/shard_map/pallas_call | solution.py:417
  (92 shorter events, 0.5 us)
Async XLA Ops:
  1.9 8.6 %collective-permute-start.4 = (f32[2,4,16]{2,1,0:T(4,128)S(1)}, f32[2,4,16]{2,1,0:T(4,128)S(1)}, u32[]{:S(2)}, u32[]{:S(2)}) collective-permute-start(f32[2,4,16]{2,1,0:T(4,128)S(1)} %pad_maximum_fusion.13), channel_id=1, source_target_pairs={{0,1},{1,0},{2,3},{3,2},{4,5},{5,4},{6,7},{7,6},{8,9},{9,8},{10,11... | collective-permute-start | bytes 1544 | tf_op jit(solution)/shard_map/ppermute | solution.py:234
  6.2 10.1 %collective-permute-start.2 = (f32[20,128]{1,0:T(8,128)S(1)}, f32[20,128]{1,0:T(8,128)S(1)}, u32[]{:S(2)}, u32[]{:S(2)}) collective-permute-start(f32[20,128]{1,0:T(8,128)S(1)} %pad_maximum_fusion.12), channel_id=1, source_target_pairs={{0,6},{1,7},{2,0},{3,1},{4,2},{5,3},{6,4},{7,5},{8,14},{9,15},{10,... | collective-permute-start | bytes 30728 | tf_op jit(solution)/shard_map/ppermute | solution.py:234
  6.6 4.2 %collective-permute-start = (f32[20,128]{1,0:T(8,128)S(1)}, f32[20,128]{1,0:T(8,128)S(1)}, u32[]{:S(2)}, u32[]{:S(2)}) collective-permute-start(f32[20,128]{1,0:T(8,128)S(1)} %pad_maximum_fusion.11), channel_id=1, source_target_pairs={{0,2},{1,3},{2,4},{3,5},{4,6},{5,7},{6,0},{7,1},{8,10},{9,11},{10,... | collective-permute-start | bytes 30728 | tf_op jit(solution)/shard_map/ppermute | solution.py:234
  10.8 6.4 %collective-permute-start.1 = (f32[32,128]{1,0:T(8,128)S(1)}, f32[32,128]{1,0:T(8,128)S(1)}, u32[]{:S(2)}, u32[]{:S(2)}) collective-permute-start(f32[32,128]{1,0:T(8,128)S(1)} %pad_maximum_fusion.9), channel_id=1, source_target_pairs={{0,12},{1,13},{2,14},{3,15},{4,8},{5,9},{6,10},{7,11},{8,20},{9,21... | collective-permute-start | bytes 49160 | tf_op jit(solution)/shard_map/ppermute | solution.py:234
  16.3 9.6 %collective-permute-start.3 = (f32[32,128]{1,0:T(8,128)S(1)}, f32[32,128]{1,0:T(8,128)S(1)}, u32[]{:S(2)}, u32[]{:S(2)}) collective-permute-start(f32[32,128]{1,0:T(8,128)S(1)} %pad_maximum_fusion.10), channel_id=1, source_target_pairs={{0,252},{1,253},{2,254},{3,255},{4,248},{5,249},{6,250},{7,251},{8... | collective-permute-start | bytes 49160 | tf_op jit(solution)/shard_map/ppermute | solution.py:234
  26.1 0.7 copy-start.5
  29.8 8.1 %copy-start = (f32[38,4,16,128]{3,2,1,0:T(8,128)S(1)}, f32[38,4,16,128]{3,2,1,0:T(8,128)}, u32[]{:S(2)}) copy-start(f32[38,4,16,128]{3,2,1,0:T(8,128)} %get-tuple-element.7.post_ref) | copy-start | bytes 3735556
  37.9 20.6 %copy-start.4 = (f32[10,16,128]{2,1,0:T(8,128)S(1)}, f32[10,16,128]{2,1,0:T(8,128)}, u32[]{:S(2)}) copy-start(f32[10,16,128]{2,1,0:T(8,128)} %get-tuple-element.9) | copy-start | bytes 245764
  37.9 20.6 %copy-start.9 = (f32[10,4,128]{2,1,0:T(4,128)S(1)}, f32[10,4,128]{2,1,0:T(4,128)}, u32[]{:S(2)}) copy-start(f32[10,4,128]{2,1,0:T(4,128)} %get-tuple-element.8) | copy-start | bytes 61444
  37.9 20.7 %copy-start.3 = (f32[10,16,128]{2,1,0:T(8,128)S(1)}, f32[10,16,128]{2,1,0:T(8,128)}, u32[]{:S(2)}) copy-start(f32[10,16,128]{2,1,0:T(8,128)} %get-tuple-element.10) | copy-start | bytes 245764
  37.9 20.7 %copy-start.8 = (f32[10,4,128]{2,1,0:T(4,128)S(1)}, f32[10,4,128]{2,1,0:T(4,128)}, u32[]{:S(2)}) copy-start(f32[10,4,128]{2,1,0:T(4,128)} %get-tuple-element.11) | copy-start | bytes 61444
  37.9 23.5 %copy-start.16 = (s32[2]{0:T(128)S(1)}, s32[2]{0:T(128)}, u32[]{:S(2)}) copy-start(s32[2]{0:T(128)} %constant.441) | copy-start | bytes 28
  37.9 25.0 %copy-start.15 = (s32[2]{0:T(128)S(1)}, s32[2]{0:T(128)}, u32[]{:S(2)}) copy-start(s32[2]{0:T(128)} %constant.417) | copy-start | bytes 28
  38.0 26.4 %copy-start.14 = (s32[2]{0:T(128)S(1)}, s32[2]{0:T(128)}, u32[]{:S(2)}) copy-start(s32[2]{0:T(128)} %constant.392) | copy-start | bytes 28
  38.0 27.8 %copy-start.13 = (s32[2]{0:T(128)S(1)}, s32[2]{0:T(128)}, u32[]{:S(2)}) copy-start(s32[2]{0:T(128)} %constant.429) | copy-start | bytes 28
  38.0 29.2 %copy-start.12 = (s32[2]{0:T(128)S(1)}, s32[2]{0:T(128)}, u32[]{:S(2)}) copy-start(s32[2]{0:T(128)} %constant.405) | copy-start | bytes 28
  38.0 30.7 %copy-start.11 = (s32[2]{0:T(128)S(1)}, s32[2]{0:T(128)}, u32[]{:S(2)}) copy-start(s32[2]{0:T(128)} %constant.380) | copy-start | bytes 28
  38.0 32.1 %copy-start.10 = (s32[2]{0:T(128)S(1)}, s32[2]{0:T(128)}, u32[]{:S(2)}) copy-start(s32[2]{0:T(128)} %constant.364) | copy-start | bytes 28
  38.0 48.5 %copy-start.23 = (pred[20]{0:T(512)(128)(4,1)S(1)}, pred[20]{0:T(512)(128)(4,1)}, u32[]{:S(2)}) copy-start(pred[20]{0:T(512)(128)(4,1)} %constant.195) | copy-start | bytes 64
  38.0 48.5 %copy-start.24 = (pred[20]{0:T(512)(128)(4,1)S(1)}, pred[20]{0:T(512)(128)(4,1)}, u32[]{:S(2)}) copy-start(pred[20]{0:T(512)(128)(4,1)} %constant.186) | copy-start | bytes 64
  38.0 50.3 %copy-start.21 = (pred[10]{0:T(512)(128)(4,1)S(1)}, pred[10]{0:T(512)(128)(4,1)}, u32[]{:S(2)}) copy-start(pred[10]{0:T(512)(128)(4,1)} %constant.159) | copy-start | bytes 34
  38.1 50.3 %copy-start.22 = (pred[10]{0:T(512)(128)(4,1)S(1)}, pred[10]{0:T(512)(128)(4,1)}, u32[]{:S(2)}) copy-start(pred[10]{0:T(512)(128)(4,1)} %constant.158) | copy-start | bytes 34
  38.1 50.5 %copy-start.19 = (pred[10]{0:T(512)(128)(4,1)S(1)}, pred[10]{0:T(512)(128)(4,1)}, u32[]{:S(2)}) copy-start(pred[10]{0:T(512)(128)(4,1)} %constant.160) | copy-start | bytes 34
  38.1 50.5 %copy-start.20 = (pred[10]{0:T(512)(128)(4,1)S(1)}, pred[10]{0:T(512)(128)(4,1)}, u32[]{:S(2)}) copy-start(pred[10]{0:T(512)(128)(4,1)} %constant.138) | copy-start | bytes 34
  38.1 56.1 %copy-start.17 = (pred[20]{0:T(512)(128)(4,1)S(1)}, pred[20]{0:T(512)(128)(4,1)}, u32[]{:S(2)}) copy-start(pred[20]{0:T(512)(128)(4,1)} %constant.200) | copy-start | bytes 64
  38.1 56.0 %copy-start.18 = (pred[20]{0:T(512)(128)(4,1)S(1)}, pred[20]{0:T(512)(128)(4,1)}, u32[]{:S(2)}) copy-start(pred[20]{0:T(512)(128)(4,1)} %constant.185) | copy-start | bytes 64
  57.3 28.3 %collective-permute-start.6 = (f32[20,4,16]{2,1,0:T(4,128)S(1)}, f32[20,4,16]{2,1,0:T(4,128)S(1)}, u32[]{:S(2)}, u32[]{:S(2)}) collective-permute-start(f32[20,4,16]{2,1,0:T(4,128)S(1)} %pad_maximum_fusion.2), channel_id=1, source_target_pairs={{0,1},{1,0},{2,3},{3,2},{4,5},{5,4},{6,7},{7,6},{8,9},{9,8},{10,11... | collective-permute-start | bytes 15368 | tf_op jit(solution)/shard_map/ppermute | solution.py:234
  58.5 29.6 %collective-permute-start.7 = (f32[200,128]{1,0:T(8,128)S(1)}, f32[200,128]{1,0:T(8,128)S(1)}, u32[]{:S(2)}, u32[]{:S(2)}) collective-permute-start(f32[200,128]{1,0:T(8,128)S(1)} %pad_maximum_fusion), channel_id=1, source_target_pairs={{0,2},{1,3},{2,4},{3,5},{4,6},{5,7},{6,0},{7,1},{8,10},{9,11},{10,... | collective-permute-start | bytes 307208 | tf_op jit(solution)/shard_map/ppermute | solution.py:234
  58.7 29.6 %collective-permute-start.10 = (f32[200,128]{1,0:T(8,128)S(1)}, f32[200,128]{1,0:T(8,128)S(1)}, u32[]{:S(2)}, u32[]{:S(2)}) collective-permute-start(f32[200,128]{1,0:T(8,128)S(1)} %pad_maximum_fusion.1), channel_id=1, source_target_pairs={{0,6},{1,7},{2,0},{3,1},{4,2},{5,3},{6,4},{7,5},{8,14},{9,15},{10,... | collective-permute-start | bytes 307208 | tf_op jit(solution)/shard_map/ppermute | solution.py:234
  71.6 7.3 %collective-permute-start.5 = (f32[8,128]{1,0:T(8,128)S(1)}, f32[8,128]{1,0:T(8,128)S(1)}, u32[]{:S(2)}, u32[]{:S(2)}) collective-permute-start(f32[8,128]{1,0:T(8,128)S(1)} %select_maximum_fusion.3), channel_id=1, source_target_pairs={{0,3},{1,2},{2,5},{3,4},{4,7},{5,6},{6,1},{7,0},{8,11},{9,10},{10,... | collective-permute-start | bytes 12296 | tf_op jit(solution)/shard_map/ppermute | solution.py:234
  76.6 7.3 %collective-permute-start.9 = (f32[8,128]{1,0:T(8,128)S(1)}, f32[8,128]{1,0:T(8,128)S(1)}, u32[]{:S(2)}, u32[]{:S(2)}) collective-permute-start(f32[8,128]{1,0:T(8,128)S(1)} %select_maximum_fusion), channel_id=1, source_target_pairs={{0,7},{1,6},{2,1},{3,0},{4,3},{5,2},{6,5},{7,4},{8,15},{9,14},{10,... | collective-permute-start | bytes 12296 | tf_op jit(solution)/shard_map/ppermute | solution.py:234
  88.2 17.2 %copy-start.1 = (f32[200,128]{1,0:T(8,128)}, f32[200,128]{1,0:T(8,128)S(1)}, u32[]{:S(2)}) copy-start(f32[200,128]{1,0:T(8,128)S(1)} %collective-permute-done.7.hym_ref) | copy-start | bytes 307204
  88.2 17.2 %copy-start.2 = (f32[200,128]{1,0:T(8,128)}, f32[200,128]{1,0:T(8,128)S(1)}, u32[]{:S(2)}) copy-start(f32[200,128]{1,0:T(8,128)S(1)} %collective-permute-done.10.hyp_ref) | copy-start | bytes 307204
  88.7 6.9 %collective-permute-start.8 = (f32[160,128]{1,0:T(8,128)S(1)}, f32[160,128]{1,0:T(8,128)S(1)}, u32[]{:S(2)}, u32[]{:S(2)}) collective-permute-start(f32[160,128]{1,0:T(8,128)S(1)} %bitcast.85), channel_id=1, source_target_pairs={{0,12},{1,13},{2,14},{3,15},{4,8},{5,9},{6,10},{7,11},{8,20},{9,21... | collective-permute-start | bytes 245768 | tf_op jit(solution)/shard_map/ppermute | solution.py:234
  94.1 10.2 %collective-permute-start.11 = (f32[160,128]{1,0:T(8,128)S(1)}, f32[160,128]{1,0:T(8,128)S(1)}, u32[]{:S(2)}, u32[]{:S(2)}) collective-permute-start(f32[160,128]{1,0:T(8,128)S(1)} %bitcast.84), channel_id=1, source_target_pairs={{0,252},{1,253},{2,254},{3,255},{4,248},{5,249},{6,250},{7,251},{8... | collective-permute-start | bytes 245768 | tf_op jit(solution)/shard_map/ppermute | solution.py:234
  95.6 9.8 %copy-start.6 = (f32[160,128]{1,0:T(8,128)}, f32[160,128]{1,0:T(8,128)S(1)}, u32[]{:S(2)}) copy-start(f32[160,128]{1,0:T(8,128)S(1)} %collective-permute-done.8) | copy-start | bytes 245764
  104.3 1.1 %copy-start.7 = (f32[160,128]{1,0:T(8,128)}, f32[160,128]{1,0:T(8,128)S(1)}, u32[]{:S(2)}) copy-start(f32[160,128]{1,0:T(8,128)S(1)} %collective-permute-done.11) | copy-start | bytes 245764

commit v13 on v12

--- a/solution.py
+++ b/solution.py
@@ -325,8 +325,8 @@
             ypops = [n for n in (yz_up if dy == 1 else yz_dn) if vel[n][2] == dz]
             xpops = [n for n in (xz_up if dy == 1 else xz_dn) if vel[n][2] == dz]
             yrow, xrow, zl = (ny - 1, nx - 1, nz - 1 if dz == 1 else 0) if dy == 1 else (0, 0, nz - 1 if dz == 1 else 0)
-            ys = post[jnp.array([slot[n] for n in ypops]), :, yrow, zl]
-            xs = post[jnp.array([slot[n] for n in xpops]), xrow, :, zl]
+            ys = jnp.stack([post[slot[n], :, yrow, zl] for n in ypops])
+            xs = jnp.stack([post[slot[n], xrow, :, zl] for n in xpops])
             sends.append((jnp.concatenate([lanes(ys), lanes(xs)]), (0, dy, dz)))
             diag_keys.append((dy, dz, ypops, xpops))
     got = exchange(sends)

time: 109 us -> 68 us (0.62)
  the two profiles are of different devices: /device:TPU:123 before, /device:TPU:251 now
where the time goes in v13:
time: 68 us; the launch traced here: 67.6 us
  starting transfers between devices  23.7 us (35%)
  waiting for transfers between devices  22.3 us (33%)
  local copies, waits for them, and re-layouts  10.1 us (15%)
  Pallas kernels  5.85 us (9%)
  other arithmetic  3.89 us (6%)
  between operations  1.86 us (3%)
    ppermute x12, starting transfers between devices, exchange(): got = lax.ppermute(joined, AXES, pairs)  23.7 us
    ppermute x12, waiting for transfers between devices, exchange(): got = lax.ppermute(joined, AXES, pairs)  22.3 us
    pallas_call x1, Pallas kernels, local(): pl.pallas_call(collide_kernel, out_shape=(jax.ShapeDtypeStruct((2 * pops,...  3.02 us
    pallas_call x1, Pallas kernels, local(): pl.pallas_call(stream_kernel, out_shape=(jax.ShapeDtypeStruct((pops, nx,...  2.83 us
    slice x1, local copies, waits for them, and re-layouts, local(): post[:len(z_up), :, :, -1]  1.47 us
  transfers between devices with their start and end apart: 12, of which 5 were waited for; matrix products, arithmetic and copies ran while one was open for 10% of the time, Pallas kernels for 0%

profile of v13, /device:TPU:251, one launch (start us, length us, event | category | flops | bytes accessed | tf_op | source)
XLA Modules:
  0.0 67.6 jit_solution(13004852947512275824)
XLA Ops:
  0.6 0.0 copy-start.18
  0.6 0.0 copy-start.17
  0.7 0.0 copy-start.15
  0.7 0.0 copy-start.16
  0.7 1.1 %reduce_sum.9 = f32[4,16,128]{2,1,0:T(8,128)S(1)} reduce(f32[19,4,16,128]{3,2,1,0:T(8,128)} %g_ref.1, f32[]{:T(128)} %constant.24.clone.1), dimensions={0}, to_apply=%region_0.0 | reduce | flops 147456 | bytes 655364 | tf_op jit(solution)/shard_map/reduce_sum | solution.py:250
  1.8 0.2 slice_reduce_fusion.3
  2.0 1.2 %collective-permute-start.4 = (f32[2,4,16]{2,1,0:T(4,128)S(1)}, f32[2,4,16]{2,1,0:T(4,128)S(1)}, u32[]{:S(2)}, u32[]{:S(2)}) collective-permute-start(f32[2,4,16]{2,1,0:T(4,128)S(1)} %pad_maximum_fusion.13), channel_id=1, source_target_pairs={{0,1},{1,0},{2,3},{3,2},{4,5},{5,4},{6,7},{7,6},{8,9},{9,8},{10,11... | collective-permute-start | bytes 1544 | tf_op jit(solution)/shard_map/ppermute | solution.py:234
  3.3 0.3 collective-permute-start.2
  3.6 1.2 %collective-permute-start = (f32[20,128]{1,0:T(8,128)S(1)}, f32[20,128]{1,0:T(8,128)S(1)}, u32[]{:S(2)}, u32[]{:S(2)}) collective-permute-start(f32[20,128]{1,0:T(8,128)S(1)} %pad_maximum_fusion.11), channel_id=1, source_target_pairs={{0,2},{1,3},{2,4},{3,5},{4,6},{5,7},{6,0},{7,1},{8,10},{9,11},{10,... | collective-permute-start | bytes 30728 | tf_op jit(solution)/shard_map/ppermute | solution.py:234
  4.8 0.1 slice_bitcast_fusion.1
  5.7 2.8 %collective-permute-done.4 = f32[2,4,16]{2,1,0:T(4,128)S(1)} collective-permute-done((f32[2,4,16]{2,1,0:T(4,128)S(1)}, f32[2,4,16]{2,1,0:T(4,128)S(1)}, u32[]{:S(2)}, u32[]{:S(2)}) %collective-permute-start.4) | collective-permute-done | bytes 544 | tf_op jit(solution)/shard_map/ppermute | solution.py:234
  8.4 0.1 copy.42
  8.5 0.1 copy.43
  8.7 4.6 %collective-permute-start.1 = (f32[32,128]{1,0:T(8,128)S(1)}, f32[32,128]{1,0:T(8,128)S(1)}, u32[]{:S(2)}, u32[]{:S(2)}) collective-permute-start(f32[32,128]{1,0:T(8,128)S(1)} %pad_maximum_fusion.9), channel_id=1, source_target_pairs={{0,12},{1,13},{2,14},{3,15},{4,8},{5,9},{6,10},{7,11},{8,20},{9,21... | collective-permute-start | bytes 49160 | tf_op jit(solution)/shard_map/ppermute | solution.py:234
  13.3 0.1 collective-permute-start.3
  13.4 0.7 %collective-permute-done.1 = f32[32,128]{1,0:T(8,128)S(1)} collective-permute-done((f32[32,128]{1,0:T(8,128)S(1)}, f32[32,128]{1,0:T(8,128)S(1)}, u32[]{:S(2)}, u32[]{:S(2)}) %collective-permute-start.1) | collective-permute-done | bytes 16416 | tf_op jit(solution)/shard_map/ppermute | solution.py:234
  14.2 8.7 %collective-permute-done.3 = f32[32,128]{1,0:T(8,128)S(1)} collective-permute-done((f32[32,128]{1,0:T(8,128)S(1)}, f32[32,128]{1,0:T(8,128)S(1)}, u32[]{:S(2)}, u32[]{:S(2)}) %collective-permute-start.3) | collective-permute-done | bytes 16416 | tf_op jit(solution)/shard_map/ppermute | solution.py:234
  22.9 0.1 fusion.5
  23.0 0.1 multiply_dynamic-update-slice_fusion.nb_ref
  23.1 0.0 copy-start.4
  23.1 0.7 copy-done.4
  23.8 3.0 %shard_map.149 = (f32[38,4,16,128]{3,2,1,0:T(8,128)}, f32[10,16,128]{2,1,0:T(8,128)}, f32[10,16,128]{2,1,0:T(8,128)}, f32[10,4,128]{2,1,0:T(4,128)}, f32[10,4,128]{2,1,0:T(4,128)}) custom-call(f32[19,4,16,128]{3,2,1,0:T(8,128)} %f_ref.1, f32[19,4,16,128]{3,2,1,0:T(8,128)} %g_ref.1, f32[5,4,16,128]{3,2,1,0:T(8,128)} %copy-done.4), custom_call_target="tpu_custom_call" | custom-call | tf_op jit(solution)/shard_map/pallas_call | solution.py:279
  26.8 0.0 copy-start.14
  26.8 1.0 %slice_reduce_fusion.15 = (f32[4]{0:T(128)S(1)}, f32[4]{0:T(128)S(1)}, f32[4]{0:T(128)S(1)}, f32[4]{0:T(128)S(1)}, f32[4]{0:T(128)S(1)}, /*index=5*/f32[4]{0:T(128)S(1)}, f32[4]{0:T(128)S(1)}, f32[4]{0:T(128)S(1)}) fusion(f32[38,4,16,128]{3,2,1,0:T(8,128)} %get-tuple-element.7.post_ref), kind=kLoop, calls=%fused_computation.78 | loop fusion | bytes 256 | tf_op jit(solution)/shard_map/slice | solution.py:328
  27.9 1.1 %slice_reduce_fusion.7 = (f32[16]{0:T(128)S(1)}, f32[16]{0:T(128)S(1)}, f32[16]{0:T(128)S(1)}, f32[16]{0:T(128)S(1)}, f32[16]{0:T(128)S(1)}, /*index=5*/f32[16]{0:T(128)S(1)}, f32[16]{0:T(128)S(1)}, f32[16]{0:T(128)S(1)}) fusion(f32[38,4,16,128]{3,2,1,0:T(8,128)} %get-tuple-element.7.post_ref), kind=kLoop, calls=%fused_computation.57 | loop fusion | bytes 1024 | tf_op jit(solution)/shard_map/slice | solution.py:329
  29.0 1.5 %slice_reduce_fusion.1 = (f32[10,4,16]{2,1,0:T(4,128)S(1)}, f32[10,4,16]{2,1,0:T(4,128)S(1)}) fusion(f32[38,4,16,128]{3,2,1,0:T(8,128)} %get-tuple-element.7.post_ref), kind=kLoop, calls=%fused_computation.6 | loop fusion | bytes 10240 | tf_op jit(solution)/shard_map/slice | solution.py:317
  30.4 0.0 copy-start.3
  30.5 5.0 %collective-permute-start.5 = (f32[8,128]{1,0:T(8,128)S(1)}, f32[8,128]{1,0:T(8,128)S(1)}, u32[]{:S(2)}, u32[]{:S(2)}) collective-permute-start(f32[8,128]{1,0:T(8,128)S(1)} %pad_maximum_fusion.14), channel_id=1, source_target_pairs={{0,3},{1,2},{2,5},{3,4},{4,7},{5,6},{6,1},{7,0},{8,11},{9,10},{10,... | collective-permute-start | bytes 12296 | tf_op jit(solution)/shard_map/ppermute | solution.py:234
  35.5 1.4 %collective-permute-start.9 = (f32[8,128]{1,0:T(8,128)S(1)}, f32[8,128]{1,0:T(8,128)S(1)}, u32[]{:S(2)}, u32[]{:S(2)}) collective-permute-start(f32[8,128]{1,0:T(8,128)S(1)} %pad_maximum_fusion.15), channel_id=1, source_target_pairs={{0,7},{1,6},{2,1},{3,0},{4,3},{5,2},{6,5},{7,4},{8,15},{9,14},{10,... | collective-permute-start | bytes 12296 | tf_op jit(solution)/shard_map/ppermute | solution.py:234
  37.0 2.7 %collective-permute-start.6 = (f32[20,4,16]{2,1,0:T(4,128)S(1)}, f32[20,4,16]{2,1,0:T(4,128)S(1)}, u32[]{:S(2)}, u32[]{:S(2)}) collective-permute-start(f32[20,4,16]{2,1,0:T(4,128)S(1)} %pad_maximum_fusion.2), channel_id=1, source_target_pairs={{0,1},{1,0},{2,3},{3,2},{4,5},{5,4},{6,7},{7,6},{8,9},{9,8},{10,11... | collective-permute-start | bytes 15368 | tf_op jit(solution)/shard_map/ppermute | solution.py:234
  39.7 0.9 %pad_maximum_fusion = f32[200,128]{1,0:T(8,128)S(1)} fusion(f32[160,128]{1,0:T(8,128)} %bitcast.95, f32[40,128]{1,0:T(8,128)} %bitcast.107), kind=kLoop, calls=%fused_computation.13 | loop fusion | flops 25600 | bytes 204800 | tf_op jit(solution)/shard_map/concatenate | solution.py:319
  40.6 2.7 %collective-permute-start.7 = (f32[200,128]{1,0:T(8,128)S(1)}, f32[200,128]{1,0:T(8,128)S(1)}, u32[]{:S(2)}, u32[]{:S(2)}) collective-permute-start(f32[200,128]{1,0:T(8,128)S(1)} %pad_maximum_fusion), channel_id=1, source_target_pairs={{0,2},{1,3},{2,4},{3,5},{4,6},{5,7},{6,0},{7,1},{8,10},{9,11},{10,... | collective-permute-start | bytes 307208 | tf_op jit(solution)/shard_map/ppermute | solution.py:234
  43.3 0.8 %pad_maximum_fusion.1 = f32[200,128]{1,0:T(8,128)S(1)} fusion(f32[160,128]{1,0:T(8,128)S(1)} %bitcast.94, f32[40,128]{1,0:T(8,128)} %bitcast.106), kind=kLoop, calls=%fused_computation.14 | loop fusion | flops 25600 | bytes 204800 | tf_op jit(solution)/shard_map/concatenate | solution.py:320
  44.1 0.0 collective-permute-done.9
  44.1 0.6 gather_fusion.4
  44.7 0.2 copy.51
  45.0 0.6 gather_fusion.2
  45.5 0.2 copy.49
  45.8 0.1 maximum_maximum_fusion.1
  45.9 0.1 constant_dynamic-slice_fusion
  45.9 0.6 gather_fusion.3
  46.5 0.1 fusion.9
  46.6 0.2 maximum_select_fusion.4
  46.8 0.1 maximum_maximum_fusion
  46.9 0.1 constant_dynamic-slice_fusion.1
  47.0 0.6 gather_fusion
  47.6 0.0 copy-start.9
  47.6 0.0 copy-start.10
  47.6 0.6 gather_fusion.1
  48.1 0.1 copy.44
  48.3 0.1 copy.46
  48.5 0.0 copy-start.7
  48.5 0.0 copy-start.8
  48.6 0.1 fusion.2
  48.7 0.1 fusion.6
  48.9 0.2 maximum_select_fusion.2
  49.0 0.0 copy-done
  49.1 0.1 copy-done.1
  49.1 4.4 %collective-permute-start.8 = (f32[160,128]{1,0:T(8,128)S(1)}, f32[160,128]{1,0:T(8,128)S(1)}, u32[]{:S(2)}, u32[]{:S(2)}) collective-permute-start(f32[160,128]{1,0:T(8,128)S(1)} %bitcast.101), channel_id=1, source_target_pairs={{0,12},{1,13},{2,14},{3,15},{4,8},{5,9},{6,10},{7,11},{8,20},{9,21... | collective-permute-start | bytes 245768 | tf_op jit(solution)/shard_map/ppermute | solution.py:234
  53.5 0.1 select_select_fusion
  53.6 1.4 %collective-permute-done.8 = f32[160,128]{1,0:T(8,128)S(1)} collective-permute-done((f32[160,128]{1,0:T(8,128)S(1)}, f32[160,128]{1,0:T(8,128)S(1)}, u32[]{:S(2)}, u32[]{:S(2)}) %collective-permute-start.8) | collective-permute-done | bytes 81952 | tf_op jit(solution)/shard_map/ppermute | solution.py:234
  55.0 8.7 %collective-permute-done.11 = f32[160,128]{1,0:T(8,128)S(1)} collective-permute-done((f32[160,128]{1,0:T(8,128)S(1)}, f32[160,128]{1,0:T(8,128)S(1)}, u32[]{:S(2)}, u32[]{:S(2)}) %collective-permute-start.11) | collective-permute-done | bytes 81952 | tf_op jit(solution)/shard_map/ppermute | solution.py:234
  63.7 1.1 %broadcast_in_dim.125.col_ref = f32[20,4,16,128]{3,2,1,0:T(8,128)} broadcast(f32[20,4,16]{2,1,0:T(4,128)S(1)} %select_select_fusion), dimensions={0,1,2} | broadcast | bytes 660480 | tf_op jit(solution)/shard_map/broadcast_in_dim | solution.py:415
  64.8 2.8 %shard_map.150 = (f32[19,4,16,128]{3,2,1,0:T(8,128)}, f32[19,4,16,128]{3,2,1,0:T(8,128)}) custom-call(f32[38,4,16,128]{3,2,1,0:T(8,128)} %get-tuple-element.7.post_ref, f32[10,16,128]{2,1,0:T(8,128)} %bitcast.98, f32[10,16,128]{2,1,0:T(8,128)} %bitcast.99, f32[200,128]{1,0:T(8,128)} %copy-done, f32[200,128]{1,0:T(8,128)} %copy-done.1, ...), custom_call_target="tpu_custom_call" | custom-call | tf_op jit(solution)/shard_map/pallas_call | solution.py:417
  (76 shorter events, 0.5 us)
Async XLA Ops:
  0.6 4.9 %copy-start.18 = (s32[10]{0:T(128)S(1)}, s32[10]{0:T(128)}, u32[]{:S(2)}) copy-start(s32[10]{0:T(128)} %constant.127) | copy-start | bytes 124
  0.6 4.9 %copy-start.17 = (s32[20]{0:T(128)S(1)}, s32[20]{0:T(128)}, u32[]{:S(2)}) copy-start(s32[20]{0:T(128)} %constant.130) | copy-start | bytes 244
  0.7 5.0 %copy-start.15 = (s32[20]{0:T(128)S(1)}, s32[20]{0:T(128)}, u32[]{:S(2)}) copy-start(s32[20]{0:T(128)} %constant.131) | copy-start | bytes 244
  0.7 5.0 %copy-start.16 = (s32[20]{0:T(128)S(1)}, s32[20]{0:T(128)}, u32[]{:S(2)}) copy-start(s32[20]{0:T(128)} %constant.129) | copy-start | bytes 244
  2.0 6.5 %collective-permute-start.4 = (f32[2,4,16]{2,1,0:T(4,128)S(1)}, f32[2,4,16]{2,1,0:T(4,128)S(1)}, u32[]{:S(2)}, u32[]{:S(2)}) collective-permute-start(f32[2,4,16]{2,1,0:T(4,128)S(1)} %pad_maximum_fusion.13), channel_id=1, source_target_pairs={{0,1},{1,0},{2,3},{3,2},{4,5},{5,4},{6,7},{7,6},{8,9},{9,8},{10,11... | collective-permute-start | bytes 1544 | tf_op jit(solution)/shard_map/ppermute | solution.py:234
  3.3 10.0 %collective-permute-start.2 = (f32[20,128]{1,0:T(8,128)S(1)}, f32[20,128]{1,0:T(8,128)S(1)}, u32[]{:S(2)}, u32[]{:S(2)}) collective-permute-start(f32[20,128]{1,0:T(8,128)S(1)} %pad_maximum_fusion.12), channel_id=1, source_target_pairs={{0,6},{1,7},{2,0},{3,1},{4,2},{5,3},{6,4},{7,5},{8,14},{9,15},{10,... | collective-permute-start | bytes 30728 | tf_op jit(solution)/shard_map/ppermute | solution.py:234
  3.6 5.1 %collective-permute-start = (f32[20,128]{1,0:T(8,128)S(1)}, f32[20,128]{1,0:T(8,128)S(1)}, u32[]{:S(2)}, u32[]{:S(2)}) collective-permute-start(f32[20,128]{1,0:T(8,128)S(1)} %pad_maximum_fusion.11), channel_id=1, source_target_pairs={{0,2},{1,3},{2,4},{3,5},{4,6},{5,7},{6,0},{7,1},{8,10},{9,11},{10,... | collective-permute-start | bytes 30728 | tf_op jit(solution)/shard_map/ppermute | solution.py:234
  8.7 5.5 %collective-permute-start.1 = (f32[32,128]{1,0:T(8,128)S(1)}, f32[32,128]{1,0:T(8,128)S(1)}, u32[]{:S(2)}, u32[]{:S(2)}) collective-permute-start(f32[32,128]{1,0:T(8,128)S(1)} %pad_maximum_fusion.9), channel_id=1, source_target_pairs={{0,12},{1,13},{2,14},{3,15},{4,8},{5,9},{6,10},{7,11},{8,20},{9,21... | collective-permute-start | bytes 49160 | tf_op jit(solution)/shard_map/ppermute | solution.py:234
  13.3 9.6 %collective-permute-start.3 = (f32[32,128]{1,0:T(8,128)S(1)}, f32[32,128]{1,0:T(8,128)S(1)}, u32[]{:S(2)}, u32[]{:S(2)}) collective-permute-start(f32[32,128]{1,0:T(8,128)S(1)} %pad_maximum_fusion.10), channel_id=1, source_target_pairs={{0,252},{1,253},{2,254},{3,255},{4,248},{5,249},{6,250},{7,251},{8... | collective-permute-start | bytes 49160 | tf_op jit(solution)/shard_map/ppermute | solution.py:234
  23.1 0.7 copy-start.4
  26.8 16.5 %copy-start.2 = (f32[10,16,128]{2,1,0:T(8,128)S(1)}, f32[10,16,128]{2,1,0:T(8,128)}, u32[]{:S(2)}) copy-start(f32[10,16,128]{2,1,0:T(8,128)} %get-tuple-element.10) | copy-start | bytes 245764
  26.8 19.8 %copy-start.13 = (pred[20]{0:T(512)(128)(4,1)S(1)}, pred[20]{0:T(512)(128)(4,1)}, u32[]{:S(2)}) copy-start(pred[20]{0:T(512)(128)(4,1)} %constant.121) | copy-start | bytes 64
  26.8 19.9 %copy-start.14 = (pred[20]{0:T(512)(128)(4,1)S(1)}, pred[20]{0:T(512)(128)(4,1)}, u32[]{:S(2)}) copy-start(pred[20]{0:T(512)(128)(4,1)} %constant.112) | copy-start | bytes 64
  30.4 18.0 %copy-start.3 = (f32[10,16,128]{2,1,0:T(8,128)S(1)}, f32[10,16,128]{2,1,0:T(8,128)}, u32[]{:S(2)}) copy-start(f32[10,16,128]{2,1,0:T(8,128)} %get-tuple-element.9) | copy-start | bytes 245764
  30.5 13.5 %collective-permute-start.5 = (f32[8,128]{1,0:T(8,128)S(1)}, f32[8,128]{1,0:T(8,128)S(1)}, u32[]{:S(2)}, u32[]{:S(2)}) collective-permute-start(f32[8,128]{1,0:T(8,128)S(1)} %pad_maximum_fusion.14), channel_id=1, source_target_pairs={{0,3},{1,2},{2,5},{3,4},{4,7},{5,6},{6,1},{7,0},{8,11},{9,10},{10,... | collective-permute-start | bytes 12296 | tf_op jit(solution)/shard_map/ppermute | solution.py:234
  35.5 8.5 %collective-permute-start.9 = (f32[8,128]{1,0:T(8,128)S(1)}, f32[8,128]{1,0:T(8,128)S(1)}, u32[]{:S(2)}, u32[]{:S(2)}) collective-permute-start(f32[8,128]{1,0:T(8,128)S(1)} %pad_maximum_fusion.15), channel_id=1, source_target_pairs={{0,7},{1,6},{2,1},{3,0},{4,3},{5,2},{6,5},{7,4},{8,15},{9,14},{10,... | collective-permute-start | bytes 12296 | tf_op jit(solution)/shard_map/ppermute | solution.py:234
  37.0 8.8 %collective-permute-start.6 = (f32[20,4,16]{2,1,0:T(4,128)S(1)}, f32[20,4,16]{2,1,0:T(4,128)S(1)}, u32[]{:S(2)}, u32[]{:S(2)}) collective-permute-start(f32[20,4,16]{2,1,0:T(4,128)S(1)} %pad_maximum_fusion.2), channel_id=1, source_target_pairs={{0,1},{1,0},{2,3},{3,2},{4,5},{5,4},{6,7},{7,6},{8,9},{9,8},{10,11... | collective-permute-start | bytes 15368 | tf_op jit(solution)/shard_map/ppermute | solution.py:234
  40.6 7.8 %collective-permute-start.7 = (f32[200,128]{1,0:T(8,128)S(1)}, f32[200,128]{1,0:T(8,128)S(1)}, u32[]{:S(2)}, u32[]{:S(2)}) collective-permute-start(f32[200,128]{1,0:T(8,128)S(1)} %pad_maximum_fusion), channel_id=1, source_target_pairs={{0,2},{1,3},{2,4},{3,5},{4,6},{5,7},{6,0},{7,1},{8,10},{9,11},{10,... | collective-permute-start | bytes 307208 | tf_op jit(solution)/shard_map/ppermute | solution.py:234
  43.3 5.3 %copy-start.11 = (pred[10]{0:T(512)(128)(4,1)S(1)}, pred[10]{0:T(512)(128)(4,1)}, u32[]{:S(2)}) copy-start(pred[10]{0:T(512)(128)(4,1)} %constant.105) | copy-start | bytes 34
  43.3 5.3 %copy-start.12 = (pred[10]{0:T(512)(128)(4,1)S(1)}, pred[10]{0:T(512)(128)(4,1)}, u32[]{:S(2)}) copy-start(pred[10]{0:T(512)(128)(4,1)} %constant.104) | copy-start | bytes 34
  44.0 4.5 %collective-permute-start.10 = (f32[200,128]{1,0:T(8,128)S(1)}, f32[200,128]{1,0:T(8,128)S(1)}, u32[]{:S(2)}, u32[]{:S(2)}) collective-permute-start(f32[200,128]{1,0:T(8,128)S(1)} %pad_maximum_fusion.1), channel_id=1, source_target_pairs={{0,6},{1,7},{2,0},{3,1},{4,2},{5,3},{6,4},{7,5},{8,14},{9,15},{10,... | collective-permute-start | bytes 307208 | tf_op jit(solution)/shard_map/ppermute | solution.py:234
  47.6 1.3 %copy-start.9 = (pred[10]{0:T(512)(128)(4,1)S(1)}, pred[10]{0:T(512)(128)(4,1)}, u32[]{:S(2)}) copy-start(pred[10]{0:T(512)(128)(4,1)} %constant.106) | copy-start | bytes 34
  47.6 1.3 %copy-start.10 = (pred[10]{0:T(512)(128)(4,1)S(1)}, pred[10]{0:T(512)(128)(4,1)}, u32[]{:S(2)}) copy-start(pred[10]{0:T(512)(128)(4,1)} %constant.99) | copy-start | bytes 34
  48.4 0.6 copy-start
  48.5 0.6 copy-start.1
  48.5 5.0 %copy-start.7 = (pred[20]{0:T(512)(128)(4,1)S(1)}, pred[20]{0:T(512)(128)(4,1)}, u32[]{:S(2)}) copy-start(pred[20]{0:T(512)(128)(4,1)} %constant.126) | copy-start | bytes 64
  48.5 5.0 %copy-start.8 = (pred[20]{0:T(512)(128)(4,1)S(1)}, pred[20]{0:T(512)(128)(4,1)}, u32[]{:S(2)}) copy-start(pred[20]{0:T(512)(128)(4,1)} %constant.111) | copy-start | bytes 64
  49.1 5.9 %collective-permute-start.8 = (f32[160,128]{1,0:T(8,128)S(1)}, f32[160,128]{1,0:T(8,128)S(1)}, u32[]{:S(2)}, u32[]{:S(2)}) collective-permute-start(f32[160,128]{1,0:T(8,128)S(1)} %bitcast.101), channel_id=1, source_target_pairs={{0,12},{1,13},{2,14},{3,15},{4,8},{5,9},{6,10},{7,11},{8,20},{9,21... | collective-permute-start | bytes 245768 | tf_op jit(solution)/shard_map/ppermute | solution.py:234
  53.5 10.2 %collective-permute-start.11 = (f32[160,128]{1,0:T(8,128)S(1)}, f32[160,128]{1,0:T(8,128)S(1)}, u32[]{:S(2)}, u32[]{:S(2)}) collective-permute-start(f32[160,128]{1,0:T(8,128)S(1)} %bitcast.100), channel_id=1, source_target_pairs={{0,252},{1,253},{2,254},{3,255},{4,248},{5,249},{6,250},{7,251},{8... | collective-permute-start | bytes 245768 | tf_op jit(solution)/shard_map/ppermute | solution.py:234
  55.0 9.8 %copy-start.5 = (f32[160,128]{1,0:T(8,128)}, f32[160,128]{1,0:T(8,128)S(1)}, u32[]{:S(2)}) copy-start(f32[160,128]{1,0:T(8,128)S(1)} %collective-permute-done.8) | copy-start | bytes 245764
  63.7 1.1 %copy-start.6 = (f32[160,128]{1,0:T(8,128)}, f32[160,128]{1,0:T(8,128)S(1)}, u32[]{:S(2)}) copy-start(f32[160,128]{1,0:T(8,128)S(1)} %collective-permute-done.11) | copy-start | bytes 245764

commit v14 on v10

--- a/solution.py
+++ b/solution.py
@@ -151,26 +151,32 @@
 
 def collide_kernel(f_ref, g_ref, nb_ref, post_ref, xu_ref, xd_ref, yu_ref, yd_ref):
     pops = f_ref.shape[0]
-    nx, ny = f_ref.shape[1], f_ref.shape[2]
+    ny = f_ref.shape[2]
+    nx = pl.num_programs(0)
+    x = pl.program_id(0)
     vel, groups, slot = pop_groups(pops)
-    for x in range(nx):
-        f_planes = [f_ref[n, x] for n in range(pops)]
-        g_planes = [g_ref[n, x] for n in range(pops)]
-        slopes = [nb_ref[2 + a, x] for a in range(3)]
-        f_posts, g_posts = collide_lists(f_planes, g_planes, nb_ref[0, x], nb_ref[1, x], slopes)
-        planes = f_posts + g_posts
-        for n in range(2 * pops):
-            post_ref[slot[n], x] = planes[n]
-        if x == nx - 1:
-            for k, n in enumerate(groups["x_up"]):
-                xu_ref[k] = planes[n]
-        if x == 0:
-            for k, n in enumerate(groups["x_dn"]):
-                xd_ref[k] = planes[n]
-        for k, n in enumerate(groups["y_up"]):
-            yu_ref[k, pl.ds(x, 1), :] = planes[n][ny - 1 : ny, :]
-        for k, n in enumerate(groups["y_dn"]):
-            yd_ref[k, pl.ds(x, 1), :] = planes[n][0:1, :]
+    f_planes = [f_ref[n, 0] for n in range(pops)]
+    g_planes = [g_ref[n, 0] for n in range(pops)]
+    slopes = [nb_ref[2 + a, 0] for a in range(3)]
+    f_posts, g_posts = collide_lists(f_planes, g_planes, nb_ref[0, 0], nb_ref[1, 0], slopes)
+    planes = f_posts + g_posts
+    for n in range(2 * pops):
+        post_ref[slot[n], 0] = planes[n]
+
+    @pl.when(x == nx - 1)
+    def _():
+        for k, n in enumerate(groups["x_up"]):
+            xu_ref[k] = planes[n]
+
+    @pl.when(x == 0)
+    def _():
+        for k, n in enumerate(groups["x_dn"]):
+            xd_ref[k] = planes[n]
+
+    for k, n in enumerate(groups["y_up"]):
+        yu_ref[0, pl.ds(k, 1), :] = planes[n][ny - 1 : ny, :]
+    for k, n in enumerate(groups["y_dn"]):
+        yd_ref[0, pl.ds(k, 1), :] = planes[n][0:1, :]
 
 
 def stream_kernel(post_ref, xlow_ref, xhigh_ref, hym_ref, hyp_ref, col_ref, f_ref, g_ref):
@@ -196,10 +202,10 @@
             else:
                 tile = post_ref[pop_groups(pops)[2][n], src]
                 if cy == 1:
-                    edge = jnp.broadcast_to(hym_ref[pl.ds(y_up.index(n) * nx + src, 1), :], (ny, nz))
+                    edge = jnp.broadcast_to(hym_ref[pl.ds(src * len(y_up) + y_up.index(n), 1), :], (ny, nz))
                     tile = jnp.where(row == 0, edge, pltpu.roll(tile, 1, 0))
                 elif cy == -1:
-                    edge = jnp.broadcast_to(hyp_ref[pl.ds(y_dn.index(n) * nx + src, 1), :], (ny, nz))
+                    edge = jnp.broadcast_to(hyp_ref[pl.ds(src * len(y_dn) + y_dn.index(n), 1), :], (ny, nz))
                     tile = jnp.where(row == ny - 1, edge, pltpu.roll(tile, ny - 1, 0))
             if 0 <= src < nx and cz == 1:
                 tile = jnp.where(lane == 0, col_ref[z_any.index(n), x], pltpu.roll(tile, 1, 1))
@@ -276,14 +282,29 @@
     pops = f_pop.shape[0]
     _, groups, slot = pop_groups(pops)
     n_xu, n_xd, n_yu, n_yd = (len(groups[k]) for k in ("x_up", "x_dn", "y_up", "y_dn"))
+    def plane_block(count):
+        return pl.BlockSpec((count, 1, ny, nz), lambda x: (0, x, 0, 0))
+
+    def whole(shape):
+        return pl.BlockSpec(shape, lambda x: (0,) * len(shape))
+
     post, face_xu, face_xd, face_yu, face_yd = pl.pallas_call(
         collide_kernel,
+        grid=(nx,),
+        in_specs=[plane_block(pops), plane_block(pops), plane_block(nb.shape[0])],
+        out_specs=(
+            plane_block(2 * pops),
+            whole((n_xu, ny, nz)),
+            whole((n_xd, ny, nz)),
+            pl.BlockSpec((1, n_yu, nz), lambda x: (x, 0, 0)),
+            pl.BlockSpec((1, n_yd, nz), lambda x: (x, 0, 0)),
+        ),
         out_shape=(
             jax.ShapeDtypeStruct((2 * pops, nx, ny, nz), jnp.float32),
             jax.ShapeDtypeStruct((n_xu, ny, nz), jnp.float32),
             jax.ShapeDtypeStruct((n_xd, ny, nz), jnp.float32),
-            jax.ShapeDtypeStruct((n_yu, nx, nz), jnp.float32),
-            jax.ShapeDtypeStruct((n_yd, nx, nz), jnp.float32),
+            jax.ShapeDtypeStruct((nx, n_yu, nz), jnp.float32),
+            jax.ShapeDtypeStruct((nx, n_yd, nz), jnp.float32),
         ),
         interpret=INTERPRET,
     )(f_pop, g_pop, nb)

time: 65.3 us -> 65.5 us (level)
  waiting for transfers between devices: 13.9 us -> 12.3 us
  local copies, waits for them, and re-layouts: 8.78 us -> 10.3 us
  Pallas kernels: 5.87 us -> 6.79 us
  other arithmetic: 3.13 us -> 2.24 us
    ppermute x10, waiting for transfers between devices: 13.9 us -> 12.3 us  [exchange(): got = lax.ppermute(joined, AXES, pairs)]
    reshape x0 -> x2, local copies, waits for them, and re-layouts: none -> 1.52 us  [packed(): face.reshape(-1, nz)]
    pallas_call x1, Pallas kernels: 3.04 us -> 3.96 us  [local(): pl.pallas_call(collide_kernel, grid=(nx,), in_specs=[plane_block(pops), p...]
    concatenate x1, other arithmetic: 0.91 us -> 0.01 us  [local(): jnp.concatenate([send_yd, send_dn])]
  transfers between devices with their start and end apart: 10 -> 10, of which waited for: 7 -> 7; matrix products, arithmetic and copies ran while one was open for 4% -> 6% of each run, Pallas kernels for 0% -> 0%
where the time goes in v14:
time: 65.5 us; the launch traced here: 65 us
  starting transfers between devices  31.5 us (48%)
  waiting for transfers between devices  12.3 us (19%)
  local copies, waits for them, and re-layouts  10.3 us (16%)
  Pallas kernels  6.79 us (10%)
  other arithmetic  2.24 us (3%)
  between operations  1.82 us (3%)
    ppermute x10, starting transfers between devices, exchange(): got = lax.ppermute(joined, AXES, pairs)  31.5 us
    ppermute x10, waiting for transfers between devices, exchange(): got = lax.ppermute(joined, AXES, pairs)  12.3 us
    pallas_call x1, Pallas kernels, local(): pl.pallas_call(collide_kernel, grid=(nx,), in_specs=[plane_block(pops), p...  3.96 us
    pallas_call x1, Pallas kernels, local(): pl.pallas_call(stream_kernel, out_shape=(jax.ShapeDtypeStruct((pops, nx,...  2.83 us
    reshape x2, local copies, waits for them, and re-layouts, packed(): face.reshape(-1, nz)  1.52 us
    slice x1, local copies, waits for them, and re-layouts, local(): post[:len(z_up), :, :, -1]  1.52 us
  transfers between devices with their start and end apart: 10, of which 7 were waited for; matrix products, arithmetic and copies ran while one was open for 6% of the time, Pallas kernels for 0%

profile of v14, /device:TPU:2, one launch (start us, length us, event | category | flops | bytes accessed | tf_op | source)
XLA Modules:
  0.0 65.0 jit_solution(6296259724685016252)
XLA Ops:
  0.6 0.0 copy-start.18
  0.6 0.0 copy-start.17
  0.7 0.0 copy-start.16
  0.7 1.1 %reduce_sum.9 = f32[4,16,128]{2,1,0:T(8,128)S(1)} reduce(f32[19,4,16,128]{3,2,1,0:T(8,128)} %g_ref.1, f32[]{:T(128)} %constant.24.clone.1), dimensions={0}, to_apply=%region_0.0 | reduce | flops 147456 | bytes 655364 | tf_op jit(solution)/shard_map/reduce_sum | solution.py:256
  1.8 0.2 slice_reduce_fusion.3
  2.0 7.3 %collective-permute-start.4 = (f32[2,4,16]{2,1,0:T(4,128)S(1)}, f32[2,4,16]{2,1,0:T(4,128)S(1)}, u32[]{:S(2)}, u32[]{:S(2)}) collective-permute-start(f32[2,4,16]{2,1,0:T(4,128)S(1)} %pad_maximum_fusion.13), channel_id=1, source_target_pairs={{0,1},{1,0},{2,3},{3,2},{4,5},{5,4},{6,7},{7,6},{8,9},{9,8},{10,11... | collective-permute-start | bytes 1544 | tf_op jit(solution)/shard_map/ppermute | solution.py:240
  9.3 0.6 collective-permute-start.2
  9.9 1.5 %collective-permute-start = (f32[20,128]{1,0:T(8,128)S(1)}, f32[20,128]{1,0:T(8,128)S(1)}, u32[]{:S(2)}, u32[]{:S(2)}) collective-permute-start(f32[20,128]{1,0:T(8,128)S(1)} %pad_maximum_fusion.11), channel_id=1, source_target_pairs={{0,2},{1,3},{2,4},{3,5},{4,6},{5,7},{6,0},{7,1},{8,10},{9,11},{10,... | collective-permute-start | bytes 30728 | tf_op jit(solution)/shard_map/ppermute | solution.py:240
  11.4 0.1 slice_bitcast_fusion.1
  12.2 0.1 copy.42
  12.3 0.1 copy.43
  12.4 1.9 %collective-permute-done = f32[20,128]{1,0:T(8,128)S(1)} collective-permute-done((f32[20,128]{1,0:T(8,128)S(1)}, f32[20,128]{1,0:T(8,128)S(1)}, u32[]{:S(2)}, u32[]{:S(2)}) %collective-permute-start) | collective-permute-done | bytes 10272 | tf_op jit(solution)/shard_map/ppermute | solution.py:240
  14.3 0.1 collective-permute-start.1
  14.5 8.0 %collective-permute-start.3 = (f32[32,128]{1,0:T(8,128)S(1)}, f32[32,128]{1,0:T(8,128)S(1)}, u32[]{:S(2)}, u32[]{:S(2)}) collective-permute-start(f32[32,128]{1,0:T(8,128)S(1)} %pad_maximum_fusion.10), channel_id=1, source_target_pairs={{0,252},{1,253},{2,254},{3,255},{4,248},{5,249},{6,250},{7,251},{8... | collective-permute-start | bytes 49160 | tf_op jit(solution)/shard_map/ppermute | solution.py:240
  22.5 1.3 %collective-permute-done.1 = f32[32,128]{1,0:T(8,128)S(1)} collective-permute-done((f32[32,128]{1,0:T(8,128)S(1)}, f32[32,128]{1,0:T(8,128)S(1)}, u32[]{:S(2)}, u32[]{:S(2)}) %collective-permute-start.1) | collective-permute-done | bytes 16416 | tf_op jit(solution)/shard_map/ppermute | solution.py:240
  23.8 0.1 collective-permute-done.3
  23.9 0.1 fusion.5
  24.0 0.0 copy-start.15
  24.1 0.1 multiply_dynamic-update-slice_fusion.nb_ref
  24.2 0.7 %copy-done.4 = f32[5,4,16,128]{3,2,1,0:T(8,128)} copy-done((f32[5,4,16,128]{3,2,1,0:T(8,128)}, f32[5,4,16,128]{3,2,1,0:T(8,128)S(1)}, u32[]{:S(2)}) %copy-start.4) | copy-done | bytes 163864
  24.8 4.0 %shard_map.149 = (f32[38,4,16,128]{3,2,1,0:T(8,128)}, f32[10,16,128]{2,1,0:T(8,128)}, f32[10,16,128]{2,1,0:T(8,128)}, f32[4,10,128]{2,1,0:T(8,128)}, f32[4,10,128]{2,1,0:T(8,128)}) custom-call(f32[19,4,16,128]{3,2,1,0:T(8,128)} %f_ref.1, f32[19,4,16,128]{3,2,1,0:T(8,128)} %g_ref.1, f32[5,4,16,128]{3,2,1,0:T(8,128)} %copy-done.4), custom_call_target="tpu_custom_call" | custom-call | tf_op jit(solution)/shard_map/pallas_call | solution.py:291
  28.8 0.0 copy-start.13
  28.8 0.0 copy-start.14
  28.8 1.5 %slice_reduce_fusion.1 = (f32[10,4,16]{2,1,0:T(4,128)S(1)}, f32[10,4,16]{2,1,0:T(4,128)S(1)}) fusion(f32[38,4,16,128]{3,2,1,0:T(8,128)} %get-tuple-element.7.post_ref), kind=kLoop, calls=%fused_computation.6 | loop fusion | bytes 10240 | tf_op jit(solution)/shard_map/slice | solution.py:330
  30.4 2.8 %collective-permute-start.5 = (f32[20,4,16]{2,1,0:T(4,128)S(1)}, f32[20,4,16]{2,1,0:T(4,128)S(1)}, u32[]{:S(2)}, u32[]{:S(2)}) collective-permute-start(f32[20,4,16]{2,1,0:T(4,128)S(1)} %pad_maximum_fusion.2), channel_id=1, source_target_pairs={{0,1},{1,0},{2,3},{3,2},{4,5},{5,4},{6,7},{7,6},{8,9},{9,8},{10,11... | collective-permute-start | bytes 15368 | tf_op jit(solution)/shard_map/ppermute | solution.py:240
  33.2 0.8 %reshape.440 = f32[40,128]{1,0:T(8,128)S(1)} reshape(f32[4,10,128]{2,1,0:T(8,128)} %get-tuple-element.8) | data formatting | bytes 40960 | tf_op jit(solution)/shard_map/reshape | solution.py:342
  34.0 0.8 %reshape.445 = f32[40,128]{1,0:T(8,128)S(1)} reshape(f32[4,10,128]{2,1,0:T(8,128)} %get-tuple-element.10) | data formatting | bytes 40960 | tf_op jit(solution)/shard_map/reshape | solution.py:342
  34.8 4.0 %collective-permute-done.5 = f32[20,4,16]{2,1,0:T(4,128)S(1)} collective-permute-done((f32[20,4,16]{2,1,0:T(4,128)S(1)}, f32[20,4,16]{2,1,0:T(4,128)S(1)}, u32[]{:S(2)}, u32[]{:S(2)}) %collective-permute-start.5) | collective-permute-done | bytes 5152 | tf_op jit(solution)/shard_map/ppermute | solution.py:240
  38.8 0.6 gather_fusion.3
  39.4 0.1 fusion.9
  39.5 0.1 slice_reduce_fusion.6
  39.6 0.2 slice_reduce_fusion.4
  39.8 0.0 copy-start.11
  39.9 2.9 %collective-permute-start.8 = (f32[208,128]{1,0:T(8,128)S(1)}, f32[208,128]{1,0:T(8,128)S(1)}, u32[]{:S(2)}, u32[]{:S(2)}) collective-permute-start(f32[208,128]{1,0:T(8,128)S(1)} %pad_maximum_fusion.1), channel_id=1, source_target_pairs={{0,6},{1,7},{2,0},{3,1},{4,2},{5,3},{6,4},{7,5},{8,14},{9,15},{10,... | collective-permute-start | bytes 319496 | tf_op jit(solution)/shard_map/ppermute | solution.py:240
  42.8 0.2 slice_reduce_fusion.8
  43.0 0.2 slice_reduce_fusion.10
  43.3 0.1 collective-permute-start.6
  43.4 1.7 %collective-permute-done.8.hyp_ref = f32[208,128]{1,0:T(8,128)S(1)} collective-permute-done((f32[208,128]{1,0:T(8,128)S(1)}, f32[208,128]{1,0:T(8,128)S(1)}, u32[]{:S(2)}, u32[]{:S(2)}) %collective-permute-start.8) | collective-permute-done | bytes 106528 | tf_op jit(solution)/shard_map/ppermute | solution.py:240
  45.1 0.1 pad_maximum_fusion.14
  45.2 0.1 constant_dynamic-slice_fusion
  45.3 0.6 gather_fusion.4
  45.8 0.2 copy.51
  46.1 0.6 gather_fusion.1
  46.6 0.1 copy.46
  46.8 1.3 %collective-permute-done.6.hym_ref = f32[208,128]{1,0:T(8,128)S(1)} collective-permute-done((f32[208,128]{1,0:T(8,128)S(1)}, f32[208,128]{1,0:T(8,128)S(1)}, u32[]{:S(2)}, u32[]{:S(2)}) %collective-permute-start.6) | collective-permute-done | bytes 106528 | tf_op jit(solution)/shard_map/ppermute | solution.py:240
  48.1 0.1 maximum_maximum_fusion
  48.2 0.1 constant_dynamic-slice_fusion.1
  48.3 0.6 gather_fusion
  48.8 0.6 gather_fusion.2
  49.4 0.2 copy.49
  49.6 0.1 copy.44
  49.8 0.2 maximum_select_fusion.4
  50.1 0.1 fusion.2
  50.3 0.1 fusion.6
  50.4 0.1 fusion.7
  50.4 0.1 copy-done.9
  50.6 0.0 copy-done.10
  50.6 0.2 maximum_select_fusion.2
  50.8 0.1 collective-permute-start.7
  50.9 8.0 %collective-permute-start.9 = (f32[160,128]{1,0:T(8,128)S(1)}, f32[160,128]{1,0:T(8,128)S(1)}, u32[]{:S(2)}, u32[]{:S(2)}) collective-permute-start(f32[160,128]{1,0:T(8,128)S(1)} %bitcast.106), channel_id=1, source_target_pairs={{0,252},{1,253},{2,254},{3,255},{4,248},{5,249},{6,250},{7,251},{8... | collective-permute-start | bytes 245768 | tf_op jit(solution)/shard_map/ppermute | solution.py:240
  58.9 0.1 select_select_fusion
  59.0 2.0 %collective-permute-done.7 = f32[160,128]{1,0:T(8,128)S(1)} collective-permute-done((f32[160,128]{1,0:T(8,128)S(1)}, f32[160,128]{1,0:T(8,128)S(1)}, u32[]{:S(2)}, u32[]{:S(2)}) %collective-permute-start.7) | collective-permute-done | bytes 81952 | tf_op jit(solution)/shard_map/ppermute | solution.py:240
  61.0 1.1 %broadcast_in_dim.125.col_ref = f32[20,4,16,128]{3,2,1,0:T(8,128)} broadcast(f32[20,4,16]{2,1,0:T(4,128)S(1)} %select_select_fusion), dimensions={0,1,2} | broadcast | bytes 660480 | tf_op jit(solution)/shard_map/broadcast_in_dim | solution.py:423
  62.2 2.8 %shard_map.150 = (f32[19,4,16,128]{3,2,1,0:T(8,128)}, f32[19,4,16,128]{3,2,1,0:T(8,128)}) custom-call(f32[38,4,16,128]{3,2,1,0:T(8,128)} %get-tuple-element.7.post_ref, f32[10,16,128]{2,1,0:T(8,128)} %bitcast.104, f32[10,16,128]{2,1,0:T(8,128)} %bitcast.105, f32[208,128]{1,0:T(8,128)} %copy-done.1, f32[208,128]{1,0:T(8,128)} %copy-done, ...), custom_call_target="tpu_custom_call" | custom-call | tf_op jit(solution)/shard_map/pallas_call | solution.py:425
  (76 shorter events, 0.5 us)
Async XLA Ops:
  0.6 11.5 %copy-start.18 = (s32[10]{0:T(128)S(1)}, s32[10]{0:T(128)}, u32[]{:S(2)}) copy-start(s32[10]{0:T(128)} %constant.123) | copy-start | bytes 124
  0.6 11.5 %copy-start.17 = (s32[20]{0:T(128)S(1)}, s32[20]{0:T(128)}, u32[]{:S(2)}) copy-start(s32[20]{0:T(128)} %constant.125) | copy-start | bytes 244
  0.7 11.5 %copy-start.16 = (s32[20]{0:T(128)S(1)}, s32[20]{0:T(128)}, u32[]{:S(2)}) copy-start(s32[20]{0:T(128)} %constant.126) | copy-start | bytes 244
  2.0 10.2 %collective-permute-start.4 = (f32[2,4,16]{2,1,0:T(4,128)S(1)}, f32[2,4,16]{2,1,0:T(4,128)S(1)}, u32[]{:S(2)}, u32[]{:S(2)}) collective-permute-start(f32[2,4,16]{2,1,0:T(4,128)S(1)} %pad_maximum_fusion.13), channel_id=1, source_target_pairs={{0,1},{1,0},{2,3},{3,2},{4,5},{5,4},{6,7},{7,6},{8,9},{9,8},{10,11... | collective-permute-start | bytes 1544 | tf_op jit(solution)/shard_map/ppermute | solution.py:240
  9.3 5.2 %collective-permute-start.2 = (f32[20,128]{1,0:T(8,128)S(1)}, f32[20,128]{1,0:T(8,128)S(1)}, u32[]{:S(2)}, u32[]{:S(2)}) collective-permute-start(f32[20,128]{1,0:T(8,128)S(1)} %pad_maximum_fusion.12), channel_id=1, source_target_pairs={{0,6},{1,7},{2,0},{3,1},{4,2},{5,3},{6,4},{7,5},{8,14},{9,15},{10,... | collective-permute-start | bytes 30728 | tf_op jit(solution)/shard_map/ppermute | solution.py:240
  9.9 4.4 %collective-permute-start = (f32[20,128]{1,0:T(8,128)S(1)}, f32[20,128]{1,0:T(8,128)S(1)}, u32[]{:S(2)}, u32[]{:S(2)}) collective-permute-start(f32[20,128]{1,0:T(8,128)S(1)} %pad_maximum_fusion.11), channel_id=1, source_target_pairs={{0,2},{1,3},{2,4},{3,5},{4,6},{5,7},{6,0},{7,1},{8,10},{9,11},{10,... | collective-permute-start | bytes 30728 | tf_op jit(solution)/shard_map/ppermute | solution.py:240
  14.3 9.5 %collective-permute-start.1 = (f32[32,128]{1,0:T(8,128)S(1)}, f32[32,128]{1,0:T(8,128)S(1)}, u32[]{:S(2)}, u32[]{:S(2)}) collective-permute-start(f32[32,128]{1,0:T(8,128)S(1)} %pad_maximum_fusion.9), channel_id=1, source_target_pairs={{0,12},{1,13},{2,14},{3,15},{4,8},{5,9},{6,10},{7,11},{8,20},{9,21... | collective-permute-start | bytes 49160 | tf_op jit(solution)/shard_map/ppermute | solution.py:240
  14.5 9.4 %collective-permute-start.3 = (f32[32,128]{1,0:T(8,128)S(1)}, f32[32,128]{1,0:T(8,128)S(1)}, u32[]{:S(2)}, u32[]{:S(2)}) collective-permute-start(f32[32,128]{1,0:T(8,128)S(1)} %pad_maximum_fusion.10), channel_id=1, source_target_pairs={{0,252},{1,253},{2,254},{3,255},{4,248},{5,249},{6,250},{7,251},{8... | collective-permute-start | bytes 49160 | tf_op jit(solution)/shard_map/ppermute | solution.py:240
  24.0 9.2 %copy-start.15 = (s32[20]{0:T(128)S(1)}, s32[20]{0:T(128)}, u32[]{:S(2)}) copy-start(s32[20]{0:T(128)} %constant.127) | copy-start | bytes 244
  24.2 0.7 %copy-start.4 = (f32[5,4,16,128]{3,2,1,0:T(8,128)}, f32[5,4,16,128]{3,2,1,0:T(8,128)S(1)}, u32[]{:S(2)}) copy-start(f32[5,4,16,128]{3,2,1,0:T(8,128)S(1)} %multiply_dynamic-update-slice_fusion.nb_ref) | copy-start | bytes 491524
  28.8 11.0 %copy-start.3 = (f32[10,16,128]{2,1,0:T(8,128)S(1)}, f32[10,16,128]{2,1,0:T(8,128)}, u32[]{:S(2)}) copy-start(f32[10,16,128]{2,1,0:T(8,128)} %get-tuple-element.11) | copy-start | bytes 245764
  28.8 14.5 %copy-start.2 = (f32[10,16,128]{2,1,0:T(8,128)S(1)}, f32[10,16,128]{2,1,0:T(8,128)}, u32[]{:S(2)}) copy-start(f32[10,16,128]{2,1,0:T(8,128)} %get-tuple-element.9) | copy-start | bytes 245764
  28.8 21.0 %copy-start.13 = (pred[20]{0:T(512)(128)(4,1)S(1)}, pred[20]{0:T(512)(128)(4,1)}, u32[]{:S(2)}) copy-start(pred[20]{0:T(512)(128)(4,1)} %constant.117) | copy-start | bytes 64
  28.8 20.9 %copy-start.14 = (pred[20]{0:T(512)(128)(4,1)S(1)}, pred[20]{0:T(512)(128)(4,1)}, u32[]{:S(2)}) copy-start(pred[20]{0:T(512)(128)(4,1)} %constant.108) | copy-start | bytes 64
  30.4 8.4 %collective-permute-start.5 = (f32[20,4,16]{2,1,0:T(4,128)S(1)}, f32[20,4,16]{2,1,0:T(4,128)S(1)}, u32[]{:S(2)}, u32[]{:S(2)}) collective-permute-start(f32[20,4,16]{2,1,0:T(4,128)S(1)} %pad_maximum_fusion.2), channel_id=1, source_target_pairs={{0,1},{1,0},{2,3},{3,2},{4,5},{5,4},{6,7},{7,6},{8,9},{9,8},{10,11... | collective-permute-start | bytes 15368 | tf_op jit(solution)/shard_map/ppermute | solution.py:240
  39.8 10.3 %copy-start.11 = (pred[10]{0:T(512)(128)(4,1)S(1)}, pred[10]{0:T(512)(128)(4,1)}, u32[]{:S(2)}) copy-start(pred[10]{0:T(512)(128)(4,1)} %constant.101) | copy-start | bytes 34
  39.8 10.3 %copy-start.12 = (pred[10]{0:T(512)(128)(4,1)S(1)}, pred[10]{0:T(512)(128)(4,1)}, u32[]{:S(2)}) copy-start(pred[10]{0:T(512)(128)(4,1)} %constant.100) | copy-start | bytes 34
  39.9 5.2 %collective-permute-start.8 = (f32[208,128]{1,0:T(8,128)S(1)}, f32[208,128]{1,0:T(8,128)S(1)}, u32[]{:S(2)}, u32[]{:S(2)}) collective-permute-start(f32[208,128]{1,0:T(8,128)S(1)} %pad_maximum_fusion.1), channel_id=1, source_target_pairs={{0,6},{1,7},{2,0},{3,1},{4,2},{5,3},{6,4},{7,5},{8,14},{9,15},{10,... | collective-permute-start | bytes 319496 | tf_op jit(solution)/shard_map/ppermute | solution.py:240
  43.3 4.8 %collective-permute-start.6 = (f32[208,128]{1,0:T(8,128)S(1)}, f32[208,128]{1,0:T(8,128)S(1)}, u32[]{:S(2)}, u32[]{:S(2)}) collective-permute-start(f32[208,128]{1,0:T(8,128)S(1)} %pad_maximum_fusion), channel_id=1, source_target_pairs={{0,2},{1,3},{2,4},{3,5},{4,6},{5,7},{6,0},{7,1},{8,10},{9,11},{10,... | collective-permute-start | bytes 319496 | tf_op jit(solution)/shard_map/ppermute | solution.py:240
  45.1 5.2 %copy-start = (f32[208,128]{1,0:T(8,128)}, f32[208,128]{1,0:T(8,128)S(1)}, u32[]{:S(2)}) copy-start(f32[208,128]{1,0:T(8,128)S(1)} %collective-permute-done.8.hyp_ref) | copy-start | bytes 319492
  48.1 2.3 %copy-start.1 = (f32[208,128]{1,0:T(8,128)}, f32[208,128]{1,0:T(8,128)S(1)}, u32[]{:S(2)}) copy-start(f32[208,128]{1,0:T(8,128)S(1)} %collective-permute-done.6.hym_ref) | copy-start | bytes 319492
  49.9 0.7 %copy-start.9 = (pred[10]{0:T(512)(128)(4,1)S(1)}, pred[10]{0:T(512)(128)(4,1)}, u32[]{:S(2)}) copy-start(pred[10]{0:T(512)(128)(4,1)} %constant.102) | copy-start | bytes 34
  49.9 0.7 %copy-start.10 = (pred[10]{0:T(512)(128)(4,1)S(1)}, pred[10]{0:T(512)(128)(4,1)}, u32[]{:S(2)}) copy-start(pred[10]{0:T(512)(128)(4,1)} %constant.95) | copy-start | bytes 34
  50.1 8.9 %copy-start.7 = (pred[20]{0:T(512)(128)(4,1)S(1)}, pred[20]{0:T(512)(128)(4,1)}, u32[]{:S(2)}) copy-start(pred[20]{0:T(512)(128)(4,1)} %constant.122) | copy-start | bytes 64
  50.1 8.9 %copy-start.8 = (pred[20]{0:T(512)(128)(4,1)S(1)}, pred[20]{0:T(512)(128)(4,1)}, u32[]{:S(2)}) copy-start(pred[20]{0:T(512)(128)(4,1)} %constant.107) | copy-start | bytes 64
  50.8 10.3 %collective-permute-start.7 = (f32[160,128]{1,0:T(8,128)S(1)}, f32[160,128]{1,0:T(8,128)S(1)}, u32[]{:S(2)}, u32[]{:S(2)}) collective-permute-start(f32[160,128]{1,0:T(8,128)S(1)} %bitcast.107), channel_id=1, source_target_pairs={{0,12},{1,13},{2,14},{3,15},{4,8},{5,9},{6,10},{7,11},{8,20},{9,21... | collective-permute-start | bytes 245768 | tf_op jit(solution)/shard_map/ppermute | solution.py:240
  50.9 10.2 %collective-permute-start.9 = (f32[160,128]{1,0:T(8,128)S(1)}, f32[160,128]{1,0:T(8,128)S(1)}, u32[]{:S(2)}, u32[]{:S(2)}) collective-permute-start(f32[160,128]{1,0:T(8,128)S(1)} %bitcast.106), channel_id=1, source_target_pairs={{0,252},{1,253},{2,254},{3,255},{4,248},{5,249},{6,250},{7,251},{8... | collective-permute-start | bytes 245768 | tf_op jit(solution)/shard_map/ppermute | solution.py:240
  61.0 1.1 %copy-start.5 = (f32[160,128]{1,0:T(8,128)}, f32[160,128]{1,0:T(8,128)S(1)}, u32[]{:S(2)}) copy-start(f32[160,128]{1,0:T(8,128)S(1)} %collective-permute-done.7) | copy-start | bytes 245764
  61.0 1.1 %copy-start.6 = (f32[160,128]{1,0:T(8,128)}, f32[160,128]{1,0:T(8,128)S(1)}, u32[]{:S(2)}) copy-start(f32[160,128]{1,0:T(8,128)S(1)} %collective-permute-done.9) | copy-start | bytes 245764

commit v15 on v10

--- a/solution.py
+++ b/solution.py
@@ -250,16 +250,16 @@
     phi = jnp.sum(g_pop, axis=0)
     up1, dn1, pzm, pzp = exchange(
         [
-            (jnp.concatenate([phi[:, -1], phi[-1]]), (0, 1, 0)),
-            (jnp.concatenate([phi[:, 0], phi[0]]), (0, -1, 0)),
+            (jnp.concatenate([phi[:, -1], phi[0]]), (0, 1, 0)),
+            (jnp.concatenate([phi[:, 0], phi[-1]]), (0, -1, 0)),
             (phi[:, :, -1][None], (0, 0, 1)),
             (phi[:, :, 0][None], (0, 0, -1)),
         ]
     )
     low_pair, high_pair = exchange(
         [
-            (jnp.concatenate([up1[nx:], phi[-1]]), (1, q, 0)),
-            (jnp.concatenate([phi[0], dn1[nx:]]), (-1, -q, 0)),
+            (jnp.concatenate([phi[-1], dn1[nx:]]), (1, q + 1, 0)),
+            (jnp.concatenate([up1[nx:], phi[0]]), (-1, -q - 1, 0)),
         ]
     )
     low = lax.dynamic_slice_in_dim(low_pair, ny - rem, ny, 0)[None]
@@ -327,8 +327,8 @@
     n_yu, n_yd = send_yu.shape[0], send_yd.shape[0]
     up2, dn2 = exchange(
         [
-            (jnp.concatenate([send_yu, send_up]), (0, 1, 0)),
-            (jnp.concatenate([send_yd, send_dn]), (0, -1, 0)),
+            (jnp.concatenate([send_yu, send_dn]), (0, 1, 0)),
+            (jnp.concatenate([send_yd, send_up]), (0, -1, 0)),
         ]
     )
     hy_m, hy_p = up2[:n_yu], dn2[:n_yd]
@@ -368,8 +368,8 @@
 
     low2, high2 = exchange(
         [
-            (window(up2[n_yu:], send_up, x_up, xz_up, ny - rem), (1, q, 0)),
-            (window(send_dn, dn2[n_yd:], x_dn, xz_dn, rem), (-1, -q, 0)),
+            (window(send_up, dn2[n_yd:], x_up, xz_up, ny - rem), (1, q + 1, 0)),
+            (window(up2[n_yu:], send_dn, x_dn, xz_dn, rem), (-1, -q - 1, 0)),
         ]
     )
     hy_m, cy_m = unpack_y(hy_m, len(y_up))

time: 65.3 us -> 64.3 us (0.985)
  the two profiles are of different devices: /device:TPU:2 before, /device:TPU:121 now
where the time goes in v15:
time: 64.3 us; the launch traced here: 64.1 us
  waiting for transfers between devices  24.6 us (38%)
  starting transfers between devices  19.8 us (31%)
  local copies, waits for them, and re-layouts  8.79 us (14%)
  Pallas kernels  5.87 us (9%)
  other arithmetic  3.13 us (5%)
  between operations  1.86 us (3%)
    ppermute x10, waiting for transfers between devices, exchange(): got = lax.ppermute(joined, AXES, pairs)  24.6 us
    ppermute x10, starting transfers between devices, exchange(): got = lax.ppermute(joined, AXES, pairs)  19.8 us
    pallas_call x1, Pallas kernels, local(): pl.pallas_call(collide_kernel, out_shape=(jax.ShapeDtypeStruct((2 * pops,...  3.04 us
    pallas_call x1, Pallas kernels, local(): pl.pallas_call(stream_kernel, out_shape=(jax.ShapeDtypeStruct((pops, nx,...  2.83 us
    slice x1, local copies, waits for them, and re-layouts, local(): post[:len(z_up), :, :, -1]  1.51 us
  transfers between devices with their start and end apart: 10, of which 6 were waited for; matrix products, arithmetic and copies ran while one was open for 4% of the time, Pallas kernels for 0%

profile of v15, /device:TPU:121, one launch (start us, length us, event | category | flops | bytes accessed | tf_op | source)
XLA Modules:
  0.0 64.1 jit_solution(7508095263841524918)
XLA Ops:
  0.6 0.0 copy-start.19
  0.6 0.0 copy-start.18
  0.7 1.1 %reduce_sum.9 = f32[4,16,128]{2,1,0:T(8,128)S(1)} reduce(f32[19,4,16,128]{3,2,1,0:T(8,128)} %g_ref.1, f32[]{:T(128)} %constant.24.clone.1), dimensions={0}, to_apply=%region_0.0 | reduce | flops 147456 | bytes 655364 | tf_op jit(solution)/shard_map/reduce_sum | solution.py:250
  1.8 0.2 slice_reduce_fusion.3
  2.0 4.3 %collective-permute-start.4 = (f32[2,4,16]{2,1,0:T(4,128)S(1)}, f32[2,4,16]{2,1,0:T(4,128)S(1)}, u32[]{:S(2)}, u32[]{:S(2)}) collective-permute-start(f32[2,4,16]{2,1,0:T(4,128)S(1)} %pad_maximum_fusion.13), channel_id=1, source_target_pairs={{0,1},{1,0},{2,3},{3,2},{4,5},{5,4},{6,7},{7,6},{8,9},{9,8},{10,11... | collective-permute-start | bytes 1544 | tf_op jit(solution)/shard_map/ppermute | solution.py:234
  6.3 1.3 %collective-permute-start.2 = (f32[20,128]{1,0:T(8,128)S(1)}, f32[20,128]{1,0:T(8,128)S(1)}, u32[]{:S(2)}, u32[]{:S(2)}) collective-permute-start(f32[20,128]{1,0:T(8,128)S(1)} %pad_maximum_fusion.12), channel_id=1, source_target_pairs={{0,2},{1,3},{2,4},{3,5},{4,6},{5,7},{6,0},{7,1},{8,10},{9,11},{10,... | collective-permute-start | bytes 30728 | tf_op jit(solution)/shard_map/ppermute | solution.py:234
  7.6 1.5 %collective-permute-start = (f32[20,128]{1,0:T(8,128)S(1)}, f32[20,128]{1,0:T(8,128)S(1)}, u32[]{:S(2)}, u32[]{:S(2)}) collective-permute-start(f32[20,128]{1,0:T(8,128)S(1)} %pad_maximum_fusion.11), channel_id=1, source_target_pairs={{0,6},{1,7},{2,0},{3,1},{4,2},{5,3},{6,4},{7,5},{8,14},{9,15},{10,... | collective-permute-start | bytes 30728 | tf_op jit(solution)/shard_map/ppermute | solution.py:234
  9.1 0.1 slice_bitcast_fusion.1
  9.9 0.1 copy.42
  10.0 0.1 copy.43
  10.1 0.0 collective-permute-done
  10.1 5.9 %collective-permute-start.1 = (f32[32,128]{1,0:T(8,128)S(1)}, f32[32,128]{1,0:T(8,128)S(1)}, u32[]{:S(2)}, u32[]{:S(2)}) collective-permute-start(f32[32,128]{1,0:T(8,128)S(1)} %pad_maximum_fusion.9), channel_id=1, source_target_pairs={{0,14},{1,15},{2,8},{3,9},{4,10},{5,11},{6,12},{7,13},{8,22},{9,23... | collective-permute-start | bytes 49160 | tf_op jit(solution)/shard_map/ppermute | solution.py:234
  16.1 0.1 collective-permute-start.3
  16.2 0.7 %collective-permute-done.1 = f32[32,128]{1,0:T(8,128)S(1)} collective-permute-done((f32[32,128]{1,0:T(8,128)S(1)}, f32[32,128]{1,0:T(8,128)S(1)}, u32[]{:S(2)}, u32[]{:S(2)}) %collective-permute-start.1) | collective-permute-done | bytes 16416 | tf_op jit(solution)/shard_map/ppermute | solution.py:234
  17.0 8.4 %collective-permute-done.3 = f32[32,128]{1,0:T(8,128)S(1)} collective-permute-done((f32[32,128]{1,0:T(8,128)S(1)}, f32[32,128]{1,0:T(8,128)S(1)}, u32[]{:S(2)}, u32[]{:S(2)}) %collective-permute-start.3) | collective-permute-done | bytes 16416 | tf_op jit(solution)/shard_map/ppermute | solution.py:234
  25.4 0.1 fusion.5
  25.5 0.0 copy-start.16
  25.5 0.1 multiply_dynamic-update-slice_fusion.nb_ref
  25.6 0.7 %copy-done.4 = f32[5,4,16,128]{3,2,1,0:T(8,128)} copy-done((f32[5,4,16,128]{3,2,1,0:T(8,128)}, f32[5,4,16,128]{3,2,1,0:T(8,128)S(1)}, u32[]{:S(2)}) %copy-start.4) | copy-done | bytes 163864
  26.3 3.0 %shard_map.149 = (f32[38,4,16,128]{3,2,1,0:T(8,128)}, f32[10,16,128]{2,1,0:T(8,128)}, f32[10,16,128]{2,1,0:T(8,128)}, f32[10,4,128]{2,1,0:T(4,128)}, f32[10,4,128]{2,1,0:T(4,128)}) custom-call(f32[19,4,16,128]{3,2,1,0:T(8,128)} %f_ref.1, f32[19,4,16,128]{3,2,1,0:T(8,128)} %g_ref.1, f32[5,4,16,128]{3,2,1,0:T(8,128)} %copy-done.4), custom_call_target="tpu_custom_call" | custom-call | tf_op jit(solution)/shard_map/pallas_call | solution.py:279
  29.3 0.0 copy-start.15
  29.3 1.5 %slice_reduce_fusion.1 = (f32[10,4,16]{2,1,0:T(4,128)S(1)}, f32[10,4,16]{2,1,0:T(4,128)S(1)}) fusion(f32[38,4,16,128]{3,2,1,0:T(8,128)} %get-tuple-element.7.post_ref), kind=kLoop, calls=%fused_computation.6 | loop fusion | bytes 10240 | tf_op jit(solution)/shard_map/slice | solution.py:309
  30.9 2.1 %collective-permute-start.5 = (f32[20,4,16]{2,1,0:T(4,128)S(1)}, f32[20,4,16]{2,1,0:T(4,128)S(1)}, u32[]{:S(2)}, u32[]{:S(2)}) collective-permute-start(f32[20,4,16]{2,1,0:T(4,128)S(1)} %pad_maximum_fusion.2), channel_id=1, source_target_pairs={{0,1},{1,0},{2,3},{3,2},{4,5},{5,4},{6,7},{7,6},{8,9},{9,8},{10,11... | collective-permute-start | bytes 15368 | tf_op jit(solution)/shard_map/ppermute | solution.py:234
  33.0 4.7 %collective-permute-done.5 = f32[20,4,16]{2,1,0:T(4,128)S(1)} collective-permute-done((f32[20,4,16]{2,1,0:T(4,128)S(1)}, f32[20,4,16]{2,1,0:T(4,128)S(1)}, u32[]{:S(2)}, u32[]{:S(2)}) %collective-permute-start.5) | collective-permute-done | bytes 5152 | tf_op jit(solution)/shard_map/ppermute | solution.py:234
  37.7 0.6 gather_fusion.3
  38.3 0.1 fusion.9
  38.4 0.2 slice_reduce_fusion.6
  38.6 0.2 slice_reduce_fusion.4
  38.9 0.0 copy-start.12
  38.9 0.9 %pad_maximum_fusion.1 = f32[208,128]{1,0:T(8,128)S(1)} fusion(f32[4,128]{1,0:T(4,128)S(1)} %select_maximum_fusion, f32[160,128]{1,0:T(8,128)} %bitcast.103, f32[4,128]{1,0:T(4,128)S(1)} %select_maximum_fusion.3, f32[40,128]{1,0:T(8,128)} %bitcast.115), kind=kLoop, calls=%fused_computation.14 | loop fusion | flops 79872 | bytes 212992 | tf_op jit(solution)/shard_map/concatenate | solution.py:330
  39.8 0.1 collective-permute-start.8
  39.9 0.1 slice_reduce_fusion.8
  40.1 0.2 slice_reduce_fusion.10
  40.3 2.7 %collective-permute-start.6 = (f32[208,128]{1,0:T(8,128)S(1)}, f32[208,128]{1,0:T(8,128)S(1)}, u32[]{:S(2)}, u32[]{:S(2)}) collective-permute-start(f32[208,128]{1,0:T(8,128)S(1)} %pad_maximum_fusion), channel_id=1, source_target_pairs={{0,6},{1,7},{2,0},{3,1},{4,2},{5,3},{6,4},{7,5},{8,14},{9,15},{10,... | collective-permute-start | bytes 319496 | tf_op jit(solution)/shard_map/ppermute | solution.py:234
  43.1 1.6 %collective-permute-done.8.hym_ref = f32[208,128]{1,0:T(8,128)S(1)} collective-permute-done((f32[208,128]{1,0:T(8,128)S(1)}, f32[208,128]{1,0:T(8,128)S(1)}, u32[]{:S(2)}, u32[]{:S(2)}) %collective-permute-start.8) | collective-permute-done | bytes 106528 | tf_op jit(solution)/shard_map/ppermute | solution.py:234
  44.7 0.1 maximum_maximum_fusion
  44.8 0.1 constant_dynamic-slice_fusion
  44.9 0.6 gather_fusion.2
  45.4 0.2 copy.49
  45.7 0.6 gather_fusion.1
  46.2 0.1 copy.46
  46.4 0.1 pad_maximum_fusion.14
  46.5 0.1 constant_dynamic-slice_fusion.1
  46.6 0.6 gather_fusion
  47.1 0.6 gather_fusion.4
  47.7 0.2 copy.51
  47.9 0.1 copy.44
  48.1 0.2 maximum_select_fusion.4
  48.2 0.0 copy-start.10
  48.4 0.0 copy-start.8
  48.4 0.0 copy-start.9
  48.5 0.1 fusion.2
  48.6 0.1 fusion.6
  48.7 0.1 fusion.7
  48.8 0.1 copy-done.10
  48.9 0.0 copy-done.11
  48.9 0.2 maximum_select_fusion.2
  49.1 1.2 %collective-permute-start.7 = (f32[160,128]{1,0:T(8,128)S(1)}, f32[160,128]{1,0:T(8,128)S(1)}, u32[]{:S(2)}, u32[]{:S(2)}) collective-permute-start(f32[160,128]{1,0:T(8,128)S(1)} %bitcast.109), channel_id=1, source_target_pairs={{0,14},{1,15},{2,8},{3,9},{4,10},{5,11},{6,12},{7,13},{8,22},{9,23... | collective-permute-start | bytes 245768 | tf_op jit(solution)/shard_map/ppermute | solution.py:234
  50.3 0.6 collective-permute-start.9
  50.9 0.1 select_select_fusion
  51.0 2.0 %collective-permute-done.7 = f32[160,128]{1,0:T(8,128)S(1)} collective-permute-done((f32[160,128]{1,0:T(8,128)S(1)}, f32[160,128]{1,0:T(8,128)S(1)}, u32[]{:S(2)}, u32[]{:S(2)}) %collective-permute-start.7) | collective-permute-done | bytes 81952 | tf_op jit(solution)/shard_map/ppermute | solution.py:234
  53.0 7.1 %collective-permute-done.9 = f32[160,128]{1,0:T(8,128)S(1)} collective-permute-done((f32[160,128]{1,0:T(8,128)S(1)}, f32[160,128]{1,0:T(8,128)S(1)}, u32[]{:S(2)}, u32[]{:S(2)}) %collective-permute-start.9) | collective-permute-done | bytes 81952 | tf_op jit(solution)/shard_map/ppermute | solution.py:234
  60.2 1.1 %broadcast_in_dim.125.col_ref = f32[20,4,16,128]{3,2,1,0:T(8,128)} broadcast(f32[20,4,16]{2,1,0:T(4,128)S(1)} %select_select_fusion), dimensions={0,1,2} | broadcast | bytes 660480 | tf_op jit(solution)/shard_map/broadcast_in_dim | solution.py:402
  61.3 2.8 %shard_map.150 = (f32[19,4,16,128]{3,2,1,0:T(8,128)}, f32[19,4,16,128]{3,2,1,0:T(8,128)}) custom-call(f32[38,4,16,128]{3,2,1,0:T(8,128)} %get-tuple-element.7.post_ref, f32[10,16,128]{2,1,0:T(8,128)} %bitcast.106, f32[10,16,128]{2,1,0:T(8,128)} %bitcast.107, f32[208,128]{1,0:T(8,128)} %copy-done, f32[208,128]{1,0:T(8,128)} %copy-done.1, ...), custom_call_target="tpu_custom_call" | custom-call | tf_op jit(solution)/shard_map/pallas_call | solution.py:404
  (76 shorter events, 0.5 us)
Async XLA Ops:
  0.6 9.2 %copy-start.19 = (s32[10]{0:T(128)S(1)}, s32[10]{0:T(128)}, u32[]{:S(2)}) copy-start(s32[10]{0:T(128)} %constant.123) | copy-start | bytes 124
  0.6 9.2 %copy-start.18 = (s32[20]{0:T(128)S(1)}, s32[20]{0:T(128)}, u32[]{:S(2)}) copy-start(s32[20]{0:T(128)} %constant.125) | copy-start | bytes 244
  0.7 9.2 %copy-start.17 = (s32[20]{0:T(128)S(1)}, s32[20]{0:T(128)}, u32[]{:S(2)}) copy-start(s32[20]{0:T(128)} %constant.126) | copy-start | bytes 244
  2.0 7.9 %collective-permute-start.4 = (f32[2,4,16]{2,1,0:T(4,128)S(1)}, f32[2,4,16]{2,1,0:T(4,128)S(1)}, u32[]{:S(2)}, u32[]{:S(2)}) collective-permute-start(f32[2,4,16]{2,1,0:T(4,128)S(1)} %pad_maximum_fusion.13), channel_id=1, source_target_pairs={{0,1},{1,0},{2,3},{3,2},{4,5},{5,4},{6,7},{7,6},{8,9},{9,8},{10,11... | collective-permute-start | bytes 1544 | tf_op jit(solution)/shard_map/ppermute | solution.py:234
  6.3 9.8 %collective-permute-start.2 = (f32[20,128]{1,0:T(8,128)S(1)}, f32[20,128]{1,0:T(8,128)S(1)}, u32[]{:S(2)}, u32[]{:S(2)}) collective-permute-start(f32[20,128]{1,0:T(8,128)S(1)} %pad_maximum_fusion.12), channel_id=1, source_target_pairs={{0,2},{1,3},{2,4},{3,5},{4,6},{5,7},{6,0},{7,1},{8,10},{9,11},{10,... | collective-permute-start | bytes 30728 | tf_op jit(solution)/shard_map/ppermute | solution.py:234
  7.6 2.5 %collective-permute-start = (f32[20,128]{1,0:T(8,128)S(1)}, f32[20,128]{1,0:T(8,128)S(1)}, u32[]{:S(2)}, u32[]{:S(2)}) collective-permute-start(f32[20,128]{1,0:T(8,128)S(1)} %pad_maximum_fusion.11), channel_id=1, source_target_pairs={{0,6},{1,7},{2,0},{3,1},{4,2},{5,3},{6,4},{7,5},{8,14},{9,15},{10,... | collective-permute-start | bytes 30728 | tf_op jit(solution)/shard_map/ppermute | solution.py:234
  10.1 6.8 %collective-permute-start.1 = (f32[32,128]{1,0:T(8,128)S(1)}, f32[32,128]{1,0:T(8,128)S(1)}, u32[]{:S(2)}, u32[]{:S(2)}) collective-permute-start(f32[32,128]{1,0:T(8,128)S(1)} %pad_maximum_fusion.9), channel_id=1, source_target_pairs={{0,14},{1,15},{2,8},{3,9},{4,10},{5,11},{6,12},{7,13},{8,22},{9,23... | collective-permute-start | bytes 49160 | tf_op jit(solution)/shard_map/ppermute | solution.py:234
  16.1 9.3 %collective-permute-start.3 = (f32[32,128]{1,0:T(8,128)S(1)}, f32[32,128]{1,0:T(8,128)S(1)}, u32[]{:S(2)}, u32[]{:S(2)}) collective-permute-start(f32[32,128]{1,0:T(8,128)S(1)} %pad_maximum_fusion.10), channel_id=1, source_target_pairs={{0,250},{1,251},{2,252},{3,253},{4,254},{5,255},{6,248},{7,249},{8... | collective-permute-start | bytes 49160 | tf_op jit(solution)/shard_map/ppermute | solution.py:234
  25.5 7.5 %copy-start.16 = (s32[20]{0:T(128)S(1)}, s32[20]{0:T(128)}, u32[]{:S(2)}) copy-start(s32[20]{0:T(128)} %constant.127) | copy-start | bytes 244
  25.6 0.7 %copy-start.4 = (f32[5,4,16,128]{3,2,1,0:T(8,128)}, f32[5,4,16,128]{3,2,1,0:T(8,128)S(1)}, u32[]{:S(2)}) copy-start(f32[5,4,16,128]{3,2,1,0:T(8,128)S(1)} %multiply_dynamic-update-slice_fusion.nb_ref) | copy-start | bytes 491524
  29.3 11.0 %copy-start.2 = (f32[10,16,128]{2,1,0:T(8,128)S(1)}, f32[10,16,128]{2,1,0:T(8,128)}, u32[]{:S(2)}) copy-start(f32[10,16,128]{2,1,0:T(8,128)} %get-tuple-element.9) | copy-start | bytes 245764
  29.3 11.0 %copy-start.7 = (f32[10,4,128]{2,1,0:T(4,128)S(1)}, f32[10,4,128]{2,1,0:T(4,128)}, u32[]{:S(2)}) copy-start(f32[10,4,128]{2,1,0:T(4,128)} %get-tuple-element.8) | copy-start | bytes 61444
  29.3 18.8 %copy-start.14 = (pred[20]{0:T(512)(128)(4,1)S(1)}, pred[20]{0:T(512)(128)(4,1)}, u32[]{:S(2)}) copy-start(pred[20]{0:T(512)(128)(4,1)} %constant.117) | copy-start | bytes 64
  29.3 18.8 %copy-start.15 = (pred[20]{0:T(512)(128)(4,1)S(1)}, pred[20]{0:T(512)(128)(4,1)}, u32[]{:S(2)}) copy-start(pred[20]{0:T(512)(128)(4,1)} %constant.108) | copy-start | bytes 64
  30.9 17.5 %copy-start.3 = (f32[10,16,128]{2,1,0:T(8,128)S(1)}, f32[10,16,128]{2,1,0:T(8,128)}, u32[]{:S(2)}) copy-start(f32[10,16,128]{2,1,0:T(8,128)} %get-tuple-element.11) | copy-start | bytes 245764
  30.9 6.8 %collective-permute-start.5 = (f32[20,4,16]{2,1,0:T(4,128)S(1)}, f32[20,4,16]{2,1,0:T(4,128)S(1)}, u32[]{:S(2)}, u32[]{:S(2)}) collective-permute-start(f32[20,4,16]{2,1,0:T(4,128)S(1)} %pad_maximum_fusion.2), channel_id=1, source_target_pairs={{0,1},{1,0},{2,3},{3,2},{4,5},{5,4},{6,7},{7,6},{8,9},{9,8},{10,11... | collective-permute-start | bytes 15368 | tf_op jit(solution)/shard_map/ppermute | solution.py:234
  38.9 9.5 %copy-start.12 = (pred[10]{0:T(512)(128)(4,1)S(1)}, pred[10]{0:T(512)(128)(4,1)}, u32[]{:S(2)}) copy-start(pred[10]{0:T(512)(128)(4,1)} %constant.101) | copy-start | bytes 34
  38.9 9.5 %copy-start.13 = (pred[10]{0:T(512)(128)(4,1)S(1)}, pred[10]{0:T(512)(128)(4,1)}, u32[]{:S(2)}) copy-start(pred[10]{0:T(512)(128)(4,1)} %constant.100) | copy-start | bytes 34
  39.8 4.8 %collective-permute-start.8 = (f32[208,128]{1,0:T(8,128)S(1)}, f32[208,128]{1,0:T(8,128)S(1)}, u32[]{:S(2)}, u32[]{:S(2)}) collective-permute-start(f32[208,128]{1,0:T(8,128)S(1)} %pad_maximum_fusion.1), channel_id=1, source_target_pairs={{0,2},{1,3},{2,4},{3,5},{4,6},{5,7},{6,0},{7,1},{8,10},{9,11},{10,... | collective-permute-start | bytes 319496 | tf_op jit(solution)/shard_map/ppermute | solution.py:234
  40.3 6.1 %collective-permute-start.6 = (f32[208,128]{1,0:T(8,128)S(1)}, f32[208,128]{1,0:T(8,128)S(1)}, u32[]{:S(2)}, u32[]{:S(2)}) collective-permute-start(f32[208,128]{1,0:T(8,128)S(1)} %pad_maximum_fusion), channel_id=1, source_target_pairs={{0,6},{1,7},{2,0},{3,1},{4,2},{5,3},{6,4},{7,5},{8,14},{9,15},{10,... | collective-permute-start | bytes 319496 | tf_op jit(solution)/shard_map/ppermute | solution.py:234
  44.7 3.9 %copy-start = (f32[208,128]{1,0:T(8,128)}, f32[208,128]{1,0:T(8,128)S(1)}, u32[]{:S(2)}) copy-start(f32[208,128]{1,0:T(8,128)S(1)} %collective-permute-done.8.hym_ref) | copy-start | bytes 319492
  46.4 2.3 %copy-start.1 = (f32[208,128]{1,0:T(8,128)}, f32[208,128]{1,0:T(8,128)S(1)}, u32[]{:S(2)}) copy-start(f32[208,128]{1,0:T(8,128)S(1)} %collective-permute-done.6.hyp_ref) | copy-start | bytes 319492
  48.2 0.7 %copy-start.10 = (pred[10]{0:T(512)(128)(4,1)S(1)}, pred[10]{0:T(512)(128)(4,1)}, u32[]{:S(2)}) copy-start(pred[10]{0:T(512)(128)(4,1)} %constant.102) | copy-start | bytes 34
  48.3 0.7 %copy-start.11 = (pred[10]{0:T(512)(128)(4,1)S(1)}, pred[10]{0:T(512)(128)(4,1)}, u32[]{:S(2)}) copy-start(pred[10]{0:T(512)(128)(4,1)} %constant.95) | copy-start | bytes 34
  48.4 2.5 %copy-start.8 = (pred[20]{0:T(512)(128)(4,1)S(1)}, pred[20]{0:T(512)(128)(4,1)}, u32[]{:S(2)}) copy-start(pred[20]{0:T(512)(128)(4,1)} %constant.122) | copy-start | bytes 64
  48.4 2.5 %copy-start.9 = (pred[20]{0:T(512)(128)(4,1)S(1)}, pred[20]{0:T(512)(128)(4,1)}, u32[]{:S(2)}) copy-start(pred[20]{0:T(512)(128)(4,1)} %constant.107) | copy-start | bytes 64
  49.1 3.9 %collective-permute-start.7 = (f32[160,128]{1,0:T(8,128)S(1)}, f32[160,128]{1,0:T(8,128)S(1)}, u32[]{:S(2)}, u32[]{:S(2)}) collective-permute-start(f32[160,128]{1,0:T(8,128)S(1)} %bitcast.109), channel_id=1, source_target_pairs={{0,14},{1,15},{2,8},{3,9},{4,10},{5,11},{6,12},{7,13},{8,22},{9,23... | collective-permute-start | bytes 245768 | tf_op jit(solution)/shard_map/ppermute | solution.py:234
  50.3 9.9 %collective-permute-start.9 = (f32[160,128]{1,0:T(8,128)S(1)}, f32[160,128]{1,0:T(8,128)S(1)}, u32[]{:S(2)}, u32[]{:S(2)}) collective-permute-start(f32[160,128]{1,0:T(8,128)S(1)} %bitcast.108), channel_id=1, source_target_pairs={{0,250},{1,251},{2,252},{3,253},{4,254},{5,255},{6,248},{7,249},{8... | collective-permute-start | bytes 245768 | tf_op jit(solution)/shard_map/ppermute | solution.py:234
  53.0 8.2 %copy-start.5 = (f32[160,128]{1,0:T(8,128)}, f32[160,128]{1,0:T(8,128)S(1)}, u32[]{:S(2)}) copy-start(f32[160,128]{1,0:T(8,128)S(1)} %collective-permute-done.7) | copy-start | bytes 245764
  60.2 1.1 %copy-start.6 = (f32[160,128]{1,0:T(8,128)}, f32[160,128]{1,0:T(8,128)S(1)}, u32[]{:S(2)}) copy-start(f32[160,128]{1,0:T(8,128)S(1)} %collective-permute-done.9) | copy-start | bytes 245764
